TPU v7x, 32 devices: a whole 2x2x4 slice. The times are simulated.
32 devices in a mesh: seq: 8 (over y, x, core), head: 4 (over z).
Axes of the slice: x: 2, y: 2, z: 4, core: 2. Of those that a mesh axis runs over, the one named last changes fastest.
Arguments:
- tokens: bfloat16 [16384, 768], P(('seq', 'head')), may hold values from -16 to 16
- w_qkv: bfloat16 [768, 3, 768], replicated, may hold values from -0.21875 to 0.21875
- w_out: bfloat16 [768, 768], replicated, may hold values from -0.21875 to 0.21875
- neighbours: int32 [128, 12], P('seq'), may hold values from 0 to 127, as said below
- near_count: int32 [128], P('seq'), may hold values from 1 to 12
- anchors: int32 [128, 8], P('seq'), may hold values from 0 to 112, as said below
Outputs:
- mixed_out: bfloat16 [16384, 768], P(('seq', 'head'))
Inputs may be any that keep to these rules, and one draw needn't show every extreme that they name: `neighbours`: entry 0 of row b is b itself; the entries of a row are distinct and lie within 32 blocks of b. `anchors`: every entry is a multiple of 16; the entries of a row are distinct.
All inputs are finite; a program needn't handle non-finite values.
Results may differ from a plain program's by a relative error of at most 0.006.
The roundings to bfloat16 on the way count: a program that leaves them out, or rounds other values in their place, can miss the bound.
Values may be sent and summed in bfloat16 or wider, within the bound.
No kernel may reach another device: no remote copies, remote signals or barrier semaphores. Data moves between devices by JAX's collectives and lax.ppermute only.
A program may use at most 128 MiB of HBM per device.

v0:
```python
import functools

import jax
import jax.numpy as jnp
from jax import lax
from jax.experimental import pallas as pl
from jax.experimental.pallas import tpu as pltpu
from jax.sharding import PartitionSpec as P

D = 768
HDIM = 64
BLK = 128


def shifted(x, axis, by):
    size = lax.axis_size(axis)
    pairs = [(i, i + by) for i in range(size) if 0 <= i + by < size]
    return lax.ppermute(x, axis, pairs)


def gather_all(x, axis):
    size = lax.axis_size(axis)
    rank = lax.axis_index(axis)
    held = x[None]
    step = 1
    while step < size:
        pairs = [(i, (i + step) % size) for i in range(size)]
        got = lax.ppermute(held, axis, pairs)
        held = jnp.concatenate([got, held], axis=0)
        step *= 2
    return held


def attention_kernel(count, from_anchor, rows, q_ref, win_ref, anc_ref, o_ref,
                     kv_ref, sc_ref, m_ref, l_ref, acc_ref, *, heads, group, groups, scale):
    b = pl.program_id(0)
    width = heads * HDIM
    used = count[b]
    span = group * BLK

    @pl.when(b == 0)
    def _():
        kv_ref[...] = jnp.zeros_like(kv_ref)

    def fetch(j, carry):
        dst = pl.ds(pl.multiple_of(j * BLK, BLK), BLK)
        row = rows[b, j]

        @pl.when(from_anchor[b, j] == 0)
        def _():
            kv_ref[dst, :] = win_ref[row]

        @pl.when(from_anchor[b, j] != 0)
        def _():
            kv_ref[dst, :] = anc_ref[row]

        return carry

    lax.fori_loop(0, used, fetch, 0)
    limit = used * BLK
    for h in range(heads):
        qcols = slice(h * HDIM, (h + 1) * HDIM)
        kcols = slice(h * HDIM, (h + 1) * HDIM)
        vcols = slice(width + h * HDIM, width + (h + 1) * HDIM)
        qh = q_ref[0, :, qcols]

        def scores_of(c):
            k = kv_ref[c * span:(c + 1) * span, kcols]
            s = lax.dot_general(qh, k, (((1,), (1,)), ((), ())),
                                preferred_element_type=jnp.float32)
            col = c * span + lax.broadcasted_iota(jnp.int32, s.shape, 1)
            return jnp.where(col < limit, s, -jnp.inf)

        first = scores_of(0)
        sc_ref[:, 0:span] = first
        m_ref[...] = first
        for c in range(1, groups):
            @pl.when(c * group < used)
            def _():
                s = scores_of(c)
                sc_ref[:, c * span:(c + 1) * span] = s
                m_ref[...] = jnp.maximum(m_ref[...], s)

        peak = jnp.max(m_ref[...], axis=-1, keepdims=True)
        l_ref[...] = jnp.zeros_like(l_ref)
        acc_ref[...] = jnp.zeros_like(acc_ref)
        for c in range(groups):
            @pl.when(c * group < used)
            def _():
                e = jnp.exp((sc_ref[:, c * span:(c + 1) * span] - peak) * scale)
                l_ref[...] += e
                v = kv_ref[c * span:(c + 1) * span, vcols]
                acc_ref[...] += jnp.dot(e.astype(jnp.bfloat16), v,
                                        preferred_element_type=jnp.float32)

        totals = jnp.sum(l_ref[...], axis=-1, keepdims=True)
        o_ref[0, :, qcols] = (acc_ref[...] / totals).astype(o_ref.dtype)


def attention(queries, window, anchor_table, count, from_anchor, rows):
    block_count, _, width = queries.shape
    heads = width // HDIM
    slots = rows.shape[1]
    group = 4
    groups = -(-slots // group)
    kernel = functools.partial(attention_kernel, heads=heads, group=group, groups=groups,
                               scale=HDIM ** (-0.5))
    whole = pl.BlockSpec(memory_space=pltpu.VMEM)
    return pl.pallas_call(
        kernel,
        out_shape=jax.ShapeDtypeStruct(queries.shape, jnp.bfloat16),
        grid_spec=pltpu.PrefetchScalarGridSpec(
            num_scalar_prefetch=3,
            grid=(block_count,),
            in_specs=[
                pl.BlockSpec((1, BLK, width), lambda b, *_: (b, 0, 0)),
                whole,
                whole,
            ],
            out_specs=pl.BlockSpec((1, BLK, width), lambda b, *_: (b, 0, 0)),
            scratch_shapes=[
                pltpu.VMEM((groups * group * BLK, 2 * width), jnp.bfloat16),
                pltpu.VMEM((BLK, groups * group * BLK), jnp.float32),
                pltpu.VMEM((BLK, group * BLK), jnp.float32),
                pltpu.VMEM((BLK, group * BLK), jnp.float32),
                pltpu.VMEM((BLK, HDIM), jnp.float32),
            ],
        ),
        compiler_params=pltpu.CompilerParams(vmem_limit_bytes=60 * 1024 * 1024),
    )(count, from_anchor, rows, queries, window, anchor_table)


def shards(tokens, w_qkv, w_out, neighbours, near_count, anchors):
    gathered = lax.all_gather(tokens, "head", axis=0, tiled=True)
    head_count = lax.axis_size("head")
    head_rank = lax.axis_index("head")
    width_here = D // head_count
    row_count = gathered.shape[0]
    block_count = row_count // BLK
    neigh = neighbours.shape[1]
    col_start = head_rank * width_here
    query_cols = lax.dynamic_slice_in_dim(w_qkv[:, 0], col_start, width_here, 1)
    key_cols = lax.dynamic_slice_in_dim(w_qkv[:, 1], col_start, width_here, 1)
    value_cols = lax.dynamic_slice_in_dim(w_qkv[:, 2], col_start, width_here, 1)
    own_weights = jnp.concatenate([query_cols, key_cols, value_cols], axis=1)
    projected = jnp.dot(gathered, own_weights, preferred_element_type=jnp.float32).astype(
        jnp.bfloat16
    )
    queries = projected[:, :width_here].reshape(block_count, BLK, width_here)
    keyval = projected[:, width_here:]
    seq_count = lax.axis_size("seq")
    seq_rank = lax.axis_index("seq")
    beside = {}
    for offset in (2, 1, -1, -2):
        beside[offset] = shifted(keyval, "seq", offset)
    window = jnp.concatenate([beside[2], beside[1], keyval, beside[-1], beside[-2]], axis=0)
    window = window.reshape(5 * block_count, BLK, 2 * width_here)
    anchor_table = gather_all(keyval[:BLK].reshape(BLK, 2 * width_here), "seq")
    held_count = anchor_table.shape[0]
    first_block = (seq_rank - 2) * block_count

    near_idx = jnp.clip(neighbours - first_block, 0, 5 * block_count - 1).astype(jnp.int32)
    owner = jnp.clip(anchors // block_count, 0, seq_count - 1)
    anch_idx = ((owner - seq_rank + held_count - 1) % seq_count).astype(jnp.int32)
    near_used = jnp.arange(neigh)[None, :] < near_count[:, None]
    repeated = jnp.any(
        (anchors[:, :, None] == neighbours[:, None, :]) & near_used[:, None, :], axis=2
    )
    valid = jnp.concatenate([near_used, jnp.logical_not(repeated)], axis=1)
    order = jnp.argsort(jnp.logical_not(valid).astype(jnp.int32), axis=1, stable=True)
    every_row = jnp.concatenate([near_idx, anch_idx], axis=1)
    rows = jnp.take_along_axis(every_row, order, axis=1).astype(jnp.int32)
    from_anchor = (order >= neigh).astype(jnp.int32)
    count = jnp.sum(valid.astype(jnp.int32), axis=1).astype(jnp.int32)

    attended = attention(queries, window, anchor_table, count, from_anchor, rows)
    attended = attended.reshape(row_count, width_here)
    mine = lax.all_to_all(attended, "head", 0, 1, tiled=True)
    mixed_out = jnp.dot(mine, w_out, preferred_element_type=jnp.float32).astype(jnp.bfloat16)
    return mixed_out


def solution(mesh):
    placed = (P(("seq", "head"), None), P(), P(), P("seq", None), P("seq"), P("seq", None))
    return jax.shard_map(
        shards, mesh=mesh, in_specs=placed, out_specs=P(("seq", "head"), None), check_vma=False
    )
```

profile of v0, /device:TPU:2, one launch (start us, length us, event | category | flops | bytes accessed | tf_op | source)
XLA Modules:
  0.0 353.5 jit_solution(3135312974796984329)
XLA Ops:
  6.5 0.7 all-gather.2.cloned.1.call-update
  7.3 0.8 copy.33
  8.0 1.4 copy.38
  9.4 0.7 iota_compare_fusion
  10.1 0.7 and_reduce_fusion
  10.8 0.8 sort.17
  11.6 0.1 copy.34
  11.7 2.2 fusion.12
  13.9 0.9 dynamic-slice_bitcast_fusion.2
  14.8 1.2 dynamic-slice_bitcast_fusion
  16.0 0.6 bitcast_or_fusion
  16.6 57.1 %all-gather.2.cloned.1.call-done = bf16[2048,768]{1,0:T(8,128)(2,1)} async-done(((bf16[512,768]{1,0:T(8,128)(2,1)}), bf16[2048,768]{1,0:T(8,128)(2,1)}) %all-gather.2.cloned.1.call-update) | async-done | bytes 3145744 | tf_op jit(solution)/shard_map/all_gather | solution.py:134
  73.7 4.8 %convolution_convert_fusion = bf16[576,2048]{1,0:T(8,128)(2,1)S(1)} fusion(bf16[2048,768]{1,0:T(8,128)(2,1)} %all-gather.2.cloned.1.call-done, bf16[768,192]{1,0:T(8,128)(2,1)} %get-tuple-element.10, bf16[768,192]{1,0:T(8,128)(2,1)} %get-tuple-element.11, bf16[768,192]{1,0:T(8,128)(2,1)} %dynamic-slice_bitcast_fusion.2), kind=kOutput, calls=%fused_computation.1 | convolution fusion | flops 1815773184 | bytes 6389760 | tf_op jit(solution)/shard_map/dot_general | solution.py:146
  78.5 2.6 copy.42
  81.1 2.4 slice.28
  83.5 3.4 collective-permute-start
  86.8 1.9 collective-permute-start.1
  88.8 1.0 slice_bitcast_fusion
  89.8 1.6 collective-permute-start.4
  91.5 47.9 %collective-permute-done.4 = bf16[1,128,384]{2,1,0:T(8,128)(2,1)S(1)} collective-permute-done((bf16[1,128,384]{2,1,0:T(8,128)(2,1)S(1)}, bf16[1,128,384]{2,1,0:T(8,128)(2,1)S(1)}, u32[]{:S(2)}, u32[]{:S(2)}) %collective-permute-start.4) | collective-permute-done | bytes 98336 | tf_op jit(solution)/shard_map/ppermute | solution.py:28
  139.4 2.4 collective-permute-start.5
  141.8 0.1 reshape.44
  141.9 0.1 pad_add_fusion.1
  142.0 2.5 gather_fusion
  144.5 0.1 reshape.47
  144.6 0.6 convert_reduce_fusion.count
  145.2 1.9 collective-permute-start.2
  147.1 0.0 collective-permute-done.5
  147.1 0.1 pad_maximum_fusion.1
  147.2 0.1 collective-permute-start.6
  147.3 0.6 and_select_fusion.rows
  147.9 3.7 %collective-permute-start.3 = (bf16[2048,384]{1,0:T(8,128)(2,1)S(1)}, bf16[2048,384]{1,0:T(8,128)(2,1)S(1)}, u32[]{:S(2)}, u32[]{:S(2)}) collective-permute-start(bf16[2048,384]{1,0:T(8,128)(2,1)S(1)} %slice.28), channel_id=1, source_target_pairs={{8,0},{12,4},{16,8},{20,12},{24,16},{28,20},{9,1},{13,5},{17,9},{2... | collective-permute-start | bytes 4718600 | tf_op jit(solution)/shard_map/ppermute | solution.py:18
  151.6 0.6 compare_convert_fusion.from_anchor
  152.2 2.3 slice.27
  154.4 53.8 %collective-permute-done.6 = bf16[4,128,384]{2,1,0:T(8,128)(2,1)S(1)} collective-permute-done((bf16[4,128,384]{2,1,0:T(8,128)(2,1)S(1)}, bf16[4,128,384]{2,1,0:T(8,128)(2,1)S(1)}, u32[]{:S(2)}, u32[]{:S(2)}) %collective-permute-start.6) | collective-permute-done | bytes 393248 | tf_op jit(solution)/shard_map/ppermute | solution.py:28
  208.2 1.0 pad_maximum_fusion.anc_ref
  209.2 0.0 collective-permute-done
  209.2 2.7 constant_dynamic-update-slice_fusion.4
  212.0 0.0 collective-permute-done.1
  212.0 2.9 constant_dynamic-update-slice_fusion.3
  214.8 1.9 constant_dynamic-update-slice_fusion.2
  216.7 1.3 constant_dynamic-update-slice_fusion.1
  218.0 0.0 collective-permute-done.3
  218.0 1.3 constant_dynamic-update-slice_fusion
  219.3 105.4 %shard_map.64 = bf16[16,128,192]{2,1,0:T(8,128)(2,1)} custom-call(s32[16]{0:T(128)} %convert_reduce_fusion.count, s32[16,20]{1,0:T(8,128)} %compare_convert_fusion.from_anchor, s32[16,20]{1,0:T(8,128)} %and_select_fusion.rows, bf16[16,128,192]{2,1,0:T(8,128)(2,1)} %bitcast.27, bf16[80,128,384]{2,1,0:T(8,128)(2,1)} %bitcast.6.win_ref, ...), custom_call_target="tpu_custom_call" | custom-call | tf_op jit(solution)/shard_map/pallas_call | solution.py:109
  324.7 1.5 copy.43
  326.2 18.8 %all_to_all.19 = bf16[4,512,192]{1,2,0:T(8,128)(2,1)S(1)} all-to-all(bf16[4,512,192]{1,2,0:T(8,128)(2,1)S(1)} %copy.43), channel_id=1, replica_groups=mesh['seq'=8,'head'=4] {'head'}, dimensions={0} | all-to-all | bytes 1572864 | tf_op jit(solution)/shard_map/all_to_all | solution.py:178
  345.0 1.7 convolution_convert_fusion.1
  (18 shorter events, 0.1 us)
Async XLA Ops:
  6.5 338.4 %copy-start = (bf16[768,768]{1,0:T(8,128)(2,1)S(1)}, bf16[768,768]{1,0:T(8,128)(2,1)}, u32[]{:S(2)}) copy-start(bf16[768,768]{1,0:T(8,128)(2,1)} %param.8) | copy-start | bytes 3538948
  6.5 67.2 %all-gather.2.cloned.1.call-start = ((), (), s32[]{:S(2)}) async-start(), calls=%async_computation.1 | async-start | bytes 3932160 | tf_op jit(solution)/shard_map/all_gather | solution.py:134
  81.1 10.4 %copy-start.4 = (s32[16,8]{1,0:T(8,128)S(1)}, s32[16,8]{1,0:T(8,128)}, u32[]{:S(2)}) copy-start(s32[16,8]{1,0:T(8,128)} %copy.38) | copy-start | bytes 1540
  81.1 60.7 %copy-start.3 = (s32[16,12]{1,0:T(8,128)S(1)}, s32[16,12]{1,0:T(8,128)}, u32[]{:S(2)}) copy-start(s32[16,12]{1,0:T(8,128)} %param.9) | copy-start | bytes 2308
  81.1 60.7 %copy-start.2 = (s32[16,20,1]{1,0,2:T(8,128)S(1)}, s32[16,20,1]{1,0,2:T(8,128)}, u32[]{:S(2)}) copy-start(s32[16,20,1]{1,0,2:T(8,128)} %bitcast_or_fusion) | copy-start | bytes 3844
  83.5 125.8 %collective-permute-start = (bf16[2048,384]{1,0:T(8,128)(2,1)S(1)}, bf16[2048,384]{1,0:T(8,128)(2,1)}, u32[]{:S(2)}, u32[]{:S(2)}) collective-permute-start(bf16[2048,384]{1,0:T(8,128)(2,1)S(1)} %slice.28), channel_id=1, source_target_pairs={{0,8},{4,12},{8,16},{12,20},{16,24},{20,28},{1,9},{5,13},{9,17},{1... | collective-permute-start | bytes 4718600 | tf_op jit(solution)/shard_map/ppermute | solution.py:18
  86.8 125.1 %collective-permute-start.1 = (bf16[2048,384]{1,0:T(8,128)(2,1)S(1)}, bf16[2048,384]{1,0:T(8,128)(2,1)}, u32[]{:S(2)}, u32[]{:S(2)}) collective-permute-start(bf16[2048,384]{1,0:T(8,128)(2,1)S(1)} %slice.28), channel_id=1, source_target_pairs={{0,4},{4,8},{8,12},{12,16},{16,20},{20,24},{24,28},{1,5},{5,9},{9,... | collective-permute-start | bytes 4718600 | tf_op jit(solution)/shard_map/ppermute | solution.py:18
  89.8 49.6 %collective-permute-start.4 = (bf16[1,128,384]{2,1,0:T(8,128)(2,1)S(1)}, bf16[1,128,384]{2,1,0:T(8,128)(2,1)S(1)}, u32[]{:S(2)}, u32[]{:S(2)}) collective-permute-start(bf16[1,128,384]{2,1,0:T(8,128)(2,1)S(1)} %slice_bitcast_fusion), channel_id=1, source_target_pairs={{0,4},{4,8},{8,12},{12,16},{16,20},{20,24},{24,28},{28,0},{1,5},{5... | collective-permute-start | bytes 294920 | tf_op jit(solution)/shard_map/ppermute | solution.py:28
  139.4 7.7 %collective-permute-start.5 = (bf16[2,128,384]{2,1,0:T(8,128)(2,1)S(1)}, bf16[2,128,384]{2,1,0:T(8,128)(2,1)S(1)}, u32[]{:S(2)}, u32[]{:S(2)}) collective-permute-start(bf16[2,128,384]{2,1,0:T(8,128)(2,1)S(1)} %pad_maximum_fusion.2), channel_id=1, source_target_pairs={{0,8},{4,12},{8,16},{12,20},{16,24},{20,28},{24,0},{28,4},{1,9},{5... | collective-permute-start | bytes 589832 | tf_op jit(solution)/shard_map/ppermute | solution.py:28
  145.2 71.5 %collective-permute-start.2 = (bf16[2048,384]{1,0:T(8,128)(2,1)S(1)}, bf16[2048,384]{1,0:T(8,128)(2,1)S(1)}, u32[]{:S(2)}, u32[]{:S(2)}) collective-permute-start(bf16[2048,384]{1,0:T(8,128)(2,1)S(1)} %slice.28), channel_id=1, source_target_pairs={{4,0},{8,4},{12,8},{16,12},{20,16},{24,20},{28,24},{5,1},{9,5},{13... | collective-permute-start | bytes 4718600 | tf_op jit(solution)/shard_map/ppermute | solution.py:18
  147.2 61.0 %collective-permute-start.6 = (bf16[4,128,384]{2,1,0:T(8,128)(2,1)S(1)}, bf16[4,128,384]{2,1,0:T(8,128)(2,1)S(1)}, u32[]{:S(2)}, u32[]{:S(2)}) collective-permute-start(bf16[4,128,384]{2,1,0:T(8,128)(2,1)S(1)} %pad_maximum_fusion.1), channel_id=1, source_target_pairs={{0,16},{4,20},{8,24},{12,28},{16,0},{20,4},{24,8},{28,12},{1,17},{... | collective-permute-start | bytes 1179656 | tf_op jit(solution)/shard_map/ppermute | solution.py:28
  147.9 70.2 %collective-permute-start.3 = (bf16[2048,384]{1,0:T(8,128)(2,1)S(1)}, bf16[2048,384]{1,0:T(8,128)(2,1)S(1)}, u32[]{:S(2)}, u32[]{:S(2)}) collective-permute-start(bf16[2048,384]{1,0:T(8,128)(2,1)S(1)} %slice.28), channel_id=1, source_target_pairs={{8,0},{12,4},{16,8},{20,12},{24,16},{28,20},{9,1},{13,5},{17,9},{2... | collective-permute-start | bytes 4718600 | tf_op jit(solution)/shard_map/ppermute | solution.py:18
  212.0 2.9 copy-start.1
Sparse Core Ops, SparseCore 0:
  8.9 64.7 all-gather.1
where the time goes:
time: 356 us; the launch traced here: 354 us
  waiting for transfers between devices  159 us (45%)
  Pallas kernels  105 us (29%)
  local copies, waits for them, and re-layouts  29.1 us (8%)
  blocking collectives  18.8 us (5%)
  starting transfers between devices  15 us (4%)
  between operations  13.5 us (4%)
  matrix products  6.47 us (2%)
  other arithmetic  5.79 us (2%)
    pallas_call x1, Pallas kernels, attention(): pl.pallas_call(kernel, out_shape=jax.ShapeDtypeStruct(queries.shape, jnp....  105 us
    ppermute x3, waiting for transfers between devices, gather_all(): got = lax.ppermute(held, axis, pairs)  102 us
    all_gather x1, waiting for transfers between devices, shards(): gathered = lax.all_gather(tokens, 'head', axis=0, tiled=True)  57.1 us
    all_to_all x1, blocking collectives, shards(): mine = lax.all_to_all(attended, 'head', 0, 1, tiled=True)  18.8 us
    unnamed x16, local copies, waits for them, and re-layouts  10.9 us
    ppermute x4, starting transfers between devices, shifted(): return lax.ppermute(x, axis, pairs)  10.9 us
  transfers between devices with their start and end apart: 8, of which 3 were waited for; matrix products, arithmetic and copies ran while one was open for 8% of the time, Pallas kernels for 0%

commit v1 on v0

--- a/solution.py
+++ b/solution.py
@@ -31,45 +31,46 @@
     return held
 
 
-def attention_kernel(count, from_anchor, rows, q_ref, win_ref, anc_ref, o_ref,
-                     kv_ref, sc_ref, m_ref, l_ref, acc_ref, *, heads, group, groups, scale):
+def attention_kernel(count, from_anchor, rows, q_ref, kwin_ref, vwin_ref, kanc_ref, vanc_ref,
+                     o_ref, kt_ref, v_ref, sc_ref, m_ref, l_ref, acc_ref,
+                     *, heads, group, groups, scale):
     b = pl.program_id(0)
-    width = heads * HDIM
     used = count[b]
     span = group * BLK
 
     @pl.when(b == 0)
     def _():
-        kv_ref[...] = jnp.zeros_like(kv_ref)
+        kt_ref[...] = jnp.zeros_like(kt_ref)
+        v_ref[...] = jnp.zeros_like(v_ref)
 
     def fetch(j, carry):
-        dst = pl.ds(pl.multiple_of(j * BLK, BLK), BLK)
+        at = pl.multiple_of(j * BLK, BLK)
         row = rows[b, j]
 
         @pl.when(from_anchor[b, j] == 0)
         def _():
-            kv_ref[dst, :] = win_ref[row]
+            kt_ref[:, pl.ds(at, BLK)] = kwin_ref[row]
+            v_ref[pl.ds(at, BLK), :] = vwin_ref[row]
 
         @pl.when(from_anchor[b, j] != 0)
         def _():
-            kv_ref[dst, :] = anc_ref[row]
+            kt_ref[:, pl.ds(at, BLK)] = kanc_ref[row]
+            v_ref[pl.ds(at, BLK), :] = vanc_ref[row]
 
         return carry
 
     lax.fori_loop(0, used, fetch, 0)
     limit = used * BLK
+    lane = lax.broadcasted_iota(jnp.int32, (1, span), 1)
     for h in range(heads):
-        qcols = slice(h * HDIM, (h + 1) * HDIM)
-        kcols = slice(h * HDIM, (h + 1) * HDIM)
-        vcols = slice(width + h * HDIM, width + (h + 1) * HDIM)
-        qh = q_ref[0, :, qcols]
+        cols = slice(h * HDIM, (h + 1) * HDIM)
+        qh = (q_ref[0, :, cols].astype(jnp.float32) * scale).astype(jnp.bfloat16)
 
         def scores_of(c):
-            k = kv_ref[c * span:(c + 1) * span, kcols]
-            s = lax.dot_general(qh, k, (((1,), (1,)), ((), ())),
-                                preferred_element_type=jnp.float32)
-            col = c * span + lax.broadcasted_iota(jnp.int32, s.shape, 1)
-            return jnp.where(col < limit, s, -jnp.inf)
+            s = jnp.dot(qh, kt_ref[cols, c * span:(c + 1) * span],
+                        preferred_element_type=jnp.float32)
+            bias = jnp.where(lane < limit - c * span, 0.0, -jnp.inf)
+            return s + bias
 
         first = scores_of(0)
         sc_ref[:, 0:span] = first
@@ -87,17 +88,17 @@
         for c in range(groups):
             @pl.when(c * group < used)
             def _():
-                e = jnp.exp((sc_ref[:, c * span:(c + 1) * span] - peak) * scale)
+                e = jnp.exp(sc_ref[:, c * span:(c + 1) * span] - peak)
                 l_ref[...] += e
-                v = kv_ref[c * span:(c + 1) * span, vcols]
-                acc_ref[...] += jnp.dot(e.astype(jnp.bfloat16), v,
+                acc_ref[...] += jnp.dot(e.astype(jnp.bfloat16),
+                                        v_ref[c * span:(c + 1) * span, cols],
                                         preferred_element_type=jnp.float32)
 
         totals = jnp.sum(l_ref[...], axis=-1, keepdims=True)
-        o_ref[0, :, qcols] = (acc_ref[...] / totals).astype(o_ref.dtype)
-
-
-def attention(queries, window, anchor_table, count, from_anchor, rows):
+        o_ref[0, :, cols] = (acc_ref[...] / totals).astype(o_ref.dtype)
+
+
+def attention(queries, kwin, vwin, kanc, vanc, count, from_anchor, rows):
     block_count, _, width = queries.shape
     heads = width // HDIM
     slots = rows.shape[1]
@@ -106,6 +107,7 @@
     kernel = functools.partial(attention_kernel, heads=heads, group=group, groups=groups,
                                scale=HDIM ** (-0.5))
     whole = pl.BlockSpec(memory_space=pltpu.VMEM)
+    keys = groups * group * BLK
     return pl.pallas_call(
         kernel,
         out_shape=jax.ShapeDtypeStruct(queries.shape, jnp.bfloat16),
@@ -116,18 +118,21 @@
                 pl.BlockSpec((1, BLK, width), lambda b, *_: (b, 0, 0)),
                 whole,
                 whole,
+                whole,
+                whole,
             ],
             out_specs=pl.BlockSpec((1, BLK, width), lambda b, *_: (b, 0, 0)),
             scratch_shapes=[
-                pltpu.VMEM((groups * group * BLK, 2 * width), jnp.bfloat16),
-                pltpu.VMEM((BLK, groups * group * BLK), jnp.float32),
+                pltpu.VMEM((width, keys), jnp.bfloat16),
+                pltpu.VMEM((keys, width), jnp.bfloat16),
+                pltpu.VMEM((BLK, keys), jnp.float32),
                 pltpu.VMEM((BLK, group * BLK), jnp.float32),
                 pltpu.VMEM((BLK, group * BLK), jnp.float32),
                 pltpu.VMEM((BLK, HDIM), jnp.float32),
             ],
         ),
         compiler_params=pltpu.CompilerParams(vmem_limit_bytes=60 * 1024 * 1024),
-    )(count, from_anchor, rows, queries, window, anchor_table)
+    )(count, from_anchor, rows, queries, kwin, vwin, kanc, vanc)
 
 
 def shards(tokens, w_qkv, w_out, neighbours, near_count, anchors):
@@ -147,16 +152,25 @@
         jnp.bfloat16
     )
     queries = projected[:, :width_here].reshape(block_count, BLK, width_here)
-    keyval = projected[:, width_here:]
+    keys_t = jnp.transpose(
+        projected[:, width_here:2 * width_here].reshape(block_count, BLK, width_here), (0, 2, 1)
+    )
+    values = projected[:, 2 * width_here:].reshape(block_count, BLK, width_here)
     seq_count = lax.axis_size("seq")
     seq_rank = lax.axis_index("seq")
-    beside = {}
-    for offset in (2, 1, -1, -2):
-        beside[offset] = shifted(keyval, "seq", offset)
-    window = jnp.concatenate([beside[2], beside[1], keyval, beside[-1], beside[-2]], axis=0)
-    window = window.reshape(5 * block_count, BLK, 2 * width_here)
-    anchor_table = gather_all(keyval[:BLK].reshape(BLK, 2 * width_here), "seq")
-    held_count = anchor_table.shape[0]
+    kparts, vparts = [], []
+    for offset in (2, 1, 0, -1, -2):
+        if offset == 0:
+            kparts.append(keys_t)
+            vparts.append(values)
+        else:
+            kparts.append(shifted(keys_t, "seq", offset))
+            vparts.append(shifted(values, "seq", offset))
+    kwin = jnp.concatenate(kparts, axis=0)
+    vwin = jnp.concatenate(vparts, axis=0)
+    kanc = gather_all(keys_t[0], "seq")
+    vanc = gather_all(values[0], "seq")
+    held_count = kanc.shape[0]
     first_block = (seq_rank - 2) * block_count
 
     near_idx = jnp.clip(neighbours - first_block, 0, 5 * block_count - 1).astype(jnp.int32)
@@ -173,7 +187,7 @@
     from_anchor = (order >= neigh).astype(jnp.int32)
     count = jnp.sum(valid.astype(jnp.int32), axis=1).astype(jnp.int32)
 
-    attended = attention(queries, window, anchor_table, count, from_anchor, rows)
+    attended = attention(queries, kwin, vwin, kanc, vanc, count, from_anchor, rows)
     attended = attended.reshape(row_count, width_here)
     mine = lax.all_to_all(attended, "head", 0, 1, tiled=True)
     mixed_out = jnp.dot(mine, w_out, preferred_element_type=jnp.float32).astype(jnp.bfloat16)

time: 356 us -> 334 us (0.938)
  waiting for transfers between devices: 159 us -> 125 us
  local copies, waits for them, and re-layouts: 29.1 us -> 45.3 us
  Pallas kernels: 105 us -> 90 us
  starting transfers between devices: 15 us -> 25.1 us
    ppermute x3 -> x6, waiting for transfers between devices: 102 us -> 52.5 us  [gather_all(): got = lax.ppermute(held, axis, pairs)]
    pallas_call x1, Pallas kernels: 105 us -> 90 us  [attention(): pl.pallas_call(kernel, out_shape=jax.ShapeDtypeStruct(queries.shape, jnp....]
    ppermute x4 -> x8, waiting for transfers between devices: 0.01 us -> 12.1 us  [shifted(): return lax.ppermute(x, axis, pairs)]
    ppermute x4 -> x8, starting transfers between devices: 10.9 us -> 20.8 us  [shifted(): return lax.ppermute(x, axis, pairs)]
    ppermute x0 -> x4, local copies, waits for them, and re-layouts: none -> 8.18 us  [shifted(): return lax.ppermute(x, axis, pairs)]
    unnamed x16 -> x24, local copies, waits for them, and re-layouts: 10.9 us -> 14.9 us
  transfers between devices with their start and end apart: 8 -> 15, of which waited for: 3 -> 7; matrix products, arithmetic and copies ran while one was open for 8% -> 13% of each run, Pallas kernels for 0% -> 0%
where the time goes in v1:
time: 334 us; the launch traced here: 329 us
  waiting for transfers between devices  125 us (37%)
  Pallas kernels  90 us (27%)
  local copies, waits for them, and re-layouts  45.3 us (14%)
  starting transfers between devices  25.1 us (8%)
  blocking collectives  17.1 us (5%)
  between operations  13.6 us (4%)
  matrix products  7.57 us (2%)
  other arithmetic  5.85 us (2%)
    pallas_call x1, Pallas kernels, attention(): pl.pallas_call(kernel, out_shape=jax.ShapeDtypeStruct(queries.shape, jnp....  90 us
    all_gather x1, waiting for transfers between devices, shards(): gathered = lax.all_gather(tokens, 'head', axis=0, tiled=True)  59.7 us
    ppermute x6, waiting for transfers between devices, gather_all(): got = lax.ppermute(held, axis, pairs)  52.5 us
    ppermute x8, starting transfers between devices, shifted(): return lax.ppermute(x, axis, pairs)  20.8 us
    all_to_all x1, blocking collectives, shards(): mine = lax.all_to_all(attended, 'head', 0, 1, tiled=True)  17.1 us
    unnamed x24, local copies, waits for them, and re-layouts  14.9 us
    ppermute x8, waiting for transfers between devices, shifted(): return lax.ppermute(x, axis, pairs)  12.1 us
    ppermute x4, local copies, waits for them, and re-layouts, shifted(): return lax.ppermute(x, axis, pairs)  8.18 us
  transfers between devices with their start and end apart: 15, of which 7 were waited for; matrix products, arithmetic and copies ran while one was open for 13% of the time, Pallas kernels for 0%

profile of v1, /device:TPU:2, one launch (start us, length us, event | category | flops | bytes accessed | tf_op | source)
XLA Modules:
  0.0 329.5 jit_solution(4305433915139567965)
XLA Ops:
  7.3 0.8 copy.65
  10.2 0.8 sort.17
  11.2 2.2 fusion.12
  14.0 59.7 %all-gather.2.cloned.1.call-done = bf16[2048,768]{1,0:T(8,128)(2,1)} async-done(((bf16[512,768]{1,0:T(8,128)(2,1)}), bf16[2048,768]{1,0:T(8,128)(2,1)}) %all-gather.2.cloned.1.call-update) | async-done | bytes 3145744 | tf_op jit(solution)/shard_map/all_gather | solution.py:139
  73.7 5.9 %convolution_convert_fusion = bf16[576,2048]{1,0:T(8,128)(2,1)} fusion(bf16[2048,768]{1,0:T(8,128)(2,1)} %all-gather.2.cloned.1.call-done, bf16[768,192]{1,0:T(8,128)(2,1)S(1)} %get-tuple-element.13, bf16[768,192]{1,0:T(8,128)(2,1)S(1)} %get-tuple-element.14, bf16[768,192]{1,0:T(8,128)(2,1)S(1)} %dynamic-slice_bitcast_fusion.2), kind=kOutput, calls=%fused_computation.1 | convolution fusion | flops 1815773184 | bytes 6389760 | tf_op jit(solution)/shard_map/dot_general | solution.py:151
  79.6 4.4 %copy.74 = bf16[576,2048]{0,1:T(8,128)(2,1)} copy(bf16[576,2048]{1,0:T(8,128)(2,1)} %convolution_convert_fusion) | data formatting | bytes 4718592 | tf_op jit(solution)/shard_map/convert_element_type | solution.py:151
  83.9 0.8 slice_bitcast_fusion
  84.8 3.5 %fusion.13 = (bf16[2048,192]{1,0:T(8,128)(2,1)S(1)}, bf16[2048,192]{1,0:T(8,128)(2,1)S(1)}, bf16[2048,192]{1,0:T(8,128)(2,1)}) fusion(bf16[2048,576]{1,0:T(8,128)(2,1)} %bitcast.26), kind=kLoop, calls=%fused_computation.55 | loop fusion | bytes 4718592 | tf_op jit(solution)/shard_map/slice | solution.py:158
  88.3 1.3 copy.76
  89.6 3.4 %collective-permute-start.4 = (bf16[16,128,192]{1,2,0:T(8,128)(2,1)}, bf16[16,128,192]{1,2,0:T(8,128)(2,1)}, u32[]{:S(2)}, u32[]{:S(2)}) collective-permute-start(bf16[16,128,192]{1,2,0:T(8,128)(2,1)} %copy.76), channel_id=1, source_target_pairs={{0,8},{4,12},{8,16},{12,20},{16,24},{20,28},{1,9},{5,13},{9,17},{1... | collective-permute-start | bytes 2359304 | tf_op jit(solution)/shard_map/ppermute | solution.py:18
  93.0 3.2 collective-permute-start.5
  96.2 1.3 copy.75
  97.4 0.8 slice.42
  98.9 23.6 %collective-permute-done.8 = bf16[1,192,128]{2,1,0:T(8,128)(2,1)S(1)} collective-permute-done((bf16[1,192,128]{2,1,0:T(8,128)(2,1)S(1)}, bf16[1,192,128]{2,1,0:T(8,128)(2,1)S(1)}, u32[]{:S(2)}, u32[]{:S(2)}) %collective-permute-start.8) | collective-permute-done | bytes 49184 | tf_op jit(solution)/shard_map/ppermute | solution.py:28
  122.5 2.4 collective-permute-start.9
  125.0 2.1 collective-permute-done.9
  127.2 1.2 collective-permute-start.10
  128.4 1.9 collective-permute-start.6
  130.3 3.8 %collective-permute-done.13 = bf16[4,128,192]{2,1,0:T(8,128)(2,1)S(1)} collective-permute-done((bf16[4,128,192]{2,1,0:T(8,128)(2,1)S(1)}, bf16[4,128,192]{2,1,0:T(8,128)(2,1)S(1)}, u32[]{:S(2)}, u32[]{:S(2)}) %collective-permute-start.13) | collective-permute-done | bytes 196640 | tf_op jit(solution)/shard_map/ppermute | solution.py:28
  134.1 1.9 collective-permute-start.7
  136.0 23.1 %collective-permute-done.10 = bf16[4,192,128]{2,1,0:T(8,128)(2,1)S(1)} collective-permute-done((bf16[4,192,128]{2,1,0:T(8,128)(2,1)S(1)}, bf16[4,192,128]{2,1,0:T(8,128)(2,1)S(1)}, u32[]{:S(2)}, u32[]{:S(2)}) %collective-permute-start.10) | collective-permute-done | bytes 196640 | tf_op jit(solution)/shard_map/ppermute | solution.py:28
  159.8 1.9 collective-permute-start
  161.8 2.5 gather_fusion
  164.4 1.9 collective-permute-start.1
  166.9 3.6 %collective-permute-start.2 = (bf16[16,192,128]{2,1,0:T(8,128)(2,1)}, bf16[16,192,128]{2,1,0:T(8,128)(2,1)}, u32[]{:S(2)}, u32[]{:S(2)}) collective-permute-start(bf16[16,192,128]{2,1,0:T(8,128)(2,1)} %bitcast.7), channel_id=1, source_target_pairs={{4,0},{8,4},{12,8},{16,12},{20,16},{24,20},{28,24},{5,1},{9,5},{13... | collective-permute-start | bytes 2359304 | tf_op jit(solution)/shard_map/ppermute | solution.py:18
  171.7 0.8 pad_maximum_fusion.1.kanc_ref
  172.5 0.9 pad_maximum_fusion.vanc_ref
  173.4 1.4 copy.80
  174.8 2.3 copy.81
  177.1 2.9 collective-permute-start.3
  180.0 2.2 copy.82
  182.3 2.2 copy.83
  184.5 2.2 constant_dynamic-update-slice_fusion.4
  186.7 2.1 constant_dynamic-update-slice_fusion.3
  188.8 2.1 constant_dynamic-update-slice_fusion.2
  190.9 5.6 %collective-permute-done.2 = bf16[16,192,128]{2,1,0:T(8,128)(2,1)} collective-permute-done((bf16[16,192,128]{2,1,0:T(8,128)(2,1)}, bf16[16,192,128]{2,1,0:T(8,128)(2,1)}, u32[]{:S(2)}, u32[]{:S(2)}) %collective-permute-start.2) | collective-permute-done | bytes 786464 | tf_op jit(solution)/shard_map/ppermute | solution.py:18
  196.5 2.1 constant_dynamic-update-slice_fusion.1
  198.6 1.0 constant_dynamic-update-slice_fusion.9
  199.7 1.1 constant_dynamic-update-slice_fusion.8
  200.7 1.0 constant_dynamic-update-slice_fusion.7
  201.8 1.1 constant_dynamic-update-slice_fusion.6
  202.9 1.0 constant_dynamic-update-slice_fusion.5.vwin_ref
  203.9 6.4 %collective-permute-done.3 = bf16[16,192,128]{2,1,0:T(8,128)(2,1)} collective-permute-done((bf16[16,192,128]{2,1,0:T(8,128)(2,1)}, bf16[16,192,128]{2,1,0:T(8,128)(2,1)}, u32[]{:S(2)}, u32[]{:S(2)}) %collective-permute-start.3) | collective-permute-done | bytes 786464 | tf_op jit(solution)/shard_map/ppermute | solution.py:18
  210.3 2.2 constant_dynamic-update-slice_fusion.kwin_ref
  212.4 90.0 %shard_map.64 = bf16[16,128,192]{2,1,0:T(8,128)(2,1)} custom-call(s32[16]{0:T(128)} %convert_reduce_fusion.count, s32[16,20]{1,0:T(8,128)} %compare_convert_fusion.from_anchor, s32[16,20]{1,0:T(8,128)} %and_select_fusion.rows, bf16[16,128,192]{2,1,0:T(8,128)(2,1)} %bitcast.30, bf16[80,192,128]{2,1,0:T(8,128)(2,1)} %constant_dynamic-update-slice_fusion.kwin_ref, ...), custom_call_target="tpu_custom_call" | custom-call | tf_op jit(solution)/shard_map/pallas_call | solution.py:111
  302.4 1.5 copy.84
  303.9 17.1 %all_to_all.19 = bf16[4,512,192]{1,2,0:T(8,128)(2,1)S(1)} all-to-all(bf16[4,512,192]{1,2,0:T(8,128)(2,1)S(1)} %copy.84), channel_id=1, replica_groups=mesh['seq'=8,'head'=4] {'head'}, dimensions={0} | all-to-all | bytes 1572864 | tf_op jit(solution)/shard_map/all_to_all | solution.py:192
  321.0 1.7 convolution_convert_fusion.1
  (50 shorter events, 7.0 us)
Async XLA Ops:
  6.5 314.4 %copy-start = (bf16[768,768]{1,0:T(8,128)(2,1)S(1)}, bf16[768,768]{1,0:T(8,128)(2,1)}, u32[]{:S(2)}) copy-start(bf16[768,768]{1,0:T(8,128)(2,1)} %param.8) | copy-start | bytes 3538948
  6.5 67.2 %all-gather.2.cloned.1.call-start = ((), (), s32[]{:S(2)}) async-start(), calls=%async_computation.1 | async-start | bytes 3932160 | tf_op jit(solution)/shard_map/all_gather | solution.py:139
  84.8 13.8 %collective-permute-start.11 = (bf16[1,128,192]{2,1,0:T(8,128)(2,1)S(1)}, bf16[1,128,192]{2,1,0:T(8,128)(2,1)S(1)}, u32[]{:S(2)}, u32[]{:S(2)}) collective-permute-start(bf16[1,128,192]{2,1,0:T(8,128)(2,1)S(1)} %slice_bitcast_fusion), channel_id=1, source_target_pairs={{0,4},{4,8},{8,12},{12,16},{16,20},{20,24},{24,28},{28,0},{1,5},{5... | collective-permute-start | bytes 147464 | tf_op jit(solution)/shard_map/ppermute | solution.py:28
  88.3 40.1 %copy-start.6 = (s32[16,12]{1,0:T(8,128)S(1)}, s32[16,12]{1,0:T(8,128)}, u32[]{:S(2)}) copy-start(s32[16,12]{1,0:T(8,128)} %param.9) | copy-start | bytes 2308
  89.6 74.8 %collective-permute-start.4 = (bf16[16,128,192]{1,2,0:T(8,128)(2,1)}, bf16[16,128,192]{1,2,0:T(8,128)(2,1)}, u32[]{:S(2)}, u32[]{:S(2)}) collective-permute-start(bf16[16,128,192]{1,2,0:T(8,128)(2,1)} %copy.76), channel_id=1, source_target_pairs={{0,8},{4,12},{8,16},{12,20},{16,24},{20,28},{1,9},{5,13},{9,17},{1... | collective-permute-start | bytes 2359304 | tf_op jit(solution)/shard_map/ppermute | solution.py:18
  93.0 74.0 %collective-permute-start.5 = (bf16[16,128,192]{1,2,0:T(8,128)(2,1)}, bf16[16,128,192]{1,2,0:T(8,128)(2,1)}, u32[]{:S(2)}, u32[]{:S(2)}) collective-permute-start(bf16[16,128,192]{1,2,0:T(8,128)(2,1)} %copy.76), channel_id=1, source_target_pairs={{0,4},{4,8},{8,12},{12,16},{16,20},{20,24},{24,28},{1,5},{5,9},{9,... | collective-permute-start | bytes 2359304 | tf_op jit(solution)/shard_map/ppermute | solution.py:18
  98.2 24.2 %collective-permute-start.8 = (bf16[1,192,128]{2,1,0:T(8,128)(2,1)S(1)}, bf16[1,192,128]{2,1,0:T(8,128)(2,1)S(1)}, u32[]{:S(2)}, u32[]{:S(2)}) collective-permute-start(bf16[1,192,128]{2,1,0:T(8,128)(2,1)S(1)} %slice.42), channel_id=1, source_target_pairs={{0,4},{4,8},{8,12},{12,16},{16,20},{20,24},{24,28},{28,0},{1,5},{5... | collective-permute-start | bytes 147464 | tf_op jit(solution)/shard_map/ppermute | solution.py:28
  98.6 26.3 %collective-permute-start.12 = (bf16[2,128,192]{2,1,0:T(8,128)(2,1)S(1)}, bf16[2,128,192]{2,1,0:T(8,128)(2,1)S(1)}, u32[]{:S(2)}, u32[]{:S(2)}) collective-permute-start(bf16[2,128,192]{2,1,0:T(8,128)(2,1)S(1)} %pad_maximum_fusion.4), channel_id=1, source_target_pairs={{0,8},{4,12},{8,16},{12,20},{16,24},{20,28},{24,0},{28,4},{1,9},{5... | collective-permute-start | bytes 294920 | tf_op jit(solution)/shard_map/ppermute | solution.py:28
  122.5 4.7 %collective-permute-start.9 = (bf16[2,192,128]{2,1,0:T(8,128)(2,1)S(1)}, bf16[2,192,128]{2,1,0:T(8,128)(2,1)S(1)}, u32[]{:S(2)}, u32[]{:S(2)}) collective-permute-start(bf16[2,192,128]{2,1,0:T(8,128)(2,1)S(1)} %pad_maximum_fusion.5), channel_id=1, source_target_pairs={{0,8},{4,12},{8,16},{12,20},{16,24},{20,28},{24,0},{28,4},{1,9},{5... | collective-permute-start | bytes 294920 | tf_op jit(solution)/shard_map/ppermute | solution.py:28
  124.9 9.2 %collective-permute-start.13 = (bf16[4,128,192]{2,1,0:T(8,128)(2,1)S(1)}, bf16[4,128,192]{2,1,0:T(8,128)(2,1)S(1)}, u32[]{:S(2)}, u32[]{:S(2)}) collective-permute-start(bf16[4,128,192]{2,1,0:T(8,128)(2,1)S(1)} %pad_maximum_fusion.2), channel_id=1, source_target_pairs={{0,16},{4,20},{8,24},{12,28},{16,0},{20,4},{24,8},{28,12},{1,17},{... | collective-permute-start | bytes 589832 | tf_op jit(solution)/shard_map/ppermute | solution.py:28
  127.2 31.9 %collective-permute-start.10 = (bf16[4,192,128]{2,1,0:T(8,128)(2,1)S(1)}, bf16[4,192,128]{2,1,0:T(8,128)(2,1)S(1)}, u32[]{:S(2)}, u32[]{:S(2)}) collective-permute-start(bf16[4,192,128]{2,1,0:T(8,128)(2,1)S(1)} %pad_maximum_fusion.3), channel_id=1, source_target_pairs={{0,16},{4,20},{8,24},{12,28},{16,0},{20,4},{24,8},{28,12},{1,17},{... | collective-permute-start | bytes 589832 | tf_op jit(solution)/shard_map/ppermute | solution.py:28
  128.4 48.7 %collective-permute-start.6 = (bf16[16,128,192]{1,2,0:T(8,128)(2,1)}, bf16[16,128,192]{1,2,0:T(8,128)(2,1)}, u32[]{:S(2)}, u32[]{:S(2)}) collective-permute-start(bf16[16,128,192]{1,2,0:T(8,128)(2,1)} %copy.76), channel_id=1, source_target_pairs={{4,0},{8,4},{12,8},{16,12},{20,16},{24,20},{28,24},{5,1},{9,5},{13... | collective-permute-start | bytes 2359304 | tf_op jit(solution)/shard_map/ppermute | solution.py:18
  134.1 48.2 %collective-permute-start.7 = (bf16[16,128,192]{1,2,0:T(8,128)(2,1)}, bf16[16,128,192]{1,2,0:T(8,128)(2,1)}, u32[]{:S(2)}, u32[]{:S(2)}) collective-permute-start(bf16[16,128,192]{1,2,0:T(8,128)(2,1)} %copy.76), channel_id=1, source_target_pairs={{8,0},{12,4},{16,8},{20,12},{24,16},{28,20},{9,1},{13,5},{17,9},{2... | collective-permute-start | bytes 2359304 | tf_op jit(solution)/shard_map/ppermute | solution.py:18
  159.1 0.7 copy-start.4
  159.8 24.7 %collective-permute-start = (bf16[16,192,128]{2,1,0:T(8,128)(2,1)}, bf16[16,192,128]{2,1,0:T(8,128)(2,1)}, u32[]{:S(2)}, u32[]{:S(2)}) collective-permute-start(bf16[16,192,128]{2,1,0:T(8,128)(2,1)} %bitcast.7), channel_id=1, source_target_pairs={{0,8},{4,12},{8,16},{12,20},{16,24},{20,28},{1,9},{5,13},{9,17},{1... | collective-permute-start | bytes 2359304 | tf_op jit(solution)/shard_map/ppermute | solution.py:18
  161.8 9.9 %copy-start.5 = (bf16[4,192,128]{2,1,0:T(8,128)(2,1)S(1)}, bf16[4,192,128]{2,1,0:T(8,128)(2,1)}, u32[]{:S(2)}) copy-start(bf16[4,192,128]{2,1,0:T(8,128)(2,1)} %copy-done.4) | copy-start | bytes 589828
  164.4 22.3 %collective-permute-start.1 = (bf16[16,192,128]{2,1,0:T(8,128)(2,1)}, bf16[16,192,128]{2,1,0:T(8,128)(2,1)}, u32[]{:S(2)}, u32[]{:S(2)}) collective-permute-start(bf16[16,192,128]{2,1,0:T(8,128)(2,1)} %bitcast.7), channel_id=1, source_target_pairs={{0,4},{4,8},{8,12},{12,16},{16,20},{20,24},{24,28},{1,5},{5,9},{9,... | collective-permute-start | bytes 2359304 | tf_op jit(solution)/shard_map/ppermute | solution.py:18
  166.9 29.6 %collective-permute-start.2 = (bf16[16,192,128]{2,1,0:T(8,128)(2,1)}, bf16[16,192,128]{2,1,0:T(8,128)(2,1)}, u32[]{:S(2)}, u32[]{:S(2)}) collective-permute-start(bf16[16,192,128]{2,1,0:T(8,128)(2,1)} %bitcast.7), channel_id=1, source_target_pairs={{4,0},{8,4},{12,8},{16,12},{20,16},{24,20},{28,24},{5,1},{9,5},{13... | collective-permute-start | bytes 2359304 | tf_op jit(solution)/shard_map/ppermute | solution.py:18
  177.1 33.2 %collective-permute-start.3 = (bf16[16,192,128]{2,1,0:T(8,128)(2,1)}, bf16[16,192,128]{2,1,0:T(8,128)(2,1)}, u32[]{:S(2)}, u32[]{:S(2)}) collective-permute-start(bf16[16,192,128]{2,1,0:T(8,128)(2,1)} %bitcast.7), channel_id=1, source_target_pairs={{8,0},{12,4},{16,8},{20,12},{24,16},{28,20},{9,1},{13,5},{17,9},{2... | collective-permute-start | bytes 2359304 | tf_op jit(solution)/shard_map/ppermute | solution.py:18
  184.5 15.2 %copy-start.1 = (bf16[16,128,192]{2,1,0:T(8,128)(2,1)S(1)}, bf16[16,128,192]{2,1,0:T(8,128)(2,1)}, u32[]{:S(2)}) copy-start(bf16[16,128,192]{2,1,0:T(8,128)(2,1)} %copy.81) | copy-start | bytes 2359300
  190.9 10.9 %copy-start.2 = (bf16[16,128,192]{2,1,0:T(8,128)(2,1)S(1)}, bf16[16,128,192]{2,1,0:T(8,128)(2,1)}, u32[]{:S(2)}) copy-start(bf16[16,128,192]{2,1,0:T(8,128)(2,1)} %copy.82) | copy-start | bytes 2359300
  198.6 4.2 %copy-start.3 = (bf16[16,128,192]{2,1,0:T(8,128)(2,1)S(1)}, bf16[16,128,192]{2,1,0:T(8,128)(2,1)}, u32[]{:S(2)}) copy-start(bf16[16,128,192]{2,1,0:T(8,128)(2,1)} %copy.83) | copy-start | bytes 2359300
Sparse Core Ops, SparseCore 0:
  8.9 64.7 all-gather.1

commit v2 on v1

--- a/solution.py
+++ b/solution.py
@@ -31,9 +31,9 @@
     return held
 
 
-def attention_kernel(count, from_anchor, rows, q_ref, kwin_ref, vwin_ref, kanc_ref, vanc_ref,
-                     o_ref, kt_ref, v_ref, sc_ref, m_ref, l_ref, acc_ref,
-                     *, heads, group, groups, scale):
+def attention_kernel(count, source, rows, q_ref, *refs, heads, group, groups, scale):
+    tables = refs[:6]
+    o_ref, kt_ref, v_ref, sc_ref, m_ref, l_ref, acc_ref = refs[6:]
     b = pl.program_id(0)
     used = count[b]
     span = group * BLK
@@ -47,15 +47,11 @@
         at = pl.multiple_of(j * BLK, BLK)
         row = rows[b, j]
 
-        @pl.when(from_anchor[b, j] == 0)
-        def _():
-            kt_ref[:, pl.ds(at, BLK)] = kwin_ref[row]
-            v_ref[pl.ds(at, BLK), :] = vwin_ref[row]
-
-        @pl.when(from_anchor[b, j] != 0)
-        def _():
-            kt_ref[:, pl.ds(at, BLK)] = kanc_ref[row]
-            v_ref[pl.ds(at, BLK), :] = vanc_ref[row]
+        for code in range(3):
+            @pl.when(source[b, j] == code)
+            def _():
+                kt_ref[:, pl.ds(at, BLK)] = tables[2 * code][row]
+                v_ref[pl.ds(at, BLK), :] = tables[2 * code + 1][row]
 
         return carry
 
@@ -98,11 +94,11 @@
         o_ref[0, :, cols] = (acc_ref[...] / totals).astype(o_ref.dtype)
 
 
-def attention(queries, kwin, vwin, kanc, vanc, count, from_anchor, rows):
+def attention(queries, tables, count, source, rows):
     block_count, _, width = queries.shape
     heads = width // HDIM
     slots = rows.shape[1]
-    group = 4
+    group = 2
     groups = -(-slots // group)
     kernel = functools.partial(attention_kernel, heads=heads, group=group, groups=groups,
                                scale=HDIM ** (-0.5))
@@ -116,11 +112,7 @@
             grid=(block_count,),
             in_specs=[
                 pl.BlockSpec((1, BLK, width), lambda b, *_: (b, 0, 0)),
-                whole,
-                whole,
-                whole,
-                whole,
-            ],
+            ] + [whole] * len(tables),
             out_specs=pl.BlockSpec((1, BLK, width), lambda b, *_: (b, 0, 0)),
             scratch_shapes=[
                 pltpu.VMEM((width, keys), jnp.bfloat16),
@@ -132,15 +124,31 @@
             ],
         ),
         compiler_params=pltpu.CompilerParams(vmem_limit_bytes=60 * 1024 * 1024),
-    )(count, from_anchor, rows, queries, kwin, vwin, kanc, vanc)
+    )(count, source, rows, queries, *tables)
+
+
+def split_kv(projected, width, block_count):
+    keys_t = jnp.transpose(
+        projected[:, width:2 * width].reshape(block_count, BLK, width), (0, 2, 1)
+    )
+    values = projected[:, 2 * width:].reshape(block_count, BLK, width)
+    return keys_t, values
+
+
+def window_of(x):
+    parts = []
+    for offset in (2, 1, 0, -1, -2):
+        parts.append(x if offset == 0 else shifted(x, "seq", offset))
+    return jnp.concatenate(parts, axis=0)
 
 
 def shards(tokens, w_qkv, w_out, neighbours, near_count, anchors):
-    gathered = lax.all_gather(tokens, "head", axis=0, tiled=True)
     head_count = lax.axis_size("head")
     head_rank = lax.axis_index("head")
     width_here = D // head_count
-    row_count = gathered.shape[0]
+    own_rows = tokens.shape[0]
+    own_blocks = own_rows // BLK
+    row_count = own_rows * head_count
     block_count = row_count // BLK
     neigh = neighbours.shape[1]
     col_start = head_rank * width_here
@@ -148,49 +156,61 @@
     key_cols = lax.dynamic_slice_in_dim(w_qkv[:, 1], col_start, width_here, 1)
     value_cols = lax.dynamic_slice_in_dim(w_qkv[:, 2], col_start, width_here, 1)
     own_weights = jnp.concatenate([query_cols, key_cols, value_cols], axis=1)
+
+    own_proj = jnp.dot(tokens, own_weights, preferred_element_type=jnp.float32).astype(
+        jnp.bfloat16
+    )
+    k_own, v_own = split_kv(own_proj, width_here, own_blocks)
+    ka, va = window_of(k_own), window_of(v_own)
+
+    gathered = lax.all_gather(tokens, "head", axis=0, tiled=True)
     projected = jnp.dot(gathered, own_weights, preferred_element_type=jnp.float32).astype(
         jnp.bfloat16
     )
     queries = projected[:, :width_here].reshape(block_count, BLK, width_here)
-    keys_t = jnp.transpose(
-        projected[:, width_here:2 * width_here].reshape(block_count, BLK, width_here), (0, 2, 1)
-    )
-    values = projected[:, 2 * width_here:].reshape(block_count, BLK, width_here)
+    rest = jnp.roll(projected, -head_rank * own_rows, axis=0)[own_rows:]
+    k_rest, v_rest = split_kv(rest, width_here, block_count - own_blocks)
+    kb, vb = window_of(k_rest), window_of(v_rest)
+
+    keys_t, values = split_kv(projected, width_here, block_count)
     seq_count = lax.axis_size("seq")
     seq_rank = lax.axis_index("seq")
-    kparts, vparts = [], []
-    for offset in (2, 1, 0, -1, -2):
-        if offset == 0:
-            kparts.append(keys_t)
-            vparts.append(values)
-        else:
-            kparts.append(shifted(keys_t, "seq", offset))
-            vparts.append(shifted(values, "seq", offset))
-    kwin = jnp.concatenate(kparts, axis=0)
-    vwin = jnp.concatenate(vparts, axis=0)
     kanc = gather_all(keys_t[0], "seq")
     vanc = gather_all(values[0], "seq")
     held_count = kanc.shape[0]
     first_block = (seq_rank - 2) * block_count
 
-    near_idx = jnp.clip(neighbours - first_block, 0, 5 * block_count - 1).astype(jnp.int32)
+    rel = jnp.clip(neighbours - first_block, 0, 5 * block_count - 1)
+    offset_idx = rel // block_count
+    within = rel % block_count
+    chunk = within // own_blocks
+    inner = within % own_blocks
+    mine = chunk == head_rank
+    row_a = offset_idx * own_blocks + inner
+    row_b = (offset_idx * (block_count - own_blocks)
+             + ((chunk - head_rank) % head_count - 1) * own_blocks + inner)
+    near_row = jnp.where(mine, row_a, row_b)
+    near_src = jnp.where(mine, 0, 1)
     owner = jnp.clip(anchors // block_count, 0, seq_count - 1)
-    anch_idx = ((owner - seq_rank + held_count - 1) % seq_count).astype(jnp.int32)
+    anch_row = (owner - seq_rank + held_count - 1) % seq_count
     near_used = jnp.arange(neigh)[None, :] < near_count[:, None]
     repeated = jnp.any(
         (anchors[:, :, None] == neighbours[:, None, :]) & near_used[:, None, :], axis=2
     )
     valid = jnp.concatenate([near_used, jnp.logical_not(repeated)], axis=1)
     order = jnp.argsort(jnp.logical_not(valid).astype(jnp.int32), axis=1, stable=True)
-    every_row = jnp.concatenate([near_idx, anch_idx], axis=1)
+    every_row = jnp.concatenate([near_row, anch_row], axis=1)
+    every_src = jnp.concatenate([near_src, jnp.full_like(anch_row, 2)], axis=1)
     rows = jnp.take_along_axis(every_row, order, axis=1).astype(jnp.int32)
-    from_anchor = (order >= neigh).astype(jnp.int32)
+    source = jnp.take_along_axis(every_src, order, axis=1).astype(jnp.int32)
     count = jnp.sum(valid.astype(jnp.int32), axis=1).astype(jnp.int32)
 
-    attended = attention(queries, kwin, vwin, kanc, vanc, count, from_anchor, rows)
+    attended = attention(queries, (ka, va, kb, vb, kanc, vanc), count, source, rows)
     attended = attended.reshape(row_count, width_here)
-    mine = lax.all_to_all(attended, "head", 0, 1, tiled=True)
-    mixed_out = jnp.dot(mine, w_out, preferred_element_type=jnp.float32).astype(jnp.bfloat16)
+    mine_rows = lax.all_to_all(attended, "head", 0, 1, tiled=True)
+    mixed_out = jnp.dot(mine_rows, w_out, preferred_element_type=jnp.float32).astype(
+        jnp.bfloat16
+    )
     return mixed_out
 
 

time: 334 us -> 376 us (1.13)
  the two profiles are of different devices: /device:TPU:2 before, /device:TPU:1 now
where the time goes in v2:
time: 376 us; the launch traced here: 375 us
  Pallas kernels  143 us (38%)
  waiting for transfers between devices  84.8 us (23%)
  starting transfers between devices  49.3 us (13%)
  local copies, waits for them, and re-layouts  47.1 us (13%)
  blocking collectives  20.9 us (6%)
  between operations  13.9 us (4%)
  other arithmetic  8.54 us (2%)
  matrix products  7.45 us (2%)
    pallas_call x1, Pallas kernels, attention(): pl.pallas_call(kernel, out_shape=jax.ShapeDtypeStruct(queries.shape, jnp....  143 us
    ppermute x16, starting transfers between devices, shifted(): return lax.ppermute(x, axis, pairs)  40.1 us
    ppermute x6, waiting for transfers between devices, gather_all(): got = lax.ppermute(held, axis, pairs)  34.8 us
    ppermute x16, waiting for transfers between devices, shifted(): return lax.ppermute(x, axis, pairs)  27.4 us
    all_gather x1, waiting for transfers between devices, shards(): gathered = lax.all_gather(tokens, 'head', axis=0, tiled=True)  21.9 us
    all_to_all x1, blocking collectives, shards(): mine_rows = lax.all_to_all(attended, 'head', 0, 1, tiled=True)  20.9 us
    unnamed x36, local copies, waits for them, and re-layouts  16.5 us
    ppermute x6, starting transfers between devices, gather_all(): got = lax.ppermute(held, axis, pairs)  9.22 us
  transfers between devices with their start and end apart: 23, of which 8 were waited for; matrix products, arithmetic and copies ran while one was open for 15% of the time, Pallas kernels for 0%

profile of v2, /device:TPU:1, one launch (start us, length us, event | category | flops | bytes accessed | tf_op | source)
XLA Modules:
  0.0 375.4 jit_solution(5067971555610506477)
XLA Ops:
  7.3 2.3 fusion.21
  11.4 4.0 %collective-permute-start.4 = (bf16[4,128,192]{2,1,0:T(8,128)(2,1)S(1)}, bf16[4,128,192]{2,1,0:T(8,128)(2,1)S(1)}, u32[]{:S(2)}, u32[]{:S(2)}) collective-permute-start(bf16[4,128,192]{2,1,0:T(8,128)(2,1)S(1)} %bitcast.53), channel_id=1, source_target_pairs={{0,8},{4,12},{8,16},{12,20},{16,24},{20,28},{1,9},{5,13},{9,17},{1... | collective-permute-start | bytes 589832 | tf_op jit(solution)/shard_map/ppermute | solution.py:18
  15.3 3.9 %collective-permute-start.5 = (bf16[4,128,192]{2,1,0:T(8,128)(2,1)S(1)}, bf16[4,128,192]{2,1,0:T(8,128)(2,1)S(1)}, u32[]{:S(2)}, u32[]{:S(2)}) collective-permute-start(bf16[4,128,192]{2,1,0:T(8,128)(2,1)S(1)} %bitcast.54), channel_id=1, source_target_pairs={{0,4},{4,8},{8,12},{12,16},{16,20},{20,24},{24,28},{1,5},{5,9},{9,... | collective-permute-start | bytes 589832 | tf_op jit(solution)/shard_map/ppermute | solution.py:18
  19.3 1.9 collective-permute-start.6
  21.9 3.1 collective-permute-start
  25.0 4.8 %collective-permute-start.1 = (bf16[4,192,128]{2,1,0:T(8,128)(2,1)}, bf16[4,192,128]{2,1,0:T(8,128)(2,1)S(1)}, u32[]{:S(2)}, u32[]{:S(2)}) collective-permute-start(bf16[4,192,128]{2,1,0:T(8,128)(2,1)} %bitcast.43), channel_id=1, source_target_pairs={{0,4},{4,8},{8,12},{12,16},{16,20},{20,24},{24,28},{1,5},{5,9},{9,... | collective-permute-start | bytes 589832 | tf_op jit(solution)/shard_map/ppermute | solution.py:18
  31.2 2.5 gather_fusion.1
  33.9 2.5 gather_fusion
  38.2 1.3 collective-permute-start.7
  40.2 1.9 collective-permute-start.2
  42.8 1.3 collective-permute-start.3
  47.0 3.4 collective-permute-done.2
  52.6 21.9 %all-gather.2.cloned.1.call-done = bf16[2048,768]{1,0:T(8,128)(2,1)} async-done(((bf16[512,768]{1,0:T(8,128)(2,1)}), bf16[2048,768]{1,0:T(8,128)(2,1)}) %all-gather.2.cloned.1.call-update) | async-done | bytes 3145744 | tf_op jit(solution)/shard_map/all_gather | solution.py:166
  74.5 4.8 %convolution_convert_fusion = bf16[576,2048]{1,0:T(8,128)(2,1)S(1)} fusion(bf16[2048,768]{1,0:T(8,128)(2,1)} %all-gather.2.cloned.1.call-done, bf16[768,192]{1,0:T(8,128)(2,1)} %copy-done.4, bf16[768,192]{1,0:T(8,128)(2,1)} %copy-done.5, bf16[768,192]{1,0:T(8,128)(2,1)} %copy-done.3), kind=kOutput, calls=%fused_computation.4 | convolution fusion | flops 1815773184 | bytes 6389760 | tf_op jit(solution)/shard_map/dot_general | solution.py:167
  79.3 2.6 copy.93
  81.9 3.2 fusion.22
  85.7 1.8 collective-permute-start.16
  87.5 4.0 %fusion = bf16[2048,576]{1,0:T(8,128)(2,1)S(1)} fusion(s32[]{:T(128)S(6)} %select_n.75, bf16[2048,576]{1,0:T(8,128)(2,1)} %bitcast.45), kind=kLoop, calls=%fused_computation.5 | loop fusion | flops 4718592 | bytes 4718596 | tf_op jit(solution)/shard_map/jit(_roll_dynamic)/concatenate | solution.py:171
  92.7 1.1 copy.96
  93.8 4.0 %collective-permute-start.8 = (bf16[12,192,128]{2,1,0:T(8,128)(2,1)}, bf16[12,192,128]{2,1,0:T(8,128)(2,1)}, u32[]{:S(2)}, u32[]{:S(2)}) collective-permute-start(bf16[12,192,128]{2,1,0:T(8,128)(2,1)} %bitcast.11), channel_id=1, source_target_pairs={{0,8},{4,12},{8,16},{12,20},{16,24},{20,28},{1,9},{5,13},{9,17},{1... | collective-permute-start | bytes 1769480 | tf_op jit(solution)/shard_map/ppermute | solution.py:18
  97.8 1.9 collective-permute-start.9
  101.5 2.2 collective-permute-start.12
  103.7 19.2 %collective-permute-done.19 = bf16[1,128,192]{2,1,0:T(8,128)(2,1)S(1)} collective-permute-done((bf16[1,128,192]{2,1,0:T(8,128)(2,1)S(1)}, bf16[1,128,192]{2,1,0:T(8,128)(2,1)S(1)}, u32[]{:S(2)}, u32[]{:S(2)}) %collective-permute-start.19) | collective-permute-done | bytes 49184 | tf_op jit(solution)/shard_map/ppermute | solution.py:28
  123.0 1.2 collective-permute-start.17
  124.2 7.2 %collective-permute-done.17 = bf16[2,192,128]{2,1,0:T(8,128)(2,1)S(1)} collective-permute-done((bf16[2,192,128]{2,1,0:T(8,128)(2,1)S(1)}, bf16[2,192,128]{2,1,0:T(8,128)(2,1)S(1)}, u32[]{:S(2)}, u32[]{:S(2)}) %collective-permute-start.17) | collective-permute-done | bytes 98336 | tf_op jit(solution)/shard_map/ppermute | solution.py:28
  131.4 1.9 collective-permute-start.20
  133.3 2.9 collective-permute-done.20
  136.2 3.5 collective-permute-start.18
  139.8 1.6 constant_dynamic-update-slice_fusion.refs_0_
  141.5 3.4 collective-permute-done.18
  144.9 2.7 collective-permute-start.13
  148.4 2.1 collective-permute-done.21
  150.5 2.6 collective-permute-start.14
  154.0 1.3 collective-permute-start.15
  155.6 1.9 collective-permute-start.10
  157.5 1.9 constant_dynamic-update-slice_fusion.14
  159.4 1.3 collective-permute-start.11
  160.7 1.9 constant_dynamic-update-slice_fusion.13
  163.7 2.0 constant_dynamic-update-slice_fusion.12
  165.6 23.9 %collective-permute-done.10 = bf16[12,192,128]{2,1,0:T(8,128)(2,1)S(1)} collective-permute-done((bf16[12,192,128]{2,1,0:T(8,128)(2,1)}, bf16[12,192,128]{2,1,0:T(8,128)(2,1)S(1)}, u32[]{:S(2)}, u32[]{:S(2)}) %collective-permute-start.10) | collective-permute-done | bytes 589856 | tf_op jit(solution)/shard_map/ppermute | solution.py:18
  190.4 1.3 copy.102
  191.7 1.3 copy.103
  193.1 2.2 copy.104
  199.1 1.9 constant_dynamic-update-slice_fusion.10.refs_2_
  201.1 143.5 %shard_map.64 = bf16[16,128,192]{2,1,0:T(8,128)(2,1)} custom-call(s32[16]{0:T(128)} %convert_reduce_fusion.count, s32[16,20]{1,0:T(8,128)} %broadcast_select_fusion.1.source, s32[16,20]{1,0:T(8,128)} %get-tuple-element.8.rows, bf16[16,128,192]{2,1,0:T(8,128)(2,1)} %bitcast.50, bf16[20,192,128]{2,1,0:T(8,128)(2,1)} %constant_dynamic-update-slice_fusion.refs_0_, ...), custom_call_target="tpu_custom_call" | custom-call | tf_op jit(solution)/shard_map/pallas_call | solution.py:107
  344.5 1.5 copy.106
  346.0 20.9 %all_to_all.19 = bf16[4,512,192]{1,2,0:T(8,128)(2,1)S(1)} all-to-all(bf16[4,512,192]{1,2,0:T(8,128)(2,1)S(1)} %copy.106), channel_id=1, replica_groups=mesh['seq'=8,'head'=4] {'head'}, dimensions={0} | all-to-all | bytes 1572864 | tf_op jit(solution)/shard_map/all_to_all | solution.py:210
  366.9 1.7 convolution_convert_fusion.1
  (90 shorter events, 24.4 us)
Async XLA Ops:
  6.5 360.4 %copy-start = (bf16[768,768]{1,0:T(8,128)(2,1)S(1)}, bf16[768,768]{1,0:T(8,128)(2,1)}, u32[]{:S(2)}) copy-start(bf16[768,768]{1,0:T(8,128)(2,1)} %param.10) | copy-start | bytes 3538948
  6.5 68.0 %all-gather.2.cloned.1.call-start = ((), (), s32[]{:S(2)}) async-start(), calls=%async_computation.1 | async-start | bytes 3932160 | tf_op jit(solution)/shard_map/all_gather | solution.py:166
  7.3 2.9 copy-start.2
  9.8 1.4 copy-start.3
  10.1 1.1 copy-start.4
  10.1 1.1 copy-start.5
  10.1 19.7 %copy-start.7 = (s32[16,8]{0,1:T(8,128)S(1)}, s32[16,8]{0,1:T(8,128)}, u32[]{:S(2)}) copy-start(s32[16,8]{0,1:T(8,128)} %param.13) | copy-start | bytes 1540
  10.1 19.8 %copy-start.6 = (s32[16,12]{1,0:T(8,128)S(1)}, s32[16,12]{1,0:T(8,128)}, u32[]{:S(2)}) copy-start(s32[16,12]{1,0:T(8,128)} %param.11) | copy-start | bytes 2308
  10.2 19.9 %copy-start.8 = (s32[16]{0:T(128)S(1)}, s32[16]{0:T(128)}, u32[]{:S(2)}) copy-start(s32[16]{0:T(128)} %param.12) | copy-start | bytes 196
  11.4 31.4 %collective-permute-start.4 = (bf16[4,128,192]{2,1,0:T(8,128)(2,1)S(1)}, bf16[4,128,192]{2,1,0:T(8,128)(2,1)S(1)}, u32[]{:S(2)}, u32[]{:S(2)}) collective-permute-start(bf16[4,128,192]{2,1,0:T(8,128)(2,1)S(1)} %bitcast.53), channel_id=1, source_target_pairs={{0,8},{4,12},{8,16},{12,20},{16,24},{20,28},{1,9},{5,13},{9,17},{1... | collective-permute-start | bytes 589832 | tf_op jit(solution)/shard_map/ppermute | solution.py:18
  15.3 30.2 %collective-permute-start.5 = (bf16[4,128,192]{2,1,0:T(8,128)(2,1)S(1)}, bf16[4,128,192]{2,1,0:T(8,128)(2,1)S(1)}, u32[]{:S(2)}, u32[]{:S(2)}) collective-permute-start(bf16[4,128,192]{2,1,0:T(8,128)(2,1)S(1)} %bitcast.54), channel_id=1, source_target_pairs={{0,4},{4,8},{8,12},{12,16},{16,20},{20,24},{24,28},{1,5},{5,9},{9,... | collective-permute-start | bytes 589832 | tf_op jit(solution)/shard_map/ppermute | solution.py:18
  19.3 31.9 %collective-permute-start.6 = (bf16[4,128,192]{2,1,0:T(8,128)(2,1)S(1)}, bf16[4,128,192]{2,1,0:T(8,128)(2,1)S(1)}, u32[]{:S(2)}, u32[]{:S(2)}) collective-permute-start(bf16[4,128,192]{2,1,0:T(8,128)(2,1)S(1)} %bitcast.55), channel_id=1, source_target_pairs={{4,0},{8,4},{12,8},{16,12},{20,16},{24,20},{28,24},{5,1},{9,5},{13... | collective-permute-start | bytes 589832 | tf_op jit(solution)/shard_map/ppermute | solution.py:18
  21.9 16.3 %collective-permute-start = (bf16[4,192,128]{2,1,0:T(8,128)(2,1)}, bf16[4,192,128]{2,1,0:T(8,128)(2,1)S(1)}, u32[]{:S(2)}, u32[]{:S(2)}) collective-permute-start(bf16[4,192,128]{2,1,0:T(8,128)(2,1)} %bitcast.43), channel_id=1, source_target_pairs={{0,8},{4,12},{8,16},{12,20},{16,24},{20,28},{1,9},{5,13},{9,17},{1... | collective-permute-start | bytes 589832 | tf_op jit(solution)/shard_map/ppermute | solution.py:18
  25.0 15.2 %collective-permute-start.1 = (bf16[4,192,128]{2,1,0:T(8,128)(2,1)}, bf16[4,192,128]{2,1,0:T(8,128)(2,1)S(1)}, u32[]{:S(2)}, u32[]{:S(2)}) collective-permute-start(bf16[4,192,128]{2,1,0:T(8,128)(2,1)} %bitcast.43), channel_id=1, source_target_pairs={{0,4},{4,8},{8,12},{12,16},{16,20},{20,24},{24,28},{1,5},{5,9},{9,... | collective-permute-start | bytes 589832 | tf_op jit(solution)/shard_map/ppermute | solution.py:18
  38.2 13.6 %collective-permute-start.7 = (bf16[4,128,192]{2,1,0:T(8,128)(2,1)S(1)}, bf16[4,128,192]{2,1,0:T(8,128)(2,1)S(1)}, u32[]{:S(2)}, u32[]{:S(2)}) collective-permute-start(bf16[4,128,192]{2,1,0:T(8,128)(2,1)S(1)} %bitcast.56), channel_id=1, source_target_pairs={{8,0},{12,4},{16,8},{20,12},{24,16},{28,20},{9,1},{13,5},{17,9},{2... | collective-permute-start | bytes 589832 | tf_op jit(solution)/shard_map/ppermute | solution.py:18
  40.2 10.2 %collective-permute-start.2 = (bf16[4,192,128]{2,1,0:T(8,128)(2,1)}, bf16[4,192,128]{2,1,0:T(8,128)(2,1)S(1)}, u32[]{:S(2)}, u32[]{:S(2)}) collective-permute-start(bf16[4,192,128]{2,1,0:T(8,128)(2,1)} %bitcast.43), channel_id=1, source_target_pairs={{4,0},{8,4},{12,8},{16,12},{20,16},{24,20},{28,24},{5,1},{9,5},{13... | collective-permute-start | bytes 589832 | tf_op jit(solution)/shard_map/ppermute | solution.py:18
  42.8 96.9 %collective-permute-start.3 = (bf16[4,192,128]{2,1,0:T(8,128)(2,1)}, bf16[4,192,128]{2,1,0:T(8,128)(2,1)}, u32[]{:S(2)}, u32[]{:S(2)}) collective-permute-start(bf16[4,192,128]{2,1,0:T(8,128)(2,1)} %bitcast.43), channel_id=1, source_target_pairs={{8,0},{12,4},{16,8},{20,12},{24,16},{28,20},{9,1},{13,5},{17,9},{2... | collective-permute-start | bytes 589832 | tf_op jit(solution)/shard_map/ppermute | solution.py:18
  85.7 15.9 %collective-permute-start.16 = (bf16[1,192,128]{2,1,0:T(8,128)(2,1)S(1)}, bf16[1,192,128]{2,1,0:T(8,128)(2,1)S(1)}, u32[]{:S(2)}, u32[]{:S(2)}) collective-permute-start(bf16[1,192,128]{2,1,0:T(8,128)(2,1)S(1)} %slice.63), channel_id=1, source_target_pairs={{0,4},{4,8},{8,12},{12,16},{16,20},{20,24},{24,28},{28,0},{1,5},{5... | collective-permute-start | bytes 147464 | tf_op jit(solution)/shard_map/ppermute | solution.py:28
  93.8 61.8 %collective-permute-start.8 = (bf16[12,192,128]{2,1,0:T(8,128)(2,1)}, bf16[12,192,128]{2,1,0:T(8,128)(2,1)}, u32[]{:S(2)}, u32[]{:S(2)}) collective-permute-start(bf16[12,192,128]{2,1,0:T(8,128)(2,1)} %bitcast.11), channel_id=1, source_target_pairs={{0,8},{4,12},{8,16},{12,20},{16,24},{20,28},{1,9},{5,13},{9,17},{1... | collective-permute-start | bytes 1769480 | tf_op jit(solution)/shard_map/ppermute | solution.py:18
  97.8 61.7 %collective-permute-start.9 = (bf16[12,192,128]{2,1,0:T(8,128)(2,1)}, bf16[12,192,128]{2,1,0:T(8,128)(2,1)}, u32[]{:S(2)}, u32[]{:S(2)}) collective-permute-start(bf16[12,192,128]{2,1,0:T(8,128)(2,1)} %bitcast.11), channel_id=1, source_target_pairs={{0,4},{4,8},{8,12},{12,16},{16,20},{20,24},{24,28},{1,5},{5,9},{9,... | collective-permute-start | bytes 1769480 | tf_op jit(solution)/shard_map/ppermute | solution.py:18
  99.7 23.3 %collective-permute-start.19 = (bf16[1,128,192]{2,1,0:T(8,128)(2,1)S(1)}, bf16[1,128,192]{2,1,0:T(8,128)(2,1)S(1)}, u32[]{:S(2)}, u32[]{:S(2)}) collective-permute-start(bf16[1,128,192]{2,1,0:T(8,128)(2,1)S(1)} %slice_bitcast_fusion.1), channel_id=1, source_target_pairs={{0,4},{4,8},{8,12},{12,16},{16,20},{20,24},{24,28},{28,0},{1,5},{5... | collective-permute-start | bytes 147464 | tf_op jit(solution)/shard_map/ppermute | solution.py:28
  101.5 52.5 %collective-permute-start.12 = (bf16[12,128,192]{1,2,0:T(8,128)(2,1)}, bf16[12,128,192]{1,2,0:T(8,128)(2,1)S(1)}, u32[]{:S(2)}, u32[]{:S(2)}) collective-permute-start(bf16[12,128,192]{1,2,0:T(8,128)(2,1)} %copy.97), channel_id=1, source_target_pairs={{0,8},{4,12},{8,16},{12,20},{16,24},{20,28},{1,9},{5,13},{9,17},{1... | collective-permute-start | bytes 1769480 | tf_op jit(solution)/shard_map/ppermute | solution.py:18
  123.0 8.4 %collective-permute-start.17 = (bf16[2,192,128]{2,1,0:T(8,128)(2,1)S(1)}, bf16[2,192,128]{2,1,0:T(8,128)(2,1)S(1)}, u32[]{:S(2)}, u32[]{:S(2)}) collective-permute-start(bf16[2,192,128]{2,1,0:T(8,128)(2,1)S(1)} %pad_maximum_fusion.8), channel_id=1, source_target_pairs={{0,8},{4,12},{8,16},{12,20},{16,24},{20,28},{24,0},{28,4},{1,9},{5... | collective-permute-start | bytes 294920 | tf_op jit(solution)/shard_map/ppermute | solution.py:28
  131.4 4.8 %collective-permute-start.20 = (bf16[2,128,192]{2,1,0:T(8,128)(2,1)S(1)}, bf16[2,128,192]{2,1,0:T(8,128)(2,1)S(1)}, u32[]{:S(2)}, u32[]{:S(2)}) collective-permute-start(bf16[2,128,192]{2,1,0:T(8,128)(2,1)S(1)} %pad_maximum_fusion.7), channel_id=1, source_target_pairs={{0,8},{4,12},{8,16},{12,20},{16,24},{20,28},{24,0},{28,4},{1,9},{5... | collective-permute-start | bytes 294920 | tf_op jit(solution)/shard_map/ppermute | solution.py:28
  136.2 8.6 %collective-permute-start.18 = (bf16[4,192,128]{2,1,0:T(8,128)(2,1)S(1)}, bf16[4,192,128]{2,1,0:T(8,128)(2,1)S(1)}, u32[]{:S(2)}, u32[]{:S(2)}) collective-permute-start(bf16[4,192,128]{2,1,0:T(8,128)(2,1)S(1)} %pad_maximum_fusion.6), channel_id=1, source_target_pairs={{0,16},{4,20},{8,24},{12,28},{16,0},{20,4},{24,8},{28,12},{1,17},{... | collective-permute-start | bytes 589832 | tf_op jit(solution)/shard_map/ppermute | solution.py:28
  139.8 10.7 %collective-permute-start.21 = (bf16[4,128,192]{2,1,0:T(8,128)(2,1)S(1)}, bf16[4,128,192]{2,1,0:T(8,128)(2,1)S(1)}, u32[]{:S(2)}, u32[]{:S(2)}) collective-permute-start(bf16[4,128,192]{2,1,0:T(8,128)(2,1)S(1)} %pad_maximum_fusion.5), channel_id=1, source_target_pairs={{0,16},{4,20},{8,24},{12,28},{16,0},{20,4},{24,8},{28,12},{1,17},{... | collective-permute-start | bytes 589832 | tf_op jit(solution)/shard_map/ppermute | solution.py:28
  144.9 45.5 %collective-permute-start.13 = (bf16[12,128,192]{1,2,0:T(8,128)(2,1)}, bf16[12,128,192]{1,2,0:T(8,128)(2,1)}, u32[]{:S(2)}, u32[]{:S(2)}) collective-permute-start(bf16[12,128,192]{1,2,0:T(8,128)(2,1)} %copy.97), channel_id=1, source_target_pairs={{0,4},{4,8},{8,12},{12,16},{16,20},{20,24},{24,28},{1,5},{5,9},{9,... | collective-permute-start | bytes 1769480 | tf_op jit(solution)/shard_map/ppermute | solution.py:18
  150.5 41.3 %collective-permute-start.14 = (bf16[12,128,192]{1,2,0:T(8,128)(2,1)}, bf16[12,128,192]{1,2,0:T(8,128)(2,1)}, u32[]{:S(2)}, u32[]{:S(2)}) collective-permute-start(bf16[12,128,192]{1,2,0:T(8,128)(2,1)} %copy.97), channel_id=1, source_target_pairs={{4,0},{8,4},{12,8},{16,12},{20,16},{24,20},{28,24},{5,1},{9,5},{13... | collective-permute-start | bytes 1769480 | tf_op jit(solution)/shard_map/ppermute | solution.py:18
  154.0 39.1 %collective-permute-start.15 = (bf16[12,128,192]{1,2,0:T(8,128)(2,1)}, bf16[12,128,192]{1,2,0:T(8,128)(2,1)}, u32[]{:S(2)}, u32[]{:S(2)}) collective-permute-start(bf16[12,128,192]{1,2,0:T(8,128)(2,1)} %copy.97), channel_id=1, source_target_pairs={{8,0},{12,4},{16,8},{20,12},{24,16},{28,20},{9,1},{13,5},{17,9},{2... | collective-permute-start | bytes 1769480 | tf_op jit(solution)/shard_map/ppermute | solution.py:18
  155.6 33.9 %collective-permute-start.10 = (bf16[12,192,128]{2,1,0:T(8,128)(2,1)}, bf16[12,192,128]{2,1,0:T(8,128)(2,1)S(1)}, u32[]{:S(2)}, u32[]{:S(2)}) collective-permute-start(bf16[12,192,128]{2,1,0:T(8,128)(2,1)} %bitcast.11), channel_id=1, source_target_pairs={{4,0},{8,4},{12,8},{16,12},{20,16},{24,20},{28,24},{5,1},{9,5},{13... | collective-permute-start | bytes 1769480 | tf_op jit(solution)/shard_map/ppermute | solution.py:18
  159.4 39.7 %collective-permute-start.11 = (bf16[12,192,128]{2,1,0:T(8,128)(2,1)}, bf16[12,192,128]{2,1,0:T(8,128)(2,1)}, u32[]{:S(2)}, u32[]{:S(2)}) collective-permute-start(bf16[12,192,128]{2,1,0:T(8,128)(2,1)} %bitcast.11), channel_id=1, source_target_pairs={{8,0},{12,4},{16,8},{20,12},{24,16},{28,20},{9,1},{13,5},{17,9},{2... | collective-permute-start | bytes 1769480 | tf_op jit(solution)/shard_map/ppermute | solution.py:18
  195.3 2.9 copy-start.1
Sparse Core Ops, SparseCore 0:
  8.9 65.5 all-gather.1

commit v3 on v2

--- a/solution.py
+++ b/solution.py
@@ -31,12 +31,11 @@
     return held
 
 
-def attention_kernel(count, source, rows, q_ref, *refs, heads, group, groups, scale):
+def attention_kernel(count, source, rows, q_ref, *refs, heads, widths, scale):
     tables = refs[:6]
-    o_ref, kt_ref, v_ref, sc_ref, m_ref, l_ref, acc_ref = refs[6:]
+    o_ref, kt_ref, v_ref = refs[6:]
     b = pl.program_id(0)
     used = count[b]
-    span = group * BLK
 
     @pl.when(b == 0)
     def _():
@@ -46,7 +45,6 @@
     def fetch(j, carry):
         at = pl.multiple_of(j * BLK, BLK)
         row = rows[b, j]
-
         for code in range(3):
             @pl.when(source[b, j] == code)
             def _():
@@ -57,53 +55,40 @@
 
     lax.fori_loop(0, used, fetch, 0)
     limit = used * BLK
-    lane = lax.broadcasted_iota(jnp.int32, (1, span), 1)
-    for h in range(heads):
-        cols = slice(h * HDIM, (h + 1) * HDIM)
-        qh = (q_ref[0, :, cols].astype(jnp.float32) * scale).astype(jnp.bfloat16)
-
-        def scores_of(c):
-            s = jnp.dot(qh, kt_ref[cols, c * span:(c + 1) * span],
-                        preferred_element_type=jnp.float32)
-            bias = jnp.where(lane < limit - c * span, 0.0, -jnp.inf)
-            return s + bias
-
-        first = scores_of(0)
-        sc_ref[:, 0:span] = first
-        m_ref[...] = first
-        for c in range(1, groups):
-            @pl.when(c * group < used)
-            def _():
-                s = scores_of(c)
-                sc_ref[:, c * span:(c + 1) * span] = s
-                m_ref[...] = jnp.maximum(m_ref[...], s)
-
-        peak = jnp.max(m_ref[...], axis=-1, keepdims=True)
-        l_ref[...] = jnp.zeros_like(l_ref)
-        acc_ref[...] = jnp.zeros_like(acc_ref)
-        for c in range(groups):
-            @pl.when(c * group < used)
-            def _():
-                e = jnp.exp(sc_ref[:, c * span:(c + 1) * span] - peak)
-                l_ref[...] += e
-                acc_ref[...] += jnp.dot(e.astype(jnp.bfloat16),
-                                        v_ref[c * span:(c + 1) * span, cols],
-                                        preferred_element_type=jnp.float32)
-
-        totals = jnp.sum(l_ref[...], axis=-1, keepdims=True)
-        o_ref[0, :, cols] = (acc_ref[...] / totals).astype(o_ref.dtype)
-
-
-def attention(queries, tables, count, source, rows):
+
+    def run(slots):
+        span = slots * BLK
+        lane = lax.broadcasted_iota(jnp.int32, (1, span), 1)
+        bias = jnp.where(lane < limit, 0.0, -jnp.inf)
+        for h in range(heads):
+            cols = slice(h * HDIM, (h + 1) * HDIM)
+            qh = (q_ref[0, :, cols].astype(jnp.float32) * scale).astype(jnp.bfloat16)
+            s = jnp.dot(qh, kt_ref[cols, 0:span], preferred_element_type=jnp.float32) + bias
+            peak = jnp.max(s, axis=-1, keepdims=True)
+            e = jnp.exp(s - peak)
+            totals = jnp.sum(e, axis=-1, keepdims=True)
+            summed = jnp.dot(e.astype(jnp.bfloat16), v_ref[0:span, cols],
+                             preferred_element_type=jnp.float32)
+            o_ref[0, :, cols] = (summed / totals).astype(o_ref.dtype)
+
+    low = 0
+    for slots in widths:
+        @pl.when((used > low) & (used <= slots))
+        def _():
+            run(slots)
+        low = slots
+
+
+def attention(queries, tables, count, source, rows, widths=None):
     block_count, _, width = queries.shape
     heads = width // HDIM
     slots = rows.shape[1]
-    group = 2
-    groups = -(-slots // group)
-    kernel = functools.partial(attention_kernel, heads=heads, group=group, groups=groups,
+    if widths is None:
+        widths = tuple(w for w in (8, 12, 16) if w < slots) + (slots,)
+    kernel = functools.partial(attention_kernel, heads=heads, widths=widths,
                                scale=HDIM ** (-0.5))
     whole = pl.BlockSpec(memory_space=pltpu.VMEM)
-    keys = groups * group * BLK
+    keys = slots * BLK
     return pl.pallas_call(
         kernel,
         out_shape=jax.ShapeDtypeStruct(queries.shape, jnp.bfloat16),
@@ -117,10 +102,6 @@
             scratch_shapes=[
                 pltpu.VMEM((width, keys), jnp.bfloat16),
                 pltpu.VMEM((keys, width), jnp.bfloat16),
-                pltpu.VMEM((BLK, keys), jnp.float32),
-                pltpu.VMEM((BLK, group * BLK), jnp.float32),
-                pltpu.VMEM((BLK, group * BLK), jnp.float32),
-                pltpu.VMEM((BLK, HDIM), jnp.float32),
             ],
         ),
         compiler_params=pltpu.CompilerParams(vmem_limit_bytes=60 * 1024 * 1024),

time: 376 us -> 278 us (0.74)
  the two profiles are of different devices: /device:TPU:1 before, /device:TPU:2 now
where the time goes in v3:
time: 278 us; the launch traced here: 273 us
  waiting for transfers between devices  81.5 us (29%)
  starting transfers between devices  49.9 us (18%)
  local copies, waits for them, and re-layouts  47.1 us (17%)
  Pallas kernels  44.1 us (16%)
  blocking collectives  20.4 us (7%)
  between operations  13.9 us (5%)
  other arithmetic  8.55 us (3%)
  matrix products  7.45 us (3%)
    pallas_call x1, Pallas kernels, attention(): pl.pallas_call(kernel, out_shape=jax.ShapeDtypeStruct(queries.shape, jnp....  44.1 us
    ppermute x16, starting transfers between devices, shifted(): return lax.ppermute(x, axis, pairs)  41.8 us
    ppermute x6, waiting for transfers between devices, gather_all(): got = lax.ppermute(held, axis, pairs)  34.5 us
    all_gather x1, waiting for transfers between devices, shards(): gathered = lax.all_gather(tokens, 'head', axis=0, tiled=True)  24.2 us
    ppermute x16, waiting for transfers between devices, shifted(): return lax.ppermute(x, axis, pairs)  22.1 us
    all_to_all x1, blocking collectives, shards(): mine_rows = lax.all_to_all(attended, 'head', 0, 1, tiled=True)  20.4 us
    unnamed x36, local copies, waits for them, and re-layouts  16.5 us
    ppermute x6, starting transfers between devices, gather_all(): got = lax.ppermute(held, axis, pairs)  8.14 us
  transfers between devices with their start and end apart: 23, of which 8 were waited for; matrix products, arithmetic and copies ran while one was open for 21% of the time, Pallas kernels for 0%

profile of v3, /device:TPU:2, one launch (start us, length us, event | category | flops | bytes accessed | tf_op | source)
XLA Modules:
  0.0 272.9 jit_solution(2340730365827355944)
XLA Ops:
  7.3 2.3 fusion.21
  11.4 3.4 %collective-permute-start.4 = (bf16[4,128,192]{2,1,0:T(8,128)(2,1)S(1)}, bf16[4,128,192]{2,1,0:T(8,128)(2,1)S(1)}, u32[]{:S(2)}, u32[]{:S(2)}) collective-permute-start(bf16[4,128,192]{2,1,0:T(8,128)(2,1)S(1)} %bitcast.53), channel_id=1, source_target_pairs={{0,8},{4,12},{8,16},{12,20},{16,24},{20,28},{1,9},{5,13},{9,17},{1... | collective-permute-start | bytes 589832 | tf_op jit(solution)/shard_map/ppermute | solution.py:18
  14.8 1.9 collective-permute-start.5
  16.7 3.6 %collective-permute-start.6 = (bf16[4,128,192]{2,1,0:T(8,128)(2,1)S(1)}, bf16[4,128,192]{2,1,0:T(8,128)(2,1)S(1)}, u32[]{:S(2)}, u32[]{:S(2)}) collective-permute-start(bf16[4,128,192]{2,1,0:T(8,128)(2,1)S(1)} %bitcast.55), channel_id=1, source_target_pairs={{4,0},{8,4},{12,8},{16,12},{20,16},{24,20},{28,24},{5,1},{9,5},{13... | collective-permute-start | bytes 589832 | tf_op jit(solution)/shard_map/ppermute | solution.py:18
  21.1 4.3 %collective-permute-start = (bf16[4,192,128]{2,1,0:T(8,128)(2,1)}, bf16[4,192,128]{2,1,0:T(8,128)(2,1)S(1)}, u32[]{:S(2)}, u32[]{:S(2)}) collective-permute-start(bf16[4,192,128]{2,1,0:T(8,128)(2,1)} %bitcast.43), channel_id=1, source_target_pairs={{0,8},{4,12},{8,16},{12,20},{16,24},{20,28},{1,9},{5,13},{9,17},{1... | collective-permute-start | bytes 589832 | tf_op jit(solution)/shard_map/ppermute | solution.py:18
  25.3 1.9 collective-permute-start.1
  28.7 2.5 gather_fusion.1
  31.3 2.5 gather_fusion
  35.6 1.9 collective-permute-start.7
  38.3 3.0 %collective-permute-start.2 = (bf16[4,192,128]{2,1,0:T(8,128)(2,1)}, bf16[4,192,128]{2,1,0:T(8,128)(2,1)S(1)}, u32[]{:S(2)}, u32[]{:S(2)}) collective-permute-start(bf16[4,192,128]{2,1,0:T(8,128)(2,1)} %bitcast.43), channel_id=1, source_target_pairs={{4,0},{8,4},{12,8},{16,12},{20,16},{24,20},{28,24},{5,1},{9,5},{13... | collective-permute-start | bytes 589832 | tf_op jit(solution)/shard_map/ppermute | solution.py:18
  41.9 1.9 collective-permute-start.3
  49.5 24.2 %all-gather.2.cloned.1.call-done = bf16[2048,768]{1,0:T(8,128)(2,1)} async-done(((bf16[512,768]{1,0:T(8,128)(2,1)}), bf16[2048,768]{1,0:T(8,128)(2,1)}) %all-gather.2.cloned.1.call-update) | async-done | bytes 3145744 | tf_op jit(solution)/shard_map/all_gather | solution.py:147
  73.7 4.8 %convolution_convert_fusion = bf16[576,2048]{1,0:T(8,128)(2,1)S(1)} fusion(bf16[2048,768]{1,0:T(8,128)(2,1)} %all-gather.2.cloned.1.call-done, bf16[768,192]{1,0:T(8,128)(2,1)} %copy-done.4, bf16[768,192]{1,0:T(8,128)(2,1)} %copy-done.5, bf16[768,192]{1,0:T(8,128)(2,1)} %copy-done.3), kind=kOutput, calls=%fused_computation.4 | convolution fusion | flops 1815773184 | bytes 6389760 | tf_op jit(solution)/shard_map/dot_general | solution.py:148
  78.5 2.6 copy.93
  81.1 3.2 %fusion.22 = (bf16[2048,192]{1,0:T(8,128)(2,1)S(1)}, bf16[2048,192]{1,0:T(8,128)(2,1)}) fusion(bf16[2048,576]{1,0:T(8,128)(2,1)} %bitcast.44), kind=kLoop, calls=%fused_computation.99 | loop fusion | bytes 3145728 | tf_op jit(solution)/shard_map/slice | solution.py:113
  84.9 4.0 %fusion = bf16[2048,576]{1,0:T(8,128)(2,1)S(1)} fusion(s32[]{:T(128)S(6)} %select_n.75, bf16[2048,576]{1,0:T(8,128)(2,1)} %bitcast.45), kind=kLoop, calls=%fused_computation.5 | loop fusion | flops 4718592 | bytes 4718596 | tf_op jit(solution)/shard_map/jit(_roll_dynamic)/concatenate | solution.py:152
  90.1 1.1 copy.96
  91.2 3.4 %collective-permute-start.8 = (bf16[12,192,128]{2,1,0:T(8,128)(2,1)}, bf16[12,192,128]{2,1,0:T(8,128)(2,1)}, u32[]{:S(2)}, u32[]{:S(2)}) collective-permute-start(bf16[12,192,128]{2,1,0:T(8,128)(2,1)} %bitcast.11), channel_id=1, source_target_pairs={{0,8},{4,12},{8,16},{12,20},{16,24},{20,28},{1,9},{5,13},{9,17},{1... | collective-permute-start | bytes 1769480 | tf_op jit(solution)/shard_map/ppermute | solution.py:18
  94.6 3.2 %collective-permute-start.9 = (bf16[12,192,128]{2,1,0:T(8,128)(2,1)}, bf16[12,192,128]{2,1,0:T(8,128)(2,1)}, u32[]{:S(2)}, u32[]{:S(2)}) collective-permute-start(bf16[12,192,128]{2,1,0:T(8,128)(2,1)} %bitcast.11), channel_id=1, source_target_pairs={{0,4},{4,8},{8,12},{12,16},{16,20},{20,24},{24,28},{1,5},{5,9},{9,... | collective-permute-start | bytes 1769480 | tf_op jit(solution)/shard_map/ppermute | solution.py:18
  98.1 1.1 copy.97
  99.2 2.1 collective-permute-start.12
  101.4 21.4 %collective-permute-done.19 = bf16[1,128,192]{2,1,0:T(8,128)(2,1)S(1)} collective-permute-done((bf16[1,128,192]{2,1,0:T(8,128)(2,1)S(1)}, bf16[1,128,192]{2,1,0:T(8,128)(2,1)S(1)}, u32[]{:S(2)}, u32[]{:S(2)}) %collective-permute-start.19) | collective-permute-done | bytes 49184 | tf_op jit(solution)/shard_map/ppermute | solution.py:28
  122.9 2.4 collective-permute-start.17
  125.2 3.3 %collective-permute-done.17 = bf16[2,192,128]{2,1,0:T(8,128)(2,1)S(1)} collective-permute-done((bf16[2,192,128]{2,1,0:T(8,128)(2,1)S(1)}, bf16[2,192,128]{2,1,0:T(8,128)(2,1)S(1)}, u32[]{:S(2)}, u32[]{:S(2)}) %collective-permute-start.17) | collective-permute-done | bytes 98336 | tf_op jit(solution)/shard_map/ppermute | solution.py:28
  128.6 3.3 %collective-permute-start.20 = (bf16[2,128,192]{2,1,0:T(8,128)(2,1)S(1)}, bf16[2,128,192]{2,1,0:T(8,128)(2,1)S(1)}, u32[]{:S(2)}, u32[]{:S(2)}) collective-permute-start(bf16[2,128,192]{2,1,0:T(8,128)(2,1)S(1)} %pad_maximum_fusion.7), channel_id=1, source_target_pairs={{0,8},{4,12},{8,16},{12,20},{16,24},{20,28},{24,0},{28,4},{1,9},{5... | collective-permute-start | bytes 294920 | tf_op jit(solution)/shard_map/ppermute | solution.py:28
  131.9 3.3 %collective-permute-done.20 = bf16[2,128,192]{2,1,0:T(8,128)(2,1)S(1)} collective-permute-done((bf16[2,128,192]{2,1,0:T(8,128)(2,1)S(1)}, bf16[2,128,192]{2,1,0:T(8,128)(2,1)S(1)}, u32[]{:S(2)}, u32[]{:S(2)}) %collective-permute-start.20) | collective-permute-done | bytes 98336 | tf_op jit(solution)/shard_map/ppermute | solution.py:28
  135.9 1.4 collective-permute-start.21
  137.3 1.6 constant_dynamic-update-slice_fusion.refs_0_
  138.9 4.0 %collective-permute-done.18 = bf16[4,192,128]{2,1,0:T(8,128)(2,1)S(1)} collective-permute-done((bf16[4,192,128]{2,1,0:T(8,128)(2,1)S(1)}, bf16[4,192,128]{2,1,0:T(8,128)(2,1)S(1)}, u32[]{:S(2)}, u32[]{:S(2)}) %collective-permute-start.18) | collective-permute-done | bytes 196640 | tf_op jit(solution)/shard_map/ppermute | solution.py:28
  142.9 2.1 collective-permute-start.13
  145.8 2.5 collective-permute-done.21
  148.3 3.2 %collective-permute-start.14 = (bf16[12,128,192]{1,2,0:T(8,128)(2,1)}, bf16[12,128,192]{1,2,0:T(8,128)(2,1)}, u32[]{:S(2)}, u32[]{:S(2)}) collective-permute-start(bf16[12,128,192]{1,2,0:T(8,128)(2,1)} %copy.97), channel_id=1, source_target_pairs={{4,0},{8,4},{12,8},{16,12},{20,16},{24,20},{28,24},{5,1},{9,5},{13... | collective-permute-start | bytes 1769480 | tf_op jit(solution)/shard_map/ppermute | solution.py:18
  152.5 1.9 collective-permute-start.15
  154.7 1.9 collective-permute-start.10
  156.6 1.9 constant_dynamic-update-slice_fusion.14
  158.6 1.9 collective-permute-start.11
  160.5 1.9 constant_dynamic-update-slice_fusion.13
  162.4 1.0 constant_dynamic-update-slice_fusion.19
  163.4 2.0 constant_dynamic-update-slice_fusion.12
  165.4 21.5 %collective-permute-done.10 = bf16[12,192,128]{2,1,0:T(8,128)(2,1)S(1)} collective-permute-done((bf16[12,192,128]{2,1,0:T(8,128)(2,1)}, bf16[12,192,128]{2,1,0:T(8,128)(2,1)S(1)}, u32[]{:S(2)}, u32[]{:S(2)}) %collective-permute-start.10) | collective-permute-done | bytes 589856 | tf_op jit(solution)/shard_map/ppermute | solution.py:18
  187.7 1.3 copy.102
  189.1 1.3 copy.103
  190.4 2.2 copy.104
  196.5 1.9 constant_dynamic-update-slice_fusion.10.refs_2_
  198.4 44.1 %shard_map.64 = bf16[16,128,192]{2,1,0:T(8,128)(2,1)} custom-call(s32[16]{0:T(128)} %convert_reduce_fusion.count, s32[16,20]{1,0:T(8,128)} %broadcast_select_fusion.1.source, s32[16,20]{1,0:T(8,128)} %get-tuple-element.8.rows, bf16[16,128,192]{2,1,0:T(8,128)(2,1)} %bitcast.50, bf16[20,192,128]{2,1,0:T(8,128)(2,1)} %constant_dynamic-update-slice_fusion.refs_0_, ...), custom_call_target="tpu_custom_call" | custom-call | tf_op jit(solution)/shard_map/pallas_call | solution.py:92
  242.5 1.5 copy.106
  244.0 20.4 %all_to_all.19 = bf16[4,512,192]{1,2,0:T(8,128)(2,1)S(1)} all-to-all(bf16[4,512,192]{1,2,0:T(8,128)(2,1)S(1)} %copy.106), channel_id=1, replica_groups=mesh['seq'=8,'head'=4] {'head'}, dimensions={0} | all-to-all | bytes 1572864 | tf_op jit(solution)/shard_map/all_to_all | solution.py:191
  264.4 1.7 convolution_convert_fusion.1
  (90 shorter events, 23.2 us)
Async XLA Ops:
  6.5 257.9 %copy-start = (bf16[768,768]{1,0:T(8,128)(2,1)S(1)}, bf16[768,768]{1,0:T(8,128)(2,1)}, u32[]{:S(2)}) copy-start(bf16[768,768]{1,0:T(8,128)(2,1)} %param.10) | copy-start | bytes 3538948
  6.5 67.2 %all-gather.2.cloned.1.call-start = ((), (), s32[]{:S(2)}) async-start(), calls=%async_computation.1 | async-start | bytes 3932160 | tf_op jit(solution)/shard_map/all_gather | solution.py:147
  7.3 2.9 %copy-start.2 = (bf16[512,768]{1,0:T(8,128)(2,1)S(1)}, bf16[512,768]{1,0:T(8,128)(2,1)}, u32[]{:S(2)}) copy-start(bf16[512,768]{1,0:T(8,128)(2,1)} %param.8) | copy-start | bytes 2359300
  9.8 1.4 copy-start.3
  10.1 1.1 copy-start.4
  10.1 1.1 copy-start.5
  10.1 17.1 %copy-start.7 = (s32[16,8]{0,1:T(8,128)S(1)}, s32[16,8]{0,1:T(8,128)}, u32[]{:S(2)}) copy-start(s32[16,8]{0,1:T(8,128)} %param.13) | copy-start | bytes 1540
  10.1 17.2 %copy-start.6 = (s32[16,12]{1,0:T(8,128)S(1)}, s32[16,12]{1,0:T(8,128)}, u32[]{:S(2)}) copy-start(s32[16,12]{1,0:T(8,128)} %param.11) | copy-start | bytes 2308
  10.2 17.3 %copy-start.8 = (s32[16]{0:T(128)S(1)}, s32[16]{0:T(128)}, u32[]{:S(2)}) copy-start(s32[16]{0:T(128)} %param.12) | copy-start | bytes 196
  11.4 30.6 %collective-permute-start.4 = (bf16[4,128,192]{2,1,0:T(8,128)(2,1)S(1)}, bf16[4,128,192]{2,1,0:T(8,128)(2,1)S(1)}, u32[]{:S(2)}, u32[]{:S(2)}) collective-permute-start(bf16[4,128,192]{2,1,0:T(8,128)(2,1)S(1)} %bitcast.53), channel_id=1, source_target_pairs={{0,8},{4,12},{8,16},{12,20},{16,24},{20,28},{1,9},{5,13},{9,17},{1... | collective-permute-start | bytes 589832 | tf_op jit(solution)/shard_map/ppermute | solution.py:18
  14.8 30.5 %collective-permute-start.5 = (bf16[4,128,192]{2,1,0:T(8,128)(2,1)S(1)}, bf16[4,128,192]{2,1,0:T(8,128)(2,1)S(1)}, u32[]{:S(2)}, u32[]{:S(2)}) collective-permute-start(bf16[4,128,192]{2,1,0:T(8,128)(2,1)S(1)} %bitcast.54), channel_id=1, source_target_pairs={{0,4},{4,8},{8,12},{12,16},{16,20},{20,24},{24,28},{1,5},{5,9},{9,... | collective-permute-start | bytes 589832 | tf_op jit(solution)/shard_map/ppermute | solution.py:18
  16.7 31.4 %collective-permute-start.6 = (bf16[4,128,192]{2,1,0:T(8,128)(2,1)S(1)}, bf16[4,128,192]{2,1,0:T(8,128)(2,1)S(1)}, u32[]{:S(2)}, u32[]{:S(2)}) collective-permute-start(bf16[4,128,192]{2,1,0:T(8,128)(2,1)S(1)} %bitcast.55), channel_id=1, source_target_pairs={{4,0},{8,4},{12,8},{16,12},{20,16},{24,20},{28,24},{5,1},{9,5},{13... | collective-permute-start | bytes 589832 | tf_op jit(solution)/shard_map/ppermute | solution.py:18
  21.1 14.6 %collective-permute-start = (bf16[4,192,128]{2,1,0:T(8,128)(2,1)}, bf16[4,192,128]{2,1,0:T(8,128)(2,1)S(1)}, u32[]{:S(2)}, u32[]{:S(2)}) collective-permute-start(bf16[4,192,128]{2,1,0:T(8,128)(2,1)} %bitcast.43), channel_id=1, source_target_pairs={{0,8},{4,12},{8,16},{12,20},{16,24},{20,28},{1,9},{5,13},{9,17},{1... | collective-permute-start | bytes 589832 | tf_op jit(solution)/shard_map/ppermute | solution.py:18
  25.3 12.9 %collective-permute-start.1 = (bf16[4,192,128]{2,1,0:T(8,128)(2,1)}, bf16[4,192,128]{2,1,0:T(8,128)(2,1)S(1)}, u32[]{:S(2)}, u32[]{:S(2)}) collective-permute-start(bf16[4,192,128]{2,1,0:T(8,128)(2,1)} %bitcast.43), channel_id=1, source_target_pairs={{0,4},{4,8},{8,12},{12,16},{16,20},{20,24},{24,28},{1,5},{5,9},{9,... | collective-permute-start | bytes 589832 | tf_op jit(solution)/shard_map/ppermute | solution.py:18
  35.6 13.2 %collective-permute-start.7 = (bf16[4,128,192]{2,1,0:T(8,128)(2,1)S(1)}, bf16[4,128,192]{2,1,0:T(8,128)(2,1)S(1)}, u32[]{:S(2)}, u32[]{:S(2)}) collective-permute-start(bf16[4,128,192]{2,1,0:T(8,128)(2,1)S(1)} %bitcast.56), channel_id=1, source_target_pairs={{8,0},{12,4},{16,8},{20,12},{24,16},{28,20},{9,1},{13,5},{17,9},{2... | collective-permute-start | bytes 589832 | tf_op jit(solution)/shard_map/ppermute | solution.py:18
  38.3 9.1 %collective-permute-start.2 = (bf16[4,192,128]{2,1,0:T(8,128)(2,1)}, bf16[4,192,128]{2,1,0:T(8,128)(2,1)S(1)}, u32[]{:S(2)}, u32[]{:S(2)}) collective-permute-start(bf16[4,192,128]{2,1,0:T(8,128)(2,1)} %bitcast.43), channel_id=1, source_target_pairs={{4,0},{8,4},{12,8},{16,12},{20,16},{24,20},{28,24},{5,1},{9,5},{13... | collective-permute-start | bytes 589832 | tf_op jit(solution)/shard_map/ppermute | solution.py:18
  41.9 94.0 %collective-permute-start.3 = (bf16[4,192,128]{2,1,0:T(8,128)(2,1)}, bf16[4,192,128]{2,1,0:T(8,128)(2,1)}, u32[]{:S(2)}, u32[]{:S(2)}) collective-permute-start(bf16[4,192,128]{2,1,0:T(8,128)(2,1)} %bitcast.43), channel_id=1, source_target_pairs={{8,0},{12,4},{16,8},{20,12},{24,16},{28,20},{9,1},{13,5},{17,9},{2... | collective-permute-start | bytes 589832 | tf_op jit(solution)/shard_map/ppermute | solution.py:18
  84.9 14.4 %collective-permute-start.16 = (bf16[1,192,128]{2,1,0:T(8,128)(2,1)S(1)}, bf16[1,192,128]{2,1,0:T(8,128)(2,1)S(1)}, u32[]{:S(2)}, u32[]{:S(2)}) collective-permute-start(bf16[1,192,128]{2,1,0:T(8,128)(2,1)S(1)} %slice.63), channel_id=1, source_target_pairs={{0,4},{4,8},{8,12},{12,16},{16,20},{20,24},{24,28},{28,0},{1,5},{5... | collective-permute-start | bytes 147464 | tf_op jit(solution)/shard_map/ppermute | solution.py:28
  91.2 63.5 %collective-permute-start.8 = (bf16[12,192,128]{2,1,0:T(8,128)(2,1)}, bf16[12,192,128]{2,1,0:T(8,128)(2,1)}, u32[]{:S(2)}, u32[]{:S(2)}) collective-permute-start(bf16[12,192,128]{2,1,0:T(8,128)(2,1)} %bitcast.11), channel_id=1, source_target_pairs={{0,8},{4,12},{8,16},{12,20},{16,24},{20,28},{1,9},{5,13},{9,17},{1... | collective-permute-start | bytes 1769480 | tf_op jit(solution)/shard_map/ppermute | solution.py:18
  94.6 64.0 %collective-permute-start.9 = (bf16[12,192,128]{2,1,0:T(8,128)(2,1)}, bf16[12,192,128]{2,1,0:T(8,128)(2,1)}, u32[]{:S(2)}, u32[]{:S(2)}) collective-permute-start(bf16[12,192,128]{2,1,0:T(8,128)(2,1)} %bitcast.11), channel_id=1, source_target_pairs={{0,4},{4,8},{8,12},{12,16},{16,20},{20,24},{24,28},{1,5},{5,9},{9,... | collective-permute-start | bytes 1769480 | tf_op jit(solution)/shard_map/ppermute | solution.py:18
  97.8 25.1 %collective-permute-start.19 = (bf16[1,128,192]{2,1,0:T(8,128)(2,1)S(1)}, bf16[1,128,192]{2,1,0:T(8,128)(2,1)S(1)}, u32[]{:S(2)}, u32[]{:S(2)}) collective-permute-start(bf16[1,128,192]{2,1,0:T(8,128)(2,1)S(1)} %slice_bitcast_fusion.1), channel_id=1, source_target_pairs={{0,4},{4,8},{8,12},{12,16},{16,20},{20,24},{24,28},{28,0},{1,5},{5... | collective-permute-start | bytes 147464 | tf_op jit(solution)/shard_map/ppermute | solution.py:28
  99.2 53.2 %collective-permute-start.12 = (bf16[12,128,192]{1,2,0:T(8,128)(2,1)}, bf16[12,128,192]{1,2,0:T(8,128)(2,1)S(1)}, u32[]{:S(2)}, u32[]{:S(2)}) collective-permute-start(bf16[12,128,192]{1,2,0:T(8,128)(2,1)} %copy.97), channel_id=1, source_target_pairs={{0,8},{4,12},{8,16},{12,20},{16,24},{20,28},{1,9},{5,13},{9,17},{1... | collective-permute-start | bytes 1769480 | tf_op jit(solution)/shard_map/ppermute | solution.py:18
  122.9 5.7 %collective-permute-start.17 = (bf16[2,192,128]{2,1,0:T(8,128)(2,1)S(1)}, bf16[2,192,128]{2,1,0:T(8,128)(2,1)S(1)}, u32[]{:S(2)}, u32[]{:S(2)}) collective-permute-start(bf16[2,192,128]{2,1,0:T(8,128)(2,1)S(1)} %pad_maximum_fusion.8), channel_id=1, source_target_pairs={{0,8},{4,12},{8,16},{12,20},{16,24},{20,28},{24,0},{28,4},{1,9},{5... | collective-permute-start | bytes 294920 | tf_op jit(solution)/shard_map/ppermute | solution.py:28
  128.6 6.6 %collective-permute-start.20 = (bf16[2,128,192]{2,1,0:T(8,128)(2,1)S(1)}, bf16[2,128,192]{2,1,0:T(8,128)(2,1)S(1)}, u32[]{:S(2)}, u32[]{:S(2)}) collective-permute-start(bf16[2,128,192]{2,1,0:T(8,128)(2,1)S(1)} %pad_maximum_fusion.7), channel_id=1, source_target_pairs={{0,8},{4,12},{8,16},{12,20},{16,24},{20,28},{24,0},{28,4},{1,9},{5... | collective-permute-start | bytes 294920 | tf_op jit(solution)/shard_map/ppermute | solution.py:28
  135.1 7.8 %collective-permute-start.18 = (bf16[4,192,128]{2,1,0:T(8,128)(2,1)S(1)}, bf16[4,192,128]{2,1,0:T(8,128)(2,1)S(1)}, u32[]{:S(2)}, u32[]{:S(2)}) collective-permute-start(bf16[4,192,128]{2,1,0:T(8,128)(2,1)S(1)} %pad_maximum_fusion.6), channel_id=1, source_target_pairs={{0,16},{4,20},{8,24},{12,28},{16,0},{20,4},{24,8},{28,12},{1,17},{... | collective-permute-start | bytes 589832 | tf_op jit(solution)/shard_map/ppermute | solution.py:28
  135.9 12.4 %collective-permute-start.21 = (bf16[4,128,192]{2,1,0:T(8,128)(2,1)S(1)}, bf16[4,128,192]{2,1,0:T(8,128)(2,1)S(1)}, u32[]{:S(2)}, u32[]{:S(2)}) collective-permute-start(bf16[4,128,192]{2,1,0:T(8,128)(2,1)S(1)} %pad_maximum_fusion.5), channel_id=1, source_target_pairs={{0,16},{4,20},{8,24},{12,28},{16,0},{20,4},{24,8},{28,12},{1,17},{... | collective-permute-start | bytes 589832 | tf_op jit(solution)/shard_map/ppermute | solution.py:28
  142.9 44.8 %collective-permute-start.13 = (bf16[12,128,192]{1,2,0:T(8,128)(2,1)}, bf16[12,128,192]{1,2,0:T(8,128)(2,1)}, u32[]{:S(2)}, u32[]{:S(2)}) collective-permute-start(bf16[12,128,192]{1,2,0:T(8,128)(2,1)} %copy.97), channel_id=1, source_target_pairs={{0,4},{4,8},{8,12},{12,16},{16,20},{20,24},{24,28},{1,5},{5,9},{9,... | collective-permute-start | bytes 1769480 | tf_op jit(solution)/shard_map/ppermute | solution.py:18
  148.3 40.8 %collective-permute-start.14 = (bf16[12,128,192]{1,2,0:T(8,128)(2,1)}, bf16[12,128,192]{1,2,0:T(8,128)(2,1)}, u32[]{:S(2)}, u32[]{:S(2)}) collective-permute-start(bf16[12,128,192]{1,2,0:T(8,128)(2,1)} %copy.97), channel_id=1, source_target_pairs={{4,0},{8,4},{12,8},{16,12},{20,16},{24,20},{28,24},{5,1},{9,5},{13... | collective-permute-start | bytes 1769480 | tf_op jit(solution)/shard_map/ppermute | solution.py:18
  152.5 38.0 %collective-permute-start.15 = (bf16[12,128,192]{1,2,0:T(8,128)(2,1)}, bf16[12,128,192]{1,2,0:T(8,128)(2,1)}, u32[]{:S(2)}, u32[]{:S(2)}) collective-permute-start(bf16[12,128,192]{1,2,0:T(8,128)(2,1)} %copy.97), channel_id=1, source_target_pairs={{8,0},{12,4},{16,8},{20,12},{24,16},{28,20},{9,1},{13,5},{17,9},{2... | collective-permute-start | bytes 1769480 | tf_op jit(solution)/shard_map/ppermute | solution.py:18
  154.7 32.2 %collective-permute-start.10 = (bf16[12,192,128]{2,1,0:T(8,128)(2,1)}, bf16[12,192,128]{2,1,0:T(8,128)(2,1)S(1)}, u32[]{:S(2)}, u32[]{:S(2)}) collective-permute-start(bf16[12,192,128]{2,1,0:T(8,128)(2,1)} %bitcast.11), channel_id=1, source_target_pairs={{4,0},{8,4},{12,8},{16,12},{20,16},{24,20},{28,24},{5,1},{9,5},{13... | collective-permute-start | bytes 1769480 | tf_op jit(solution)/shard_map/ppermute | solution.py:18
  158.6 37.9 %collective-permute-start.11 = (bf16[12,192,128]{2,1,0:T(8,128)(2,1)}, bf16[12,192,128]{2,1,0:T(8,128)(2,1)}, u32[]{:S(2)}, u32[]{:S(2)}) collective-permute-start(bf16[12,192,128]{2,1,0:T(8,128)(2,1)} %bitcast.11), channel_id=1, source_target_pairs={{8,0},{12,4},{16,8},{20,12},{24,16},{28,20},{9,1},{13,5},{17,9},{2... | collective-permute-start | bytes 1769480 | tf_op jit(solution)/shard_map/ppermute | solution.py:18
  192.7 2.9 %copy-start.1 = (bf16[12,128,192]{2,1,0:T(8,128)(2,1)S(1)}, bf16[12,128,192]{2,1,0:T(8,128)(2,1)}, u32[]{:S(2)}) copy-start(bf16[12,128,192]{2,1,0:T(8,128)(2,1)} %copy.104) | copy-start | bytes 1769476
Sparse Core Ops, SparseCore 0:
  8.9 64.7 all-gather.1

commit v4 on v3

--- a/solution.py
+++ b/solution.py
@@ -48,8 +48,9 @@
         for code in range(3):
             @pl.when(source[b, j] == code)
             def _():
-                kt_ref[:, pl.ds(at, BLK)] = tables[2 * code][row]
-                v_ref[pl.ds(at, BLK), :] = tables[2 * code + 1][row]
+                start = pl.multiple_of(row * BLK, BLK)
+                kt_ref[:, pl.ds(at, BLK)] = tables[2 * code][:, pl.ds(start, BLK)]
+                v_ref[pl.ds(at, BLK), :] = tables[2 * code + 1][pl.ds(start, BLK), :]
 
         return carry
 
@@ -108,19 +109,18 @@
     )(count, source, rows, queries, *tables)
 
 
-def split_kv(projected, width, block_count):
-    keys_t = jnp.transpose(
-        projected[:, width:2 * width].reshape(block_count, BLK, width), (0, 2, 1)
-    )
-    values = projected[:, 2 * width:].reshape(block_count, BLK, width)
+def project_kv(x, key_w, value_w):
+    keys_t = lax.dot_general(key_w, x, (((0,), (1,)), ((), ())),
+                             preferred_element_type=jnp.float32).astype(jnp.bfloat16)
+    values = jnp.dot(x, value_w, preferred_element_type=jnp.float32).astype(jnp.bfloat16)
     return keys_t, values
 
 
-def window_of(x):
+def window_of(x, axis):
     parts = []
     for offset in (2, 1, 0, -1, -2):
         parts.append(x if offset == 0 else shifted(x, "seq", offset))
-    return jnp.concatenate(parts, axis=0)
+    return jnp.concatenate(parts, axis=axis)
 
 
 def shards(tokens, w_qkv, w_out, neighbours, near_count, anchors):
@@ -133,33 +133,36 @@
     block_count = row_count // BLK
     neigh = neighbours.shape[1]
     col_start = head_rank * width_here
-    query_cols = lax.dynamic_slice_in_dim(w_qkv[:, 0], col_start, width_here, 1)
-    key_cols = lax.dynamic_slice_in_dim(w_qkv[:, 1], col_start, width_here, 1)
-    value_cols = lax.dynamic_slice_in_dim(w_qkv[:, 2], col_start, width_here, 1)
-    own_weights = jnp.concatenate([query_cols, key_cols, value_cols], axis=1)
-
-    own_proj = jnp.dot(tokens, own_weights, preferred_element_type=jnp.float32).astype(
+    query_w = lax.dynamic_slice_in_dim(w_qkv[:, 0], col_start, width_here, 1)
+    key_w = lax.dynamic_slice_in_dim(w_qkv[:, 1], col_start, width_here, 1)
+    value_w = lax.dynamic_slice_in_dim(w_qkv[:, 2], col_start, width_here, 1)
+
+    k_own, v_own = project_kv(tokens, key_w, value_w)
+    ka, va = window_of(k_own, 1), window_of(v_own, 0)
+
+    gathered = lax.all_gather(tokens, "head", axis=0, tiled=True)
+    rest_tokens = jnp.roll(gathered, -head_rank * own_rows, axis=0)[own_rows:]
+    k_rest, v_rest = project_kv(rest_tokens, key_w, value_w)
+    kb, vb = window_of(k_rest, 1), window_of(v_rest, 0)
+    rolled_tokens = jnp.concatenate([tokens, rest_tokens], axis=0)
+    queries = jnp.dot(rolled_tokens, query_w, preferred_element_type=jnp.float32).astype(
         jnp.bfloat16
-    )
-    k_own, v_own = split_kv(own_proj, width_here, own_blocks)
-    ka, va = window_of(k_own), window_of(v_own)
-
-    gathered = lax.all_gather(tokens, "head", axis=0, tiled=True)
-    projected = jnp.dot(gathered, own_weights, preferred_element_type=jnp.float32).astype(
-        jnp.bfloat16
-    )
-    queries = projected[:, :width_here].reshape(block_count, BLK, width_here)
-    rest = jnp.roll(projected, -head_rank * own_rows, axis=0)[own_rows:]
-    k_rest, v_rest = split_kv(rest, width_here, block_count - own_blocks)
-    kb, vb = window_of(k_rest), window_of(v_rest)
-
-    keys_t, values = split_kv(projected, width_here, block_count)
+    ).reshape(block_count, BLK, width_here)
+
     seq_count = lax.axis_size("seq")
     seq_rank = lax.axis_index("seq")
-    kanc = gather_all(keys_t[0], "seq")
-    vanc = gather_all(values[0], "seq")
+    k_first, v_first = project_kv(gathered[:BLK], key_w, value_w)
+    kanc = gather_all(k_first, "seq")
+    vanc = gather_all(v_first, "seq")
     held_count = kanc.shape[0]
+    kanc = jnp.transpose(kanc, (1, 0, 2)).reshape(width_here, held_count * BLK)
+    vanc = vanc.reshape(held_count * BLK, width_here)
     first_block = (seq_rank - 2) * block_count
+
+    shift = -head_rank * own_blocks
+    neighbours = jnp.roll(neighbours, shift, axis=0)
+    near_count = jnp.roll(near_count, shift, axis=0)
+    anchors = jnp.roll(anchors, shift, axis=0)
 
     rel = jnp.clip(neighbours - first_block, 0, 5 * block_count - 1)
     offset_idx = rel // block_count
@@ -187,7 +190,7 @@
     count = jnp.sum(valid.astype(jnp.int32), axis=1).astype(jnp.int32)
 
     attended = attention(queries, (ka, va, kb, vb, kanc, vanc), count, source, rows)
-    attended = attended.reshape(row_count, width_here)
+    attended = jnp.roll(attended.reshape(row_count, width_here), head_rank * own_rows, axis=0)
     mine_rows = lax.all_to_all(attended, "head", 0, 1, tiled=True)
     mixed_out = jnp.dot(mine_rows, w_out, preferred_element_type=jnp.float32).astype(
         jnp.bfloat16

time: 278 us -> 264 us (0.950)
  waiting for transfers between devices: 81.5 us -> 53 us
  matrix products: 7.45 us -> 13.4 us
  starting transfers between devices: 49.9 us -> 52.8 us
  local copies, waits for them, and re-layouts: 47.1 us -> 49.9 us
    ppermute x6, waiting for transfers between devices: 34.5 us -> 19.8 us  [gather_all(): got = lax.ppermute(held, axis, pairs)]
    all_gather x1, waiting for transfers between devices: 24.2 us -> 16 us  [shards(): gathered = lax.all_gather(tokens, 'head', axis=0, tiled=True)]
    unnamed x36 -> x31, local copies, waits for them, and re-layouts: 16.5 us -> 23.3 us
    dot_general x2 -> x7, matrix products: 5.76 us -> 11.7 us  [the longest x3 4.76 us: project_kv(): lax.dot_general(key_w, x, (((0,), (1,)), ((), ())), preferred_element_typ...]
    ppermute x16, waiting for transfers between devices: 22.1 us -> 16.5 us  [shifted(): return lax.ppermute(x, axis, pairs)]
    slice x7 -> x1, local copies, waits for them, and re-layouts: 6.82 us -> 3.32 us  [shards(): value_w = lax.dynamic_slice_in_dim(w_qkv[:, 2], col_start, width_here, 1)]
    ppermute x16, starting transfers between devices: 41.8 us -> 44.7 us  [shifted(): return lax.ppermute(x, axis, pairs)]
    concatenate x4 -> x5, local copies, waits for them, and re-layouts: 5.18 us -> 6.34 us  [the longest x4 5.32 us: window_of(): return jnp.concatenate(parts, axis=axis)]
  transfers between devices with their start and end apart: 23 -> 23, of which waited for: 8 -> 4; matrix products, arithmetic and copies ran while one was open for 21% -> 23% of each run, Pallas kernels for 0% -> 0%
where the time goes in v4:
time: 264 us; the launch traced here: 260 us
  waiting for transfers between devices  53 us (20%)
  starting transfers between devices  52.8 us (20%)
  local copies, waits for them, and re-layouts  49.9 us (19%)
  Pallas kernels  43.6 us (17%)
  blocking collectives  22.4 us (8%)
  between operations  13.8 us (5%)
  matrix products  13.4 us (5%)
  other arithmetic  10.8 us (4%)
    ppermute x16, starting transfers between devices, shifted(): return lax.ppermute(x, axis, pairs)  44.7 us
    pallas_call x1, Pallas kernels, attention(): pl.pallas_call(kernel, out_shape=jax.ShapeDtypeStruct(queries.shape, jnp....  43.6 us
    unnamed x31, local copies, waits for them, and re-layouts  23.3 us
    all_to_all x1, blocking collectives, shards(): mine_rows = lax.all_to_all(attended, 'head', 0, 1, tiled=True)  22.4 us
    ppermute x6, waiting for transfers between devices, gather_all(): got = lax.ppermute(held, axis, pairs)  19.8 us
    ppermute x16, waiting for transfers between devices, shifted(): return lax.ppermute(x, axis, pairs)  16.5 us
    all_gather x1, waiting for transfers between devices, shards(): gathered = lax.all_gather(tokens, 'head', axis=0, tiled=True)  16 us
    ppermute x6, starting transfers between devices, gather_all(): got = lax.ppermute(held, axis, pairs)  8.09 us
  transfers between devices with their start and end apart: 23, of which 4 were waited for; matrix products, arithmetic and copies ran while one was open for 23% of the time, Pallas kernels for 0%

profile of v4, /device:TPU:2, one launch (start us, length us, event | category | flops | bytes accessed | tf_op | source)
XLA Modules:
  0.0 259.8 jit_solution(12577365410740383100)
XLA Ops:
  7.3 3.3 %fusion.54 = (bf16[768,1,768]{2,0,1:T(8,128)(2,1)S(1)}, bf16[768,1,768]{2,0,1:T(8,128)(2,1)}, bf16[768,1,768]{2,0,1:T(8,128)(2,1)S(1)}) fusion(bf16[768,3,768]{2,0,1:T(8,128)(2,1)} %param.9), kind=kLoop, calls=%fused_computation.134 | loop fusion | bytes 7077888 | tf_op jit(solution)/shard_map/slice | solution.py:138
  12.0 1.9 collective-permute-start.3
  13.9 1.9 collective-permute-start.2
  15.8 2.4 collective-permute-start.1
  18.2 4.8 %collective-permute-start = (bf16[192,512]{1,0:T(8,128)(2,1)}, bf16[192,512]{1,0:T(8,128)(2,1)}, u32[]{:S(2)}, u32[]{:S(2)}) collective-permute-start(bf16[192,512]{1,0:T(8,128)(2,1)} %convolution_convert_fusion.4), channel_id=1, source_target_pairs={{0,8},{4,12},{8,16},{12,20},{16,24},{20,28},{1,9},{5,13},{9,17},{1... | collective-permute-start | bytes 589832 | tf_op jit(solution)/shard_map/ppermute | solution.py:18
  25.5 3.8 %collective-permute-start.4 = (bf16[512,192]{1,0:T(8,128)(2,1)S(1)}, bf16[512,192]{1,0:T(8,128)(2,1)}, u32[]{:S(2)}, u32[]{:S(2)}) collective-permute-start(bf16[512,192]{1,0:T(8,128)(2,1)S(1)} %bitcast.57), channel_id=1, source_target_pairs={{0,8},{4,12},{8,16},{12,20},{16,24},{20,28},{1,9},{5,13},{9,17},{1... | collective-permute-start | bytes 589832 | tf_op jit(solution)/shard_map/ppermute | solution.py:18
  31.0 2.5 gather_fusion.1
  33.6 2.5 gather_fusion
  38.0 1.9 collective-permute-start.5
  39.9 1.6 constant_dynamic-update-slice_fusion.4
  41.6 3.0 %collective-permute-start.7 = (bf16[512,192]{1,0:T(8,128)(2,1)S(1)}, bf16[512,192]{1,0:T(8,128)(2,1)S(1)}, u32[]{:S(2)}, u32[]{:S(2)}) collective-permute-start(bf16[512,192]{1,0:T(8,128)(2,1)S(1)} %bitcast.59), channel_id=1, source_target_pairs={{8,0},{12,4},{16,8},{20,12},{24,16},{28,20},{9,1},{13,5},{17,9},{2... | collective-permute-start | bytes 589832 | tf_op jit(solution)/shard_map/ppermute | solution.py:18
  44.6 1.7 constant_dynamic-update-slice_fusion.9
  46.3 1.9 collective-permute-start.6
  49.7 1.6 constant_dynamic-update-slice_fusion.3
  51.3 1.7 constant_dynamic-update-slice_fusion.2
  52.9 1.6 constant_dynamic-update-slice_fusion.1
  54.6 1.7 constant_dynamic-update-slice_fusion.refs_0_
  57.7 16.0 %all-gather.2.cloned.1.call-done = bf16[2048,768]{1,0:T(8,128)(2,1)} async-done(((bf16[512,768]{1,0:T(8,128)(2,1)}), bf16[2048,768]{1,0:T(8,128)(2,1)}) %all-gather.2.cloned.1.call-update) | async-done | bytes 3145744 | tf_op jit(solution)/shard_map/all_gather | solution.py:143
  73.7 4.0 %fusion.7 = bf16[1536,768]{1,0:T(8,128)(2,1)S(1)} fusion(s32[]{:T(128)S(6)} %add.116, bf16[2048,768]{1,0:T(8,128)(2,1)} %all-gather.2.cloned.1.call-done), kind=kLoop, calls=%fused_computation.11 | loop fusion | flops 4718592 | bytes 5505028 | tf_op jit(solution)/shard_map/jit(_roll_dynamic)/concatenate | solution.py:144
  77.7 2.0 convolution_convert_fusion.1
  79.7 1.9 convolution_convert_fusion
  81.6 1.9 collective-permute-start.13
  83.5 3.4 %collective-permute-start.12 = (bf16[1536,192]{0,1:T(8,128)(2,1)}, bf16[1536,192]{0,1:T(8,128)(2,1)}, u32[]{:S(2)}, u32[]{:S(2)}) collective-permute-start(bf16[1536,192]{0,1:T(8,128)(2,1)} %convolution_convert_fusion), channel_id=1, source_target_pairs={{0,8},{4,12},{8,16},{12,20},{16,24},{20,28},{1,9},{5,13},{9,17},{1... | collective-permute-start | bytes 1769480 | tf_op jit(solution)/shard_map/ppermute | solution.py:18
  91.4 1.9 collective-permute-start.8
  93.3 17.1 %collective-permute-done.19 = bf16[1,128,192]{1,2,0:T(8,128)(2,1)S(1)} collective-permute-done((bf16[1,128,192]{1,2,0:T(8,128)(2,1)S(1)}, bf16[1,128,192]{1,2,0:T(8,128)(2,1)S(1)}, u32[]{:S(2)}, u32[]{:S(2)}) %collective-permute-start.19) | collective-permute-done | bytes 49184 | tf_op jit(solution)/shard_map/ppermute | solution.py:28
  110.5 2.4 collective-permute-start.20
  113.9 2.7 %collective-permute-done.20 = bf16[2,128,192]{1,2,0:T(8,128)(2,1)S(1)} collective-permute-done((bf16[2,128,192]{1,2,0:T(8,128)(2,1)S(1)}, bf16[2,128,192]{1,2,0:T(8,128)(2,1)S(1)}, u32[]{:S(2)}, u32[]{:S(2)}) %collective-permute-start.20) | collective-permute-done | bytes 98336 | tf_op jit(solution)/shard_map/ppermute | solution.py:28
  117.3 1.5 collective-permute-start.21
  118.8 1.5 collective-permute-start.18
  120.3 2.3 fusion.4
  125.3 3.9 %collective-permute-start.15 = (bf16[1536,192]{0,1:T(8,128)(2,1)}, bf16[1536,192]{0,1:T(8,128)(2,1)}, u32[]{:S(2)}, u32[]{:S(2)}) collective-permute-start(bf16[1536,192]{0,1:T(8,128)(2,1)} %convolution_convert_fusion), channel_id=1, source_target_pairs={{8,0},{12,4},{16,8},{20,12},{24,16},{28,20},{9,1},{13,5},{17,9},{2... | collective-permute-start | bytes 1769480 | tf_op jit(solution)/shard_map/ppermute | solution.py:18
  131.1 4.8 %collective-permute-start.14 = (bf16[1536,192]{0,1:T(8,128)(2,1)}, bf16[1536,192]{0,1:T(8,128)(2,1)}, u32[]{:S(2)}, u32[]{:S(2)}) collective-permute-start(bf16[1536,192]{0,1:T(8,128)(2,1)} %convolution_convert_fusion), channel_id=1, source_target_pairs={{4,0},{8,4},{12,8},{16,12},{20,16},{24,20},{28,24},{5,1},{9,5},{13... | collective-permute-start | bytes 1769480 | tf_op jit(solution)/shard_map/ppermute | solution.py:18
  136.0 1.7 copy_bitcast_fusion.1.refs_4_
  137.7 2.6 %collective-permute-start.9 = (bf16[192,1536]{1,0:T(8,128)(2,1)}, bf16[192,1536]{1,0:T(8,128)(2,1)}, u32[]{:S(2)}, u32[]{:S(2)}) collective-permute-start(bf16[192,1536]{1,0:T(8,128)(2,1)} %convolution_convert_fusion.1), channel_id=1, source_target_pairs={{0,4},{4,8},{8,12},{12,16},{16,20},{20,24},{24,28},{1,5},{5,9},{9,... | collective-permute-start | bytes 1769480 | tf_op jit(solution)/shard_map/ppermute | solution.py:18
  140.4 2.0 constant_dynamic-update-slice_fusion.14
  142.3 2.4 collective-permute-start.11
  146.1 2.1 collective-permute-start.10
  148.2 2.2 copy.105
  150.4 2.1 constant_dynamic-update-slice_fusion.19
  153.5 1.9 constant_dynamic-update-slice_fusion.13
  155.4 1.9 constant_dynamic-update-slice_fusion.12
  158.3 16.4 %collective-permute-done.10 = bf16[192,1536]{1,0:T(8,128)(2,1)} collective-permute-done((bf16[192,1536]{1,0:T(8,128)(2,1)}, bf16[192,1536]{1,0:T(8,128)(2,1)}, u32[]{:S(2)}, u32[]{:S(2)}) %collective-permute-start.10) | collective-permute-done | bytes 589856 | tf_op jit(solution)/shard_map/ppermute | solution.py:18
  174.7 2.0 constant_dynamic-update-slice_fusion.11
  181.2 2.0 constant_dynamic-update-slice_fusion.10.refs_2_
  183.2 43.6 %shard_map.64 = bf16[16,128,192]{2,1,0:T(8,128)(2,1)} custom-call(s32[16]{0:T(128)} %convert_reduce_fusion.count, s32[16,20]{1,0:T(8,128)} %broadcast_select_fusion.1.source, s32[16,20]{1,0:T(8,128)} %get-tuple-element.8.rows, bf16[16,128,192]{2,1,0:T(8,128)(2,1)} %bitcast.52, bf16[192,2560]{1,0:T(8,128)(2,1)} %constant_dynamic-update-slice_fusion.refs_0_, ...), custom_call_target="tpu_custom_call" | custom-call | tf_op jit(solution)/shard_map/pallas_call | solution.py:93
  226.9 1.4 copy.112
  228.8 22.4 %all_to_all.19 = bf16[4,512,192]{1,2,0:T(8,128)(2,1)S(1)} all-to-all(bf16[4,512,192]{1,2,0:T(8,128)(2,1)S(1)} %bitcast.55), channel_id=1, replica_groups=mesh['seq'=8,'head'=4] {'head'}, dimensions={0} | all-to-all | bytes 1572864 | tf_op jit(solution)/shard_map/all_to_all | solution.py:194
  251.2 1.7 convolution_convert_fusion.2
  (89 shorter events, 30.1 us)
Async XLA Ops:
  6.5 244.7 %copy-start = (bf16[768,768]{1,0:T(8,128)(2,1)S(1)}, bf16[768,768]{1,0:T(8,128)(2,1)}, u32[]{:S(2)}) copy-start(bf16[768,768]{1,0:T(8,128)(2,1)} %param.10) | copy-start | bytes 3538948
  6.5 67.2 %all-gather.2.cloned.1.call-start = ((), (), s32[]{:S(2)}) async-start(), calls=%async_computation.1 | async-start | bytes 3932160 | tf_op jit(solution)/shard_map/all_gather | solution.py:143
  7.3 3.3 %copy-start.1 = (bf16[512,768]{1,0:T(8,128)(2,1)S(1)}, bf16[512,768]{1,0:T(8,128)(2,1)}, u32[]{:S(2)}) copy-start(bf16[512,768]{1,0:T(8,128)(2,1)} %param.8) | copy-start | bytes 2359300
  10.6 12.5 %copy-start.2 = (bf16[768,1,768]{2,0,1:T(8,128)(2,1)}, bf16[768,1,768]{2,0,1:T(8,128)(2,1)S(1)}, u32[]{:S(2)}) copy-start(bf16[768,1,768]{2,0,1:T(8,128)(2,1)S(1)} %get-tuple-element.12) | copy-start | bytes 3538948
  10.6 18.7 %copy-start.6 = (s32[16]{0:T(128)S(1)}, s32[16]{0:T(128)}, u32[]{:S(2)}) copy-start(s32[16]{0:T(128)} %param.12) | copy-start | bytes 196
  10.6 18.9 %copy-start.5 = (s32[16,8]{0,1:T(8,128)S(1)}, s32[16,8]{0,1:T(8,128)}, u32[]{:S(2)}) copy-start(s32[16,8]{0,1:T(8,128)} %param.13) | copy-start | bytes 1540
  10.6 19.1 %copy-start.4 = (s32[16,12]{1,0:T(8,128)S(1)}, s32[16,12]{1,0:T(8,128)}, u32[]{:S(2)}) copy-start(s32[16,12]{1,0:T(8,128)} %param.11) | copy-start | bytes 2308
  12.0 42.6 %collective-permute-start.3 = (bf16[192,512]{1,0:T(8,128)(2,1)}, bf16[192,512]{1,0:T(8,128)(2,1)}, u32[]{:S(2)}, u32[]{:S(2)}) collective-permute-start(bf16[192,512]{1,0:T(8,128)(2,1)} %convolution_convert_fusion.4), channel_id=1, source_target_pairs={{8,0},{12,4},{16,8},{20,12},{24,16},{28,20},{9,1},{13,5},{17,9},{2... | collective-permute-start | bytes 589832 | tf_op jit(solution)/shard_map/ppermute | solution.py:18
  13.9 39.1 %collective-permute-start.2 = (bf16[192,512]{1,0:T(8,128)(2,1)}, bf16[192,512]{1,0:T(8,128)(2,1)}, u32[]{:S(2)}, u32[]{:S(2)}) collective-permute-start(bf16[192,512]{1,0:T(8,128)(2,1)} %convolution_convert_fusion.4), channel_id=1, source_target_pairs={{4,0},{8,4},{12,8},{16,12},{20,16},{24,20},{28,24},{5,1},{9,5},{13... | collective-permute-start | bytes 589832 | tf_op jit(solution)/shard_map/ppermute | solution.py:18
  15.8 33.8 %collective-permute-start.1 = (bf16[192,512]{1,0:T(8,128)(2,1)}, bf16[192,512]{1,0:T(8,128)(2,1)}, u32[]{:S(2)}, u32[]{:S(2)}) collective-permute-start(bf16[192,512]{1,0:T(8,128)(2,1)} %convolution_convert_fusion.4), channel_id=1, source_target_pairs={{0,4},{4,8},{8,12},{12,16},{16,20},{20,24},{24,28},{1,5},{5,9},{9,... | collective-permute-start | bytes 589832 | tf_op jit(solution)/shard_map/ppermute | solution.py:18
  18.2 19.8 %collective-permute-start = (bf16[192,512]{1,0:T(8,128)(2,1)}, bf16[192,512]{1,0:T(8,128)(2,1)}, u32[]{:S(2)}, u32[]{:S(2)}) collective-permute-start(bf16[192,512]{1,0:T(8,128)(2,1)} %convolution_convert_fusion.4), channel_id=1, source_target_pairs={{0,8},{4,12},{8,16},{12,20},{16,24},{20,28},{1,9},{5,13},{9,17},{1... | collective-permute-start | bytes 589832 | tf_op jit(solution)/shard_map/ppermute | solution.py:18
  25.5 16.1 %collective-permute-start.4 = (bf16[512,192]{1,0:T(8,128)(2,1)S(1)}, bf16[512,192]{1,0:T(8,128)(2,1)}, u32[]{:S(2)}, u32[]{:S(2)}) collective-permute-start(bf16[512,192]{1,0:T(8,128)(2,1)S(1)} %bitcast.57), channel_id=1, source_target_pairs={{0,8},{4,12},{8,16},{12,20},{16,24},{20,28},{1,9},{5,13},{9,17},{1... | collective-permute-start | bytes 589832 | tf_op jit(solution)/shard_map/ppermute | solution.py:18
  38.0 8.3 %collective-permute-start.5 = (bf16[512,192]{1,0:T(8,128)(2,1)S(1)}, bf16[512,192]{1,0:T(8,128)(2,1)S(1)}, u32[]{:S(2)}, u32[]{:S(2)}) collective-permute-start(bf16[512,192]{1,0:T(8,128)(2,1)S(1)} %bitcast.58), channel_id=1, source_target_pairs={{0,4},{4,8},{8,12},{12,16},{16,20},{20,24},{24,28},{1,5},{5,9},{9,... | collective-permute-start | bytes 589832 | tf_op jit(solution)/shard_map/ppermute | solution.py:18
  41.6 15.4 %collective-permute-start.7 = (bf16[512,192]{1,0:T(8,128)(2,1)S(1)}, bf16[512,192]{1,0:T(8,128)(2,1)S(1)}, u32[]{:S(2)}, u32[]{:S(2)}) collective-permute-start(bf16[512,192]{1,0:T(8,128)(2,1)S(1)} %bitcast.59), channel_id=1, source_target_pairs={{8,0},{12,4},{16,8},{20,12},{24,16},{28,20},{9,1},{13,5},{17,9},{2... | collective-permute-start | bytes 589832 | tf_op jit(solution)/shard_map/ppermute | solution.py:18
  46.3 10.0 %collective-permute-start.6 = (bf16[512,192]{1,0:T(8,128)(2,1)S(1)}, bf16[512,192]{1,0:T(8,128)(2,1)S(1)}, u32[]{:S(2)}, u32[]{:S(2)}) collective-permute-start(bf16[512,192]{1,0:T(8,128)(2,1)S(1)} %bitcast.60), channel_id=1, source_target_pairs={{4,0},{8,4},{12,8},{16,12},{20,16},{24,20},{28,24},{5,1},{9,5},{13... | collective-permute-start | bytes 589832 | tf_op jit(solution)/shard_map/ppermute | solution.py:18
  77.7 2.0 copy-start.3
  81.6 60.7 %collective-permute-start.13 = (bf16[1536,192]{0,1:T(8,128)(2,1)}, bf16[1536,192]{0,1:T(8,128)(2,1)}, u32[]{:S(2)}, u32[]{:S(2)}) collective-permute-start(bf16[1536,192]{0,1:T(8,128)(2,1)} %convolution_convert_fusion), channel_id=1, source_target_pairs={{0,4},{4,8},{8,12},{12,16},{16,20},{20,24},{24,28},{1,5},{5,9},{9,... | collective-permute-start | bytes 1769480 | tf_op jit(solution)/shard_map/ppermute | solution.py:18
  83.5 62.6 %collective-permute-start.12 = (bf16[1536,192]{0,1:T(8,128)(2,1)}, bf16[1536,192]{0,1:T(8,128)(2,1)}, u32[]{:S(2)}, u32[]{:S(2)}) collective-permute-start(bf16[1536,192]{0,1:T(8,128)(2,1)} %convolution_convert_fusion), channel_id=1, source_target_pairs={{0,8},{4,12},{8,16},{12,20},{16,24},{20,28},{1,9},{5,13},{9,17},{1... | collective-permute-start | bytes 1769480 | tf_op jit(solution)/shard_map/ppermute | solution.py:18
  88.3 22.1 %collective-permute-start.19 = (bf16[1,128,192]{1,2,0:T(8,128)(2,1)S(1)}, bf16[1,128,192]{1,2,0:T(8,128)(2,1)S(1)}, u32[]{:S(2)}, u32[]{:S(2)}) collective-permute-start(bf16[1,128,192]{1,2,0:T(8,128)(2,1)S(1)} %fusion.9), channel_id=1, source_target_pairs={{0,4},{4,8},{8,12},{12,16},{16,20},{20,24},{24,28},{28,0},{1,5},{5... | collective-permute-start | bytes 147464 | tf_op jit(solution)/shard_map/ppermute | solution.py:28
  91.0 21.8 %collective-permute-start.16 = (bf16[1,192,128]{2,1,0:T(8,128)(2,1)S(1)}, bf16[1,192,128]{2,1,0:T(8,128)(2,1)S(1)}, u32[]{:S(2)}, u32[]{:S(2)}) collective-permute-start(bf16[1,192,128]{2,1,0:T(8,128)(2,1)S(1)} %fusion.8), channel_id=1, source_target_pairs={{0,4},{4,8},{8,12},{12,16},{16,20},{20,24},{24,28},{28,0},{1,5},{5... | collective-permute-start | bytes 147464 | tf_op jit(solution)/shard_map/ppermute | solution.py:28
  91.4 46.3 %collective-permute-start.8 = (bf16[192,1536]{1,0:T(8,128)(2,1)}, bf16[192,1536]{1,0:T(8,128)(2,1)}, u32[]{:S(2)}, u32[]{:S(2)}) collective-permute-start(bf16[192,1536]{1,0:T(8,128)(2,1)} %convolution_convert_fusion.1), channel_id=1, source_target_pairs={{0,8},{4,12},{8,16},{12,20},{16,24},{20,28},{1,9},{5,13},{9,17},{1... | collective-permute-start | bytes 1769480 | tf_op jit(solution)/shard_map/ppermute | solution.py:18
  110.5 6.2 %collective-permute-start.20 = (bf16[2,128,192]{1,2,0:T(8,128)(2,1)S(1)}, bf16[2,128,192]{1,2,0:T(8,128)(2,1)S(1)}, u32[]{:S(2)}, u32[]{:S(2)}) collective-permute-start(bf16[2,128,192]{1,2,0:T(8,128)(2,1)S(1)} %pad_maximum_fusion.4), channel_id=1, source_target_pairs={{0,8},{4,12},{8,16},{12,20},{16,24},{20,28},{24,0},{28,4},{1,9},{5... | collective-permute-start | bytes 294920 | tf_op jit(solution)/shard_map/ppermute | solution.py:28
  112.9 5.9 %collective-permute-start.17 = (bf16[2,192,128]{2,1,0:T(8,128)(2,1)S(1)}, bf16[2,192,128]{2,1,0:T(8,128)(2,1)S(1)}, u32[]{:S(2)}, u32[]{:S(2)}) collective-permute-start(bf16[2,192,128]{2,1,0:T(8,128)(2,1)S(1)} %pad_maximum_fusion.3), channel_id=1, source_target_pairs={{0,8},{4,12},{8,16},{12,20},{16,24},{20,28},{24,0},{28,4},{1,9},{5... | collective-permute-start | bytes 294920 | tf_op jit(solution)/shard_map/ppermute | solution.py:28
  117.3 7.9 %collective-permute-start.21 = (bf16[4,128,192]{1,2,0:T(8,128)(2,1)}, bf16[4,128,192]{1,2,0:T(8,128)(2,1)}, u32[]{:S(2)}, u32[]{:S(2)}) collective-permute-start(bf16[4,128,192]{1,2,0:T(8,128)(2,1)} %pad_maximum_fusion.2), channel_id=1, source_target_pairs={{0,16},{4,20},{8,24},{12,28},{16,0},{20,4},{24,8},{28,12},{1,17},{... | collective-permute-start | bytes 589832 | tf_op jit(solution)/shard_map/ppermute | solution.py:28
  118.8 12.3 %collective-permute-start.18 = (bf16[4,192,128]{2,1,0:T(8,128)(2,1)S(1)}, bf16[4,192,128]{2,1,0:T(8,128)(2,1)}, u32[]{:S(2)}, u32[]{:S(2)}) collective-permute-start(bf16[4,192,128]{2,1,0:T(8,128)(2,1)S(1)} %pad_maximum_fusion.1), channel_id=1, source_target_pairs={{0,16},{4,20},{8,24},{12,28},{16,0},{20,4},{24,8},{28,12},{1,17},{... | collective-permute-start | bytes 589832 | tf_op jit(solution)/shard_map/ppermute | solution.py:28
  125.3 51.4 %collective-permute-start.15 = (bf16[1536,192]{0,1:T(8,128)(2,1)}, bf16[1536,192]{0,1:T(8,128)(2,1)}, u32[]{:S(2)}, u32[]{:S(2)}) collective-permute-start(bf16[1536,192]{0,1:T(8,128)(2,1)} %convolution_convert_fusion), channel_id=1, source_target_pairs={{8,0},{12,4},{16,8},{20,12},{24,16},{28,20},{9,1},{13,5},{17,9},{2... | collective-permute-start | bytes 1769480 | tf_op jit(solution)/shard_map/ppermute | solution.py:18
  131.1 46.9 %collective-permute-start.14 = (bf16[1536,192]{0,1:T(8,128)(2,1)}, bf16[1536,192]{0,1:T(8,128)(2,1)}, u32[]{:S(2)}, u32[]{:S(2)}) collective-permute-start(bf16[1536,192]{0,1:T(8,128)(2,1)} %convolution_convert_fusion), channel_id=1, source_target_pairs={{4,0},{8,4},{12,8},{16,12},{20,16},{24,20},{28,24},{5,1},{9,5},{13... | collective-permute-start | bytes 1769480 | tf_op jit(solution)/shard_map/ppermute | solution.py:18
  137.7 15.8 %collective-permute-start.9 = (bf16[192,1536]{1,0:T(8,128)(2,1)}, bf16[192,1536]{1,0:T(8,128)(2,1)}, u32[]{:S(2)}, u32[]{:S(2)}) collective-permute-start(bf16[192,1536]{1,0:T(8,128)(2,1)} %convolution_convert_fusion.1), channel_id=1, source_target_pairs={{0,4},{4,8},{8,12},{12,16},{16,20},{20,24},{24,28},{1,5},{5,9},{9,... | collective-permute-start | bytes 1769480 | tf_op jit(solution)/shard_map/ppermute | solution.py:18
  142.3 38.9 %collective-permute-start.11 = (bf16[192,1536]{1,0:T(8,128)(2,1)}, bf16[192,1536]{1,0:T(8,128)(2,1)}, u32[]{:S(2)}, u32[]{:S(2)}) collective-permute-start(bf16[192,1536]{1,0:T(8,128)(2,1)} %convolution_convert_fusion.1), channel_id=1, source_target_pairs={{8,0},{12,4},{16,8},{20,12},{24,16},{28,20},{9,1},{13,5},{17,9},{2... | collective-permute-start | bytes 1769480 | tf_op jit(solution)/shard_map/ppermute | solution.py:18
  146.1 28.7 %collective-permute-start.10 = (bf16[192,1536]{1,0:T(8,128)(2,1)}, bf16[192,1536]{1,0:T(8,128)(2,1)}, u32[]{:S(2)}, u32[]{:S(2)}) collective-permute-start(bf16[192,1536]{1,0:T(8,128)(2,1)} %convolution_convert_fusion.1), channel_id=1, source_target_pairs={{4,0},{8,4},{12,8},{16,12},{20,16},{24,20},{28,24},{5,1},{9,5},{13... | collective-permute-start | bytes 1769480 | tf_op jit(solution)/shard_map/ppermute | solution.py:18
Sparse Core Ops, SparseCore 0:
  8.9 64.7 all-gather.1

commit v5 on v4

--- a/solution.py
+++ b/solution.py
@@ -32,8 +32,8 @@
 
 
 def attention_kernel(count, source, rows, q_ref, *refs, heads, widths, scale):
-    tables = refs[:6]
-    o_ref, kt_ref, v_ref = refs[6:]
+    tables = refs[:-3]
+    o_ref, kt_ref, v_ref = refs[-3:]
     b = pl.program_id(0)
     used = count[b]
 
@@ -45,7 +45,7 @@
     def fetch(j, carry):
         at = pl.multiple_of(j * BLK, BLK)
         row = rows[b, j]
-        for code in range(3):
+        for code in range(len(tables) // 2):
             @pl.when(source[b, j] == code)
             def _():
                 start = pl.multiple_of(row * BLK, BLK)
@@ -129,6 +129,9 @@
     width_here = D // head_count
     own_rows = tokens.shape[0]
     own_blocks = own_rows // BLK
+    parts = 2 if own_blocks % 2 == 0 else 1
+    part_rows = own_rows // parts
+    part_blocks = own_blocks // parts
     row_count = own_rows * head_count
     block_count = row_count // BLK
     neigh = neighbours.shape[1]
@@ -138,12 +141,20 @@
     value_w = lax.dynamic_slice_in_dim(w_qkv[:, 2], col_start, width_here, 1)
 
     k_own, v_own = project_kv(tokens, key_w, value_w)
-    ka, va = window_of(k_own, 1), window_of(v_own, 0)
-
-    gathered = lax.all_gather(tokens, "head", axis=0, tiled=True)
-    rest_tokens = jnp.roll(gathered, -head_rank * own_rows, axis=0)[own_rows:]
-    k_rest, v_rest = project_kv(rest_tokens, key_w, value_w)
-    kb, vb = window_of(k_rest, 1), window_of(v_rest, 0)
+    tables = [window_of(k_own, 1), window_of(v_own, 0)]
+
+    rest_parts = []
+    first_rows = None
+    for p in range(parts):
+        piece = tokens[p * part_rows:(p + 1) * part_rows]
+        gathered = lax.all_gather(piece, "head", axis=0, tiled=True)
+        if p == 0:
+            first_rows = gathered[:BLK]
+        rest = jnp.roll(gathered, -head_rank * part_rows, axis=0)[part_rows:]
+        k_rest, v_rest = project_kv(rest, key_w, value_w)
+        tables += [window_of(k_rest, 1), window_of(v_rest, 0)]
+        rest_parts.append(rest.reshape(head_count - 1, part_rows, D))
+    rest_tokens = jnp.concatenate(rest_parts, axis=1).reshape((head_count - 1) * own_rows, D)
     rolled_tokens = jnp.concatenate([tokens, rest_tokens], axis=0)
     queries = jnp.dot(rolled_tokens, query_w, preferred_element_type=jnp.float32).astype(
         jnp.bfloat16
@@ -151,12 +162,13 @@
 
     seq_count = lax.axis_size("seq")
     seq_rank = lax.axis_index("seq")
-    k_first, v_first = project_kv(gathered[:BLK], key_w, value_w)
+    k_first, v_first = project_kv(first_rows, key_w, value_w)
     kanc = gather_all(k_first, "seq")
     vanc = gather_all(v_first, "seq")
     held_count = kanc.shape[0]
     kanc = jnp.transpose(kanc, (1, 0, 2)).reshape(width_here, held_count * BLK)
     vanc = vanc.reshape(held_count * BLK, width_here)
+    tables += [kanc, vanc]
     first_block = (seq_rank - 2) * block_count
 
     shift = -head_rank * own_blocks
@@ -171,10 +183,10 @@
     inner = within % own_blocks
     mine = chunk == head_rank
     row_a = offset_idx * own_blocks + inner
-    row_b = (offset_idx * (block_count - own_blocks)
-             + ((chunk - head_rank) % head_count - 1) * own_blocks + inner)
+    row_b = (offset_idx * (head_count - 1) * part_blocks
+             + ((chunk - head_rank) % head_count - 1) * part_blocks + inner % part_blocks)
     near_row = jnp.where(mine, row_a, row_b)
-    near_src = jnp.where(mine, 0, 1)
+    near_src = jnp.where(mine, 0, 1 + inner // part_blocks)
     owner = jnp.clip(anchors // block_count, 0, seq_count - 1)
     anch_row = (owner - seq_rank + held_count - 1) % seq_count
     near_used = jnp.arange(neigh)[None, :] < near_count[:, None]
@@ -184,12 +196,12 @@
     valid = jnp.concatenate([near_used, jnp.logical_not(repeated)], axis=1)
     order = jnp.argsort(jnp.logical_not(valid).astype(jnp.int32), axis=1, stable=True)
     every_row = jnp.concatenate([near_row, anch_row], axis=1)
-    every_src = jnp.concatenate([near_src, jnp.full_like(anch_row, 2)], axis=1)
+    every_src = jnp.concatenate([near_src, jnp.full_like(anch_row, 1 + parts)], axis=1)
     rows = jnp.take_along_axis(every_row, order, axis=1).astype(jnp.int32)
     source = jnp.take_along_axis(every_src, order, axis=1).astype(jnp.int32)
     count = jnp.sum(valid.astype(jnp.int32), axis=1).astype(jnp.int32)
 
-    attended = attention(queries, (ka, va, kb, vb, kanc, vanc), count, source, rows)
+    attended = attention(queries, tuple(tables), count, source, rows)
     attended = jnp.roll(attended.reshape(row_count, width_here), head_rank * own_rows, axis=0)
     mine_rows = lax.all_to_all(attended, "head", 0, 1, tiled=True)
     mixed_out = jnp.dot(mine_rows, w_out, preferred_element_type=jnp.float32).astype(

time: 264 us -> 297 us (1.12)
  starting transfers between devices: 52.8 us -> 81.2 us
  waiting for transfers between devices: 53 us -> 60.6 us
  local copies, waits for them, and re-layouts: 49.9 us -> 42.8 us
  matrix products: 13.4 us -> 17.5 us
    ppermute x16 -> x24, starting transfers between devices: 44.7 us -> 65.7 us  [shifted(): return lax.ppermute(x, axis, pairs)]
    ppermute x16 -> x24, waiting for transfers between devices: 16.5 us -> 28.5 us  [shifted(): return lax.ppermute(x, axis, pairs)]
    ppermute x6, starting transfers between devices: 8.09 us -> 15.4 us  [gather_all(): got = lax.ppermute(held, axis, pairs)]
    ppermute x6, waiting for transfers between devices: 19.8 us -> 13.6 us  [gather_all(): got = lax.ppermute(held, axis, pairs)]
    ppermute x4 -> x0, local copies, waits for them, and re-layouts: 6.22 us -> none  [shifted(): return lax.ppermute(x, axis, pairs)]
    all_gather x1 -> x2, waiting for transfers between devices: 16 us -> 18.4 us  [shards(): gathered = lax.all_gather(piece, 'head', axis=0, tiled=True)]
    dot_general x3 -> x4, matrix products: 4.76 us -> 6.94 us  [project_kv(): lax.dot_general(key_w, x, (((0,), (1,)), ((), ())), preferred_element_typ...]
    dot_general x3 -> x4, matrix products: 4.6 us -> 6.49 us  [project_kv(): jnp.dot(x, value_w, preferred_element_type=jnp.float32).astype(jnp.bfloat16)]
  transfers between devices with their start and end apart: 23 -> 32, of which waited for: 4 -> 15; matrix products, arithmetic and copies ran while one was open for 23% -> 20% of each run, Pallas kernels for 0% -> 0%
where the time goes in v5:
time: 297 us; the launch traced here: 293 us
  starting transfers between devices  81.2 us (27%)
  waiting for transfers between devices  60.6 us (20%)
  Pallas kernels  43.7 us (15%)
  local copies, waits for them, and re-layouts  42.8 us (14%)
  blocking collectives  22.4 us (8%)
  matrix products  17.5 us (6%)
  between operations  14 us (5%)
  other arithmetic  11.1 us (4%)
    ppermute x24, starting transfers between devices, shifted(): return lax.ppermute(x, axis, pairs)  65.7 us
    pallas_call x1, Pallas kernels, attention(): pl.pallas_call(kernel, out_shape=jax.ShapeDtypeStruct(queries.shape, jnp....  43.7 us
    ppermute x24, waiting for transfers between devices, shifted(): return lax.ppermute(x, axis, pairs)  28.5 us
    all_to_all x1, blocking collectives, shards(): mine_rows = lax.all_to_all(attended, 'head', 0, 1, tiled=True)  22.4 us
    unnamed x49, local copies, waits for them, and re-layouts  21.9 us
    all_gather x2, waiting for transfers between devices, shards(): gathered = lax.all_gather(piece, 'head', axis=0, tiled=True)  18.4 us
    ppermute x6, starting transfers between devices, gather_all(): got = lax.ppermute(held, axis, pairs)  15.4 us
    ppermute x6, waiting for transfers between devices, gather_all(): got = lax.ppermute(held, axis, pairs)  13.6 us
  transfers between devices with their start and end apart: 32, of which 15 were waited for; matrix products, arithmetic and copies ran while one was open for 20% of the time, Pallas kernels for 0%

profile of v5, /device:TPU:2, one launch (start us, length us, event | category | flops | bytes accessed | tf_op | source)
XLA Modules:
  0.0 293.2 jit_solution(10361348610662229837)
XLA Ops:
  6.5 2.1 fusion.65
  8.8 3.3 %fusion.64 = (bf16[768,1,768]{2,0,1:T(8,128)(2,1)S(1)}, bf16[768,1,768]{2,0,1:T(8,128)(2,1)}, bf16[768,1,768]{2,0,1:T(8,128)(2,1)S(1)}) fusion(bf16[768,3,768]{2,0,1:T(8,128)(2,1)} %param.11), kind=kLoop, calls=%fused_computation.164 | loop fusion | bytes 7077888 | tf_op jit(solution)/shard_map/slice | solution.py:141
  13.6 2.0 collective-permute-start.3
  15.6 1.9 collective-permute-start.2
  17.6 2.4 collective-permute-start.1
  20.0 4.8 %collective-permute-start = (bf16[192,512]{1,0:T(8,128)(2,1)}, bf16[192,512]{1,0:T(8,128)(2,1)}, u32[]{:S(2)}, u32[]{:S(2)}) collective-permute-start(bf16[192,512]{1,0:T(8,128)(2,1)} %convolution_convert_fusion.6), channel_id=1, source_target_pairs={{0,8},{4,12},{8,16},{12,20},{16,24},{20,28},{1,9},{5,13},{9,17},{1... | collective-permute-start | bytes 589832 | tf_op jit(solution)/shard_map/ppermute | solution.py:18
  27.2 3.8 %collective-permute-start.4 = (bf16[512,192]{1,0:T(8,128)(2,1)S(1)}, bf16[512,192]{1,0:T(8,128)(2,1)S(1)}, u32[]{:S(2)}, u32[]{:S(2)}) collective-permute-start(bf16[512,192]{1,0:T(8,128)(2,1)S(1)} %bitcast.69), channel_id=1, source_target_pairs={{0,8},{4,12},{8,16},{12,20},{16,24},{20,28},{1,9},{5,13},{9,17},{1... | collective-permute-start | bytes 589832 | tf_op jit(solution)/shard_map/ppermute | solution.py:18
  32.9 2.5 gather_fusion.1
  35.4 2.5 gather_fusion
  39.9 1.9 collective-permute-start.5
  43.5 2.3 collective-permute-start.7
  47.6 1.9 collective-permute-start.6
  59.0 2.4 fusion.8
  61.5 2.6 convolution_convert_fusion.4
  64.0 2.4 convolution_convert_fusion.2
  66.4 18.4 %all-gather.5.cloned.1.call-done = bf16[1024,768]{1,0:T(8,128)(2,1)} async-done(((bf16[256,768]{1,0:T(8,128)(2,1)}), bf16[1024,768]{1,0:T(8,128)(2,1)}) %all-gather.5.cloned.1.call-update) | async-done | bytes 1572880 | tf_op jit(solution)/shard_map/all_gather | solution.py:150
  84.8 2.5 fusion.7
  90.2 2.5 collective-permute-start.11
  92.7 1.9 collective-permute-start.10
  94.6 2.4 collective-permute-start.13
  97.0 4.3 %collective-permute-start.12 = (bf16[768,192]{1,0:T(8,128)(2,1)}, bf16[768,192]{1,0:T(8,128)(2,1)}, u32[]{:S(2)}, u32[]{:S(2)}) collective-permute-start(bf16[768,192]{1,0:T(8,128)(2,1)} %convolution_convert_fusion.2), channel_id=1, source_target_pairs={{0,8},{4,12},{8,16},{12,20},{16,24},{20,28},{1,9},{5,13},{9,17},{1... | collective-permute-start | bytes 884744 | tf_op jit(solution)/shard_map/ppermute | solution.py:18
  103.5 2.3 fusion.4
  108.6 4.3 %collective-permute-done.27 = bf16[1,128,192]{1,2,0:T(8,128)(2,1)S(1)} collective-permute-done((bf16[1,128,192]{1,2,0:T(8,128)(2,1)S(1)}, bf16[1,128,192]{1,2,0:T(8,128)(2,1)S(1)}, u32[]{:S(2)}, u32[]{:S(2)}) %collective-permute-start.27) | collective-permute-done | bytes 49184 | tf_op jit(solution)/shard_map/ppermute | solution.py:28
  112.9 2.6 collective-permute-start.24
  116.4 6.8 %collective-permute-start.28 = (bf16[2,128,192]{1,2,0:T(8,128)(2,1)S(1)}, bf16[2,128,192]{1,2,0:T(8,128)(2,1)S(1)}, u32[]{:S(2)}, u32[]{:S(2)}) collective-permute-start(bf16[2,128,192]{1,2,0:T(8,128)(2,1)S(1)} %pad_maximum_fusion.5), channel_id=1, source_target_pairs={{0,8},{4,12},{8,16},{12,20},{16,24},{20,28},{24,0},{28,4},{1,9},{5... | collective-permute-start | bytes 294920 | tf_op jit(solution)/shard_map/ppermute | solution.py:28
  123.1 2.2 collective-permute-done.28
  125.3 3.3 %collective-permute-start.25 = (bf16[2,192,128]{2,1,0:T(8,128)(2,1)S(1)}, bf16[2,192,128]{2,1,0:T(8,128)(2,1)S(1)}, u32[]{:S(2)}, u32[]{:S(2)}) collective-permute-start(bf16[2,192,128]{2,1,0:T(8,128)(2,1)S(1)} %pad_maximum_fusion.4), channel_id=1, source_target_pairs={{0,8},{4,12},{8,16},{12,20},{16,24},{20,28},{24,0},{28,4},{1,9},{5... | collective-permute-start | bytes 294920 | tf_op jit(solution)/shard_map/ppermute | solution.py:28
  128.7 2.2 collective-permute-done.25
  130.9 1.9 collective-permute-start.21
  133.5 5.2 %collective-permute-start.20 = (bf16[768,192]{1,0:T(8,128)(2,1)S(1)}, bf16[768,192]{1,0:T(8,128)(2,1)S(1)}, u32[]{:S(2)}, u32[]{:S(2)}) collective-permute-start(bf16[768,192]{1,0:T(8,128)(2,1)S(1)} %copy-done.8), channel_id=1, source_target_pairs={{0,8},{4,12},{8,16},{12,20},{16,24},{20,28},{1,9},{5,13},{9,17},{1... | collective-permute-start | bytes 884744 | tf_op jit(solution)/shard_map/ppermute | solution.py:18
  139.8 2.1 collective-permute-start.15
  143.9 4.4 %collective-permute-done.20 = bf16[768,192]{1,0:T(8,128)(2,1)S(1)} collective-permute-done((bf16[768,192]{1,0:T(8,128)(2,1)S(1)}, bf16[768,192]{1,0:T(8,128)(2,1)S(1)}, u32[]{:S(2)}, u32[]{:S(2)}) %collective-permute-start.20) | collective-permute-done | bytes 294944 | tf_op jit(solution)/shard_map/ppermute | solution.py:18
  148.3 1.9 collective-permute-start.14
  151.0 6.3 %collective-permute-start.16 = (bf16[192,768]{1,0:T(8,128)(2,1)}, bf16[192,768]{1,0:T(8,128)(2,1)S(1)}, u32[]{:S(2)}, u32[]{:S(2)}) collective-permute-start(bf16[192,768]{1,0:T(8,128)(2,1)} %convolution_convert_fusion.3), channel_id=1, source_target_pairs={{0,8},{4,12},{8,16},{12,20},{16,24},{20,28},{1,9},{5,13},{9,17},{1... | collective-permute-start | bytes 884744 | tf_op jit(solution)/shard_map/ppermute | solution.py:18
  158.9 6.2 %collective-permute-done.14 = bf16[768,192]{1,0:T(8,128)(2,1)S(1)} collective-permute-done((bf16[768,192]{1,0:T(8,128)(2,1)}, bf16[768,192]{1,0:T(8,128)(2,1)S(1)}, u32[]{:S(2)}, u32[]{:S(2)}) %collective-permute-start.14) | collective-permute-done | bytes 294944 | tf_op jit(solution)/shard_map/ppermute | solution.py:18
  165.1 1.9 collective-permute-start.17
  167.1 1.9 collective-permute-start.9
  170.2 2.5 collective-permute-start.22
  173.4 4.0 %collective-permute-start.8 = (bf16[192,768]{1,0:T(8,128)(2,1)}, bf16[192,768]{1,0:T(8,128)(2,1)S(1)}, u32[]{:S(2)}, u32[]{:S(2)}) collective-permute-start(bf16[192,768]{1,0:T(8,128)(2,1)} %convolution_convert_fusion.4), channel_id=1, source_target_pairs={{0,8},{4,12},{8,16},{12,20},{16,24},{20,28},{1,9},{5,13},{9,17},{1... | collective-permute-start | bytes 884744 | tf_op jit(solution)/shard_map/ppermute | solution.py:18
  179.1 1.9 collective-permute-start.19
  181.8 3.3 %collective-permute-done.8 = bf16[192,768]{1,0:T(8,128)(2,1)S(1)} collective-permute-done((bf16[192,768]{1,0:T(8,128)(2,1)}, bf16[192,768]{1,0:T(8,128)(2,1)S(1)}, u32[]{:S(2)}, u32[]{:S(2)}) %collective-permute-start.8) | collective-permute-done | bytes 294944 | tf_op jit(solution)/shard_map/ppermute | solution.py:18
  187.8 1.9 collective-permute-start.23
  192.3 4.8 %collective-permute-done.18 = bf16[192,768]{1,0:T(8,128)(2,1)S(1)} collective-permute-done((bf16[192,768]{1,0:T(8,128)(2,1)}, bf16[192,768]{1,0:T(8,128)(2,1)S(1)}, u32[]{:S(2)}, u32[]{:S(2)}) %collective-permute-start.18) | collective-permute-done | bytes 294944 | tf_op jit(solution)/shard_map/ppermute | solution.py:18
  197.1 2.1 collective-permute-start.29
  199.2 6.3 %collective-permute-done.23 = bf16[768,192]{1,0:T(8,128)(2,1)S(1)} collective-permute-done((bf16[768,192]{1,0:T(8,128)(2,1)S(1)}, bf16[768,192]{1,0:T(8,128)(2,1)S(1)}, u32[]{:S(2)}, u32[]{:S(2)}) %collective-permute-start.23) | collective-permute-done | bytes 294944 | tf_op jit(solution)/shard_map/ppermute | solution.py:18
  209.7 4.0 %collective-permute-done.29 = bf16[4,128,192]{1,2,0:T(8,128)(2,1)S(1)} collective-permute-done((bf16[4,128,192]{1,2,0:T(8,128)(2,1)S(1)}, bf16[4,128,192]{1,2,0:T(8,128)(2,1)S(1)}, u32[]{:S(2)}, u32[]{:S(2)}) %collective-permute-start.29) | collective-permute-done | bytes 196640 | tf_op jit(solution)/shard_map/ppermute | solution.py:28
  216.6 43.7 %shard_map.64 = bf16[16,128,192]{2,1,0:T(8,128)(2,1)} custom-call(s32[16]{0:T(128)} %convert_reduce_fusion.count, s32[16,20]{1,0:T(8,128)} %broadcast_select_fusion.1.source, s32[16,20]{1,0:T(8,128)} %get-tuple-element.9.rows, bf16[16,128,192]{2,1,0:T(8,128)(2,1)} %bitcast.63, bf16[192,2560]{1,0:T(8,128)(2,1)} %constant_dynamic-update-slice_fusion.refs_0_, ...), custom_call_target="tpu_custom_call" | custom-call | tf_op jit(solution)/shard_map/pallas_call | solution.py:93
  262.2 22.4 %all_to_all.19 = bf16[4,512,192]{1,2,0:T(8,128)(2,1)S(1)} all-to-all(bf16[4,512,192]{1,2,0:T(8,128)(2,1)S(1)} %bitcast.66), channel_id=1, replica_groups=mesh['seq'=8,'head'=4] {'head'}, dimensions={0} | all-to-all | bytes 1572864 | tf_op jit(solution)/shard_map/all_to_all | solution.py:206
  (128 shorter events, 55.9 us)
Async XLA Ops:
  6.5 278.1 %copy-start = (bf16[768,768]{1,0:T(8,128)(2,1)S(1)}, bf16[768,768]{1,0:T(8,128)(2,1)}, u32[]{:S(2)}) copy-start(bf16[768,768]{1,0:T(8,128)(2,1)} %param.12) | copy-start | bytes 3538948
  6.5 52.5 %all-gather.3.cloned.1.call-start = ((), (), s32[]{:S(2)}) async-start(), calls=%async_computation.1 | async-start | bytes 1966080 | tf_op jit(solution)/shard_map/all_gather | solution.py:150
  8.7 76.1 %all-gather.5.cloned.1.call-start = ((), (), s32[]{:S(2)}) async-start(), calls=%async_computation.2 | async-start | bytes 1966080 | tf_op jit(solution)/shard_map/all_gather | solution.py:150
  8.8 3.4 %copy-start.1 = (bf16[512,768]{1,0:T(8,128)(2,1)S(1)}, bf16[512,768]{1,0:T(8,128)(2,1)}, u32[]{:S(2)}) copy-start(bf16[512,768]{1,0:T(8,128)(2,1)} %param.10) | copy-start | bytes 2359300
  12.1 12.7 %copy-start.4 = (bf16[768,1,768]{2,0,1:T(8,128)(2,1)}, bf16[768,1,768]{2,0,1:T(8,128)(2,1)S(1)}, u32[]{:S(2)}) copy-start(bf16[768,1,768]{2,0,1:T(8,128)(2,1)S(1)} %get-tuple-element.13) | copy-start | bytes 3538948
  12.1 15.1 %copy-start.2 = (bf16[768,1,768]{2,0,1:T(8,128)(2,1)}, bf16[768,1,768]{2,0,1:T(8,128)(2,1)S(1)}, u32[]{:S(2)}) copy-start(bf16[768,1,768]{2,0,1:T(8,128)(2,1)S(1)} %get-tuple-element.15) | copy-start | bytes 3538948
  13.6 17.6 %copy-start.9 = (s32[16,12]{1,0:T(8,128)S(1)}, s32[16,12]{1,0:T(8,128)}, u32[]{:S(2)}) copy-start(s32[16,12]{1,0:T(8,128)} %param.13) | copy-start | bytes 2308
  13.6 17.7 %copy-start.11 = (s32[16]{0:T(128)S(1)}, s32[16]{0:T(128)}, u32[]{:S(2)}) copy-start(s32[16]{0:T(128)} %param.14) | copy-start | bytes 196
  13.6 17.9 %copy-start.10 = (s32[16,8]{0,1:T(8,128)S(1)}, s32[16,8]{0,1:T(8,128)}, u32[]{:S(2)}) copy-start(s32[16,8]{0,1:T(8,128)} %param.15) | copy-start | bytes 1540
  13.6 42.3 %collective-permute-start.3 = (bf16[192,512]{1,0:T(8,128)(2,1)}, bf16[192,512]{1,0:T(8,128)(2,1)}, u32[]{:S(2)}, u32[]{:S(2)}) collective-permute-start(bf16[192,512]{1,0:T(8,128)(2,1)} %convolution_convert_fusion.6), channel_id=1, source_target_pairs={{8,0},{12,4},{16,8},{20,12},{24,16},{28,20},{9,1},{13,5},{17,9},{2... | collective-permute-start | bytes 589832 | tf_op jit(solution)/shard_map/ppermute | solution.py:18
  15.6 38.6 %collective-permute-start.2 = (bf16[192,512]{1,0:T(8,128)(2,1)}, bf16[192,512]{1,0:T(8,128)(2,1)}, u32[]{:S(2)}, u32[]{:S(2)}) collective-permute-start(bf16[192,512]{1,0:T(8,128)(2,1)} %convolution_convert_fusion.6), channel_id=1, source_target_pairs={{4,0},{8,4},{12,8},{16,12},{20,16},{24,20},{28,24},{5,1},{9,5},{13... | collective-permute-start | bytes 589832 | tf_op jit(solution)/shard_map/ppermute | solution.py:18
  17.6 33.4 %collective-permute-start.1 = (bf16[192,512]{1,0:T(8,128)(2,1)}, bf16[192,512]{1,0:T(8,128)(2,1)}, u32[]{:S(2)}, u32[]{:S(2)}) collective-permute-start(bf16[192,512]{1,0:T(8,128)(2,1)} %convolution_convert_fusion.6), channel_id=1, source_target_pairs={{0,4},{4,8},{8,12},{12,16},{16,20},{20,24},{24,28},{1,5},{5,9},{9,... | collective-permute-start | bytes 589832 | tf_op jit(solution)/shard_map/ppermute | solution.py:18
  20.0 19.9 %collective-permute-start = (bf16[192,512]{1,0:T(8,128)(2,1)}, bf16[192,512]{1,0:T(8,128)(2,1)}, u32[]{:S(2)}, u32[]{:S(2)}) collective-permute-start(bf16[192,512]{1,0:T(8,128)(2,1)} %convolution_convert_fusion.6), channel_id=1, source_target_pairs={{0,8},{4,12},{8,16},{12,20},{16,24},{20,28},{1,9},{5,13},{9,17},{1... | collective-permute-start | bytes 589832 | tf_op jit(solution)/shard_map/ppermute | solution.py:18
  27.2 16.3 %collective-permute-start.4 = (bf16[512,192]{1,0:T(8,128)(2,1)S(1)}, bf16[512,192]{1,0:T(8,128)(2,1)S(1)}, u32[]{:S(2)}, u32[]{:S(2)}) collective-permute-start(bf16[512,192]{1,0:T(8,128)(2,1)S(1)} %bitcast.69), channel_id=1, source_target_pairs={{0,8},{4,12},{8,16},{12,20},{16,24},{20,28},{1,9},{5,13},{9,17},{1... | collective-permute-start | bytes 589832 | tf_op jit(solution)/shard_map/ppermute | solution.py:18
  39.9 7.7 %collective-permute-start.5 = (bf16[512,192]{1,0:T(8,128)(2,1)S(1)}, bf16[512,192]{1,0:T(8,128)(2,1)S(1)}, u32[]{:S(2)}, u32[]{:S(2)}) collective-permute-start(bf16[512,192]{1,0:T(8,128)(2,1)S(1)} %bitcast.70), channel_id=1, source_target_pairs={{0,4},{4,8},{8,12},{12,16},{16,20},{20,24},{24,28},{1,5},{5,9},{9,... | collective-permute-start | bytes 589832 | tf_op jit(solution)/shard_map/ppermute | solution.py:18
  43.5 14.8 %collective-permute-start.7 = (bf16[512,192]{1,0:T(8,128)(2,1)S(1)}, bf16[512,192]{1,0:T(8,128)(2,1)S(1)}, u32[]{:S(2)}, u32[]{:S(2)}) collective-permute-start(bf16[512,192]{1,0:T(8,128)(2,1)S(1)} %bitcast.71), channel_id=1, source_target_pairs={{8,0},{12,4},{16,8},{20,12},{24,16},{28,20},{9,1},{13,5},{17,9},{2... | collective-permute-start | bytes 589832 | tf_op jit(solution)/shard_map/ppermute | solution.py:18
  47.6 10.0 %collective-permute-start.6 = (bf16[512,192]{1,0:T(8,128)(2,1)S(1)}, bf16[512,192]{1,0:T(8,128)(2,1)S(1)}, u32[]{:S(2)}, u32[]{:S(2)}) collective-permute-start(bf16[512,192]{1,0:T(8,128)(2,1)S(1)} %bitcast.72), channel_id=1, source_target_pairs={{4,0},{8,4},{12,8},{16,12},{20,16},{24,20},{28,24},{5,1},{9,5},{13... | collective-permute-start | bytes 589832 | tf_op jit(solution)/shard_map/ppermute | solution.py:18
  84.8 2.5 copy-start.3
  87.4 1.5 copy-start.5
  90.2 117.8 %collective-permute-start.11 = (bf16[192,768]{1,0:T(8,128)(2,1)}, bf16[192,768]{1,0:T(8,128)(2,1)}, u32[]{:S(2)}, u32[]{:S(2)}) collective-permute-start(bf16[192,768]{1,0:T(8,128)(2,1)} %convolution_convert_fusion.4), channel_id=1, source_target_pairs={{8,0},{12,4},{16,8},{20,12},{24,16},{28,20},{9,1},{13,5},{17,9},{2... | collective-permute-start | bytes 884744 | tf_op jit(solution)/shard_map/ppermute | solution.py:18
  92.7 113.6 %collective-permute-start.10 = (bf16[192,768]{1,0:T(8,128)(2,1)}, bf16[192,768]{1,0:T(8,128)(2,1)}, u32[]{:S(2)}, u32[]{:S(2)}) collective-permute-start(bf16[192,768]{1,0:T(8,128)(2,1)} %convolution_convert_fusion.4), channel_id=1, source_target_pairs={{4,0},{8,4},{12,8},{16,12},{20,16},{24,20},{28,24},{5,1},{9,5},{13... | collective-permute-start | bytes 884744 | tf_op jit(solution)/shard_map/ppermute | solution.py:18
  94.6 45.2 %collective-permute-start.13 = (bf16[768,192]{1,0:T(8,128)(2,1)}, bf16[768,192]{1,0:T(8,128)(2,1)}, u32[]{:S(2)}, u32[]{:S(2)}) collective-permute-start(bf16[768,192]{1,0:T(8,128)(2,1)} %convolution_convert_fusion.2), channel_id=1, source_target_pairs={{0,4},{4,8},{8,12},{12,16},{16,20},{20,24},{24,28},{1,5},{5,9},{9,... | collective-permute-start | bytes 884744 | tf_op jit(solution)/shard_map/ppermute | solution.py:18
  97.0 36.5 %collective-permute-start.12 = (bf16[768,192]{1,0:T(8,128)(2,1)}, bf16[768,192]{1,0:T(8,128)(2,1)}, u32[]{:S(2)}, u32[]{:S(2)}) collective-permute-start(bf16[768,192]{1,0:T(8,128)(2,1)} %convolution_convert_fusion.2), channel_id=1, source_target_pairs={{0,8},{4,12},{8,16},{12,20},{16,24},{20,28},{1,9},{5,13},{9,17},{1... | collective-permute-start | bytes 884744 | tf_op jit(solution)/shard_map/ppermute | solution.py:18
  102.7 10.2 %collective-permute-start.27 = (bf16[1,128,192]{1,2,0:T(8,128)(2,1)S(1)}, bf16[1,128,192]{1,2,0:T(8,128)(2,1)S(1)}, u32[]{:S(2)}, u32[]{:S(2)}) collective-permute-start(bf16[1,128,192]{1,2,0:T(8,128)(2,1)S(1)} %fusion.10), channel_id=1, source_target_pairs={{0,4},{4,8},{8,12},{12,16},{16,20},{20,24},{24,28},{28,0},{1,5},{5... | collective-permute-start | bytes 147464 | tf_op jit(solution)/shard_map/ppermute | solution.py:28
  105.8 25.0 %copy-start.8 = (bf16[768,192]{1,0:T(8,128)(2,1)S(1)}, bf16[768,192]{1,0:T(8,128)(2,1)}, u32[]{:S(2)}) copy-start(bf16[768,192]{1,0:T(8,128)(2,1)} %convolution_convert_fusion.1) | copy-start | bytes 884740
  112.9 3.5 %collective-permute-start.24 = (bf16[1,192,128]{2,1,0:T(8,128)(2,1)S(1)}, bf16[1,192,128]{2,1,0:T(8,128)(2,1)S(1)}, u32[]{:S(2)}, u32[]{:S(2)}) collective-permute-start(bf16[1,192,128]{2,1,0:T(8,128)(2,1)S(1)} %fusion.9), channel_id=1, source_target_pairs={{0,4},{4,8},{8,12},{12,16},{16,20},{20,24},{24,28},{28,0},{1,5},{5... | collective-permute-start | bytes 147464 | tf_op jit(solution)/shard_map/ppermute | solution.py:28
  116.4 9.0 %collective-permute-start.28 = (bf16[2,128,192]{1,2,0:T(8,128)(2,1)S(1)}, bf16[2,128,192]{1,2,0:T(8,128)(2,1)S(1)}, u32[]{:S(2)}, u32[]{:S(2)}) collective-permute-start(bf16[2,128,192]{1,2,0:T(8,128)(2,1)S(1)} %pad_maximum_fusion.5), channel_id=1, source_target_pairs={{0,8},{4,12},{8,16},{12,20},{16,24},{20,28},{24,0},{28,4},{1,9},{5... | collective-permute-start | bytes 294920 | tf_op jit(solution)/shard_map/ppermute | solution.py:28
  125.3 5.5 %collective-permute-start.25 = (bf16[2,192,128]{2,1,0:T(8,128)(2,1)S(1)}, bf16[2,192,128]{2,1,0:T(8,128)(2,1)S(1)}, u32[]{:S(2)}, u32[]{:S(2)}) collective-permute-start(bf16[2,192,128]{2,1,0:T(8,128)(2,1)S(1)} %pad_maximum_fusion.4), channel_id=1, source_target_pairs={{0,8},{4,12},{8,16},{12,20},{16,24},{20,28},{24,0},{28,4},{1,9},{5... | collective-permute-start | bytes 294920 | tf_op jit(solution)/shard_map/ppermute | solution.py:28
  130.9 20.1 %collective-permute-start.21 = (bf16[768,192]{1,0:T(8,128)(2,1)S(1)}, bf16[768,192]{1,0:T(8,128)(2,1)S(1)}, u32[]{:S(2)}, u32[]{:S(2)}) collective-permute-start(bf16[768,192]{1,0:T(8,128)(2,1)S(1)} %copy-done.8), channel_id=1, source_target_pairs={{0,4},{4,8},{8,12},{12,16},{16,20},{20,24},{24,28},{1,5},{5,9},{9,... | collective-permute-start | bytes 884744 | tf_op jit(solution)/shard_map/ppermute | solution.py:18
  133.5 14.8 %collective-permute-start.20 = (bf16[768,192]{1,0:T(8,128)(2,1)S(1)}, bf16[768,192]{1,0:T(8,128)(2,1)S(1)}, u32[]{:S(2)}, u32[]{:S(2)}) collective-permute-start(bf16[768,192]{1,0:T(8,128)(2,1)S(1)} %copy-done.8), channel_id=1, source_target_pairs={{0,8},{4,12},{8,16},{12,20},{16,24},{20,28},{1,9},{5,13},{9,17},{1... | collective-permute-start | bytes 884744 | tf_op jit(solution)/shard_map/ppermute | solution.py:18
  139.8 27.3 %collective-permute-start.15 = (bf16[768,192]{1,0:T(8,128)(2,1)}, bf16[768,192]{1,0:T(8,128)(2,1)S(1)}, u32[]{:S(2)}, u32[]{:S(2)}) collective-permute-start(bf16[768,192]{1,0:T(8,128)(2,1)} %convolution_convert_fusion.2), channel_id=1, source_target_pairs={{8,0},{12,4},{16,8},{20,12},{24,16},{28,20},{9,1},{13,5},{17,9},{2... | collective-permute-start | bytes 884744 | tf_op jit(solution)/shard_map/ppermute | solution.py:18
  148.3 16.8 %collective-permute-start.14 = (bf16[768,192]{1,0:T(8,128)(2,1)}, bf16[768,192]{1,0:T(8,128)(2,1)S(1)}, u32[]{:S(2)}, u32[]{:S(2)}) collective-permute-start(bf16[768,192]{1,0:T(8,128)(2,1)} %convolution_convert_fusion.2), channel_id=1, source_target_pairs={{4,0},{8,4},{12,8},{16,12},{20,16},{24,20},{28,24},{5,1},{9,5},{13... | collective-permute-start | bytes 884744 | tf_op jit(solution)/shard_map/ppermute | solution.py:18
  151.0 19.3 %collective-permute-start.16 = (bf16[192,768]{1,0:T(8,128)(2,1)}, bf16[192,768]{1,0:T(8,128)(2,1)S(1)}, u32[]{:S(2)}, u32[]{:S(2)}) collective-permute-start(bf16[192,768]{1,0:T(8,128)(2,1)} %convolution_convert_fusion.3), channel_id=1, source_target_pairs={{0,8},{4,12},{8,16},{12,20},{16,24},{20,28},{1,9},{5,13},{9,17},{1... | collective-permute-start | bytes 884744 | tf_op jit(solution)/shard_map/ppermute | solution.py:18
  165.1 8.3 %collective-permute-start.17 = (bf16[192,768]{1,0:T(8,128)(2,1)}, bf16[192,768]{1,0:T(8,128)(2,1)S(1)}, u32[]{:S(2)}, u32[]{:S(2)}) collective-permute-start(bf16[192,768]{1,0:T(8,128)(2,1)} %convolution_convert_fusion.3), channel_id=1, source_target_pairs={{0,4},{4,8},{8,12},{12,16},{16,20},{20,24},{24,28},{1,5},{5,9},{9,... | collective-permute-start | bytes 884744 | tf_op jit(solution)/shard_map/ppermute | solution.py:18
  167.1 20.7 %collective-permute-start.9 = (bf16[192,768]{1,0:T(8,128)(2,1)}, bf16[192,768]{1,0:T(8,128)(2,1)S(1)}, u32[]{:S(2)}, u32[]{:S(2)}) collective-permute-start(bf16[192,768]{1,0:T(8,128)(2,1)} %convolution_convert_fusion.4), channel_id=1, source_target_pairs={{0,4},{4,8},{8,12},{12,16},{16,20},{20,24},{24,28},{1,5},{5,9},{9,... | collective-permute-start | bytes 884744 | tf_op jit(solution)/shard_map/ppermute | solution.py:18
  169.0 18.8 %copy-start.6 = (bf16[3840,192]{1,0:T(8,128)(2,1)}, bf16[3840,192]{1,0:T(8,128)(2,1)S(1)}, u32[]{:S(2)}) copy-start(bf16[3840,192]{1,0:T(8,128)(2,1)S(1)} %constant_dynamic-update-slice_fusion.15.refs_3_) | copy-start | bytes 4423684
  170.2 8.9 %collective-permute-start.22 = (bf16[768,192]{1,0:T(8,128)(2,1)S(1)}, bf16[768,192]{1,0:T(8,128)(2,1)S(1)}, u32[]{:S(2)}, u32[]{:S(2)}) collective-permute-start(bf16[768,192]{1,0:T(8,128)(2,1)S(1)} %copy-done.8), channel_id=1, source_target_pairs={{4,0},{8,4},{12,8},{16,12},{20,16},{24,20},{28,24},{5,1},{9,5},{13... | collective-permute-start | bytes 884744 | tf_op jit(solution)/shard_map/ppermute | solution.py:18
  173.4 11.7 %collective-permute-start.8 = (bf16[192,768]{1,0:T(8,128)(2,1)}, bf16[192,768]{1,0:T(8,128)(2,1)S(1)}, u32[]{:S(2)}, u32[]{:S(2)}) collective-permute-start(bf16[192,768]{1,0:T(8,128)(2,1)} %convolution_convert_fusion.4), channel_id=1, source_target_pairs={{0,8},{4,12},{8,16},{12,20},{16,24},{20,28},{1,9},{5,13},{9,17},{1... | collective-permute-start | bytes 884744 | tf_op jit(solution)/shard_map/ppermute | solution.py:18
  179.1 18.0 %collective-permute-start.19 = (bf16[192,768]{1,0:T(8,128)(2,1)}, bf16[192,768]{1,0:T(8,128)(2,1)S(1)}, u32[]{:S(2)}, u32[]{:S(2)}) collective-permute-start(bf16[192,768]{1,0:T(8,128)(2,1)} %convolution_convert_fusion.3), channel_id=1, source_target_pairs={{8,0},{12,4},{16,8},{20,12},{24,16},{28,20},{9,1},{13,5},{17,9},{2... | collective-permute-start | bytes 884744 | tf_op jit(solution)/shard_map/ppermute | solution.py:18
  185.1 11.9 %collective-permute-start.18 = (bf16[192,768]{1,0:T(8,128)(2,1)}, bf16[192,768]{1,0:T(8,128)(2,1)S(1)}, u32[]{:S(2)}, u32[]{:S(2)}) collective-permute-start(bf16[192,768]{1,0:T(8,128)(2,1)} %convolution_convert_fusion.3), channel_id=1, source_target_pairs={{4,0},{8,4},{12,8},{16,12},{20,16},{24,20},{28,24},{5,1},{9,5},{13... | collective-permute-start | bytes 884744 | tf_op jit(solution)/shard_map/ppermute | solution.py:18
  187.8 17.7 %collective-permute-start.23 = (bf16[768,192]{1,0:T(8,128)(2,1)S(1)}, bf16[768,192]{1,0:T(8,128)(2,1)S(1)}, u32[]{:S(2)}, u32[]{:S(2)}) collective-permute-start(bf16[768,192]{1,0:T(8,128)(2,1)S(1)} %copy-done.8), channel_id=1, source_target_pairs={{8,0},{12,4},{16,8},{20,12},{24,16},{28,20},{9,1},{13,5},{17,9},{2... | collective-permute-start | bytes 884744 | tf_op jit(solution)/shard_map/ppermute | solution.py:18
  197.1 17.8 %collective-permute-start.26 = (bf16[4,192,128]{2,1,0:T(8,128)(2,1)}, bf16[4,192,128]{2,1,0:T(8,128)(2,1)}, u32[]{:S(2)}, u32[]{:S(2)}) collective-permute-start(bf16[4,192,128]{2,1,0:T(8,128)(2,1)} %pad_maximum_fusion.2), channel_id=1, source_target_pairs={{0,16},{4,20},{8,24},{12,28},{16,0},{20,4},{24,8},{28,12},{1,17},{... | collective-permute-start | bytes 589832 | tf_op jit(solution)/shard_map/ppermute | solution.py:28
  197.1 16.7 %collective-permute-start.29 = (bf16[4,128,192]{1,2,0:T(8,128)(2,1)S(1)}, bf16[4,128,192]{1,2,0:T(8,128)(2,1)S(1)}, u32[]{:S(2)}, u32[]{:S(2)}) collective-permute-start(bf16[4,128,192]{1,2,0:T(8,128)(2,1)S(1)} %pad_maximum_fusion.3), channel_id=1, source_target_pairs={{0,16},{4,20},{8,24},{12,28},{16,0},{20,4},{24,8},{28,12},{1,17},{... | collective-permute-start | bytes 589832 | tf_op jit(solution)/shard_map/ppermute | solution.py:28
  199.2 15.6 %copy-start.7 = (bf16[192,3840]{1,0:T(8,128)(2,1)}, bf16[192,3840]{1,0:T(8,128)(2,1)S(1)}, u32[]{:S(2)}) copy-start(bf16[192,3840]{1,0:T(8,128)(2,1)S(1)} %constant_dynamic-update-slice_fusion.20.refs_4_) | copy-start | bytes 4423684
Sparse Core Ops, SparseCore 0:
  8.9 38.3 all-gather.2
  48.8 35.9 all-gather.4

commit v6 on v4

--- a/solution.py
+++ b/solution.py
@@ -32,30 +32,30 @@
 
 
 def attention_kernel(count, source, rows, q_ref, *refs, heads, widths, scale):
-    tables = refs[:6]
-    o_ref, kt_ref, v_ref = refs[6:]
+    tables = refs[:-2]
+    o_ref, kv_ref = refs[-2:]
     b = pl.program_id(0)
     used = count[b]
 
     @pl.when(b == 0)
     def _():
-        kt_ref[...] = jnp.zeros_like(kt_ref)
-        v_ref[...] = jnp.zeros_like(v_ref)
+        kv_ref[...] = jnp.zeros_like(kv_ref)
 
     def fetch(j, carry):
         at = pl.multiple_of(j * BLK, BLK)
         row = rows[b, j]
-        for code in range(3):
+        for code in range(len(tables)):
             @pl.when(source[b, j] == code)
             def _():
                 start = pl.multiple_of(row * BLK, BLK)
-                kt_ref[:, pl.ds(at, BLK)] = tables[2 * code][:, pl.ds(start, BLK)]
-                v_ref[pl.ds(at, BLK), :] = tables[2 * code + 1][pl.ds(start, BLK), :]
+                kv_ref[pl.ds(at, BLK), :] = tables[code][pl.ds(start, BLK), :]
 
         return carry
 
     lax.fori_loop(0, used, fetch, 0)
     limit = used * BLK
+
+    width = heads * HDIM
 
     def run(slots):
         span = slots * BLK
@@ -64,11 +64,13 @@
         for h in range(heads):
             cols = slice(h * HDIM, (h + 1) * HDIM)
             qh = (q_ref[0, :, cols].astype(jnp.float32) * scale).astype(jnp.bfloat16)
-            s = jnp.dot(qh, kt_ref[cols, 0:span], preferred_element_type=jnp.float32) + bias
+            s = lax.dot_general(qh, kv_ref[0:span, cols], (((1,), (1,)), ((), ())),
+                                preferred_element_type=jnp.float32) + bias
             peak = jnp.max(s, axis=-1, keepdims=True)
             e = jnp.exp(s - peak)
             totals = jnp.sum(e, axis=-1, keepdims=True)
-            summed = jnp.dot(e.astype(jnp.bfloat16), v_ref[0:span, cols],
+            vcols = slice(width + h * HDIM, width + (h + 1) * HDIM)
+            summed = jnp.dot(e.astype(jnp.bfloat16), kv_ref[0:span, vcols],
                              preferred_element_type=jnp.float32)
             o_ref[0, :, cols] = (summed / totals).astype(o_ref.dtype)
 
@@ -101,19 +103,15 @@
             ] + [whole] * len(tables),
             out_specs=pl.BlockSpec((1, BLK, width), lambda b, *_: (b, 0, 0)),
             scratch_shapes=[
-                pltpu.VMEM((width, keys), jnp.bfloat16),
-                pltpu.VMEM((keys, width), jnp.bfloat16),
+                pltpu.VMEM((keys, 2 * width), jnp.bfloat16),
             ],
         ),
         compiler_params=pltpu.CompilerParams(vmem_limit_bytes=60 * 1024 * 1024),
     )(count, source, rows, queries, *tables)
 
 
-def project_kv(x, key_w, value_w):
-    keys_t = lax.dot_general(key_w, x, (((0,), (1,)), ((), ())),
-                             preferred_element_type=jnp.float32).astype(jnp.bfloat16)
-    values = jnp.dot(x, value_w, preferred_element_type=jnp.float32).astype(jnp.bfloat16)
-    return keys_t, values
+def project_kv(x, kv_w):
+    return jnp.dot(x, kv_w, preferred_element_type=jnp.float32).astype(jnp.bfloat16)
 
 
 def window_of(x, axis):
@@ -137,13 +135,12 @@
     key_w = lax.dynamic_slice_in_dim(w_qkv[:, 1], col_start, width_here, 1)
     value_w = lax.dynamic_slice_in_dim(w_qkv[:, 2], col_start, width_here, 1)
 
-    k_own, v_own = project_kv(tokens, key_w, value_w)
-    ka, va = window_of(k_own, 1), window_of(v_own, 0)
+    kv_w = jnp.concatenate([key_w, value_w], axis=1)
+    kva = window_of(project_kv(tokens, kv_w), 0)
 
     gathered = lax.all_gather(tokens, "head", axis=0, tiled=True)
     rest_tokens = jnp.roll(gathered, -head_rank * own_rows, axis=0)[own_rows:]
-    k_rest, v_rest = project_kv(rest_tokens, key_w, value_w)
-    kb, vb = window_of(k_rest, 1), window_of(v_rest, 0)
+    kvb = window_of(project_kv(rest_tokens, kv_w), 0)
     rolled_tokens = jnp.concatenate([tokens, rest_tokens], axis=0)
     queries = jnp.dot(rolled_tokens, query_w, preferred_element_type=jnp.float32).astype(
         jnp.bfloat16
@@ -151,12 +148,9 @@
 
     seq_count = lax.axis_size("seq")
     seq_rank = lax.axis_index("seq")
-    k_first, v_first = project_kv(gathered[:BLK], key_w, value_w)
-    kanc = gather_all(k_first, "seq")
-    vanc = gather_all(v_first, "seq")
-    held_count = kanc.shape[0]
-    kanc = jnp.transpose(kanc, (1, 0, 2)).reshape(width_here, held_count * BLK)
-    vanc = vanc.reshape(held_count * BLK, width_here)
+    kvanc = gather_all(project_kv(gathered[:BLK], kv_w), "seq")
+    held_count = kvanc.shape[0]
+    kvanc = kvanc.reshape(held_count * BLK, 2 * width_here)
     first_block = (seq_rank - 2) * block_count
 
     shift = -head_rank * own_blocks
@@ -189,7 +183,7 @@
     source = jnp.take_along_axis(every_src, order, axis=1).astype(jnp.int32)
     count = jnp.sum(valid.astype(jnp.int32), axis=1).astype(jnp.int32)
 
-    attended = attention(queries, (ka, va, kb, vb, kanc, vanc), count, source, rows)
+    attended = attention(queries, (kva, kvb, kvanc), count, source, rows)
     attended = jnp.roll(attended.reshape(row_count, width_here), head_rank * own_rows, axis=0)
     mine_rows = lax.all_to_all(attended, "head", 0, 1, tiled=True)
     mixed_out = jnp.dot(mine_rows, w_out, preferred_element_type=jnp.float32).astype(

time: 264 us -> 255 us (0.966)
  waiting for transfers between devices: 53 us -> 90.4 us
  local copies, waits for them, and re-layouts: 49.9 us -> 30.5 us
  starting transfers between devices: 52.8 us -> 37.9 us
  blocking collectives: 22.4 us -> 15.5 us
  matrix products: 13.4 us -> 10.1 us
    all_gather x1, waiting for transfers between devices: 16 us -> 41.6 us  [shards(): gathered = lax.all_gather(tokens, 'head', axis=0, tiled=True)]
    ppermute x16 -> x8, starting transfers between devices: 44.7 us -> 34 us  [shifted(): return lax.ppermute(x, axis, pairs)]
    unnamed x31 -> x23, local copies, waits for them, and re-layouts: 23.3 us -> 14 us
    ppermute x6 -> x3, waiting for transfers between devices: 19.8 us -> 28.1 us  [gather_all(): got = lax.ppermute(held, axis, pairs)]
    all_to_all x1, blocking collectives: 22.4 us -> 15.5 us  [shards(): mine_rows = lax.all_to_all(attended, 'head', 0, 1, tiled=True)]
    ppermute x4 -> x0, local copies, waits for them, and re-layouts: 6.22 us -> none  [shifted(): return lax.ppermute(x, axis, pairs)]
    dot_general x6 -> x3, matrix products: 9.37 us -> 5.24 us  [project_kv(): jnp.dot(x, kv_w, preferred_element_type=jnp.float32).astype(jnp.bfloat16)]
    ppermute x6 -> x3, starting transfers between devices: 8.09 us -> 3.97 us  [gather_all(): got = lax.ppermute(held, axis, pairs)]
  transfers between devices with their start and end apart: 23 -> 12, of which waited for: 4 -> 5; matrix products, arithmetic and copies ran while one was open for 23% -> 18% of each run, Pallas kernels for 0% -> 0%
where the time goes in v6:
time: 255 us; the launch traced here: 253 us
  waiting for transfers between devices  90.4 us (35%)
  Pallas kernels  44.3 us (17%)
  starting transfers between devices  37.9 us (15%)
  local copies, waits for them, and re-layouts  30.5 us (12%)
  blocking collectives  15.5 us (6%)
  between operations  13.8 us (5%)
  other arithmetic  10.2 us (4%)
  matrix products  10.1 us (4%)
    pallas_call x1, Pallas kernels, attention(): pl.pallas_call(kernel, out_shape=jax.ShapeDtypeStruct(queries.shape, jnp....  44.3 us
    all_gather x1, waiting for transfers between devices, shards(): gathered = lax.all_gather(tokens, 'head', axis=0, tiled=True)  41.6 us
    ppermute x8, starting transfers between devices, shifted(): return lax.ppermute(x, axis, pairs)  34 us
    ppermute x3, waiting for transfers between devices, gather_all(): got = lax.ppermute(held, axis, pairs)  28.1 us
    ppermute x8, waiting for transfers between devices, shifted(): return lax.ppermute(x, axis, pairs)  19.9 us
    all_to_all x1, blocking collectives, shards(): mine_rows = lax.all_to_all(attended, 'head', 0, 1, tiled=True)  15.5 us
    unnamed x23, local copies, waits for them, and re-layouts  14 us
    dot_general x3, matrix products, project_kv(): jnp.dot(x, kv_w, preferred_element_type=jnp.float32).astype(jnp.bfloat16)  5.24 us
  transfers between devices with their start and end apart: 12, of which 5 were waited for; matrix products, arithmetic and copies ran while one was open for 18% of the time, Pallas kernels for 0%

profile of v6, /device:TPU:2, one launch (start us, length us, event | category | flops | bytes accessed | tf_op | source)
XLA Modules:
  0.0 252.7 jit_solution(12543028280306852242)
XLA Ops:
  6.5 0.7 all-gather.2.cloned.1.call-update
  7.3 3.3 %fusion.35 = (bf16[768,1,768]{2,0,1:T(8,128)(2,1)S(1)}, bf16[768,1,768]{2,0,1:T(8,128)(2,1)}, bf16[768,1,768]{2,0,1:T(8,128)(2,1)S(1)}) fusion(bf16[768,3,768]{2,0,1:T(8,128)(2,1)} %param.9), kind=kLoop, calls=%fused_computation.101 | loop fusion | bytes 7077888 | tf_op jit(solution)/shard_map/slice | solution.py:135
  10.6 0.3 dynamic-slice_bitcast_fusion
  10.9 1.4 fusion.8
  12.4 3.4 %collective-permute-start = (bf16[512,384]{1,0:T(8,128)(2,1)}, bf16[512,384]{1,0:T(8,128)(2,1)}, u32[]{:S(2)}, u32[]{:S(2)}) collective-permute-start(bf16[512,384]{1,0:T(8,128)(2,1)} %fusion.8), channel_id=1, source_target_pairs={{0,8},{4,12},{8,16},{12,20},{16,24},{20,28},{1,9},{5,13},{9,17},{1... | collective-permute-start | bytes 1179656 | tf_op jit(solution)/shard_map/ppermute | solution.py:18
  15.7 1.9 collective-permute-start.1
  17.7 3.6 %collective-permute-start.2 = (bf16[512,384]{1,0:T(8,128)(2,1)}, bf16[512,384]{1,0:T(8,128)(2,1)}, u32[]{:S(2)}, u32[]{:S(2)}) collective-permute-start(bf16[512,384]{1,0:T(8,128)(2,1)} %fusion.8), channel_id=1, source_target_pairs={{4,0},{8,4},{12,8},{16,12},{20,16},{24,20},{28,24},{5,1},{9,5},{13... | collective-permute-start | bytes 1179656 | tf_op jit(solution)/shard_map/ppermute | solution.py:18
  21.3 1.9 collective-permute-start.3
  23.9 0.8 sort.17
  24.8 0.1 reshape.68
  24.9 2.5 gather_fusion
  27.7 2.5 gather_fusion.1
  30.3 0.6 convert_reduce_fusion.count
  30.8 0.6 broadcast_select_fusion
  31.4 0.6 broadcast_select_fusion.1.source
  32.0 41.6 %all-gather.2.cloned.1.call-done = bf16[2048,768]{1,0:T(8,128)(2,1)} async-done(((bf16[512,768]{1,0:T(8,128)(2,1)}), bf16[2048,768]{1,0:T(8,128)(2,1)}) %all-gather.2.cloned.1.call-update) | async-done | bytes 3145744 | tf_op jit(solution)/shard_map/all_gather | solution.py:141
  73.7 4.0 %fusion.7 = bf16[1536,768]{1,0:T(8,128)(2,1)S(1)} fusion(s32[]{:T(128)S(6)} %add.116, bf16[2048,768]{1,0:T(8,128)(2,1)} %all-gather.2.cloned.1.call-done), kind=kLoop, calls=%fused_computation.10 | loop fusion | flops 4718592 | bytes 5505028 | tf_op jit(solution)/shard_map/jit(_roll_dynamic)/concatenate | solution.py:142
  77.7 2.6 %convolution_convert_fusion = bf16[1536,384]{1,0:T(8,128)(2,1)} fusion(bf16[1536,768]{1,0:T(8,128)(2,1)S(1)} %fusion.7, bf16[768,192]{1,0:T(8,128)(2,1)S(1)} %get-tuple-element.15, bf16[768,192]{1,0:T(8,128)(2,1)S(1)} %get-tuple-element.16), kind=kOutput, calls=%fused_computation.8 | convolution fusion | flops 907739136 | bytes 4128768 | tf_op jit(solution)/shard_map/dot_general | solution.py:114
  80.2 3.4 %collective-permute-start.4 = (bf16[1536,384]{1,0:T(8,128)(2,1)}, bf16[1536,384]{1,0:T(8,128)(2,1)}, u32[]{:S(2)}, u32[]{:S(2)}) collective-permute-start(bf16[1536,384]{1,0:T(8,128)(2,1)} %convolution_convert_fusion), channel_id=1, source_target_pairs={{0,8},{4,12},{8,16},{12,20},{16,24},{20,28},{1,9},{5,13},{9,17},{1... | collective-permute-start | bytes 3538952 | tf_op jit(solution)/shard_map/ppermute | solution.py:18
  83.6 1.3 fusion.9
  85.0 1.0 constant_dynamic-update-slice_fusion.4
  86.0 24.9 %collective-permute-done.8 = bf16[1,128,384]{2,1,0:T(8,128)(2,1)S(1)} collective-permute-done((bf16[1,128,384]{2,1,0:T(8,128)(2,1)S(1)}, bf16[1,128,384]{2,1,0:T(8,128)(2,1)S(1)}, u32[]{:S(2)}, u32[]{:S(2)}) %collective-permute-start.8) | collective-permute-done | bytes 98336 | tf_op jit(solution)/shard_map/ppermute | solution.py:28
  110.9 1.9 collective-permute-start.5
  112.9 2.4 collective-permute-start.9
  115.3 1.1 constant_dynamic-update-slice_fusion.3
  116.4 1.1 constant_dynamic-update-slice_fusion.2
  117.4 3.2 %collective-permute-done.9 = bf16[2,128,384]{2,1,0:T(8,128)(2,1)S(1)} collective-permute-done((bf16[2,128,384]{2,1,0:T(8,128)(2,1)S(1)}, bf16[2,128,384]{2,1,0:T(8,128)(2,1)S(1)}, u32[]{:S(2)}, u32[]{:S(2)}) %collective-permute-start.9) | collective-permute-done | bytes 196640 | tf_op jit(solution)/shard_map/ppermute | solution.py:28
  120.6 0.8 pad_maximum_fusion.2
  121.4 1.5 collective-permute-start.10
  122.9 1.1 constant_dynamic-update-slice_fusion.1
  124.0 15.7 %collective-permute-start.6 = (bf16[1536,384]{1,0:T(8,128)(2,1)}, bf16[1536,384]{1,0:T(8,128)(2,1)}, u32[]{:S(2)}, u32[]{:S(2)}) collective-permute-start(bf16[1536,384]{1,0:T(8,128)(2,1)} %convolution_convert_fusion), channel_id=1, source_target_pairs={{4,0},{8,4},{12,8},{16,12},{20,16},{24,20},{28,24},{5,1},{9,5},{13... | collective-permute-start | bytes 3538952 | tf_op jit(solution)/shard_map/ppermute | solution.py:18
  139.7 1.1 constant_dynamic-update-slice_fusion.refs_0_
  140.8 2.1 collective-permute-start.7
  142.9 3.2 %fusion.4 = bf16[2048,192]{0,1:T(8,128)(2,1)} fusion(bf16[1536,768]{1,0:T(8,128)(2,1)S(1)} %fusion.7, bf16[512,768]{1,0:T(8,128)(2,1)S(1)} %copy-done.3, bf16[768,1,768]{2,0,1:T(8,128)(2,1)} %get-tuple-element.13, s32[]{:T(128)S(6)} %select_n.109), kind=kOutput, calls=%fused_computation.9 | convolution fusion | flops 610664448 | bytes 4325380 | tf_op jit(solution)/shard_map/dot_general | solution.py:145
  146.1 2.2 copy.58
  148.4 2.0 pad_maximum_fusion
  150.4 2.4 constant_dynamic-update-slice_fusion.9
  152.8 2.4 constant_dynamic-update-slice_fusion.8
  155.2 2.4 constant_dynamic-update-slice_fusion.7
  157.6 6.2 %collective-permute-done.6 = bf16[1536,384]{1,0:T(8,128)(2,1)} collective-permute-done((bf16[1536,384]{1,0:T(8,128)(2,1)}, bf16[1536,384]{1,0:T(8,128)(2,1)}, u32[]{:S(2)}, u32[]{:S(2)}) %collective-permute-start.6) | collective-permute-done | bytes 1179680 | tf_op jit(solution)/shard_map/ppermute | solution.py:18
  163.9 2.4 constant_dynamic-update-slice_fusion.6
  166.3 13.6 %collective-permute-done.7 = bf16[1536,384]{1,0:T(8,128)(2,1)} collective-permute-done((bf16[1536,384]{1,0:T(8,128)(2,1)}, bf16[1536,384]{1,0:T(8,128)(2,1)}, u32[]{:S(2)}, u32[]{:S(2)}) %collective-permute-start.7) | collective-permute-done | bytes 1179680 | tf_op jit(solution)/shard_map/ppermute | solution.py:18
  179.9 2.5 constant_dynamic-update-slice_fusion.5.refs_1_
  182.4 44.3 %shard_map.64 = bf16[16,128,192]{2,1,0:T(8,128)(2,1)} custom-call(s32[16]{0:T(128)} %convert_reduce_fusion.count, s32[16,20]{1,0:T(8,128)} %broadcast_select_fusion.1.source, s32[16,20]{1,0:T(8,128)} %get-tuple-element.8.rows, bf16[16,128,192]{2,1,0:T(8,128)(2,1)} %bitcast.32, bf16[2560,384]{1,0:T(8,128)(2,1)} %copy-done.1, ...), custom_call_target="tpu_custom_call" | custom-call | tf_op jit(solution)/shard_map/pallas_call | solution.py:95
  226.7 1.4 copy.60
  228.2 0.4 fusion.10
  228.7 15.5 %all_to_all.19 = bf16[4,512,192]{1,2,0:T(8,128)(2,1)S(1)} all-to-all(bf16[4,512,192]{1,2,0:T(8,128)(2,1)S(1)} %bitcast.35), channel_id=1, replica_groups=mesh['seq'=8,'head'=4] {'head'}, dimensions={0} | all-to-all | bytes 1572864 | tf_op jit(solution)/shard_map/all_to_all | solution.py:188
  244.2 1.7 convolution_convert_fusion.1
  (45 shorter events, 1.1 us)
Async XLA Ops:
  6.5 237.7 %copy-start = (bf16[768,768]{1,0:T(8,128)(2,1)S(1)}, bf16[768,768]{1,0:T(8,128)(2,1)}, u32[]{:S(2)}) copy-start(bf16[768,768]{1,0:T(8,128)(2,1)} %param.10) | copy-start | bytes 3538948
  6.5 67.2 %all-gather.2.cloned.1.call-start = ((), (), s32[]{:S(2)}) async-start(), calls=%async_computation.1 | async-start | bytes 3932160 | tf_op jit(solution)/shard_map/all_gather | solution.py:141
  7.3 3.7 %copy-start.2 = (bf16[512,768]{1,0:T(8,128)(2,1)S(1)}, bf16[512,768]{1,0:T(8,128)(2,1)}, u32[]{:S(2)}) copy-start(bf16[512,768]{1,0:T(8,128)(2,1)} %param.8) | copy-start | bytes 2359300
  10.6 12.7 %copy-start.4 = (s32[16,12]{1,0:T(8,128)S(1)}, s32[16,12]{1,0:T(8,128)}, u32[]{:S(2)}) copy-start(s32[16,12]{1,0:T(8,128)} %param.11) | copy-start | bytes 2308
  10.6 12.9 %copy-start.6 = (s32[16]{0:T(128)S(1)}, s32[16]{0:T(128)}, u32[]{:S(2)}) copy-start(s32[16]{0:T(128)} %param.12) | copy-start | bytes 196
  10.6 13.0 %copy-start.5 = (s32[16,8]{0,1:T(8,128)S(1)}, s32[16,8]{0,1:T(8,128)}, u32[]{:S(2)}) copy-start(s32[16,8]{0,1:T(8,128)} %param.13) | copy-start | bytes 1540
  12.4 72.5 %collective-permute-start = (bf16[512,384]{1,0:T(8,128)(2,1)}, bf16[512,384]{1,0:T(8,128)(2,1)}, u32[]{:S(2)}, u32[]{:S(2)}) collective-permute-start(bf16[512,384]{1,0:T(8,128)(2,1)} %fusion.8), channel_id=1, source_target_pairs={{0,8},{4,12},{8,16},{12,20},{16,24},{20,28},{1,9},{5,13},{9,17},{1... | collective-permute-start | bytes 1179656 | tf_op jit(solution)/shard_map/ppermute | solution.py:18
  15.7 97.1 %collective-permute-start.1 = (bf16[512,384]{1,0:T(8,128)(2,1)}, bf16[512,384]{1,0:T(8,128)(2,1)}, u32[]{:S(2)}, u32[]{:S(2)}) collective-permute-start(bf16[512,384]{1,0:T(8,128)(2,1)} %fusion.8), channel_id=1, source_target_pairs={{0,4},{4,8},{8,12},{12,16},{16,20},{20,24},{24,28},{1,5},{5,9},{9,... | collective-permute-start | bytes 1179656 | tf_op jit(solution)/shard_map/ppermute | solution.py:18
  17.7 105.3 %collective-permute-start.2 = (bf16[512,384]{1,0:T(8,128)(2,1)}, bf16[512,384]{1,0:T(8,128)(2,1)}, u32[]{:S(2)}, u32[]{:S(2)}) collective-permute-start(bf16[512,384]{1,0:T(8,128)(2,1)} %fusion.8), channel_id=1, source_target_pairs={{4,0},{8,4},{12,8},{16,12},{20,16},{24,20},{28,24},{5,1},{9,5},{13... | collective-permute-start | bytes 1179656 | tf_op jit(solution)/shard_map/ppermute | solution.py:18
  21.3 118.4 %collective-permute-start.3 = (bf16[512,384]{1,0:T(8,128)(2,1)}, bf16[512,384]{1,0:T(8,128)(2,1)}, u32[]{:S(2)}, u32[]{:S(2)}) collective-permute-start(bf16[512,384]{1,0:T(8,128)(2,1)} %fusion.8), channel_id=1, source_target_pairs={{8,0},{12,4},{16,8},{20,12},{24,16},{28,20},{9,1},{13,5},{17,9},{2... | collective-permute-start | bytes 1179656 | tf_op jit(solution)/shard_map/ppermute | solution.py:18
  80.2 70.2 %collective-permute-start.4 = (bf16[1536,384]{1,0:T(8,128)(2,1)}, bf16[1536,384]{1,0:T(8,128)(2,1)}, u32[]{:S(2)}, u32[]{:S(2)}) collective-permute-start(bf16[1536,384]{1,0:T(8,128)(2,1)} %convolution_convert_fusion), channel_id=1, source_target_pairs={{0,8},{4,12},{8,16},{12,20},{16,24},{20,28},{1,9},{5,13},{9,17},{1... | collective-permute-start | bytes 3538952 | tf_op jit(solution)/shard_map/ppermute | solution.py:18
  84.9 26.0 %collective-permute-start.8 = (bf16[1,128,384]{2,1,0:T(8,128)(2,1)S(1)}, bf16[1,128,384]{2,1,0:T(8,128)(2,1)S(1)}, u32[]{:S(2)}, u32[]{:S(2)}) collective-permute-start(bf16[1,128,384]{2,1,0:T(8,128)(2,1)S(1)} %fusion.9), channel_id=1, source_target_pairs={{0,4},{4,8},{8,12},{12,16},{16,20},{20,24},{24,28},{28,0},{1,5},{5... | collective-permute-start | bytes 294920 | tf_op jit(solution)/shard_map/ppermute | solution.py:28
  110.9 41.9 %collective-permute-start.5 = (bf16[1536,384]{1,0:T(8,128)(2,1)}, bf16[1536,384]{1,0:T(8,128)(2,1)}, u32[]{:S(2)}, u32[]{:S(2)}) collective-permute-start(bf16[1536,384]{1,0:T(8,128)(2,1)} %convolution_convert_fusion), channel_id=1, source_target_pairs={{0,4},{4,8},{8,12},{12,16},{16,20},{20,24},{24,28},{1,5},{5,9},{9,... | collective-permute-start | bytes 3538952 | tf_op jit(solution)/shard_map/ppermute | solution.py:18
  112.9 30.1 %copy-start.3 = (bf16[512,768]{1,0:T(8,128)(2,1)S(1)}, bf16[512,768]{1,0:T(8,128)(2,1)}, u32[]{:S(2)}) copy-start(bf16[512,768]{1,0:T(8,128)(2,1)} %param.8) | copy-start | bytes 2359300
  112.9 7.8 %collective-permute-start.9 = (bf16[2,128,384]{2,1,0:T(8,128)(2,1)S(1)}, bf16[2,128,384]{2,1,0:T(8,128)(2,1)S(1)}, u32[]{:S(2)}, u32[]{:S(2)}) collective-permute-start(bf16[2,128,384]{2,1,0:T(8,128)(2,1)S(1)} %pad_maximum_fusion.3), channel_id=1, source_target_pairs={{0,8},{4,12},{8,16},{12,20},{16,24},{20,28},{24,0},{28,4},{1,9},{5... | collective-permute-start | bytes 589832 | tf_op jit(solution)/shard_map/ppermute | solution.py:28
  121.4 26.9 %collective-permute-start.10 = (bf16[4,128,384]{2,1,0:T(8,128)(2,1)}, bf16[4,128,384]{2,1,0:T(8,128)(2,1)}, u32[]{:S(2)}, u32[]{:S(2)}) collective-permute-start(bf16[4,128,384]{2,1,0:T(8,128)(2,1)} %pad_maximum_fusion.2), channel_id=1, source_target_pairs={{0,16},{4,20},{8,24},{12,28},{16,0},{20,4},{24,8},{28,12},{1,17},{... | collective-permute-start | bytes 1179656 | tf_op jit(solution)/shard_map/ppermute | solution.py:28
  124.0 39.9 %collective-permute-start.6 = (bf16[1536,384]{1,0:T(8,128)(2,1)}, bf16[1536,384]{1,0:T(8,128)(2,1)}, u32[]{:S(2)}, u32[]{:S(2)}) collective-permute-start(bf16[1536,384]{1,0:T(8,128)(2,1)} %convolution_convert_fusion), channel_id=1, source_target_pairs={{4,0},{8,4},{12,8},{16,12},{20,16},{24,20},{28,24},{5,1},{9,5},{13... | collective-permute-start | bytes 3538952 | tf_op jit(solution)/shard_map/ppermute | solution.py:18
  140.8 5.3 %copy-start.1 = (bf16[2560,384]{1,0:T(8,128)(2,1)}, bf16[2560,384]{1,0:T(8,128)(2,1)S(1)}, u32[]{:S(2)}) copy-start(bf16[2560,384]{1,0:T(8,128)(2,1)S(1)} %constant_dynamic-update-slice_fusion.refs_0_) | copy-start | bytes 5898244
  140.8 39.1 %collective-permute-start.7 = (bf16[1536,384]{1,0:T(8,128)(2,1)}, bf16[1536,384]{1,0:T(8,128)(2,1)}, u32[]{:S(2)}, u32[]{:S(2)}) collective-permute-start(bf16[1536,384]{1,0:T(8,128)(2,1)} %convolution_convert_fusion), channel_id=1, source_target_pairs={{8,0},{12,4},{16,8},{20,12},{24,16},{28,20},{9,1},{13,5},{17,9},{2... | collective-permute-start | bytes 3538952 | tf_op jit(solution)/shard_map/ppermute | solution.py:18
Sparse Core Ops, SparseCore 0:
  8.9 64.7 all-gather.1

commit v7 on v6

--- a/solution.py
+++ b/solution.py
@@ -107,6 +107,11 @@
             ],
         ),
         compiler_params=pltpu.CompilerParams(vmem_limit_bytes=60 * 1024 * 1024),
+        cost_estimate=pl.CostEstimate(
+            flops=4 * block_count * BLK * keys * width,
+            transcendentals=block_count * heads * BLK * keys,
+            bytes_accessed=sum(t.size * t.dtype.itemsize for t in tables) + 2 * queries.size * 2,
+        ),
     )(count, source, rows, queries, *tables)
 
 
@@ -183,10 +188,20 @@
     source = jnp.take_along_axis(every_src, order, axis=1).astype(jnp.int32)
     count = jnp.sum(valid.astype(jnp.int32), axis=1).astype(jnp.int32)
 
-    attended = attention(queries, (kva, kvb, kvanc), count, source, rows)
-    attended = jnp.roll(attended.reshape(row_count, width_here), head_rank * own_rows, axis=0)
-    mine_rows = lax.all_to_all(attended, "head", 0, 1, tiled=True)
-    mixed_out = jnp.dot(mine_rows, w_out, preferred_element_type=jnp.float32).astype(
+    tables = (kva, kvb, kvanc)
+    away = attention(queries[own_blocks:], tables, count[own_blocks:], source[own_blocks:],
+                     rows[own_blocks:])
+    away = away.reshape(head_count - 1, own_rows, width_here)
+    received = [None] * head_count
+    for j in range(1, head_count):
+        pairs = [(z, (z + j) % head_count) for z in range(head_count)]
+        received[j] = lax.ppermute(away[j - 1], "head", pairs)
+    received[0] = attention(queries[:own_blocks], tables, count[:own_blocks],
+                            source[:own_blocks], rows[:own_blocks]).reshape(own_rows, width_here)
+    mine_rows = jnp.concatenate(received, axis=1)
+    groups = (head_rank - jnp.arange(head_count)) % head_count
+    out_w = jnp.take(w_out.reshape(head_count, width_here, D), groups, axis=0).reshape(D, D)
+    mixed_out = jnp.dot(mine_rows, out_w, preferred_element_type=jnp.float32).astype(
         jnp.bfloat16
     )
     return mixed_out

time: 255 us -> 254 us (level); the launches traced: 253 us -> 254 us
  blocking collectives: 15.5 us -> 0 us
  local copies, waits for them, and re-layouts: 30.5 us -> 40.3 us
  Pallas kernels: 44.3 us -> 50.4 us
  starting transfers between devices: 37.9 us -> 43.7 us
  waiting for transfers between devices: 90.4 us -> 87.7 us
    all_to_all x1 -> x0, blocking collectives: 15.5 us -> none  [shards(): mine_rows = lax.all_to_all(attended, 'head', 0, 1, tiled=True)]
    slice x0 -> x10, local copies, waits for them, and re-layouts: none -> 7.95 us  [the longest x1 2 us: shards(): received[j] = lax.ppermute(away[j - 1], 'head', pairs)]
    pallas_call x1 -> x2, Pallas kernels: 44.3 us -> 50.4 us  [attention(): pl.pallas_call(kernel, out_shape=jax.ShapeDtypeStruct(queries.shape, jnp....]
    ppermute x0 -> x3, starting transfers between devices: none -> 5.82 us  [shards(): received[j] = lax.ppermute(away[j - 1], 'head', pairs)]
    unnamed x23 -> x47, local copies, waits for them, and re-layouts: 14 us -> 18.4 us
  transfers between devices with their start and end apart: 12 -> 15, of which waited for: 5 -> 5; matrix products, arithmetic and copies ran while one was open for 18% -> 20% of each run, Pallas kernels for 0% -> 6%
where the time goes in v7:
time: 254 us
  waiting for transfers between devices  87.7 us (35%)
  Pallas kernels  50.4 us (20%)
  starting transfers between devices  43.7 us (17%)
  local copies, waits for them, and re-layouts  40.3 us (16%)
  between operations  13.9 us (5%)
  matrix products  9.43 us (4%)
  other arithmetic  9 us (4%)
    pallas_call x2, Pallas kernels, attention(): pl.pallas_call(kernel, out_shape=jax.ShapeDtypeStruct(queries.shape, jnp....  50.4 us
    all_gather x1, waiting for transfers between devices, shards(): gathered = lax.all_gather(tokens, 'head', axis=0, tiled=True)  39.8 us
    ppermute x8, starting transfers between devices, shifted(): return lax.ppermute(x, axis, pairs)  33.9 us
    ppermute x3, waiting for transfers between devices, gather_all(): got = lax.ppermute(held, axis, pairs)  25.9 us
    ppermute x8, waiting for transfers between devices, shifted(): return lax.ppermute(x, axis, pairs)  21.2 us
    unnamed x47, local copies, waits for them, and re-layouts  18.4 us
    ppermute x3, starting transfers between devices, shards(): received[j] = lax.ppermute(away[j - 1], 'head', pairs)  5.82 us
    dot_general x3, matrix products, project_kv(): jnp.dot(x, kv_w, preferred_element_type=jnp.float32).astype(jnp.bfloat16)  5.26 us
  transfers between devices with their start and end apart: 15, of which 5 were waited for; matrix products, arithmetic and copies ran while one was open for 20% of the time, Pallas kernels for 6%

profile of v7, /device:TPU:2, one launch (start us, length us, event | category | flops | bytes accessed | tf_op | source)
XLA Modules:
  0.0 254.5 jit_solution(14490361555050659887)
XLA Ops:
  6.5 0.7 all-gather.2.cloned.1.call-update
  7.3 2.3 fusion.45
  10.0 1.4 fusion.8
  11.4 3.4 %collective-permute-start = (bf16[512,384]{1,0:T(8,128)(2,1)}, bf16[512,384]{1,0:T(8,128)(2,1)}, u32[]{:S(2)}, u32[]{:S(2)}) collective-permute-start(bf16[512,384]{1,0:T(8,128)(2,1)} %fusion.8), channel_id=1, source_target_pairs={{0,8},{4,12},{8,16},{12,20},{16,24},{20,28},{1,9},{5,13},{9,17},{1... | collective-permute-start | bytes 1179656 | tf_op jit(solution)/shard_map/ppermute | solution.py:18
  14.8 1.9 collective-permute-start.1
  16.7 3.6 %collective-permute-start.2 = (bf16[512,384]{1,0:T(8,128)(2,1)}, bf16[512,384]{1,0:T(8,128)(2,1)}, u32[]{:S(2)}, u32[]{:S(2)}) collective-permute-start(bf16[512,384]{1,0:T(8,128)(2,1)} %fusion.8), channel_id=1, source_target_pairs={{4,0},{8,4},{12,8},{16,12},{20,16},{24,20},{28,24},{5,1},{9,5},{13... | collective-permute-start | bytes 1179656 | tf_op jit(solution)/shard_map/ppermute | solution.py:18
  20.4 1.9 collective-permute-start.3
  23.0 0.8 sort.17
  24.0 2.5 gather_fusion.2
  26.7 2.5 gather_fusion.1
  33.1 0.7 gather_fusion
  33.9 39.8 %all-gather.2.cloned.1.call-done = bf16[2048,768]{1,0:T(8,128)(2,1)} async-done(((bf16[512,768]{1,0:T(8,128)(2,1)}), bf16[2048,768]{1,0:T(8,128)(2,1)}) %all-gather.2.cloned.1.call-update) | async-done | bytes 3145744 | tf_op jit(solution)/shard_map/all_gather | solution.py:146
  73.7 4.1 %fusion.7 = bf16[1536,768]{1,0:T(8,128)(2,1)S(1)} fusion(s32[]{:T(128)S(6)} %add.141, bf16[2048,768]{1,0:T(8,128)(2,1)} %all-gather.2.cloned.1.call-done), kind=kLoop, calls=%fused_computation.11 | loop fusion | flops 4718592 | bytes 5505028 | tf_op jit(solution)/shard_map/jit(_roll_dynamic)/concatenate | solution.py:147
  77.8 2.6 %convolution_convert_fusion = bf16[1536,384]{1,0:T(8,128)(2,1)} fusion(bf16[1536,768]{1,0:T(8,128)(2,1)S(1)} %fusion.7, bf16[768,192]{1,0:T(8,128)(2,1)S(1)} %copy-done.11, bf16[768,192]{1,0:T(8,128)(2,1)S(1)} %copy-done.13), kind=kOutput, calls=%fused_computation.9 | convolution fusion | flops 907739136 | bytes 4128768 | tf_op jit(solution)/shard_map/dot_general | solution.py:119
  80.4 3.4 %collective-permute-start.4 = (bf16[1536,384]{1,0:T(8,128)(2,1)}, bf16[1536,384]{1,0:T(8,128)(2,1)}, u32[]{:S(2)}, u32[]{:S(2)}) collective-permute-start(bf16[1536,384]{1,0:T(8,128)(2,1)} %convolution_convert_fusion), channel_id=1, source_target_pairs={{0,8},{4,12},{8,16},{12,20},{16,24},{20,28},{1,9},{5,13},{9,17},{1... | collective-permute-start | bytes 3538952 | tf_op jit(solution)/shard_map/ppermute | solution.py:18
  83.7 1.3 fusion.9
  85.1 1.8 constant_dynamic-update-slice_fusion.4
  86.9 24.1 %collective-permute-done.8 = bf16[1,128,384]{2,1,0:T(8,128)(2,1)S(1)} collective-permute-done((bf16[1,128,384]{2,1,0:T(8,128)(2,1)S(1)}, bf16[1,128,384]{2,1,0:T(8,128)(2,1)S(1)}, u32[]{:S(2)}, u32[]{:S(2)}) %collective-permute-start.8) | collective-permute-done | bytes 98336 | tf_op jit(solution)/shard_map/ppermute | solution.py:28
  111.0 1.9 collective-permute-start.5
  113.0 2.4 collective-permute-start.9
  115.4 1.8 constant_dynamic-update-slice_fusion.3
  117.2 1.8 constant_dynamic-update-slice_fusion.2
  119.0 1.8 collective-permute-done.9
  120.8 0.8 pad_maximum_fusion.2
  121.6 1.5 collective-permute-start.10
  123.1 1.8 constant_dynamic-update-slice_fusion.1
  124.8 15.7 %collective-permute-start.6 = (bf16[1536,384]{1,0:T(8,128)(2,1)}, bf16[1536,384]{1,0:T(8,128)(2,1)}, u32[]{:S(2)}, u32[]{:S(2)}) collective-permute-start(bf16[1536,384]{1,0:T(8,128)(2,1)} %convolution_convert_fusion), channel_id=1, source_target_pairs={{4,0},{8,4},{12,8},{16,12},{20,16},{24,20},{28,24},{5,1},{9,5},{13... | collective-permute-start | bytes 3538952 | tf_op jit(solution)/shard_map/ppermute | solution.py:18
  140.6 1.8 constant_dynamic-update-slice_fusion.refs_0_
  142.4 2.1 collective-permute-start.7
  144.5 1.3 fusion.4
  145.7 0.9 copy-done.7
  146.7 1.2 copy.46
  147.9 2.0 pad_maximum_fusion
  149.9 2.4 constant_dynamic-update-slice_fusion.9
  152.3 2.4 constant_dynamic-update-slice_fusion.8
  154.8 2.4 constant_dynamic-update-slice_fusion.7
  157.2 6.8 %collective-permute-done.6 = bf16[1536,384]{1,0:T(8,128)(2,1)} collective-permute-done((bf16[1536,384]{1,0:T(8,128)(2,1)}, bf16[1536,384]{1,0:T(8,128)(2,1)}, u32[]{:S(2)}, u32[]{:S(2)}) %collective-permute-start.6) | collective-permute-done | bytes 1179680 | tf_op jit(solution)/shard_map/ppermute | solution.py:18
  164.0 2.4 constant_dynamic-update-slice_fusion.6
  166.4 14.4 %collective-permute-done.7 = bf16[1536,384]{1,0:T(8,128)(2,1)} collective-permute-done((bf16[1536,384]{1,0:T(8,128)(2,1)}, bf16[1536,384]{1,0:T(8,128)(2,1)}, u32[]{:S(2)}, u32[]{:S(2)}) %collective-permute-start.7) | collective-permute-done | bytes 1179680 | tf_op jit(solution)/shard_map/ppermute | solution.py:18
  180.8 2.4 constant_dynamic-update-slice_fusion.5.refs_1_
  183.2 34.4 %shard_map.65 = bf16[12,128,192]{2,1,0:T(8,128)(2,1)} custom-call(s32[12]{0:T(128)} %slice.67.count, s32[12,20]{1,0:T(8,128)} %slice.85.source, s32[12,20]{1,0:T(8,128)} %slice.86.rows, bf16[12,128,192]{2,1,0:T(8,128)(2,1)} %bitcast.38, bf16[2560,384]{1,0:T(8,128)(2,1)} %constant_dynamic-update-slice_fusion.refs_0_, ...), custom_call_target="tpu_custom_call" | custom-call | flops 3019898880 | bytes 9830400 | tf_op jit(solution)/shard_map/pallas_call | solution.py:95
  217.6 2.0 fusion.46
  219.6 3.6 %collective-permute-start.12 = (bf16[512,192]{1,0:T(8,128)(2,1)}, bf16[512,192]{1,0:T(8,128)(2,1)}, u32[]{:S(2)}, u32[]{:S(2)}) collective-permute-start(bf16[512,192]{1,0:T(8,128)(2,1)} %bitcast.13), channel_id=1, source_target_pairs={{0,2},{1,3},{2,0},{3,1},{4,6},{5,7},{6,4},{7,5},{8,10},{9,11},{10,... | collective-permute-start | bytes 589832 | tf_op jit(solution)/shard_map/ppermute | solution.py:198
  223.3 2.2 collective-permute-start.13
  226.9 0.9 slice.83
  227.8 0.8 copy.44
  228.7 16.0 %shard_map.64 = bf16[4,128,192]{2,1,0:T(8,128)(2,1)} custom-call(s32[4]{0:T(128)} %bitcast.40, s32[4,20]{1,0:T(4,128)} %slice.81.source, s32[4,20]{1,0:T(4,128)} %slice.82.rows, bf16[4,128,192]{2,1,0:T(8,128)(2,1)} %bitcast.37, bf16[2560,384]{1,0:T(8,128)(2,1)} %constant_dynamic-update-slice_fusion.refs_0_, ...), custom_call_target="tpu_custom_call" | custom-call | flops 1006632960 | bytes 9043968 | tf_op jit(solution)/shard_map/pallas_call | solution.py:95
  244.7 2.9 %convolution_convert_fusion.1 = bf16[512,768]{1,0:T(8,128)(2,1)} fusion(bf16[768,768]{1,0:T(8,128)(2,1)S(1)} %bitcast_select_fusion, bf16[512,192]{1,0:T(8,128)(2,1)} %collective-permute-done.13, bf16[512,192]{1,0:T(8,128)(2,1)} %collective-permute-done.12, bf16[512,192]{1,0:T(8,128)(2,1)} %collective-permute-done.11, bf16[512,192]{1,0:T(8,128)(2,1)} %bitcast.39), kind=kOutput, calls=%fused_computation.12 | convolution fusion | flops 607518720 | bytes 2752512 | tf_op jit(solution)/shard_map/dot_general | solution.py:204
  (88 shorter events, 6.8 us)
Async XLA Ops:
  6.5 26.6 %copy-start = (bf16[768,768]{1,0:T(8,128)(2,1)S(1)}, bf16[768,768]{1,0:T(8,128)(2,1)}, u32[]{:S(2)}) copy-start(bf16[768,768]{1,0:T(8,128)(2,1)} %param.10) | copy-start | bytes 3538948
  6.5 67.2 %all-gather.2.cloned.1.call-start = ((), (), s32[]{:S(2)}) async-start(), calls=%async_computation | async-start | bytes 3932160 | tf_op jit(solution)/shard_map/all_gather | solution.py:146
  7.3 2.7 %copy-start.5 = (bf16[512,768]{1,0:T(8,128)(2,1)S(1)}, bf16[512,768]{1,0:T(8,128)(2,1)}, u32[]{:S(2)}) copy-start(bf16[512,768]{1,0:T(8,128)(2,1)} %param.8) | copy-start | bytes 2359300
  9.6 12.8 %copy-start.14 = (s32[16,12]{1,0:T(8,128)S(1)}, s32[16,12]{1,0:T(8,128)}, u32[]{:S(2)}) copy-start(s32[16,12]{1,0:T(8,128)} %param.11) | copy-start | bytes 2308
  9.6 12.9 %copy-start.18 = (s32[16]{0:T(128)S(1)}, s32[16]{0:T(128)}, u32[]{:S(2)}) copy-start(s32[16]{0:T(128)} %param.12) | copy-start | bytes 196
  9.6 13.1 %copy-start.16 = (s32[16,8]{0,1:T(8,128)S(1)}, s32[16,8]{0,1:T(8,128)}, u32[]{:S(2)}) copy-start(s32[16,8]{0,1:T(8,128)} %param.13) | copy-start | bytes 1540
  9.9 1.4 copy-start.10
  10.0 4.8 %copy-start.12 = (bf16[768,192]{1,0:T(8,128)(2,1)}, bf16[768,192]{1,0:T(8,128)(2,1)S(1)}, u32[]{:S(2)}) copy-start(bf16[768,192]{1,0:T(8,128)(2,1)S(1)} %get-tuple-element.19) | copy-start | bytes 884740
  11.4 73.6 %collective-permute-start = (bf16[512,384]{1,0:T(8,128)(2,1)}, bf16[512,384]{1,0:T(8,128)(2,1)}, u32[]{:S(2)}, u32[]{:S(2)}) collective-permute-start(bf16[512,384]{1,0:T(8,128)(2,1)} %fusion.8), channel_id=1, source_target_pairs={{0,8},{4,12},{8,16},{12,20},{16,24},{20,28},{1,9},{5,13},{9,17},{1... | collective-permute-start | bytes 1179656 | tf_op jit(solution)/shard_map/ppermute | solution.py:18
  14.8 98.2 %collective-permute-start.1 = (bf16[512,384]{1,0:T(8,128)(2,1)}, bf16[512,384]{1,0:T(8,128)(2,1)}, u32[]{:S(2)}, u32[]{:S(2)}) collective-permute-start(bf16[512,384]{1,0:T(8,128)(2,1)} %fusion.8), channel_id=1, source_target_pairs={{0,4},{4,8},{8,12},{12,16},{16,20},{20,24},{24,28},{1,5},{5,9},{9,... | collective-permute-start | bytes 1179656 | tf_op jit(solution)/shard_map/ppermute | solution.py:18
  16.7 106.3 %collective-permute-start.2 = (bf16[512,384]{1,0:T(8,128)(2,1)}, bf16[512,384]{1,0:T(8,128)(2,1)}, u32[]{:S(2)}, u32[]{:S(2)}) collective-permute-start(bf16[512,384]{1,0:T(8,128)(2,1)} %fusion.8), channel_id=1, source_target_pairs={{4,0},{8,4},{12,8},{16,12},{20,16},{24,20},{28,24},{5,1},{9,5},{13... | collective-permute-start | bytes 1179656 | tf_op jit(solution)/shard_map/ppermute | solution.py:18
  20.4 120.2 %collective-permute-start.3 = (bf16[512,384]{1,0:T(8,128)(2,1)}, bf16[512,384]{1,0:T(8,128)(2,1)}, u32[]{:S(2)}, u32[]{:S(2)}) collective-permute-start(bf16[512,384]{1,0:T(8,128)(2,1)} %fusion.8), channel_id=1, source_target_pairs={{8,0},{12,4},{16,8},{20,12},{24,16},{28,20},{9,1},{13,5},{17,9},{2... | collective-permute-start | bytes 1179656 | tf_op jit(solution)/shard_map/ppermute | solution.py:18
  30.5 0.6 copy-start.17
  73.7 4.1 %copy-start.11 = (bf16[768,192]{1,0:T(8,128)(2,1)S(1)}, bf16[768,192]{1,0:T(8,128)(2,1)}, u32[]{:S(2)}) copy-start(bf16[768,192]{1,0:T(8,128)(2,1)} %copy-done.10) | copy-start | bytes 884740
  73.7 4.1 %copy-start.13 = (bf16[768,192]{1,0:T(8,128)(2,1)S(1)}, bf16[768,192]{1,0:T(8,128)(2,1)}, u32[]{:S(2)}) copy-start(bf16[768,192]{1,0:T(8,128)(2,1)} %copy-done.12) | copy-start | bytes 884740
  80.4 69.5 %collective-permute-start.4 = (bf16[1536,384]{1,0:T(8,128)(2,1)}, bf16[1536,384]{1,0:T(8,128)(2,1)}, u32[]{:S(2)}, u32[]{:S(2)}) collective-permute-start(bf16[1536,384]{1,0:T(8,128)(2,1)} %convolution_convert_fusion), channel_id=1, source_target_pairs={{0,8},{4,12},{8,16},{12,20},{16,24},{20,28},{1,9},{5,13},{9,17},{1... | collective-permute-start | bytes 3538952 | tf_op jit(solution)/shard_map/ppermute | solution.py:18
  85.0 39.8 %copy-start.1 = (bf16[1,128,384]{2,1,0:T(8,128)(2,1)}, bf16[1,128,384]{2,1,0:T(8,128)(2,1)S(1)}, u32[]{:S(2)}) copy-start(bf16[1,128,384]{2,1,0:T(8,128)(2,1)S(1)} %fusion.9) | copy-start | bytes 294916
  85.0 26.0 %collective-permute-start.8 = (bf16[1,128,384]{2,1,0:T(8,128)(2,1)S(1)}, bf16[1,128,384]{2,1,0:T(8,128)(2,1)S(1)}, u32[]{:S(2)}, u32[]{:S(2)}) collective-permute-start(bf16[1,128,384]{2,1,0:T(8,128)(2,1)S(1)} %fusion.9), channel_id=1, source_target_pairs={{0,4},{4,8},{8,12},{12,16},{16,20},{20,24},{24,28},{28,0},{1,5},{5... | collective-permute-start | bytes 294920 | tf_op jit(solution)/shard_map/ppermute | solution.py:28
  111.0 31.3 %copy-start.3 = (bf16[1,128,384]{2,1,0:T(8,128)(2,1)}, bf16[1,128,384]{2,1,0:T(8,128)(2,1)S(1)}, u32[]{:S(2)}) copy-start(bf16[1,128,384]{2,1,0:T(8,128)(2,1)S(1)} %collective-permute-done.8) | copy-start | bytes 294916
  111.0 41.3 %collective-permute-start.5 = (bf16[1536,384]{1,0:T(8,128)(2,1)}, bf16[1536,384]{1,0:T(8,128)(2,1)}, u32[]{:S(2)}, u32[]{:S(2)}) collective-permute-start(bf16[1536,384]{1,0:T(8,128)(2,1)} %convolution_convert_fusion), channel_id=1, source_target_pairs={{0,4},{4,8},{8,12},{12,16},{16,20},{20,24},{24,28},{1,5},{5,9},{9,... | collective-permute-start | bytes 3538952 | tf_op jit(solution)/shard_map/ppermute | solution.py:18
  113.0 31.5 %copy-start.6 = (bf16[512,768]{1,0:T(8,128)(2,1)S(1)}, bf16[512,768]{1,0:T(8,128)(2,1)}, u32[]{:S(2)}) copy-start(bf16[512,768]{1,0:T(8,128)(2,1)} %param.8) | copy-start | bytes 2359300
  113.0 7.8 %collective-permute-start.9 = (bf16[2,128,384]{2,1,0:T(8,128)(2,1)S(1)}, bf16[2,128,384]{2,1,0:T(8,128)(2,1)S(1)}, u32[]{:S(2)}, u32[]{:S(2)}) collective-permute-start(bf16[2,128,384]{2,1,0:T(8,128)(2,1)S(1)} %pad_maximum_fusion.3), channel_id=1, source_target_pairs={{0,8},{4,12},{8,16},{12,20},{16,24},{20,28},{24,0},{28,4},{1,9},{5... | collective-permute-start | bytes 589832 | tf_op jit(solution)/shard_map/ppermute | solution.py:28
  120.8 23.7 %copy-start.8 = (bf16[2,128,384]{2,1,0:T(8,128)(2,1)}, bf16[2,128,384]{2,1,0:T(8,128)(2,1)S(1)}, u32[]{:S(2)}) copy-start(bf16[2,128,384]{2,1,0:T(8,128)(2,1)S(1)} %collective-permute-done.9) | copy-start | bytes 589828
  121.6 26.3 %collective-permute-start.10 = (bf16[4,128,384]{2,1,0:T(8,128)(2,1)}, bf16[4,128,384]{2,1,0:T(8,128)(2,1)}, u32[]{:S(2)}, u32[]{:S(2)}) collective-permute-start(bf16[4,128,384]{2,1,0:T(8,128)(2,1)} %pad_maximum_fusion.2), channel_id=1, source_target_pairs={{0,16},{4,20},{8,24},{12,28},{16,0},{20,4},{24,8},{28,12},{1,17},{... | collective-permute-start | bytes 1179656 | tf_op jit(solution)/shard_map/ppermute | solution.py:28
  124.8 39.2 %collective-permute-start.6 = (bf16[1536,384]{1,0:T(8,128)(2,1)}, bf16[1536,384]{1,0:T(8,128)(2,1)}, u32[]{:S(2)}, u32[]{:S(2)}) collective-permute-start(bf16[1536,384]{1,0:T(8,128)(2,1)} %convolution_convert_fusion), channel_id=1, source_target_pairs={{4,0},{8,4},{12,8},{16,12},{20,16},{24,20},{28,24},{5,1},{9,5},{13... | collective-permute-start | bytes 3538952 | tf_op jit(solution)/shard_map/ppermute | solution.py:18
  142.4 38.4 %collective-permute-start.7 = (bf16[1536,384]{1,0:T(8,128)(2,1)}, bf16[1536,384]{1,0:T(8,128)(2,1)}, u32[]{:S(2)}, u32[]{:S(2)}) collective-permute-start(bf16[1536,384]{1,0:T(8,128)(2,1)} %convolution_convert_fusion), channel_id=1, source_target_pairs={{8,0},{12,4},{16,8},{20,12},{24,16},{28,20},{9,1},{13,5},{17,9},{2... | collective-permute-start | bytes 3538952 | tf_op jit(solution)/shard_map/ppermute | solution.py:18
  145.7 0.9 copy-start.7
  146.6 1.2 copy-start.2
  146.7 1.2 copy-start.4
  146.7 1.2 copy-start.9
  183.2 42.3 %copy-start.15 = (pred[768]{0:T(1024)(128)(4,1)S(1)}, pred[768]{0:T(1024)(128)(4,1)}, u32[]{:S(2)}) copy-start(pred[768]{0:T(1024)(128)(4,1)} %broadcast_in_dim.32) | copy-start | bytes 2308
  219.6 25.0 %collective-permute-start.11 = (bf16[512,192]{1,0:T(8,128)(2,1)}, bf16[512,192]{1,0:T(8,128)(2,1)}, u32[]{:S(2)}, u32[]{:S(2)}) collective-permute-start(bf16[512,192]{1,0:T(8,128)(2,1)} %bitcast.12), channel_id=1, source_target_pairs={{0,1},{1,2},{2,3},{3,0},{4,5},{5,6},{6,7},{7,4},{8,9},{9,10},{10,1... | collective-permute-start | bytes 589832 | tf_op jit(solution)/shard_map/ppermute | solution.py:198
  219.6 25.0 %collective-permute-start.12 = (bf16[512,192]{1,0:T(8,128)(2,1)}, bf16[512,192]{1,0:T(8,128)(2,1)}, u32[]{:S(2)}, u32[]{:S(2)}) collective-permute-start(bf16[512,192]{1,0:T(8,128)(2,1)} %bitcast.13), channel_id=1, source_target_pairs={{0,2},{1,3},{2,0},{3,1},{4,6},{5,7},{6,4},{7,5},{8,10},{9,11},{10,... | collective-permute-start | bytes 589832 | tf_op jit(solution)/shard_map/ppermute | solution.py:198
  223.3 21.4 %collective-permute-start.13 = (bf16[512,192]{1,0:T(8,128)(2,1)}, bf16[512,192]{1,0:T(8,128)(2,1)}, u32[]{:S(2)}, u32[]{:S(2)}) collective-permute-start(bf16[512,192]{1,0:T(8,128)(2,1)} %bitcast.14), channel_id=1, source_target_pairs={{0,3},{1,0},{2,1},{3,2},{4,7},{5,4},{6,5},{7,6},{8,11},{9,8},{10,9... | collective-permute-start | bytes 589832 | tf_op jit(solution)/shard_map/ppermute | solution.py:198
Sparse Core Ops, SparseCore 0:
  8.9 64.7 all-gather.1

commit v8 on v7

--- a/solution.py
+++ b/solution.py
@@ -120,10 +120,20 @@
 
 
 def window_of(x, axis):
-    parts = []
-    for offset in (2, 1, 0, -1, -2):
-        parts.append(x if offset == 0 else shifted(x, "seq", offset))
-    return jnp.concatenate(parts, axis=axis)
+    size = lax.axis_size("seq")
+    beside = {}
+    if size == 8:
+        plus2 = lax.ppermute(x, "seq", [(i, i + 2) for i in range(6) if i not in (2, 3)])
+        minus2 = lax.ppermute(x, "seq", [(i, i - 2) for i in range(2, 8) if i not in (4, 5)])
+        beside[2] = plus2 + lax.ppermute(minus2, "seq", [(0, 4), (1, 5)])
+        beside[-2] = minus2 + lax.ppermute(plus2, "seq", [(6, 2), (7, 3)])
+    else:
+        beside[2] = shifted(x, "seq", 2)
+        beside[-2] = shifted(x, "seq", -2)
+    beside[1] = shifted(x, "seq", 1)
+    beside[-1] = shifted(x, "seq", -1)
+    beside[0] = x
+    return jnp.concatenate([beside[k] for k in (2, 1, 0, -1, -2)], axis=axis)
 
 
 def shards(tokens, w_qkv, w_out, neighbours, near_count, anchors):

time: 254 us -> 261 us (1.028)
  the two profiles are of different devices: /device:TPU:2 before, /device:TPU:10 now
where the time goes in v8:
time: 261 us; the launch traced here: 260 us
  waiting for transfers between devices  103 us (39%)
  Pallas kernels  49 us (19%)
  starting transfers between devices  35 us (13%)
  local copies, waits for them, and re-layouts  31.2 us (12%)
  other arithmetic  18.3 us (7%)
  between operations  13.9 us (5%)
  matrix products  9.64 us (4%)
    pallas_call x2, Pallas kernels, attention(): pl.pallas_call(kernel, out_shape=jax.ShapeDtypeStruct(queries.shape, jnp....  49 us
    all_gather x1, waiting for transfers between devices, shards(): gathered = lax.all_gather(tokens, 'head', axis=0, tiled=True)  45 us
    ppermute x2, waiting for transfers between devices, window_of(): beside[-2] = minus2 + lax.ppermute(plus2, 'seq', [(6, 2), (7, 3)])  20.9 us
    unnamed x45, local copies, waits for them, and re-layouts  13.6 us
    ppermute x3, waiting for transfers between devices, gather_all(): got = lax.ppermute(held, axis, pairs)  12.9 us
    ppermute x4, starting transfers between devices, shifted(): return lax.ppermute(x, axis, pairs)  12.5 us
    ppermute x2, waiting for transfers between devices, window_of(): lax.ppermute(x, 'seq', [(i, i - 2) for i in range(2, 8) if i not in (4, 5)])  11.7 us
    ppermute x2, starting transfers between devices, window_of(): lax.ppermute(x, 'seq', [(i, i - 2) for i in range(2, 8) if i not in (4, 5)])  6.7 us
  transfers between devices with their start and end apart: 19, of which 8 were waited for; matrix products, arithmetic and copies ran while one was open for 19% of the time, Pallas kernels for 6%

profile of v8, /device:TPU:10, one launch (start us, length us, event | category | flops | bytes accessed | tf_op | source)
XLA Modules:
  0.0 260.0 jit_solution(6382086179382169812)
XLA Ops:
  7.3 2.3 fusion.45
  10.0 1.4 fusion.8
  11.4 3.2 %collective-permute-start.1 = (bf16[512,384]{1,0:T(8,128)(2,1)}, bf16[512,384]{1,0:T(8,128)(2,1)}, u32[]{:S(2)}, u32[]{:S(2)}) collective-permute-start(bf16[512,384]{1,0:T(8,128)(2,1)} %fusion.8), channel_id=1, source_target_pairs={{8,0},{12,4},{24,16},{28,20},{9,1},{13,5},{25,17},{29,21},{10,2},{... | collective-permute-start | bytes 1179656 | tf_op jit(solution)/shard_map/ppermute | solution.py:127
  14.6 1.3 collective-permute-start
  15.8 1.9 collective-permute-start.3
  17.8 4.2 %collective-permute-start.4 = (bf16[512,384]{1,0:T(8,128)(2,1)}, bf16[512,384]{1,0:T(8,128)(2,1)}, u32[]{:S(2)}, u32[]{:S(2)}) collective-permute-start(bf16[512,384]{1,0:T(8,128)(2,1)} %fusion.8), channel_id=1, source_target_pairs={{4,0},{8,4},{12,8},{16,12},{20,16},{24,20},{28,24},{5,1},{9,5},{13... | collective-permute-start | bytes 1179656 | tf_op jit(solution)/shard_map/ppermute | solution.py:18
  23.7 2.5 gather_fusion.2
  26.3 45.0 %all-gather.2.cloned.1.call-done = bf16[2048,768]{1,0:T(8,128)(2,1)} async-done(((bf16[512,768]{1,0:T(8,128)(2,1)}), bf16[2048,768]{1,0:T(8,128)(2,1)}) %all-gather.2.cloned.1.call-update) | async-done | bytes 3145744 | tf_op jit(solution)/shard_map/all_gather | solution.py:156
  71.3 3.9 %fusion.7 = bf16[1536,768]{1,0:T(8,128)(2,1)S(1)} fusion(s32[]{:T(128)S(6)} %add.157, bf16[2048,768]{1,0:T(8,128)(2,1)} %all-gather.2.cloned.1.call-done), kind=kLoop, calls=%fused_computation.11 | loop fusion | flops 4718592 | bytes 5505028 | tf_op jit(solution)/shard_map/jit(_roll_dynamic)/concatenate | solution.py:157
  75.3 2.5 convolution_convert_fusion
  77.8 3.5 %collective-permute-start.7 = (bf16[1536,384]{1,0:T(8,128)(2,1)}, bf16[1536,384]{1,0:T(8,128)(2,1)}, u32[]{:S(2)}, u32[]{:S(2)}) collective-permute-start(bf16[1536,384]{1,0:T(8,128)(2,1)} %convolution_convert_fusion), channel_id=1, source_target_pairs={{8,0},{12,4},{24,16},{28,20},{9,1},{13,5},{25,17},{29,21},{10,2},{... | collective-permute-start | bytes 3538952 | tf_op jit(solution)/shard_map/ppermute | solution.py:127
  81.3 2.5 gather_fusion.1
  84.0 1.4 collective-permute-start.2
  89.3 1.3 collective-permute-start.5
  90.6 2.0 add_dynamic-update-slice_fusion.3
  92.6 1.3 collective-permute-start.6
  93.9 11.7 %collective-permute-done.7 = bf16[1536,384]{1,0:T(8,128)(2,1)} collective-permute-done((bf16[1536,384]{1,0:T(8,128)(2,1)}, bf16[1536,384]{1,0:T(8,128)(2,1)}, u32[]{:S(2)}, u32[]{:S(2)}) %collective-permute-start.7) | collective-permute-done | bytes 1179680 | tf_op jit(solution)/shard_map/ppermute | solution.py:127
  105.6 1.7 collective-permute-start.8
  107.3 1.6 fusion.9
  108.9 1.8 constant_dynamic-update-slice_fusion.2
  110.7 12.2 %collective-permute-done.12 = bf16[1,128,384]{2,1,0:T(8,128)(2,1)S(1)} collective-permute-done((bf16[1,128,384]{2,1,0:T(8,128)(2,1)S(1)}, bf16[1,128,384]{2,1,0:T(8,128)(2,1)S(1)}, u32[]{:S(2)}, u32[]{:S(2)}) %collective-permute-start.12) | collective-permute-done | bytes 98336 | tf_op jit(solution)/shard_map/ppermute | solution.py:28
  123.0 1.8 constant_dynamic-update-slice_fusion.1
  124.8 1.8 constant_dynamic-update-slice_fusion
  126.6 3.2 %collective-permute-start.9 = (bf16[1536,384]{1,0:T(8,128)(2,1)}, bf16[1536,384]{1,0:T(8,128)(2,1)}, u32[]{:S(2)}, u32[]{:S(2)}) collective-permute-start(bf16[1536,384]{1,0:T(8,128)(2,1)} %convolution_convert_fusion), channel_id=1, source_target_pairs={{0,4},{4,8},{8,12},{12,16},{16,20},{20,24},{24,28},{1,5},{5,9},{9,... | collective-permute-start | bytes 3538952 | tf_op jit(solution)/shard_map/ppermute | solution.py:18
  130.6 1.4 collective-permute-start.14
  132.0 1.9 add_dynamic-update-slice_fusion.2.refs_0_
  133.8 3.2 %collective-permute-start.10 = (bf16[1536,384]{1,0:T(8,128)(2,1)}, bf16[1536,384]{1,0:T(8,128)(2,1)}, u32[]{:S(2)}, u32[]{:S(2)}) collective-permute-start(bf16[1536,384]{1,0:T(8,128)(2,1)} %convolution_convert_fusion), channel_id=1, source_target_pairs={{4,0},{8,4},{12,8},{16,12},{20,16},{24,20},{28,24},{5,1},{9,5},{13... | collective-permute-start | bytes 3538952 | tf_op jit(solution)/shard_map/ppermute | solution.py:18
  137.1 1.3 fusion.4
  138.3 0.9 copy-done.9
  139.3 1.2 copy.46
  141.1 2.0 pad_maximum_fusion
  143.2 1.5 collective-permute-start.11
  144.7 2.9 %add_dynamic-update-slice_fusion.1 = bf16[7680,384]{1,0:T(8,128)(2,1)} fusion(bf16[1536,384]{1,0:T(8,128)(2,1)} %collective-permute-done.6, bf16[1536,384]{1,0:T(8,128)(2,1)} %collective-permute-done.8), kind=kLoop, calls=%fused_computation.17 | loop fusion | flops 2359295 | bytes 3538944
  147.6 2.4 constant_dynamic-update-slice_fusion.5
  150.0 2.4 constant_dynamic-update-slice_fusion.4
  152.4 6.1 %collective-permute-done.10 = bf16[1536,384]{1,0:T(8,128)(2,1)} collective-permute-done((bf16[1536,384]{1,0:T(8,128)(2,1)}, bf16[1536,384]{1,0:T(8,128)(2,1)}, u32[]{:S(2)}, u32[]{:S(2)}) %collective-permute-start.10) | collective-permute-done | bytes 1179680 | tf_op jit(solution)/shard_map/ppermute | solution.py:18
  158.5 2.4 constant_dynamic-update-slice_fusion.3
  160.9 20.9 %collective-permute-done.11 = bf16[1536,384]{1,0:T(8,128)(2,1)S(1)} collective-permute-done((bf16[1536,384]{1,0:T(8,128)(2,1)}, bf16[1536,384]{1,0:T(8,128)(2,1)S(1)}, u32[]{:S(2)}, u32[]{:S(2)}) %collective-permute-start.11) | collective-permute-done | bytes 1179680 | tf_op jit(solution)/shard_map/ppermute | solution.py:129
  181.8 2.7 %add_dynamic-update-slice_fusion.refs_1_ = bf16[7680,384]{1,0:T(8,128)(2,1)} fusion(bf16[7680,384]{1,0:T(8,128)(2,1)} %constant_dynamic-update-slice_fusion.3, bf16[1536,384]{1,0:T(8,128)(2,1)} %collective-permute-done.7, bf16[1536,384]{1,0:T(8,128)(2,1)S(1)} %collective-permute-done.11), kind=kLoop, calls=%fused_computation.16 | loop fusion | flops 2359296 | bytes 3538944 | tf_op jit(solution)/shard_map/concatenate | solution.py:136
  184.5 34.5 %shard_map.65 = bf16[12,128,192]{2,1,0:T(8,128)(2,1)} custom-call(s32[12]{0:T(128)} %slice.67.count, s32[12,20]{1,0:T(8,128)} %slice.85.source, s32[12,20]{1,0:T(8,128)} %slice.86.rows, bf16[12,128,192]{2,1,0:T(8,128)(2,1)} %bitcast.38, bf16[2560,384]{1,0:T(8,128)(2,1)} %add_dynamic-update-slice_fusion.2.refs_0_, ...), custom_call_target="tpu_custom_call" | custom-call | flops 3019898880 | bytes 9830400 | tf_op jit(solution)/shard_map/pallas_call | solution.py:95
  219.0 2.0 fusion.46
  221.0 1.6 collective-permute-start.15
  222.6 4.2 %collective-permute-start.16 = (bf16[512,192]{1,0:T(8,128)(2,1)}, bf16[512,192]{1,0:T(8,128)(2,1)}, u32[]{:S(2)}, u32[]{:S(2)}) collective-permute-start(bf16[512,192]{1,0:T(8,128)(2,1)} %bitcast.13), channel_id=1, source_target_pairs={{0,2},{1,3},{2,0},{3,1},{4,6},{5,7},{6,4},{7,5},{8,10},{9,11},{10,... | collective-permute-start | bytes 589832 | tf_op jit(solution)/shard_map/ppermute | solution.py:208
  228.2 0.9 slice.83
  229.1 0.9 copy.44
  230.0 14.6 %shard_map.64 = bf16[4,128,192]{2,1,0:T(8,128)(2,1)} custom-call(s32[4]{0:T(128)} %bitcast.40, s32[4,20]{1,0:T(4,128)} %slice.81.source, s32[4,20]{1,0:T(4,128)} %slice.82.rows, bf16[4,128,192]{2,1,0:T(8,128)(2,1)} %bitcast.37, bf16[2560,384]{1,0:T(8,128)(2,1)} %add_dynamic-update-slice_fusion.2.refs_0_, ...), custom_call_target="tpu_custom_call" | custom-call | flops 1006632960 | bytes 9043968 | tf_op jit(solution)/shard_map/pallas_call | solution.py:95
  245.3 5.0 %collective-permute-done.17 = bf16[512,192]{1,0:T(8,128)(2,1)} collective-permute-done((bf16[512,192]{1,0:T(8,128)(2,1)}, bf16[512,192]{1,0:T(8,128)(2,1)}, u32[]{:S(2)}, u32[]{:S(2)}) %collective-permute-start.17) | collective-permute-done | bytes 196640 | tf_op jit(solution)/shard_map/ppermute | solution.py:208
  250.3 2.9 %convolution_convert_fusion.1 = bf16[512,768]{1,0:T(8,128)(2,1)} fusion(bf16[768,768]{1,0:T(8,128)(2,1)S(1)} %bitcast_select_fusion, bf16[512,192]{1,0:T(8,128)(2,1)} %collective-permute-done.17, bf16[512,192]{1,0:T(8,128)(2,1)} %collective-permute-done.16, bf16[512,192]{1,0:T(8,128)(2,1)} %collective-permute-done.15, bf16[512,192]{1,0:T(8,128)(2,1)} %bitcast.39), kind=kOutput, calls=%fused_computation.12 | convolution fusion | flops 607518720 | bytes 2752512 | tf_op jit(solution)/shard_map/dot_general | solution.py:214
  (96 shorter events, 10.7 us)
Async XLA Ops:
  6.5 82.0 %copy-start = (bf16[768,768]{1,0:T(8,128)(2,1)S(1)}, bf16[768,768]{1,0:T(8,128)(2,1)}, u32[]{:S(2)}) copy-start(bf16[768,768]{1,0:T(8,128)(2,1)} %param.10) | copy-start | bytes 3538948
  6.5 64.8 %all-gather.2.cloned.1.call-start = ((), (), s32[]{:S(2)}) async-start(), calls=%async_computation | async-start | bytes 3932160 | tf_op jit(solution)/shard_map/all_gather | solution.py:156
  7.3 2.7 %copy-start.7 = (bf16[512,768]{1,0:T(8,128)(2,1)S(1)}, bf16[512,768]{1,0:T(8,128)(2,1)}, u32[]{:S(2)}) copy-start(bf16[512,768]{1,0:T(8,128)(2,1)} %param.8) | copy-start | bytes 2359300
  9.6 12.4 %copy-start.14 = (s32[16,12]{1,0:T(8,128)S(1)}, s32[16,12]{1,0:T(8,128)}, u32[]{:S(2)}) copy-start(s32[16,12]{1,0:T(8,128)} %param.11) | copy-start | bytes 2308
  9.6 12.6 %copy-start.18 = (s32[16]{0:T(128)S(1)}, s32[16]{0:T(128)}, u32[]{:S(2)}) copy-start(s32[16]{0:T(128)} %param.12) | copy-start | bytes 196
  9.6 12.7 %copy-start.16 = (s32[16,8]{0,1:T(8,128)S(1)}, s32[16,8]{0,1:T(8,128)}, u32[]{:S(2)}) copy-start(s32[16,8]{0,1:T(8,128)} %param.13) | copy-start | bytes 1540
  9.9 65.3 %copy-start.12 = (bf16[768,192]{1,0:T(8,128)(2,1)}, bf16[768,192]{1,0:T(8,128)(2,1)S(1)}, u32[]{:S(2)}) copy-start(bf16[768,192]{1,0:T(8,128)(2,1)S(1)} %get-tuple-element.18) | copy-start | bytes 884740
  10.0 65.3 %copy-start.13 = (bf16[768,192]{1,0:T(8,128)(2,1)}, bf16[768,192]{1,0:T(8,128)(2,1)S(1)}, u32[]{:S(2)}) copy-start(bf16[768,192]{1,0:T(8,128)(2,1)S(1)} %get-tuple-element.19) | copy-start | bytes 884740
  11.4 72.6 %collective-permute-start.1 = (bf16[512,384]{1,0:T(8,128)(2,1)}, bf16[512,384]{1,0:T(8,128)(2,1)}, u32[]{:S(2)}, u32[]{:S(2)}) collective-permute-start(bf16[512,384]{1,0:T(8,128)(2,1)} %fusion.8), channel_id=1, source_target_pairs={{8,0},{12,4},{24,16},{28,20},{9,1},{13,5},{25,17},{29,21},{10,2},{... | collective-permute-start | bytes 1179656 | tf_op jit(solution)/shard_map/ppermute | solution.py:127
  14.6 74.8 %collective-permute-start = (bf16[512,384]{1,0:T(8,128)(2,1)}, bf16[512,384]{1,0:T(8,128)(2,1)}, u32[]{:S(2)}, u32[]{:S(2)}) collective-permute-start(bf16[512,384]{1,0:T(8,128)(2,1)} %fusion.8), channel_id=1, source_target_pairs={{0,8},{4,12},{16,24},{20,28},{1,9},{5,13},{17,25},{21,29},{2,10},{... | collective-permute-start | bytes 1179656 | tf_op jit(solution)/shard_map/ppermute | solution.py:126
  15.8 93.0 %collective-permute-start.3 = (bf16[512,384]{1,0:T(8,128)(2,1)}, bf16[512,384]{1,0:T(8,128)(2,1)}, u32[]{:S(2)}, u32[]{:S(2)}) collective-permute-start(bf16[512,384]{1,0:T(8,128)(2,1)} %fusion.8), channel_id=1, source_target_pairs={{0,4},{4,8},{8,12},{12,16},{16,20},{20,24},{24,28},{1,5},{5,9},{9,... | collective-permute-start | bytes 1179656 | tf_op jit(solution)/shard_map/ppermute | solution.py:18
  17.8 107.0 %collective-permute-start.4 = (bf16[512,384]{1,0:T(8,128)(2,1)}, bf16[512,384]{1,0:T(8,128)(2,1)}, u32[]{:S(2)}, u32[]{:S(2)}) collective-permute-start(bf16[512,384]{1,0:T(8,128)(2,1)} %fusion.8), channel_id=1, source_target_pairs={{4,0},{8,4},{12,8},{16,12},{20,16},{24,20},{28,24},{5,1},{9,5},{13... | collective-permute-start | bytes 1179656 | tf_op jit(solution)/shard_map/ppermute | solution.py:18
  75.3 2.5 copy-start.1
  77.8 27.8 %collective-permute-start.7 = (bf16[1536,384]{1,0:T(8,128)(2,1)}, bf16[1536,384]{1,0:T(8,128)(2,1)}, u32[]{:S(2)}, u32[]{:S(2)}) collective-permute-start(bf16[1536,384]{1,0:T(8,128)(2,1)} %convolution_convert_fusion), channel_id=1, source_target_pairs={{8,0},{12,4},{24,16},{28,20},{9,1},{13,5},{25,17},{29,21},{10,2},{... | collective-permute-start | bytes 3538952 | tf_op jit(solution)/shard_map/ppermute | solution.py:127
  84.0 6.7 %collective-permute-start.2 = (bf16[512,384]{1,0:T(8,128)(2,1)}, bf16[512,384]{1,0:T(8,128)(2,1)}, u32[]{:S(2)}, u32[]{:S(2)}) collective-permute-start(bf16[512,384]{1,0:T(8,128)(2,1)} %collective-permute-done.1), channel_id=1, source_target_pairs={{0,16},{4,20},{1,17},{5,21},{2,18},{6,22},{3,19},{7,23}} | collective-permute-start | bytes 1179656 | tf_op jit(solution)/shard_map/ppermute | solution.py:128
  86.6 1.9 copy-start.17
  89.3 42.6 %collective-permute-start.5 = (bf16[512,384]{1,0:T(8,128)(2,1)}, bf16[512,384]{1,0:T(8,128)(2,1)S(1)}, u32[]{:S(2)}, u32[]{:S(2)}) collective-permute-start(bf16[512,384]{1,0:T(8,128)(2,1)} %collective-permute-done), channel_id=1, source_target_pairs={{24,8},{28,12},{25,9},{29,13},{26,10},{30,14},{27,11},{31,15}} | collective-permute-start | bytes 1179656 | tf_op jit(solution)/shard_map/ppermute | solution.py:129
  92.6 50.6 %collective-permute-start.6 = (bf16[1536,384]{1,0:T(8,128)(2,1)}, bf16[1536,384]{1,0:T(8,128)(2,1)}, u32[]{:S(2)}, u32[]{:S(2)}) collective-permute-start(bf16[1536,384]{1,0:T(8,128)(2,1)} %convolution_convert_fusion), channel_id=1, source_target_pairs={{0,8},{4,12},{16,24},{20,28},{1,9},{5,13},{17,25},{21,29},{2,10},{... | collective-permute-start | bytes 3538952 | tf_op jit(solution)/shard_map/ppermute | solution.py:126
  105.6 39.1 %collective-permute-start.8 = (bf16[1536,384]{1,0:T(8,128)(2,1)}, bf16[1536,384]{1,0:T(8,128)(2,1)}, u32[]{:S(2)}, u32[]{:S(2)}) collective-permute-start(bf16[1536,384]{1,0:T(8,128)(2,1)} %collective-permute-done.7), channel_id=1, source_target_pairs={{0,16},{4,20},{1,17},{5,21},{2,18},{6,22},{3,19},{7,23}} | collective-permute-start | bytes 3538952 | tf_op jit(solution)/shard_map/ppermute | solution.py:128
  108.9 25.0 %copy-start.3 = (bf16[1,128,384]{2,1,0:T(8,128)(2,1)}, bf16[1,128,384]{2,1,0:T(8,128)(2,1)S(1)}, u32[]{:S(2)}) copy-start(bf16[1,128,384]{2,1,0:T(8,128)(2,1)S(1)} %fusion.9) | copy-start | bytes 294916
  108.9 14.0 %collective-permute-start.12 = (bf16[1,128,384]{2,1,0:T(8,128)(2,1)S(1)}, bf16[1,128,384]{2,1,0:T(8,128)(2,1)S(1)}, u32[]{:S(2)}, u32[]{:S(2)}) collective-permute-start(bf16[1,128,384]{2,1,0:T(8,128)(2,1)S(1)} %fusion.9), channel_id=1, source_target_pairs={{0,4},{4,8},{8,12},{12,16},{16,20},{20,24},{24,28},{28,0},{1,5},{5... | collective-permute-start | bytes 294920 | tf_op jit(solution)/shard_map/ppermute | solution.py:28
  110.7 26.3 %copy-start.2 = (bf16[1536,768]{1,0:T(8,128)(2,1)S(1)}, bf16[1536,768]{1,0:T(8,128)(2,1)}, u32[]{:S(2)}) copy-start(bf16[1536,768]{1,0:T(8,128)(2,1)} %copy-done.1) | copy-start | bytes 7077892
  110.7 26.3 %copy-start.8 = (bf16[512,768]{1,0:T(8,128)(2,1)S(1)}, bf16[512,768]{1,0:T(8,128)(2,1)}, u32[]{:S(2)}) copy-start(bf16[512,768]{1,0:T(8,128)(2,1)} %param.8) | copy-start | bytes 2359300
  122.9 10.9 %copy-start.5 = (bf16[1,128,384]{2,1,0:T(8,128)(2,1)}, bf16[1,128,384]{2,1,0:T(8,128)(2,1)S(1)}, u32[]{:S(2)}) copy-start(bf16[1,128,384]{2,1,0:T(8,128)(2,1)S(1)} %collective-permute-done.12) | copy-start | bytes 294916
  122.9 6.8 %collective-permute-start.13 = (bf16[2,128,384]{2,1,0:T(8,128)(2,1)S(1)}, bf16[2,128,384]{2,1,0:T(8,128)(2,1)S(1)}, u32[]{:S(2)}, u32[]{:S(2)}) collective-permute-start(bf16[2,128,384]{2,1,0:T(8,128)(2,1)S(1)} %pad_maximum_fusion.3), channel_id=1, source_target_pairs={{0,8},{4,12},{8,16},{12,20},{16,24},{20,28},{24,0},{28,4},{1,9},{5... | collective-permute-start | bytes 589832 | tf_op jit(solution)/shard_map/ppermute | solution.py:28
  126.6 21.0 %collective-permute-start.9 = (bf16[1536,384]{1,0:T(8,128)(2,1)}, bf16[1536,384]{1,0:T(8,128)(2,1)}, u32[]{:S(2)}, u32[]{:S(2)}) collective-permute-start(bf16[1536,384]{1,0:T(8,128)(2,1)} %convolution_convert_fusion), channel_id=1, source_target_pairs={{0,4},{4,8},{8,12},{12,16},{16,20},{20,24},{24,28},{1,5},{5,9},{9,... | collective-permute-start | bytes 3538952 | tf_op jit(solution)/shard_map/ppermute | solution.py:18
  129.8 7.3 %copy-start.10 = (bf16[2,128,384]{2,1,0:T(8,128)(2,1)}, bf16[2,128,384]{2,1,0:T(8,128)(2,1)S(1)}, u32[]{:S(2)}) copy-start(bf16[2,128,384]{2,1,0:T(8,128)(2,1)S(1)} %collective-permute-done.13) | copy-start | bytes 589828
  130.6 10.5 %collective-permute-start.14 = (bf16[4,128,384]{2,1,0:T(8,128)(2,1)}, bf16[4,128,384]{2,1,0:T(8,128)(2,1)}, u32[]{:S(2)}, u32[]{:S(2)}) collective-permute-start(bf16[4,128,384]{2,1,0:T(8,128)(2,1)} %pad_maximum_fusion.2), channel_id=1, source_target_pairs={{0,16},{4,20},{8,24},{12,28},{16,0},{20,4},{24,8},{28,12},{1,17},{... | collective-permute-start | bytes 1179656 | tf_op jit(solution)/shard_map/ppermute | solution.py:28
  133.8 24.7 %collective-permute-start.10 = (bf16[1536,384]{1,0:T(8,128)(2,1)}, bf16[1536,384]{1,0:T(8,128)(2,1)}, u32[]{:S(2)}, u32[]{:S(2)}) collective-permute-start(bf16[1536,384]{1,0:T(8,128)(2,1)} %convolution_convert_fusion), channel_id=1, source_target_pairs={{4,0},{8,4},{12,8},{16,12},{20,16},{24,20},{28,24},{5,1},{9,5},{13... | collective-permute-start | bytes 3538952 | tf_op jit(solution)/shard_map/ppermute | solution.py:18
  138.3 0.9 copy-start.9
  139.2 1.9 copy-start.4
  139.2 1.9 copy-start.6
  139.2 1.9 copy-start.11
  143.2 38.7 %collective-permute-start.11 = (bf16[1536,384]{1,0:T(8,128)(2,1)}, bf16[1536,384]{1,0:T(8,128)(2,1)S(1)}, u32[]{:S(2)}, u32[]{:S(2)}) collective-permute-start(bf16[1536,384]{1,0:T(8,128)(2,1)} %collective-permute-done.6), channel_id=1, source_target_pairs={{24,8},{28,12},{25,9},{29,13},{26,10},{30,14},{27,11},{31,15}} | collective-permute-start | bytes 3538952 | tf_op jit(solution)/shard_map/ppermute | solution.py:129
  184.5 42.3 %copy-start.15 = (pred[768]{0:T(1024)(128)(4,1)S(1)}, pred[768]{0:T(1024)(128)(4,1)}, u32[]{:S(2)}) copy-start(pred[768]{0:T(1024)(128)(4,1)} %broadcast_in_dim.32) | copy-start | bytes 2308
  221.0 23.6 %collective-permute-start.15 = (bf16[512,192]{1,0:T(8,128)(2,1)}, bf16[512,192]{1,0:T(8,128)(2,1)}, u32[]{:S(2)}, u32[]{:S(2)}) collective-permute-start(bf16[512,192]{1,0:T(8,128)(2,1)} %bitcast.12), channel_id=1, source_target_pairs={{0,1},{1,2},{2,3},{3,0},{4,5},{5,6},{6,7},{7,4},{8,9},{9,10},{10,1... | collective-permute-start | bytes 589832 | tf_op jit(solution)/shard_map/ppermute | solution.py:208
  222.6 22.7 %collective-permute-start.16 = (bf16[512,192]{1,0:T(8,128)(2,1)}, bf16[512,192]{1,0:T(8,128)(2,1)}, u32[]{:S(2)}, u32[]{:S(2)}) collective-permute-start(bf16[512,192]{1,0:T(8,128)(2,1)} %bitcast.13), channel_id=1, source_target_pairs={{0,2},{1,3},{2,0},{3,1},{4,6},{5,7},{6,4},{7,5},{8,10},{9,11},{10,... | collective-permute-start | bytes 589832 | tf_op jit(solution)/shard_map/ppermute | solution.py:208
  226.8 23.5 %collective-permute-start.17 = (bf16[512,192]{1,0:T(8,128)(2,1)}, bf16[512,192]{1,0:T(8,128)(2,1)}, u32[]{:S(2)}, u32[]{:S(2)}) collective-permute-start(bf16[512,192]{1,0:T(8,128)(2,1)} %bitcast.14), channel_id=1, source_target_pairs={{0,3},{1,0},{2,1},{3,2},{4,7},{5,4},{6,5},{7,6},{8,11},{9,8},{10,9... | collective-permute-start | bytes 589832 | tf_op jit(solution)/shard_map/ppermute | solution.py:208
Sparse Core Ops, SparseCore 0:
  8.9 62.3 all-gather.1

commit v9 on v7

--- a/solution.py
+++ b/solution.py
@@ -123,7 +123,7 @@
     parts = []
     for offset in (2, 1, 0, -1, -2):
         parts.append(x if offset == 0 else shifted(x, "seq", offset))
-    return jnp.concatenate(parts, axis=axis)
+    return parts
 
 
 def shards(tokens, w_qkv, w_out, neighbours, near_count, anchors):
@@ -169,11 +169,10 @@
     chunk = within // own_blocks
     inner = within % own_blocks
     mine = chunk == head_rank
-    row_a = offset_idx * own_blocks + inner
-    row_b = (offset_idx * (block_count - own_blocks)
-             + ((chunk - head_rank) % head_count - 1) * own_blocks + inner)
-    near_row = jnp.where(mine, row_a, row_b)
-    near_src = jnp.where(mine, 0, 1)
+    row_b = ((chunk - head_rank) % head_count - 1) * own_blocks + inner
+    near_row = jnp.where(mine, inner, row_b)
+    offsets = len(kva)
+    near_src = jnp.where(mine, 0, offsets) + offset_idx
     owner = jnp.clip(anchors // block_count, 0, seq_count - 1)
     anch_row = (owner - seq_rank + held_count - 1) % seq_count
     near_used = jnp.arange(neigh)[None, :] < near_count[:, None]
@@ -183,12 +182,12 @@
     valid = jnp.concatenate([near_used, jnp.logical_not(repeated)], axis=1)
     order = jnp.argsort(jnp.logical_not(valid).astype(jnp.int32), axis=1, stable=True)
     every_row = jnp.concatenate([near_row, anch_row], axis=1)
-    every_src = jnp.concatenate([near_src, jnp.full_like(anch_row, 2)], axis=1)
+    every_src = jnp.concatenate([near_src, jnp.full_like(anch_row, 2 * offsets)], axis=1)
     rows = jnp.take_along_axis(every_row, order, axis=1).astype(jnp.int32)
     source = jnp.take_along_axis(every_src, order, axis=1).astype(jnp.int32)
     count = jnp.sum(valid.astype(jnp.int32), axis=1).astype(jnp.int32)
 
-    tables = (kva, kvb, kvanc)
+    tables = tuple(kva) + tuple(kvb) + (kvanc,)
     away = attention(queries[own_blocks:], tables, count[own_blocks:], source[own_blocks:],
                      rows[own_blocks:])
     away = away.reshape(head_count - 1, own_rows, width_here)

time: 254 us -> 260 us (1.024)
  the two profiles are of different devices: /device:TPU:2 before, /device:TPU:12 now
where the time goes in v9:
time: 260 us; the launch traced here: 257 us
  waiting for transfers between devices  74 us (28%)
  Pallas kernels  64 us (25%)
  starting transfers between devices  50.5 us (19%)
  local copies, waits for them, and re-layouts  25.6 us (10%)
  other arithmetic  17.6 us (7%)
  between operations  13.9 us (5%)
  matrix products  11.5 us (4%)
    pallas_call x2, Pallas kernels, attention(): pl.pallas_call(kernel, out_shape=jax.ShapeDtypeStruct(queries.shape, jnp....  64 us
    ppermute x8, starting transfers between devices, shifted(): return lax.ppermute(x, axis, pairs)  43.6 us
    all_gather x1, waiting for transfers between devices, shards(): gathered = lax.all_gather(tokens, 'head', axis=0, tiled=True)  36.1 us
    ppermute x8, waiting for transfers between devices, shifted(): return lax.ppermute(x, axis, pairs)  32.8 us
    ppermute x3, starting transfers between devices, shards(): received[j] = lax.ppermute(away[j - 1], 'head', pairs)  6.12 us
    dot_general x3, matrix products, project_kv(): jnp.dot(x, kv_w, preferred_element_type=jnp.float32).astype(jnp.bfloat16)  5.5 us
  transfers between devices with their start and end apart: 15, of which 4 were waited for; matrix products, arithmetic and copies ran while one was open for 18% of the time, Pallas kernels for 7%

profile of v9, /device:TPU:12, one launch (start us, length us, event | category | flops | bytes accessed | tf_op | source)
XLA Modules:
  0.0 257.1 jit_solution(17904638978214089852)
XLA Ops:
  6.5 0.7 all-gather.2.cloned.1.call-update
  7.3 2.2 fusion.42
  9.9 0.8 copy-done.6
  10.6 1.4 fusion.8.refs_2_
  12.1 3.3 %collective-permute-start.3 = (bf16[512,384]{1,0:T(8,128)(2,1)}, bf16[512,384]{1,0:T(8,128)(2,1)S(1)}, u32[]{:S(2)}, u32[]{:S(2)}) collective-permute-start(bf16[512,384]{1,0:T(8,128)(2,1)} %fusion.8.refs_2_), channel_id=1, source_target_pairs={{8,0},{12,4},{16,8},{20,12},{24,16},{28,20},{9,1},{13,5},{17,9},{2... | collective-permute-start | bytes 1179656 | tf_op jit(solution)/shard_map/ppermute | solution.py:18
  15.4 1.9 collective-permute-start.2
  17.3 2.4 collective-permute-start.1
  20.1 0.7 copy.48
  20.8 1.4 add_select_fusion.2
  22.9 0.7 and_reduce_fusion
  24.8 1.5 sort.17
  26.4 1.4 copy.38
  27.7 1.3 bitcast_or_fusion
  29.0 0.8 reshape.140
  29.8 0.7 add_select_fusion
  30.5 0.8 pad_add_fusion.1
  31.3 2.5 gather_fusion.2
  33.9 1.3 broadcast_select_fusion
  35.2 36.1 %all-gather.2.cloned.1.call-done = bf16[2048,768]{1,0:T(8,128)(2,1)} async-done(((bf16[512,768]{1,0:T(8,128)(2,1)}), bf16[2048,768]{1,0:T(8,128)(2,1)}) %all-gather.2.cloned.1.call-update) | async-done | bytes 3145744 | tf_op jit(solution)/shard_map/all_gather | solution.py:146
  71.3 1.6 fusion.9
  73.0 4.0 %fusion.7 = bf16[1536,768]{1,0:T(8,128)(2,1)S(1)} fusion(s32[]{:T(128)S(6)} %add.137, bf16[2048,768]{1,0:T(8,128)(2,1)} %all-gather.2.cloned.1.call-done), kind=kLoop, calls=%fused_computation.11 | loop fusion | flops 4718592 | bytes 5505028 | tf_op jit(solution)/shard_map/jit(_roll_dynamic)/concatenate | solution.py:147
  77.0 0.9 collective-permute-done.8
  77.9 0.7 collective-permute-start.9
  78.6 2.5 convolution_convert_fusion.refs_7_
  81.1 4.2 %collective-permute-start.7 = (bf16[1536,384]{1,0:T(8,128)(2,1)}, bf16[1536,384]{1,0:T(8,128)(2,1)}, u32[]{:S(2)}, u32[]{:S(2)}) collective-permute-start(bf16[1536,384]{1,0:T(8,128)(2,1)} %convolution_convert_fusion.refs_7_), channel_id=1, source_target_pairs={{8,0},{12,4},{16,8},{20,12},{24,16},{28,20},{9,1},{13,5},{17,9},{2... | collective-permute-start | bytes 3538952 | tf_op jit(solution)/shard_map/ppermute | solution.py:18
  85.3 2.1 collective-permute-start.6
  87.5 2.2 collective-permute-start.5
  89.7 3.7 %collective-permute-start.4 = (bf16[1536,384]{1,0:T(8,128)(2,1)}, bf16[1536,384]{1,0:T(8,128)(2,1)}, u32[]{:S(2)}, u32[]{:S(2)}) collective-permute-start(bf16[1536,384]{1,0:T(8,128)(2,1)} %convolution_convert_fusion.refs_7_), channel_id=1, source_target_pairs={{0,8},{4,12},{8,16},{12,20},{16,24},{20,28},{1,9},{5,13},{9,17},{1... | collective-permute-start | bytes 3538952 | tf_op jit(solution)/shard_map/ppermute | solution.py:18
  94.0 0.8 pad_maximum_fusion.2
  97.5 0.7 concatenate.49
  98.2 2.5 gather_fusion.1
  102.0 1.3 slice.86.rows
  103.3 3.5 %collective-permute-done.10 = bf16[4,128,384]{2,1,0:T(8,128)(2,1)} collective-permute-done((bf16[4,128,384]{2,1,0:T(8,128)(2,1)}, bf16[4,128,384]{2,1,0:T(8,128)(2,1)}, u32[]{:S(2)}, u32[]{:S(2)}) %collective-permute-start.10) | collective-permute-done | bytes 393248 | tf_op jit(solution)/shard_map/ppermute | solution.py:28
  106.9 23.8 %collective-permute-start = (bf16[512,384]{1,0:T(8,128)(2,1)}, bf16[512,384]{1,0:T(8,128)(2,1)}, u32[]{:S(2)}, u32[]{:S(2)}) collective-permute-start(bf16[512,384]{1,0:T(8,128)(2,1)} %fusion.8.refs_2_), channel_id=1, source_target_pairs={{0,8},{4,12},{8,16},{12,20},{16,24},{20,28},{1,9},{5,13},{9,17},{1... | collective-permute-start | bytes 1179656 | tf_op jit(solution)/shard_map/ppermute | solution.py:18
  131.3 3.1 %fusion.4 = bf16[2048,192]{0,1:T(8,128)(2,1)S(1)} fusion(bf16[1536,768]{1,0:T(8,128)(2,1)} %copy-done.1, bf16[512,768]{1,0:T(8,128)(2,1)} %param.8, bf16[768,1,768]{2,0,1:T(8,128)(2,1)S(1)} %get-tuple-element.13, s32[]{:T(128)S(6)} %select_n.137), kind=kOutput, calls=%fused_computation.10 | convolution fusion | flops 610664448 | bytes 4325380 | tf_op jit(solution)/shard_map/dot_general | solution.py:150
  134.4 0.9 copy-done.7
  135.4 1.2 copy.46
  136.5 2.0 pad_maximum_fusion
  138.6 32.7 %collective-permute-done.refs_0_ = bf16[512,384]{1,0:T(8,128)(2,1)} collective-permute-done((bf16[512,384]{1,0:T(8,128)(2,1)}, bf16[512,384]{1,0:T(8,128)(2,1)}, u32[]{:S(2)}, u32[]{:S(2)}) %collective-permute-start) | collective-permute-done | bytes 393248 | tf_op jit(solution)/shard_map/ppermute | solution.py:18
  171.3 45.2 %shard_map.65 = bf16[12,128,192]{2,1,0:T(8,128)(2,1)} custom-call(s32[12]{0:T(128)} %slice.67.count, s32[12,20]{1,0:T(8,128)} %slice.85.source, s32[12,20]{1,0:T(8,128)} %slice.86.rows, bf16[12,128,192]{2,1,0:T(8,128)(2,1)} %bitcast.38, bf16[512,384]{1,0:T(8,128)(2,1)} %collective-permute-done.refs_0_, bf16[512,384]{1,0:T(8,128)(2,1)} %copy-done.12, ...), custom_call_target="tpu_custom_call" | custom-call | flops 3019898880 | bytes 9830400 | tf_op jit(solution)/shard_map/pallas_call | solution.py:95
  216.5 2.0 fusion.43
  218.5 3.8 %collective-permute-start.13 = (bf16[512,192]{1,0:T(8,128)(2,1)}, bf16[512,192]{1,0:T(8,128)(2,1)}, u32[]{:S(2)}, u32[]{:S(2)}) collective-permute-start(bf16[512,192]{1,0:T(8,128)(2,1)} %bitcast.14), channel_id=1, source_target_pairs={{0,3},{1,0},{2,1},{3,2},{4,7},{5,4},{6,5},{7,6},{8,11},{9,8},{10,9... | collective-permute-start | bytes 589832 | tf_op jit(solution)/shard_map/ppermute | solution.py:197
  222.3 2.4 collective-permute-start.12
  225.5 1.3 slice.82.rows
  226.7 0.9 slice.83
  227.7 0.8 copy.44
  228.5 18.9 %shard_map.64 = bf16[4,128,192]{2,1,0:T(8,128)(2,1)} custom-call(s32[4]{0:T(128)} %bitcast.40, s32[4,20]{1,0:T(4,128)} %slice.81.source, s32[4,20]{1,0:T(4,128)} %slice.82.rows, bf16[4,128,192]{2,1,0:T(8,128)(2,1)} %bitcast.37, bf16[512,384]{1,0:T(8,128)(2,1)} %collective-permute-done.refs_0_, bf16[512,384]{1,0:T(8,128)(2,1)} %copy-done.12, ...), custom_call_target="tpu_custom_call" | custom-call | flops 1006632960 | bytes 9043968 | tf_op jit(solution)/shard_map/pallas_call | solution.py:95
  247.4 2.9 %convolution_convert_fusion.1 = bf16[512,768]{1,0:T(8,128)(2,1)} fusion(bf16[768,768]{1,0:T(8,128)(2,1)S(1)} %bitcast_select_fusion, bf16[512,192]{1,0:T(8,128)(2,1)} %collective-permute-done.13, bf16[512,192]{1,0:T(8,128)(2,1)} %collective-permute-done.12, bf16[512,192]{1,0:T(8,128)(2,1)} %collective-permute-done.11, bf16[512,192]{1,0:T(8,128)(2,1)} %bitcast.39), kind=kOutput, calls=%fused_computation.12 | convolution fusion | flops 607518720 | bytes 2752512 | tf_op jit(solution)/shard_map/dot_general | solution.py:203
  (92 shorter events, 8.8 us)
Async XLA Ops:
  6.5 124.1 %copy-start = (bf16[768,768]{1,0:T(8,128)(2,1)S(1)}, bf16[768,768]{1,0:T(8,128)(2,1)}, u32[]{:S(2)}) copy-start(bf16[768,768]{1,0:T(8,128)(2,1)} %param.10) | copy-start | bytes 3538948
  6.5 64.7 %all-gather.2.cloned.1.call-start = ((), (), s32[]{:S(2)}) async-start(), calls=%async_computation | async-start | bytes 3932160 | tf_op jit(solution)/shard_map/all_gather | solution.py:146
  9.5 1.1 copy-start.6
  9.8 2.2 copy-start.13
  9.8 2.2 copy-start.15
  10.6 9.2 %copy-start.25 = (s32[16]{0:T(128)S(1)}, s32[16]{0:T(128)}, u32[]{:S(2)}) copy-start(s32[16]{0:T(128)} %param.12) | copy-start | bytes 196
  10.6 9.4 %copy-start.23 = (s32[16,8]{0,1:T(8,128)S(1)}, s32[16,8]{0,1:T(8,128)}, u32[]{:S(2)}) copy-start(s32[16,8]{0,1:T(8,128)} %param.13) | copy-start | bytes 1540
  12.1 73.2 %collective-permute-start.3 = (bf16[512,384]{1,0:T(8,128)(2,1)}, bf16[512,384]{1,0:T(8,128)(2,1)S(1)}, u32[]{:S(2)}, u32[]{:S(2)}) collective-permute-start(bf16[512,384]{1,0:T(8,128)(2,1)} %fusion.8.refs_2_), channel_id=1, source_target_pairs={{8,0},{12,4},{16,8},{20,12},{24,16},{28,20},{9,1},{13,5},{17,9},{2... | collective-permute-start | bytes 1179656 | tf_op jit(solution)/shard_map/ppermute | solution.py:18
  15.4 72.0 %collective-permute-start.2 = (bf16[512,384]{1,0:T(8,128)(2,1)}, bf16[512,384]{1,0:T(8,128)(2,1)S(1)}, u32[]{:S(2)}, u32[]{:S(2)}) collective-permute-start(bf16[512,384]{1,0:T(8,128)(2,1)} %fusion.8.refs_2_), channel_id=1, source_target_pairs={{4,0},{8,4},{12,8},{16,12},{20,16},{24,20},{28,24},{5,1},{9,5},{13... | collective-permute-start | bytes 1179656 | tf_op jit(solution)/shard_map/ppermute | solution.py:18
  17.3 77.5 %collective-permute-start.1 = (bf16[512,384]{1,0:T(8,128)(2,1)}, bf16[512,384]{1,0:T(8,128)(2,1)S(1)}, u32[]{:S(2)}, u32[]{:S(2)}) collective-permute-start(bf16[512,384]{1,0:T(8,128)(2,1)} %fusion.8.refs_2_), channel_id=1, source_target_pairs={{0,4},{4,8},{8,12},{12,16},{16,20},{20,24},{24,28},{1,5},{5,9},{9,... | collective-permute-start | bytes 1179656 | tf_op jit(solution)/shard_map/ppermute | solution.py:18
  22.2 5.5 %copy-start.17 = (s32[16,12]{1,0:T(8,128)}, s32[16,12]{1,0:T(8,128)S(1)}, u32[]{:S(2)}) copy-start(s32[16,12]{1,0:T(8,128)S(1)} %get-tuple-element.11) | copy-start | bytes 2308
  22.9 0.7 copy-start.19
  23.6 6.9 %copy-start.21 = (pred[16,8]{0,1:T(8,128)(4,1)}, pred[16,8]{0,1:T(8,128)(4,1)S(1)}, u32[]{:S(2)}) copy-start(pred[16,8]{0,1:T(8,128)(4,1)S(1)} %not.6) | copy-start | bytes 388
  72.9 21.2 %copy-start.2 = (bf16[1,128,384]{2,1,0:T(8,128)(2,1)}, bf16[1,128,384]{2,1,0:T(8,128)(2,1)S(1)}, u32[]{:S(2)}) copy-start(bf16[1,128,384]{2,1,0:T(8,128)(2,1)S(1)} %fusion.9) | copy-start | bytes 294916
  72.9 5.7 %copy-start.14 = (bf16[768,192]{1,0:T(8,128)(2,1)S(1)}, bf16[768,192]{1,0:T(8,128)(2,1)}, u32[]{:S(2)}) copy-start(bf16[768,192]{1,0:T(8,128)(2,1)} %copy-done.13) | copy-start | bytes 884740
  72.9 5.7 %copy-start.16 = (bf16[768,192]{1,0:T(8,128)(2,1)S(1)}, bf16[768,192]{1,0:T(8,128)(2,1)}, u32[]{:S(2)}) copy-start(bf16[768,192]{1,0:T(8,128)(2,1)} %copy-done.15) | copy-start | bytes 884740
  72.9 5.0 %collective-permute-start.8 = (bf16[1,128,384]{2,1,0:T(8,128)(2,1)S(1)}, bf16[1,128,384]{2,1,0:T(8,128)(2,1)S(1)}, u32[]{:S(2)}, u32[]{:S(2)}) collective-permute-start(bf16[1,128,384]{2,1,0:T(8,128)(2,1)S(1)} %fusion.9), channel_id=1, source_target_pairs={{0,4},{4,8},{8,12},{12,16},{16,20},{20,24},{24,28},{28,0},{1,5},{5... | collective-permute-start | bytes 294920 | tf_op jit(solution)/shard_map/ppermute | solution.py:28
  77.0 4.1 %copy-start.1 = (bf16[1536,768]{1,0:T(8,128)(2,1)}, bf16[1536,768]{1,0:T(8,128)(2,1)S(1)}, u32[]{:S(2)}) copy-start(bf16[1536,768]{1,0:T(8,128)(2,1)S(1)} %fusion.7) | copy-start | bytes 7077892
  77.9 16.1 %copy-start.4 = (bf16[1,128,384]{2,1,0:T(8,128)(2,1)}, bf16[1,128,384]{2,1,0:T(8,128)(2,1)S(1)}, u32[]{:S(2)}) copy-start(bf16[1,128,384]{2,1,0:T(8,128)(2,1)S(1)} %collective-permute-done.8) | copy-start | bytes 294916
  77.9 15.5 %copy-start.18 = (s32[16,12]{1,0:T(8,128)S(1)}, s32[16,12]{1,0:T(8,128)}, u32[]{:S(2)}) copy-start(s32[16,12]{1,0:T(8,128)} %copy-done.17) | copy-start | bytes 2308
  77.9 17.7 %copy-start.20 = (pred[16,12]{0,1:T(8,128)(4,1)S(1)}, pred[16,12]{0,1:T(8,128)(4,1)}, u32[]{:S(2)}) copy-start(pred[16,12]{0,1:T(8,128)(4,1)} %copy-done.19) | copy-start | bytes 580
  77.9 11.8 %collective-permute-start.9 = (bf16[2,128,384]{2,1,0:T(8,128)(2,1)S(1)}, bf16[2,128,384]{2,1,0:T(8,128)(2,1)S(1)}, u32[]{:S(2)}, u32[]{:S(2)}) collective-permute-start(bf16[2,128,384]{2,1,0:T(8,128)(2,1)S(1)} %pad_maximum_fusion.3), channel_id=1, source_target_pairs={{0,8},{4,12},{8,16},{12,20},{16,24},{20,28},{24,0},{28,4},{1,9},{5... | collective-permute-start | bytes 589832 | tf_op jit(solution)/shard_map/ppermute | solution.py:28
  81.1 90.2 %collective-permute-start.7 = (bf16[1536,384]{1,0:T(8,128)(2,1)}, bf16[1536,384]{1,0:T(8,128)(2,1)}, u32[]{:S(2)}, u32[]{:S(2)}) collective-permute-start(bf16[1536,384]{1,0:T(8,128)(2,1)} %convolution_convert_fusion.refs_7_), channel_id=1, source_target_pairs={{8,0},{12,4},{16,8},{20,12},{24,16},{28,20},{9,1},{13,5},{17,9},{2... | collective-permute-start | bytes 3538952 | tf_op jit(solution)/shard_map/ppermute | solution.py:18
  85.3 15.4 %copy-start.10 = (bf16[512,384]{1,0:T(8,128)(2,1)}, bf16[512,384]{1,0:T(8,128)(2,1)S(1)}, u32[]{:S(2)}) copy-start(bf16[512,384]{1,0:T(8,128)(2,1)S(1)} %collective-permute-done.3.refs_4_) | copy-start | bytes 1179652
  85.3 86.0 %collective-permute-start.6 = (bf16[1536,384]{1,0:T(8,128)(2,1)}, bf16[1536,384]{1,0:T(8,128)(2,1)}, u32[]{:S(2)}, u32[]{:S(2)}) collective-permute-start(bf16[1536,384]{1,0:T(8,128)(2,1)} %convolution_convert_fusion.refs_7_), channel_id=1, source_target_pairs={{4,0},{8,4},{12,8},{16,12},{20,16},{24,20},{28,24},{5,1},{9,5},{13... | collective-permute-start | bytes 3538952 | tf_op jit(solution)/shard_map/ppermute | solution.py:18
  87.5 13.2 %copy-start.11 = (bf16[512,384]{1,0:T(8,128)(2,1)}, bf16[512,384]{1,0:T(8,128)(2,1)S(1)}, u32[]{:S(2)}) copy-start(bf16[512,384]{1,0:T(8,128)(2,1)S(1)} %collective-permute-done.2.refs_3_) | copy-start | bytes 1179652
  87.5 83.9 %collective-permute-start.5 = (bf16[1536,384]{1,0:T(8,128)(2,1)}, bf16[1536,384]{1,0:T(8,128)(2,1)}, u32[]{:S(2)}, u32[]{:S(2)}) collective-permute-start(bf16[1536,384]{1,0:T(8,128)(2,1)} %convolution_convert_fusion.refs_7_), channel_id=1, source_target_pairs={{0,4},{4,8},{8,12},{12,16},{16,20},{20,24},{24,28},{1,5},{5,9},{9,... | collective-permute-start | bytes 3538952 | tf_op jit(solution)/shard_map/ppermute | solution.py:18
  89.7 5.1 %copy-start.8 = (bf16[2,128,384]{2,1,0:T(8,128)(2,1)}, bf16[2,128,384]{2,1,0:T(8,128)(2,1)S(1)}, u32[]{:S(2)}) copy-start(bf16[2,128,384]{2,1,0:T(8,128)(2,1)S(1)} %collective-permute-done.9) | copy-start | bytes 589828
  89.7 81.6 %collective-permute-start.4 = (bf16[1536,384]{1,0:T(8,128)(2,1)}, bf16[1536,384]{1,0:T(8,128)(2,1)}, u32[]{:S(2)}, u32[]{:S(2)}) collective-permute-start(bf16[1536,384]{1,0:T(8,128)(2,1)} %convolution_convert_fusion.refs_7_), channel_id=1, source_target_pairs={{0,8},{4,12},{8,16},{12,20},{16,24},{20,28},{1,9},{5,13},{9,17},{1... | collective-permute-start | bytes 3538952 | tf_op jit(solution)/shard_map/ppermute | solution.py:18
  94.8 5.9 %copy-start.12 = (bf16[512,384]{1,0:T(8,128)(2,1)}, bf16[512,384]{1,0:T(8,128)(2,1)S(1)}, u32[]{:S(2)}) copy-start(bf16[512,384]{1,0:T(8,128)(2,1)S(1)} %collective-permute-done.1.refs_1_) | copy-start | bytes 1179652
  94.8 12.0 %collective-permute-start.10 = (bf16[4,128,384]{2,1,0:T(8,128)(2,1)}, bf16[4,128,384]{2,1,0:T(8,128)(2,1)}, u32[]{:S(2)}, u32[]{:S(2)}) collective-permute-start(bf16[4,128,384]{2,1,0:T(8,128)(2,1)} %pad_maximum_fusion.2), channel_id=1, source_target_pairs={{0,16},{4,20},{8,24},{12,28},{16,0},{20,4},{24,8},{28,12},{1,17},{... | collective-permute-start | bytes 1179656 | tf_op jit(solution)/shard_map/ppermute | solution.py:28
  96.3 0.5 copy-start.24
  106.9 64.4 %collective-permute-start = (bf16[512,384]{1,0:T(8,128)(2,1)}, bf16[512,384]{1,0:T(8,128)(2,1)}, u32[]{:S(2)}, u32[]{:S(2)}) collective-permute-start(bf16[512,384]{1,0:T(8,128)(2,1)} %fusion.8.refs_2_), channel_id=1, source_target_pairs={{0,8},{4,12},{8,16},{12,20},{16,24},{20,28},{1,9},{5,13},{9,17},{1... | collective-permute-start | bytes 1179656 | tf_op jit(solution)/shard_map/ppermute | solution.py:18
  134.4 0.9 copy-start.7
  135.3 1.2 copy-start.3
  135.3 1.2 copy-start.5
  135.3 1.2 copy-start.9
  216.5 8.1 %copy-start.22 = (pred[768]{0:T(1024)(128)(4,1)S(1)}, pred[768]{0:T(1024)(128)(4,1)}, u32[]{:S(2)}) copy-start(pred[768]{0:T(1024)(128)(4,1)} %broadcast_in_dim.35) | copy-start | bytes 2308
  218.5 28.8 %collective-permute-start.13 = (bf16[512,192]{1,0:T(8,128)(2,1)}, bf16[512,192]{1,0:T(8,128)(2,1)}, u32[]{:S(2)}, u32[]{:S(2)}) collective-permute-start(bf16[512,192]{1,0:T(8,128)(2,1)} %bitcast.14), channel_id=1, source_target_pairs={{0,3},{1,0},{2,1},{3,2},{4,7},{5,4},{6,5},{7,6},{8,11},{9,8},{10,9... | collective-permute-start | bytes 589832 | tf_op jit(solution)/shard_map/ppermute | solution.py:197
  222.3 25.1 %collective-permute-start.11 = (bf16[512,192]{1,0:T(8,128)(2,1)}, bf16[512,192]{1,0:T(8,128)(2,1)}, u32[]{:S(2)}, u32[]{:S(2)}) collective-permute-start(bf16[512,192]{1,0:T(8,128)(2,1)} %bitcast.12), channel_id=1, source_target_pairs={{0,1},{1,2},{2,3},{3,0},{4,5},{5,6},{6,7},{7,4},{8,9},{9,10},{10,1... | collective-permute-start | bytes 589832 | tf_op jit(solution)/shard_map/ppermute | solution.py:197
  222.3 25.1 %collective-permute-start.12 = (bf16[512,192]{1,0:T(8,128)(2,1)}, bf16[512,192]{1,0:T(8,128)(2,1)}, u32[]{:S(2)}, u32[]{:S(2)}) collective-permute-start(bf16[512,192]{1,0:T(8,128)(2,1)} %bitcast.13), channel_id=1, source_target_pairs={{0,2},{1,3},{2,0},{3,1},{4,6},{5,7},{6,4},{7,5},{8,10},{9,11},{10,... | collective-permute-start | bytes 589832 | tf_op jit(solution)/shard_map/ppermute | solution.py:197
Sparse Core Ops, SparseCore 0:
  8.9 62.3 all-gather.1

commit v10 on v7

--- a/solution.py
+++ b/solution.py
@@ -120,10 +120,14 @@
 
 
 def window_of(x, axis):
-    parts = []
-    for offset in (2, 1, 0, -1, -2):
-        parts.append(x if offset == 0 else shifted(x, "seq", offset))
-    return jnp.concatenate(parts, axis=axis)
+    size = lax.axis_size("seq")
+    plus1 = shifted(x, "seq", 1)
+    minus1 = shifted(x, "seq", -1)
+    plus2 = lax.ppermute(x, "seq", [(i, i + 2) for i in range(0, size - 2, 2)])
+    plus2 = plus2 + lax.ppermute(plus1, "seq", [(i, i + 1) for i in range(2, size, 2)])
+    minus2 = lax.ppermute(x, "seq", [(i, i - 2) for i in range(3, size, 2)])
+    minus2 = minus2 + lax.ppermute(minus1, "seq", [(i, i - 1) for i in range(1, size - 2, 2)])
+    return jnp.concatenate([plus2, plus1, x, minus1, minus2], axis=axis)
 
 
 def shards(tokens, w_qkv, w_out, neighbours, near_count, anchors):

time: 254 us -> 261 us (1.028); the launches traced: 254 us -> 256 us
  waiting for transfers between devices: 87.7 us -> 99.1 us
  starting transfers between devices: 43.7 us -> 33.3 us
  other arithmetic: 9 us -> 19.4 us
  local copies, waits for them, and re-layouts: 40.3 us -> 31.5 us
    ppermute x8 -> x4, starting transfers between devices: 33.9 us -> 7.66 us  [shifted(): return lax.ppermute(x, axis, pairs)]
    ppermute x3, waiting for transfers between devices: 25.9 us -> 47.6 us  [gather_all(): got = lax.ppermute(held, axis, pairs)]
    ppermute x8 -> x4, waiting for transfers between devices: 21.2 us -> 0.01 us  [shifted(): return lax.ppermute(x, axis, pairs)]
    ppermute x0 -> x8, starting transfers between devices: none -> 20.2 us  [the longest x2 7.67 us: window_of(): plus2 = lax.ppermute(x, 'seq', [(i, i + 2) for i in range(0, size - 2, 2)])]
    all_gather x1, waiting for transfers between devices: 39.8 us -> 50.7 us  [shards(): gathered = lax.all_gather(tokens, 'head', axis=0, tiled=True)]
    unnamed x0 -> x2, other arithmetic: none -> 4.95 us
    unnamed x47 -> x33, local copies, waits for them, and re-layouts: 18.4 us -> 13.8 us
    concatenate x2 -> x0, local copies, waits for them, and re-layouts: 4.22 us -> none  [window_of(): return jnp.concatenate(parts, axis=axis)]
  transfers between devices with their start and end apart: 15 -> 19, of which waited for: 5 -> 4; matrix products, arithmetic and copies ran while one was open for 20% -> 20% of each run, Pallas kernels for 6% -> 6%
where the time goes in v10:
time: 261 us; the launch traced here: 256 us
  waiting for transfers between devices  99.1 us (38%)
  Pallas kernels  48.9 us (19%)
  starting transfers between devices  33.3 us (13%)
  local copies, waits for them, and re-layouts  31.5 us (12%)
  other arithmetic  19.4 us (7%)
  between operations  13.8 us (5%)
  matrix products  10 us (4%)
    all_gather x1, waiting for transfers between devices, shards(): gathered = lax.all_gather(tokens, 'head', axis=0, tiled=True)  50.7 us
    pallas_call x2, Pallas kernels, attention(): pl.pallas_call(kernel, out_shape=jax.ShapeDtypeStruct(queries.shape, jnp....  48.9 us
    ppermute x3, waiting for transfers between devices, gather_all(): got = lax.ppermute(held, axis, pairs)  47.6 us
    unnamed x33, local copies, waits for them, and re-layouts  13.8 us
    ppermute x2, starting transfers between devices, window_of(): plus2 = lax.ppermute(x, 'seq', [(i, i + 2) for i in range(0, size - 2, 2)])  7.67 us
    ppermute x4, starting transfers between devices, shifted(): return lax.ppermute(x, axis, pairs)  7.66 us
    ppermute x2, starting transfers between devices, window_of(): lax.ppermute(plus1, 'seq', [(i, i + 1) for i in range(2, size, 2)])  7.41 us
    dot_general x3, matrix products, project_kv(): jnp.dot(x, kv_w, preferred_element_type=jnp.float32).astype(jnp.bfloat16)  5.84 us
  transfers between devices with their start and end apart: 19, of which 4 were waited for; matrix products, arithmetic and copies ran while one was open for 20% of the time, Pallas kernels for 6%

profile of v10, /device:TPU:2, one launch (start us, length us, event | category | flops | bytes accessed | tf_op | source)
XLA Modules:
  0.0 255.9 jit_solution(7620045640606421981)
XLA Ops:
  7.3 2.3 fusion.45
  10.0 1.4 fusion.8
  11.4 1.9 collective-permute-start.1
  13.3 3.4 %collective-permute-start = (bf16[512,384]{1,0:T(8,128)(2,1)}, bf16[512,384]{1,0:T(8,128)(2,1)}, u32[]{:S(2)}, u32[]{:S(2)}) collective-permute-start(bf16[512,384]{1,0:T(8,128)(2,1)} %fusion.8), channel_id=1, source_target_pairs={{0,8},{8,16},{16,24},{1,9},{9,17},{17,25},{2,10},{10,18},{18,26},{... | collective-permute-start | bytes 1179656 | tf_op jit(solution)/shard_map/ppermute | solution.py:126
  16.7 1.9 collective-permute-start.3
  19.3 0.8 sort.17
  20.3 2.5 gather_fusion.2
  23.0 50.7 %all-gather.2.cloned.1.call-done = bf16[2048,768]{1,0:T(8,128)(2,1)} async-done(((bf16[512,768]{1,0:T(8,128)(2,1)}), bf16[2048,768]{1,0:T(8,128)(2,1)}) %all-gather.2.cloned.1.call-update) | async-done | bytes 3145744 | tf_op jit(solution)/shard_map/all_gather | solution.py:150
  73.7 4.0 %fusion.7 = bf16[1536,768]{1,0:T(8,128)(2,1)S(1)} fusion(s32[]{:T(128)S(6)} %add.157, bf16[2048,768]{1,0:T(8,128)(2,1)} %all-gather.2.cloned.1.call-done), kind=kLoop, calls=%fused_computation.11 | loop fusion | flops 4718592 | bytes 5505028 | tf_op jit(solution)/shard_map/jit(_roll_dynamic)/concatenate | solution.py:151
  77.7 2.5 convolution_convert_fusion
  80.2 1.9 collective-permute-start.7
  82.2 2.5 gather_fusion.1
  84.8 4.3 %collective-permute-start.2 = (bf16[512,384]{1,0:T(8,128)(2,1)}, bf16[512,384]{1,0:T(8,128)(2,1)}, u32[]{:S(2)}, u32[]{:S(2)}) collective-permute-start(bf16[512,384]{1,0:T(8,128)(2,1)} %collective-permute-done.1), channel_id=1, source_target_pairs={{8,12},{16,20},{24,28},{9,13},{17,21},{25,29},{10,14},{18,22},{26,... | collective-permute-start | bytes 1179656 | tf_op jit(solution)/shard_map/ppermute | solution.py:127
  89.7 1.9 fusion.9
  94.9 4.2 %collective-permute-done.12 = bf16[1,128,384]{2,1,0:T(8,128)(2,1)} collective-permute-done((bf16[1,128,384]{2,1,0:T(8,128)(2,1)}, bf16[1,128,384]{2,1,0:T(8,128)(2,1)}, u32[]{:S(2)}, u32[]{:S(2)}) %collective-permute-start.12) | collective-permute-done | bytes 98336 | tf_op jit(solution)/shard_map/ppermute | solution.py:28
  99.1 4.3 %collective-permute-start.6 = (bf16[1536,384]{1,0:T(8,128)(2,1)}, bf16[1536,384]{1,0:T(8,128)(2,1)}, u32[]{:S(2)}, u32[]{:S(2)}) collective-permute-start(bf16[1536,384]{1,0:T(8,128)(2,1)} %convolution_convert_fusion), channel_id=1, source_target_pairs={{0,8},{8,16},{16,24},{1,9},{9,17},{17,25},{2,10},{10,18},{18,26},{... | collective-permute-start | bytes 3538952 | tf_op jit(solution)/shard_map/ppermute | solution.py:126
  103.4 1.0 pad_maximum_fusion.3
  104.3 1.9 collective-permute-start.9
  106.9 3.2 %collective-permute-start.8 = (bf16[1536,384]{1,0:T(8,128)(2,1)}, bf16[1536,384]{1,0:T(8,128)(2,1)}, u32[]{:S(2)}, u32[]{:S(2)}) collective-permute-start(bf16[1536,384]{1,0:T(8,128)(2,1)} %collective-permute-done.7), channel_id=1, source_target_pairs={{8,12},{16,20},{24,28},{9,13},{17,21},{25,29},{10,14},{18,22},{26,... | collective-permute-start | bytes 3538952 | tf_op jit(solution)/shard_map/ppermute | solution.py:127
  110.1 2.0 add_dynamic-update-slice_fusion.3
  112.7 25.6 %collective-permute-done.13 = bf16[2,128,384]{2,1,0:T(8,128)(2,1)S(1)} collective-permute-done((bf16[2,128,384]{2,1,0:T(8,128)(2,1)S(1)}, bf16[2,128,384]{2,1,0:T(8,128)(2,1)S(1)}, u32[]{:S(2)}, u32[]{:S(2)}) %collective-permute-start.13) | collective-permute-done | bytes 196640 | tf_op jit(solution)/shard_map/ppermute | solution.py:28
  138.3 1.3 collective-permute-start.5
  139.6 1.8 constant_dynamic-update-slice_fusion.2
  141.4 1.9 constant_dynamic-update-slice_fusion.1
  143.3 1.8 constant_dynamic-update-slice_fusion
  145.1 1.7 pad_maximum_fusion.2
  146.9 1.0 collective-permute-start.14
  147.9 0.9 add_dynamic-update-slice_fusion.2.refs_0_
  148.8 1.7 collective-permute-start.10
  150.4 1.3 fusion.4
  151.7 0.9 copy-done.5
  152.6 1.2 copy.46
  153.8 17.9 %collective-permute-done.14 = bf16[4,128,384]{2,1,0:T(8,128)(2,1)} collective-permute-done((bf16[4,128,384]{2,1,0:T(8,128)(2,1)}, bf16[4,128,384]{2,1,0:T(8,128)(2,1)}, u32[]{:S(2)}, u32[]{:S(2)}) %collective-permute-start.14) | collective-permute-done | bytes 393248 | tf_op jit(solution)/shard_map/ppermute | solution.py:28
  171.7 2.1 pad_maximum_fusion
  173.8 1.5 collective-permute-start.11
  175.3 3.0 %add_dynamic-update-slice_fusion.1 = bf16[7680,384]{1,0:T(8,128)(2,1)} fusion(bf16[1536,384]{1,0:T(8,128)(2,1)} %collective-permute-done.6, bf16[1536,384]{1,0:T(8,128)(2,1)} %collective-permute-done.8), kind=kLoop, calls=%fused_computation.17 | loop fusion | flops 2359295 | bytes 3538944
  178.3 2.5 constant_dynamic-update-slice_fusion.5
  180.8 2.4 constant_dynamic-update-slice_fusion.4
  183.2 2.4 constant_dynamic-update-slice_fusion.3
  185.6 2.7 %add_dynamic-update-slice_fusion.refs_1_ = bf16[7680,384]{1,0:T(8,128)(2,1)} fusion(bf16[7680,384]{1,0:T(8,128)(2,1)} %constant_dynamic-update-slice_fusion.3, bf16[1536,384]{1,0:T(8,128)(2,1)} %collective-permute-done.10, bf16[1536,384]{1,0:T(8,128)(2,1)S(1)} %collective-permute-done.11), kind=kLoop, calls=%fused_computation.16 | loop fusion | flops 2359296 | bytes 3538944 | tf_op jit(solution)/shard_map/concatenate | solution.py:130
  188.3 34.3 %shard_map.65 = bf16[12,128,192]{2,1,0:T(8,128)(2,1)} custom-call(s32[12]{0:T(128)} %slice.67.count, s32[12,20]{1,0:T(8,128)} %slice.85.source, s32[12,20]{1,0:T(8,128)} %slice.86.rows, bf16[12,128,192]{2,1,0:T(8,128)(2,1)} %bitcast.38, bf16[2560,384]{1,0:T(8,128)(2,1)} %add_dynamic-update-slice_fusion.2.refs_0_, ...), custom_call_target="tpu_custom_call" | custom-call | flops 3019898880 | bytes 9830400 | tf_op jit(solution)/shard_map/pallas_call | solution.py:95
  222.5 2.0 fusion.46
  224.5 1.7 collective-permute-start.16
  226.3 2.1 collective-permute-start.17
  229.8 0.9 slice.83
  230.7 0.9 copy.44
  231.6 14.6 %shard_map.64 = bf16[4,128,192]{2,1,0:T(8,128)(2,1)} custom-call(s32[4]{0:T(128)} %bitcast.40, s32[4,20]{1,0:T(4,128)} %slice.81.source, s32[4,20]{1,0:T(4,128)} %slice.82.rows, bf16[4,128,192]{2,1,0:T(8,128)(2,1)} %bitcast.37, bf16[2560,384]{1,0:T(8,128)(2,1)} %add_dynamic-update-slice_fusion.2.refs_0_, ...), custom_call_target="tpu_custom_call" | custom-call | flops 1006632960 | bytes 9043968 | tf_op jit(solution)/shard_map/pallas_call | solution.py:95
  246.2 2.9 %convolution_convert_fusion.1 = bf16[512,768]{1,0:T(8,128)(2,1)} fusion(bf16[768,768]{1,0:T(8,128)(2,1)S(1)} %bitcast_select_fusion, bf16[512,192]{1,0:T(8,128)(2,1)} %collective-permute-done.17, bf16[512,192]{1,0:T(8,128)(2,1)} %collective-permute-done.16, bf16[512,192]{1,0:T(8,128)(2,1)} %collective-permute-done.15, bf16[512,192]{1,0:T(8,128)(2,1)} %bitcast.39), kind=kOutput, calls=%fused_computation.12 | convolution fusion | flops 607518720 | bytes 2752512 | tf_op jit(solution)/shard_map/dot_general | solution.py:208
  (84 shorter events, 8.8 us)
Async XLA Ops:
  6.5 87.6 %copy-start = (bf16[768,768]{1,0:T(8,128)(2,1)S(1)}, bf16[768,768]{1,0:T(8,128)(2,1)}, u32[]{:S(2)}) copy-start(bf16[768,768]{1,0:T(8,128)(2,1)} %param.10) | copy-start | bytes 3538948
  6.5 67.2 %all-gather.2.cloned.1.call-start = ((), (), s32[]{:S(2)}) async-start(), calls=%async_computation | async-start | bytes 3932160 | tf_op jit(solution)/shard_map/all_gather | solution.py:150
  7.3 2.7 %copy-start.3 = (bf16[512,768]{1,0:T(8,128)(2,1)S(1)}, bf16[512,768]{1,0:T(8,128)(2,1)}, u32[]{:S(2)}) copy-start(bf16[512,768]{1,0:T(8,128)(2,1)} %param.8) | copy-start | bytes 2359300
  9.6 9.1 %copy-start.8 = (s32[16,12]{1,0:T(8,128)S(1)}, s32[16,12]{1,0:T(8,128)}, u32[]{:S(2)}) copy-start(s32[16,12]{1,0:T(8,128)} %param.11) | copy-start | bytes 2308
  9.6 9.2 %copy-start.12 = (s32[16]{0:T(128)S(1)}, s32[16]{0:T(128)}, u32[]{:S(2)}) copy-start(s32[16]{0:T(128)} %param.12) | copy-start | bytes 196
  9.6 9.4 %copy-start.10 = (s32[16,8]{0,1:T(8,128)S(1)}, s32[16,8]{0,1:T(8,128)}, u32[]{:S(2)}) copy-start(s32[16,8]{0,1:T(8,128)} %param.13) | copy-start | bytes 1540
  11.4 73.5 %collective-permute-start.1 = (bf16[512,384]{1,0:T(8,128)(2,1)}, bf16[512,384]{1,0:T(8,128)(2,1)}, u32[]{:S(2)}, u32[]{:S(2)}) collective-permute-start(bf16[512,384]{1,0:T(8,128)(2,1)} %fusion.8), channel_id=1, source_target_pairs={{0,4},{4,8},{8,12},{12,16},{16,20},{20,24},{24,28},{1,5},{5,9},{9,... | collective-permute-start | bytes 1179656 | tf_op jit(solution)/shard_map/ppermute | solution.py:18
  13.3 91.1 %collective-permute-start = (bf16[512,384]{1,0:T(8,128)(2,1)}, bf16[512,384]{1,0:T(8,128)(2,1)}, u32[]{:S(2)}, u32[]{:S(2)}) collective-permute-start(bf16[512,384]{1,0:T(8,128)(2,1)} %fusion.8), channel_id=1, source_target_pairs={{0,8},{8,16},{16,24},{1,9},{9,17},{17,25},{2,10},{10,18},{18,26},{... | collective-permute-start | bytes 1179656 | tf_op jit(solution)/shard_map/ppermute | solution.py:126
  16.7 95.3 %collective-permute-start.3 = (bf16[512,384]{1,0:T(8,128)(2,1)}, bf16[512,384]{1,0:T(8,128)(2,1)}, u32[]{:S(2)}, u32[]{:S(2)}) collective-permute-start(bf16[512,384]{1,0:T(8,128)(2,1)} %fusion.8), channel_id=1, source_target_pairs={{4,0},{8,4},{12,8},{16,12},{20,16},{24,20},{28,24},{5,1},{9,5},{13... | collective-permute-start | bytes 1179656 | tf_op jit(solution)/shard_map/ppermute | solution.py:18
  77.7 2.5 copy-start.1
  80.2 26.7 %collective-permute-start.7 = (bf16[1536,384]{1,0:T(8,128)(2,1)}, bf16[1536,384]{1,0:T(8,128)(2,1)}, u32[]{:S(2)}, u32[]{:S(2)}) collective-permute-start(bf16[1536,384]{1,0:T(8,128)(2,1)} %convolution_convert_fusion), channel_id=1, source_target_pairs={{0,4},{4,8},{8,12},{12,16},{16,20},{20,24},{24,28},{1,5},{5,9},{9,... | collective-permute-start | bytes 3538952 | tf_op jit(solution)/shard_map/ppermute | solution.py:18
  84.8 21.4 %collective-permute-start.2 = (bf16[512,384]{1,0:T(8,128)(2,1)}, bf16[512,384]{1,0:T(8,128)(2,1)}, u32[]{:S(2)}, u32[]{:S(2)}) collective-permute-start(bf16[512,384]{1,0:T(8,128)(2,1)} %collective-permute-done.1), channel_id=1, source_target_pairs={{8,12},{16,20},{24,28},{9,13},{17,21},{25,29},{10,14},{18,22},{26,... | collective-permute-start | bytes 1179656 | tf_op jit(solution)/shard_map/ppermute | solution.py:127
  91.6 7.5 %collective-permute-start.12 = (bf16[1,128,384]{2,1,0:T(8,128)(2,1)}, bf16[1,128,384]{2,1,0:T(8,128)(2,1)}, u32[]{:S(2)}, u32[]{:S(2)}) collective-permute-start(bf16[1,128,384]{2,1,0:T(8,128)(2,1)} %fusion.9), channel_id=1, source_target_pairs={{0,4},{4,8},{8,12},{12,16},{16,20},{20,24},{24,28},{28,0},{1,5},{5... | collective-permute-start | bytes 294920 | tf_op jit(solution)/shard_map/ppermute | solution.py:28
  92.9 1.3 copy-start.11
  99.1 76.2 %collective-permute-start.6 = (bf16[1536,384]{1,0:T(8,128)(2,1)}, bf16[1536,384]{1,0:T(8,128)(2,1)}, u32[]{:S(2)}, u32[]{:S(2)}) collective-permute-start(bf16[1536,384]{1,0:T(8,128)(2,1)} %convolution_convert_fusion), channel_id=1, source_target_pairs={{0,8},{8,16},{16,24},{1,9},{9,17},{17,25},{2,10},{10,18},{18,26},{... | collective-permute-start | bytes 3538952 | tf_op jit(solution)/shard_map/ppermute | solution.py:126
  104.3 69.5 %collective-permute-start.9 = (bf16[1536,384]{1,0:T(8,128)(2,1)}, bf16[1536,384]{1,0:T(8,128)(2,1)}, u32[]{:S(2)}, u32[]{:S(2)}) collective-permute-start(bf16[1536,384]{1,0:T(8,128)(2,1)} %convolution_convert_fusion), channel_id=1, source_target_pairs={{4,0},{8,4},{12,8},{16,12},{20,16},{24,20},{28,24},{5,1},{9,5},{13... | collective-permute-start | bytes 3538952 | tf_op jit(solution)/shard_map/ppermute | solution.py:18
  106.3 32.1 %collective-permute-start.13 = (bf16[2,128,384]{2,1,0:T(8,128)(2,1)S(1)}, bf16[2,128,384]{2,1,0:T(8,128)(2,1)S(1)}, u32[]{:S(2)}, u32[]{:S(2)}) collective-permute-start(bf16[2,128,384]{2,1,0:T(8,128)(2,1)S(1)} %pad_maximum_fusion.3), channel_id=1, source_target_pairs={{0,8},{4,12},{8,16},{12,20},{16,24},{20,28},{24,0},{28,4},{1,9},{5... | collective-permute-start | bytes 589832 | tf_op jit(solution)/shard_map/ppermute | solution.py:28
  106.9 68.4 %collective-permute-start.8 = (bf16[1536,384]{1,0:T(8,128)(2,1)}, bf16[1536,384]{1,0:T(8,128)(2,1)}, u32[]{:S(2)}, u32[]{:S(2)}) collective-permute-start(bf16[1536,384]{1,0:T(8,128)(2,1)} %collective-permute-done.7), channel_id=1, source_target_pairs={{8,12},{16,20},{24,28},{9,13},{17,21},{25,29},{10,14},{18,22},{26,... | collective-permute-start | bytes 3538952 | tf_op jit(solution)/shard_map/ppermute | solution.py:127
  112.0 34.9 %collective-permute-start.4 = (bf16[512,384]{1,0:T(8,128)(2,1)}, bf16[512,384]{1,0:T(8,128)(2,1)S(1)}, u32[]{:S(2)}, u32[]{:S(2)}) collective-permute-start(bf16[512,384]{1,0:T(8,128)(2,1)} %fusion.8), channel_id=1, source_target_pairs={{12,4},{20,12},{28,20},{13,5},{21,13},{29,21},{14,6},{22,14},{30,2... | collective-permute-start | bytes 1179656 | tf_op jit(solution)/shard_map/ppermute | solution.py:128
  138.3 10.4 %copy-start.6 = (bf16[2,128,384]{2,1,0:T(8,128)(2,1)}, bf16[2,128,384]{2,1,0:T(8,128)(2,1)S(1)}, u32[]{:S(2)}) copy-start(bf16[2,128,384]{2,1,0:T(8,128)(2,1)S(1)} %collective-permute-done.13) | copy-start | bytes 589828
  138.3 9.5 %collective-permute-start.5 = (bf16[512,384]{1,0:T(8,128)(2,1)}, bf16[512,384]{1,0:T(8,128)(2,1)S(1)}, u32[]{:S(2)}, u32[]{:S(2)}) collective-permute-start(bf16[512,384]{1,0:T(8,128)(2,1)} %collective-permute-done.3), channel_id=1, source_target_pairs={{4,0},{12,8},{20,16},{5,1},{13,9},{21,17},{6,2},{14,10},{22,18},{7... | collective-permute-start | bytes 1179656 | tf_op jit(solution)/shard_map/ppermute | solution.py:129
  141.4 9.0 %copy-start.2 = (bf16[1536,768]{1,0:T(8,128)(2,1)S(1)}, bf16[1536,768]{1,0:T(8,128)(2,1)}, u32[]{:S(2)}) copy-start(bf16[1536,768]{1,0:T(8,128)(2,1)} %copy-done.1) | copy-start | bytes 7077892
  141.4 9.0 %copy-start.4 = (bf16[512,768]{1,0:T(8,128)(2,1)S(1)}, bf16[512,768]{1,0:T(8,128)(2,1)}, u32[]{:S(2)}) copy-start(bf16[512,768]{1,0:T(8,128)(2,1)} %param.8) | copy-start | bytes 2359300
  146.9 24.8 %collective-permute-start.14 = (bf16[4,128,384]{2,1,0:T(8,128)(2,1)}, bf16[4,128,384]{2,1,0:T(8,128)(2,1)}, u32[]{:S(2)}, u32[]{:S(2)}) collective-permute-start(bf16[4,128,384]{2,1,0:T(8,128)(2,1)} %pad_maximum_fusion.2), channel_id=1, source_target_pairs={{0,16},{4,20},{8,24},{12,28},{16,0},{20,4},{24,8},{28,12},{1,17},{... | collective-permute-start | bytes 1179656 | tf_op jit(solution)/shard_map/ppermute | solution.py:28
  148.8 36.8 %collective-permute-start.10 = (bf16[1536,384]{1,0:T(8,128)(2,1)}, bf16[1536,384]{1,0:T(8,128)(2,1)}, u32[]{:S(2)}, u32[]{:S(2)}) collective-permute-start(bf16[1536,384]{1,0:T(8,128)(2,1)} %convolution_convert_fusion), channel_id=1, source_target_pairs={{12,4},{20,12},{28,20},{13,5},{21,13},{29,21},{14,6},{22,14},{30,2... | collective-permute-start | bytes 3538952 | tf_op jit(solution)/shard_map/ppermute | solution.py:128
  151.7 0.9 copy-start.5
  152.6 19.1 %copy-start.7 = (bf16[2,128,384]{2,1,0:T(8,128)(2,1)S(1)}, bf16[2,128,384]{2,1,0:T(8,128)(2,1)}, u32[]{:S(2)}) copy-start(bf16[2,128,384]{2,1,0:T(8,128)(2,1)} %copy-done.6) | copy-start | bytes 589828
  173.8 11.8 %collective-permute-start.11 = (bf16[1536,384]{1,0:T(8,128)(2,1)}, bf16[1536,384]{1,0:T(8,128)(2,1)S(1)}, u32[]{:S(2)}, u32[]{:S(2)}) collective-permute-start(bf16[1536,384]{1,0:T(8,128)(2,1)} %collective-permute-done.9), channel_id=1, source_target_pairs={{4,0},{12,8},{20,16},{5,1},{13,9},{21,17},{6,2},{14,10},{22,18},{7... | collective-permute-start | bytes 3538952 | tf_op jit(solution)/shard_map/ppermute | solution.py:129
  188.3 40.1 %copy-start.9 = (pred[768]{0:T(1024)(128)(4,1)S(1)}, pred[768]{0:T(1024)(128)(4,1)}, u32[]{:S(2)}) copy-start(pred[768]{0:T(1024)(128)(4,1)} %broadcast_in_dim.32) | copy-start | bytes 2308
  224.5 21.6 %collective-permute-start.15 = (bf16[512,192]{1,0:T(8,128)(2,1)}, bf16[512,192]{1,0:T(8,128)(2,1)}, u32[]{:S(2)}, u32[]{:S(2)}) collective-permute-start(bf16[512,192]{1,0:T(8,128)(2,1)} %bitcast.12), channel_id=1, source_target_pairs={{0,1},{1,2},{2,3},{3,0},{4,5},{5,6},{6,7},{7,4},{8,9},{9,10},{10,1... | collective-permute-start | bytes 589832 | tf_op jit(solution)/shard_map/ppermute | solution.py:202
  224.5 21.6 %collective-permute-start.16 = (bf16[512,192]{1,0:T(8,128)(2,1)}, bf16[512,192]{1,0:T(8,128)(2,1)}, u32[]{:S(2)}, u32[]{:S(2)}) collective-permute-start(bf16[512,192]{1,0:T(8,128)(2,1)} %bitcast.13), channel_id=1, source_target_pairs={{0,2},{1,3},{2,0},{3,1},{4,6},{5,7},{6,4},{7,5},{8,10},{9,11},{10,... | collective-permute-start | bytes 589832 | tf_op jit(solution)/shard_map/ppermute | solution.py:202
  226.3 19.9 %collective-permute-start.17 = (bf16[512,192]{1,0:T(8,128)(2,1)}, bf16[512,192]{1,0:T(8,128)(2,1)}, u32[]{:S(2)}, u32[]{:S(2)}) collective-permute-start(bf16[512,192]{1,0:T(8,128)(2,1)} %bitcast.14), channel_id=1, source_target_pairs={{0,3},{1,0},{2,1},{3,2},{4,7},{5,4},{6,5},{7,6},{8,11},{9,8},{10,9... | collective-permute-start | bytes 589832 | tf_op jit(solution)/shard_map/ppermute | solution.py:202
Sparse Core Ops, SparseCore 0:
  8.9 64.7 all-gather.1

commit v11 on v7

--- a/solution.py
+++ b/solution.py
@@ -143,8 +143,13 @@
     kv_w = jnp.concatenate([key_w, value_w], axis=1)
     kva = window_of(project_kv(tokens, kv_w), 0)
 
-    gathered = lax.all_gather(tokens, "head", axis=0, tiled=True)
-    rest_tokens = jnp.roll(gathered, -head_rank * own_rows, axis=0)[own_rows:]
+    rest_tokens = jnp.concatenate(
+        [
+            lax.ppermute(tokens, "head", [(z, (z - k) % head_count) for z in range(head_count)])
+            for k in range(1, head_count)
+        ],
+        axis=0,
+    )
     kvb = window_of(project_kv(rest_tokens, kv_w), 0)
     rolled_tokens = jnp.concatenate([tokens, rest_tokens], axis=0)
     queries = jnp.dot(rolled_tokens, query_w, preferred_element_type=jnp.float32).astype(
@@ -153,7 +158,9 @@
 
     seq_count = lax.axis_size("seq")
     seq_rank = lax.axis_index("seq")
-    kvanc = gather_all(project_kv(gathered[:BLK], kv_w), "seq")
+    first_at = ((head_count - head_rank) % head_count) * own_rows
+    first_rows = lax.dynamic_slice_in_dim(rolled_tokens, first_at, BLK, 0)
+    kvanc = gather_all(project_kv(first_rows, kv_w), "seq")
     held_count = kvanc.shape[0]
     kvanc = kvanc.reshape(held_count * BLK, 2 * width_here)
     first_block = (seq_rank - 2) * block_count

time: 254 us -> 239 us (0.941); the launches traced: 254 us -> 237 us
  between operations: 13.9 us -> 0.48 us
  waiting for transfers between devices: 87.7 us -> 83.1 us
  starting transfers between devices: 43.7 us -> 47 us
  other arithmetic: 9 us -> 6.07 us
  matrix products: 9.43 us -> 12.3 us
    all_gather x1 -> x0, waiting for transfers between devices: 39.8 us -> none  [shards(): gathered = lax.all_gather(tokens, 'head', axis=0, tiled=True)]
    ppermute x0 -> x3, waiting for transfers between devices: none -> 36.4 us  [shards(): lax.ppermute(tokens, 'head', [(z, (z - k) % head_count) for z in range(he...]
    ppermute x0 -> x3, starting transfers between devices: none -> 4.61 us  [shards(): lax.ppermute(tokens, 'head', [(z, (z - k) % head_count) for z in range(he...]
    concatenate x1 -> x0, other arithmetic: 4.05 us -> none  [shards(): rest_tokens = jnp.roll(gathered, -head_rank * own_rows, axis=0)[own_rows:]]
    unnamed x47 -> x38, local copies, waits for them, and re-layouts: 18.4 us -> 15.2 us
  transfers between devices with their start and end apart: 15 -> 17, of which waited for: 5 -> 4; matrix products, arithmetic and copies ran while one was open for 20% -> 21% of each run, Pallas kernels for 6% -> 6%
where the time goes in v11:
time: 239 us; the launch traced here: 237 us
  waiting for transfers between devices  83.1 us (35%)
  Pallas kernels  49.3 us (21%)
  starting transfers between devices  47 us (20%)
  local copies, waits for them, and re-layouts  38.4 us (16%)
  matrix products  12.3 us (5%)
  other arithmetic  6.07 us (3%)
    pallas_call x2, Pallas kernels, attention(): pl.pallas_call(kernel, out_shape=jax.ShapeDtypeStruct(queries.shape, jnp....  49.3 us
    ppermute x3, waiting for transfers between devices, shards(): lax.ppermute(tokens, 'head', [(z, (z - k) % head_count) for z in range(he...  36.4 us
    ppermute x8, starting transfers between devices, shifted(): return lax.ppermute(x, axis, pairs)  34.9 us
    ppermute x3, waiting for transfers between devices, gather_all(): got = lax.ppermute(held, axis, pairs)  25.2 us
    ppermute x8, waiting for transfers between devices, shifted(): return lax.ppermute(x, axis, pairs)  21.5 us
    unnamed x38, local copies, waits for them, and re-layouts  15.2 us
    dot_general x3, matrix products, project_kv(): jnp.dot(x, kv_w, preferred_element_type=jnp.float32).astype(jnp.bfloat16)  7.06 us
    ppermute x3, starting transfers between devices, shards(): received[j] = lax.ppermute(away[j - 1], 'head', pairs)  4.92 us
  transfers between devices with their start and end apart: 17, of which 4 were waited for; matrix products, arithmetic and copies ran while one was open for 21% of the time, Pallas kernels for 6%

profile of v11, /device:TPU:2, one launch (start us, length us, event | category | flops | bytes accessed | tf_op | source)
XLA Modules:
  0.0 236.6 jit_solution(13982142271505408788)
XLA Ops:
  0.0 3.6 %collective-permute-start = (bf16[512,768]{1,0:T(8,128)(2,1)}, bf16[512,768]{1,0:T(8,128)(2,1)}, u32[]{:S(2)}, u32[]{:S(2)}) collective-permute-start(bf16[512,768]{1,0:T(8,128)(2,1)} %param.8), channel_id=1, source_target_pairs={{0,3},{1,0},{2,1},{3,2},{4,7},{5,4},{6,5},{7,6},{8,11},{9,8},{10,9... | collective-permute-start | bytes 2359304 | tf_op jit(solution)/shard_map/ppermute | solution.py:148
  3.6 1.0 collective-permute-start.2
  4.6 3.2 %fusion.43 = (bf16[768,1,768]{2,0,1:T(8,128)(2,1)S(1)}, bf16[768,1,768]{2,0,1:T(8,128)(2,1)}, bf16[768,1,768]{2,0,1:T(8,128)(2,1)S(1)}) fusion(bf16[768,3,768]{2,0,1:T(8,128)(2,1)} %param.9), kind=kLoop, calls=%fused_computation.123 | loop fusion | bytes 7077888 | tf_op jit(solution)/shard_map/slice | solution.py:140
  8.2 0.7 copy-done.4
  9.0 2.5 %fusion.5 = bf16[512,384]{1,0:T(8,128)(2,1)} fusion(bf16[512,768]{1,0:T(8,128)(2,1)} %param.8, bf16[768,192]{1,0:T(8,128)(2,1)S(1)} %get-tuple-element.18, bf16[768,192]{1,0:T(8,128)(2,1)S(1)} %get-tuple-element.19), kind=kOutput, calls=%fused_computation.12 | convolution fusion | flops 303366144 | bytes 1769472 | tf_op jit(solution)/shard_map/dot_general | solution.py:119
  11.5 3.4 %collective-permute-start.3 = (bf16[512,384]{1,0:T(8,128)(2,1)}, bf16[512,384]{1,0:T(8,128)(2,1)S(1)}, u32[]{:S(2)}, u32[]{:S(2)}) collective-permute-start(bf16[512,384]{1,0:T(8,128)(2,1)} %fusion.5), channel_id=1, source_target_pairs={{0,8},{4,12},{8,16},{12,20},{16,24},{20,28},{1,9},{5,13},{9,17},{1... | collective-permute-start | bytes 1179656 | tf_op jit(solution)/shard_map/ppermute | solution.py:18
  14.9 1.9 collective-permute-start.4
  17.5 0.8 sort.17
  18.6 2.5 %gather_fusion.2 = s32[320]{0:T(512)S(1)} fusion(s32[16,20]{1,0:T(8,128)S(1)} %pad_add_fusion.1, s32[320]{0:T(512)S(1)} %reshape.140), kind=kCustom, calls=%fused_computation.1.clone | custom fusion | bytes 5120 | tf_op jit(solution)/shard_map/jit(take_along_axis)/gather | solution.py:194
  21.2 2.5 %gather_fusion.1 = s32[320]{0:T(512)S(1)} fusion(s32[16,20]{1,0:T(8,128)S(1)} %concatenate.55, s32[320]{0:T(512)S(1)} %reshape.140), kind=kCustom, calls=%fused_computation.clone | custom fusion | bytes 5120 | tf_op jit(solution)/shard_map/jit(take_along_axis)/gather | solution.py:195
  25.1 0.6 slice.59.count
  25.8 0.7 broadcast_in_dim.32
  27.1 0.7 gather_fusion
  27.9 3.6 %collective-permute-start.5 = (bf16[512,384]{1,0:T(8,128)(2,1)}, bf16[512,384]{1,0:T(8,128)(2,1)S(1)}, u32[]{:S(2)}, u32[]{:S(2)}) collective-permute-start(bf16[512,384]{1,0:T(8,128)(2,1)} %fusion.5), channel_id=1, source_target_pairs={{4,0},{8,4},{12,8},{16,12},{20,16},{24,20},{28,24},{5,1},{9,5},{13... | collective-permute-start | bytes 1179656 | tf_op jit(solution)/shard_map/ppermute | solution.py:18
  31.7 1.9 collective-permute-start.6
  33.6 1.2 constant_dynamic-update-slice_fusion.2
  34.8 36.4 %collective-permute-done.1 = bf16[512,768]{1,0:T(8,128)(2,1)} collective-permute-done((bf16[512,768]{1,0:T(8,128)(2,1)}, bf16[512,768]{1,0:T(8,128)(2,1)}, u32[]{:S(2)}, u32[]{:S(2)}) %collective-permute-start.1) | collective-permute-done | bytes 786464 | tf_op jit(solution)/shard_map/ppermute | solution.py:148
  71.2 1.2 constant_dynamic-update-slice_fusion.1
  72.4 1.2 constant_dynamic-update-slice_fusion
  74.0 4.2 %convolution_convert_fusion = bf16[1536,384]{1,0:T(8,128)(2,1)} fusion(bf16[512,768]{1,0:T(8,128)(2,1)} %collective-permute-done.2, bf16[512,768]{1,0:T(8,128)(2,1)} %collective-permute-done.1, bf16[512,768]{1,0:T(8,128)(2,1)} %collective-permute-done, bf16[768,192]{1,0:T(8,128)(2,1)S(1)} %copy-done.5, bf16[768,192]{1,0:T(8,128)(2,1)S(1)} %copy-done.7), kind=kOutput, calls=%fused_computation.3 | convolution fusion | flops 914817024 | bytes 4128768 | tf_op jit(solution)/shard_map/dot_general | solution.py:119
  78.2 3.4 %collective-permute-start.7 = (bf16[1536,384]{1,0:T(8,128)(2,1)}, bf16[1536,384]{1,0:T(8,128)(2,1)}, u32[]{:S(2)}, u32[]{:S(2)}) collective-permute-start(bf16[1536,384]{1,0:T(8,128)(2,1)} %convolution_convert_fusion), channel_id=1, source_target_pairs={{0,8},{4,12},{8,16},{12,20},{16,24},{20,28},{1,9},{5,13},{9,17},{1... | collective-permute-start | bytes 3538952 | tf_op jit(solution)/shard_map/ppermute | solution.py:18
  81.6 1.1 constant_dynamic-update-slice_fusion.7
  82.7 3.2 %collective-permute-start.8 = (bf16[1536,384]{1,0:T(8,128)(2,1)}, bf16[1536,384]{1,0:T(8,128)(2,1)}, u32[]{:S(2)}, u32[]{:S(2)}) collective-permute-start(bf16[1536,384]{1,0:T(8,128)(2,1)} %convolution_convert_fusion), channel_id=1, source_target_pairs={{0,4},{4,8},{8,12},{12,16},{16,20},{20,24},{24,28},{1,5},{5,9},{9,... | collective-permute-start | bytes 3538952 | tf_op jit(solution)/shard_map/ppermute | solution.py:18
  86.5 1.1 constant_dynamic-update-slice_fusion.6
  87.6 25.2 %collective-permute-done.12 = bf16[2,128,384]{2,1,0:T(8,128)(2,1)S(1)} collective-permute-done((bf16[2,128,384]{2,1,0:T(8,128)(2,1)S(1)}, bf16[2,128,384]{2,1,0:T(8,128)(2,1)S(1)}, u32[]{:S(2)}, u32[]{:S(2)}) %collective-permute-start.12) | collective-permute-done | bytes 196640 | tf_op jit(solution)/shard_map/ppermute | solution.py:28
  112.8 0.8 pad_maximum_fusion.2
  113.6 2.0 collective-permute-start.13
  115.7 15.3 %collective-permute-start.9 = (bf16[1536,384]{1,0:T(8,128)(2,1)}, bf16[1536,384]{1,0:T(8,128)(2,1)}, u32[]{:S(2)}, u32[]{:S(2)}) collective-permute-start(bf16[1536,384]{1,0:T(8,128)(2,1)} %convolution_convert_fusion), channel_id=1, source_target_pairs={{4,0},{8,4},{12,8},{16,12},{20,16},{24,20},{28,24},{5,1},{9,5},{13... | collective-permute-start | bytes 3538952 | tf_op jit(solution)/shard_map/ppermute | solution.py:18
  131.0 2.1 collective-permute-start.10
  133.1 2.3 convolution_convert_fusion.1
  135.5 0.9 slice.78
  136.3 2.2 copy.46
  138.5 2.0 pad_maximum_fusion
  140.6 2.4 %constant_dynamic-update-slice_fusion.13 = bf16[7680,384]{1,0:T(8,128)(2,1)} fusion(bf16[1536,384]{1,0:T(8,128)(2,1)} %collective-permute-done.7), kind=kLoop, calls=%fused_computation.46 | loop fusion | bytes 2359296
  143.0 2.4 %constant_dynamic-update-slice_fusion.12 = bf16[7680,384]{1,0:T(8,128)(2,1)} fusion(bf16[7680,384]{1,0:T(8,128)(2,1)} %constant_dynamic-update-slice_fusion.13, bf16[1536,384]{1,0:T(8,128)(2,1)} %collective-permute-done.8), kind=kLoop, calls=%fused_computation.45 | loop fusion | bytes 2359296
  145.4 2.4 %constant_dynamic-update-slice_fusion.11 = bf16[7680,384]{1,0:T(8,128)(2,1)} fusion(bf16[7680,384]{1,0:T(8,128)(2,1)} %constant_dynamic-update-slice_fusion.12, bf16[1536,384]{1,0:T(8,128)(2,1)} %convolution_convert_fusion), kind=kLoop, calls=%fused_computation.44 | loop fusion | bytes 2359296
  147.8 8.4 %collective-permute-done.9 = bf16[1536,384]{1,0:T(8,128)(2,1)} collective-permute-done((bf16[1536,384]{1,0:T(8,128)(2,1)}, bf16[1536,384]{1,0:T(8,128)(2,1)}, u32[]{:S(2)}, u32[]{:S(2)}) %collective-permute-start.9) | collective-permute-done | bytes 1179680 | tf_op jit(solution)/shard_map/ppermute | solution.py:18
  156.2 2.4 %constant_dynamic-update-slice_fusion.10 = bf16[7680,384]{1,0:T(8,128)(2,1)} fusion(bf16[7680,384]{1,0:T(8,128)(2,1)} %constant_dynamic-update-slice_fusion.11, bf16[1536,384]{1,0:T(8,128)(2,1)} %collective-permute-done.9), kind=kLoop, calls=%fused_computation.43 | loop fusion | bytes 2359296
  158.7 13.1 %collective-permute-done.10 = bf16[1536,384]{1,0:T(8,128)(2,1)} collective-permute-done((bf16[1536,384]{1,0:T(8,128)(2,1)}, bf16[1536,384]{1,0:T(8,128)(2,1)}, u32[]{:S(2)}, u32[]{:S(2)}) %collective-permute-start.10) | collective-permute-done | bytes 1179680 | tf_op jit(solution)/shard_map/ppermute | solution.py:18
  171.7 2.4 %constant_dynamic-update-slice_fusion.9.refs_1_ = bf16[7680,384]{1,0:T(8,128)(2,1)} fusion(bf16[7680,384]{1,0:T(8,128)(2,1)} %constant_dynamic-update-slice_fusion.10, bf16[1536,384]{1,0:T(8,128)(2,1)} %collective-permute-done.10), kind=kLoop, calls=%fused_computation.42 | loop fusion | bytes 2359296 | tf_op jit(solution)/shard_map/concatenate | solution.py:126
  174.2 34.0 %shard_map.65 = bf16[12,128,192]{2,1,0:T(8,128)(2,1)} custom-call(s32[12]{0:T(128)} %slice.59.count, s32[12,20]{1,0:T(8,128)} %slice.76.source, s32[12,20]{1,0:T(8,128)} %slice.77.rows, bf16[12,128,192]{2,1,0:T(8,128)(2,1)} %bitcast.36, bf16[2560,384]{1,0:T(8,128)(2,1)} %copy-done.1, bf16[7680,384]{1,0:T(8,128)(2,1)} %constant_dynamic-update-slice_fusion.9.refs_1_, ...), custom_call_target="tpu_custom_call" | custom-call | flops 3019898880 | bytes 9830400 | tf_op jit(solution)/shard_map/pallas_call | solution.py:95
  208.2 2.0 fusion.44
  210.4 1.8 collective-permute-start.15
  212.1 2.9 %collective-permute-start.16 = (bf16[512,192]{1,0:T(8,128)(2,1)S(1)}, bf16[512,192]{1,0:T(8,128)(2,1)}, u32[]{:S(2)}, u32[]{:S(2)}) collective-permute-start(bf16[512,192]{1,0:T(8,128)(2,1)S(1)} %bitcast.38), channel_id=1, source_target_pairs={{0,3},{1,0},{2,1},{3,2},{4,7},{5,4},{6,5},{7,6},{8,11},{9,8},{10,9... | collective-permute-start | bytes 589832 | tf_op jit(solution)/shard_map/ppermute | solution.py:205
  215.1 1.3 bitcast_select_fusion
  217.5 0.9 copy.44
  218.4 15.3 %shard_map.64 = bf16[4,128,192]{2,1,0:T(8,128)(2,1)} custom-call(s32[4]{0:T(128)} %bitcast.39, s32[4,20]{1,0:T(4,128)} %slice.73.source, s32[4,20]{1,0:T(4,128)} %slice.74.rows, bf16[4,128,192]{2,1,0:T(8,128)(2,1)} %bitcast.35, bf16[2560,384]{1,0:T(8,128)(2,1)} %copy-done.1, bf16[7680,384]{1,0:T(8,128)(2,1)} %constant_dynamic-update-slice_fusion.9.refs_1_, ...), custom_call_target="tpu_custom_call" | custom-call | flops 1006632960 | bytes 9043968 | tf_op jit(solution)/shard_map/pallas_call | solution.py:95
  233.7 2.9 %convolution_convert_fusion.2 = bf16[512,768]{1,0:T(8,128)(2,1)} fusion(bf16[768,768]{1,0:T(8,128)(2,1)S(1)} %copy-done.2, bf16[512,192]{1,0:T(8,128)(2,1)} %collective-permute-done.16, bf16[512,192]{1,0:T(8,128)(2,1)} %collective-permute-done.15, bf16[512,192]{1,0:T(8,128)(2,1)} %collective-permute-done.14, bf16[512,192]{1,0:T(8,128)(2,1)} %bitcast.37), kind=kOutput, calls=%fused_computation.10 | convolution fusion | flops 607518720 | bytes 2752512 | tf_op jit(solution)/shard_map/dot_general | solution.py:211
  (82 shorter events, 5.9 us)
Async XLA Ops:
  0.0 27.1 %copy-start = (bf16[768,768]{1,0:T(8,128)(2,1)S(1)}, bf16[768,768]{1,0:T(8,128)(2,1)}, u32[]{:S(2)}) copy-start(bf16[768,768]{1,0:T(8,128)(2,1)} %param.10) | copy-start | bytes 3538948
  0.0 31.6 %collective-permute-start = (bf16[512,768]{1,0:T(8,128)(2,1)}, bf16[512,768]{1,0:T(8,128)(2,1)}, u32[]{:S(2)}, u32[]{:S(2)}) collective-permute-start(bf16[512,768]{1,0:T(8,128)(2,1)} %param.8), channel_id=1, source_target_pairs={{0,3},{1,0},{2,1},{3,2},{4,7},{5,4},{6,5},{7,6},{8,11},{9,8},{10,9... | collective-permute-start | bytes 2359304 | tf_op jit(solution)/shard_map/ppermute | solution.py:148
  3.6 67.6 %collective-permute-start.1 = (bf16[512,768]{1,0:T(8,128)(2,1)}, bf16[512,768]{1,0:T(8,128)(2,1)}, u32[]{:S(2)}, u32[]{:S(2)}) collective-permute-start(bf16[512,768]{1,0:T(8,128)(2,1)} %param.8), channel_id=1, source_target_pairs={{0,2},{1,3},{2,0},{3,1},{4,6},{5,7},{6,4},{7,5},{8,10},{9,11},{10,... | collective-permute-start | bytes 2359304 | tf_op jit(solution)/shard_map/ppermute | solution.py:148
  3.6 68.8 %collective-permute-start.2 = (bf16[512,768]{1,0:T(8,128)(2,1)}, bf16[512,768]{1,0:T(8,128)(2,1)}, u32[]{:S(2)}, u32[]{:S(2)}) collective-permute-start(bf16[512,768]{1,0:T(8,128)(2,1)} %param.8), channel_id=1, source_target_pairs={{0,1},{1,2},{2,3},{3,0},{4,5},{5,6},{6,7},{7,4},{8,9},{9,10},{10,1... | collective-permute-start | bytes 2359304 | tf_op jit(solution)/shard_map/ppermute | solution.py:148
  7.9 9.0 %copy-start.8 = (s32[16,12]{1,0:T(8,128)S(1)}, s32[16,12]{1,0:T(8,128)}, u32[]{:S(2)}) copy-start(s32[16,12]{1,0:T(8,128)} %param.11) | copy-start | bytes 2308
  7.9 9.2 %copy-start.10 = (s32[16,8]{0,1:T(8,128)S(1)}, s32[16,8]{0,1:T(8,128)}, u32[]{:S(2)}) copy-start(s32[16,8]{0,1:T(8,128)} %param.13) | copy-start | bytes 1540
  7.9 9.3 %copy-start.12 = (s32[16]{0:T(128)S(1)}, s32[16]{0:T(128)}, u32[]{:S(2)}) copy-start(s32[16]{0:T(128)} %param.12) | copy-start | bytes 196
  8.2 0.8 copy-start.4
  8.2 3.3 %copy-start.6 = (bf16[768,192]{1,0:T(8,128)(2,1)}, bf16[768,192]{1,0:T(8,128)(2,1)S(1)}, u32[]{:S(2)}) copy-start(bf16[768,192]{1,0:T(8,128)(2,1)S(1)} %get-tuple-element.19) | copy-start | bytes 884740
  11.5 16.4 %collective-permute-start.3 = (bf16[512,384]{1,0:T(8,128)(2,1)}, bf16[512,384]{1,0:T(8,128)(2,1)S(1)}, u32[]{:S(2)}, u32[]{:S(2)}) collective-permute-start(bf16[512,384]{1,0:T(8,128)(2,1)} %fusion.5), channel_id=1, source_target_pairs={{0,8},{4,12},{8,16},{12,20},{16,24},{20,28},{1,9},{5,13},{9,17},{1... | collective-permute-start | bytes 1179656 | tf_op jit(solution)/shard_map/ppermute | solution.py:18
  14.9 66.7 %collective-permute-start.4 = (bf16[512,384]{1,0:T(8,128)(2,1)}, bf16[512,384]{1,0:T(8,128)(2,1)}, u32[]{:S(2)}, u32[]{:S(2)}) collective-permute-start(bf16[512,384]{1,0:T(8,128)(2,1)} %fusion.5), channel_id=1, source_target_pairs={{0,4},{4,8},{8,12},{12,16},{16,20},{20,24},{24,28},{1,5},{5,9},{9,... | collective-permute-start | bytes 1179656 | tf_op jit(solution)/shard_map/ppermute | solution.py:18
  23.7 4.1 %copy-start.3 = (bf16[512,768]{1,0:T(8,128)(2,1)S(1)}, bf16[512,768]{1,0:T(8,128)(2,1)}, u32[]{:S(2)}) copy-start(bf16[512,768]{1,0:T(8,128)(2,1)} %param.8) | copy-start | bytes 2359300
  25.1 2.0 copy-start.11
  27.9 59.6 %collective-permute-start.5 = (bf16[512,384]{1,0:T(8,128)(2,1)}, bf16[512,384]{1,0:T(8,128)(2,1)S(1)}, u32[]{:S(2)}, u32[]{:S(2)}) collective-permute-start(bf16[512,384]{1,0:T(8,128)(2,1)} %fusion.5), channel_id=1, source_target_pairs={{4,0},{8,4},{12,8},{16,12},{20,16},{24,20},{28,24},{5,1},{9,5},{13... | collective-permute-start | bytes 1179656 | tf_op jit(solution)/shard_map/ppermute | solution.py:18
  31.7 83.9 %collective-permute-start.6 = (bf16[512,384]{1,0:T(8,128)(2,1)}, bf16[512,384]{1,0:T(8,128)(2,1)S(1)}, u32[]{:S(2)}, u32[]{:S(2)}) collective-permute-start(bf16[512,384]{1,0:T(8,128)(2,1)} %fusion.5), channel_id=1, source_target_pairs={{8,0},{12,4},{16,8},{20,12},{24,16},{28,20},{9,1},{13,5},{17,9},{2... | collective-permute-start | bytes 1179656 | tf_op jit(solution)/shard_map/ppermute | solution.py:18
  34.8 38.8 %copy-start.5 = (bf16[768,192]{1,0:T(8,128)(2,1)S(1)}, bf16[768,192]{1,0:T(8,128)(2,1)}, u32[]{:S(2)}) copy-start(bf16[768,192]{1,0:T(8,128)(2,1)} %copy-done.4) | copy-start | bytes 884740
  34.8 38.8 %copy-start.7 = (bf16[768,192]{1,0:T(8,128)(2,1)S(1)}, bf16[768,192]{1,0:T(8,128)(2,1)}, u32[]{:S(2)}) copy-start(bf16[768,192]{1,0:T(8,128)(2,1)} %copy-done.6) | copy-start | bytes 884740
  73.9 12.0 %collective-permute-start.11 = (bf16[1,128,384]{2,1,0:T(8,128)(2,1)S(1)}, bf16[1,128,384]{2,1,0:T(8,128)(2,1)S(1)}, u32[]{:S(2)}, u32[]{:S(2)}) collective-permute-start(bf16[1,128,384]{2,1,0:T(8,128)(2,1)S(1)} %fusion.6), channel_id=1, source_target_pairs={{0,4},{4,8},{8,12},{12,16},{16,20},{20,24},{24,28},{28,0},{1,5},{5... | collective-permute-start | bytes 294920 | tf_op jit(solution)/shard_map/ppermute | solution.py:28
  78.2 62.4 %collective-permute-start.7 = (bf16[1536,384]{1,0:T(8,128)(2,1)}, bf16[1536,384]{1,0:T(8,128)(2,1)}, u32[]{:S(2)}, u32[]{:S(2)}) collective-permute-start(bf16[1536,384]{1,0:T(8,128)(2,1)} %convolution_convert_fusion), channel_id=1, source_target_pairs={{0,8},{4,12},{8,16},{12,20},{16,24},{20,28},{1,9},{5,13},{9,17},{1... | collective-permute-start | bytes 3538952 | tf_op jit(solution)/shard_map/ppermute | solution.py:18
  82.7 60.3 %collective-permute-start.8 = (bf16[1536,384]{1,0:T(8,128)(2,1)}, bf16[1536,384]{1,0:T(8,128)(2,1)}, u32[]{:S(2)}, u32[]{:S(2)}) collective-permute-start(bf16[1536,384]{1,0:T(8,128)(2,1)} %convolution_convert_fusion), channel_id=1, source_target_pairs={{0,4},{4,8},{8,12},{12,16},{16,20},{20,24},{24,28},{1,5},{5,9},{9,... | collective-permute-start | bytes 3538952 | tf_op jit(solution)/shard_map/ppermute | solution.py:18
  85.9 26.8 %collective-permute-start.12 = (bf16[2,128,384]{2,1,0:T(8,128)(2,1)S(1)}, bf16[2,128,384]{2,1,0:T(8,128)(2,1)S(1)}, u32[]{:S(2)}, u32[]{:S(2)}) collective-permute-start(bf16[2,128,384]{2,1,0:T(8,128)(2,1)S(1)} %pad_maximum_fusion.3), channel_id=1, source_target_pairs={{0,8},{4,12},{8,16},{12,20},{16,24},{20,28},{24,0},{28,4},{1,9},{5... | collective-permute-start | bytes 589832 | tf_op jit(solution)/shard_map/ppermute | solution.py:28
  113.6 25.0 %collective-permute-start.13 = (bf16[4,128,384]{2,1,0:T(8,128)(2,1)}, bf16[4,128,384]{2,1,0:T(8,128)(2,1)}, u32[]{:S(2)}, u32[]{:S(2)}) collective-permute-start(bf16[4,128,384]{2,1,0:T(8,128)(2,1)} %pad_maximum_fusion.2), channel_id=1, source_target_pairs={{0,16},{4,20},{8,24},{12,28},{16,0},{20,4},{24,8},{28,12},{1,17},{... | collective-permute-start | bytes 1179656 | tf_op jit(solution)/shard_map/ppermute | solution.py:28
  115.7 19.8 %copy-start.1 = (bf16[2560,384]{1,0:T(8,128)(2,1)}, bf16[2560,384]{1,0:T(8,128)(2,1)S(1)}, u32[]{:S(2)}) copy-start(bf16[2560,384]{1,0:T(8,128)(2,1)S(1)} %constant_dynamic-update-slice_fusion.4.refs_0_) | copy-start | bytes 5898244
  115.7 40.6 %collective-permute-start.9 = (bf16[1536,384]{1,0:T(8,128)(2,1)}, bf16[1536,384]{1,0:T(8,128)(2,1)}, u32[]{:S(2)}, u32[]{:S(2)}) collective-permute-start(bf16[1536,384]{1,0:T(8,128)(2,1)} %convolution_convert_fusion), channel_id=1, source_target_pairs={{4,0},{8,4},{12,8},{16,12},{20,16},{24,20},{28,24},{5,1},{9,5},{13... | collective-permute-start | bytes 3538952 | tf_op jit(solution)/shard_map/ppermute | solution.py:18
  131.0 40.7 %collective-permute-start.10 = (bf16[1536,384]{1,0:T(8,128)(2,1)}, bf16[1536,384]{1,0:T(8,128)(2,1)}, u32[]{:S(2)}, u32[]{:S(2)}) collective-permute-start(bf16[1536,384]{1,0:T(8,128)(2,1)} %convolution_convert_fusion), channel_id=1, source_target_pairs={{8,0},{12,4},{16,8},{20,12},{24,16},{28,20},{9,1},{13,5},{17,9},{2... | collective-permute-start | bytes 3538952 | tf_op jit(solution)/shard_map/ppermute | solution.py:18
  174.2 40.9 %copy-start.9 = (pred[768]{0:T(1024)(128)(4,1)S(1)}, pred[768]{0:T(1024)(128)(4,1)}, u32[]{:S(2)}) copy-start(pred[768]{0:T(1024)(128)(4,1)} %broadcast_in_dim.32) | copy-start | bytes 2308
  210.1 23.5 %collective-permute-start.14 = (bf16[512,192]{1,0:T(8,128)(2,1)}, bf16[512,192]{1,0:T(8,128)(2,1)}, u32[]{:S(2)}, u32[]{:S(2)}) collective-permute-start(bf16[512,192]{1,0:T(8,128)(2,1)} %bitcast.11), channel_id=1, source_target_pairs={{0,1},{1,2},{2,3},{3,0},{4,5},{5,6},{6,7},{7,4},{8,9},{9,10},{10,1... | collective-permute-start | bytes 589832 | tf_op jit(solution)/shard_map/ppermute | solution.py:205
  210.4 23.3 %collective-permute-start.15 = (bf16[512,192]{1,0:T(8,128)(2,1)}, bf16[512,192]{1,0:T(8,128)(2,1)}, u32[]{:S(2)}, u32[]{:S(2)}) collective-permute-start(bf16[512,192]{1,0:T(8,128)(2,1)} %bitcast.12), channel_id=1, source_target_pairs={{0,2},{1,3},{2,0},{3,1},{4,6},{5,7},{6,4},{7,5},{8,10},{9,11},{10,... | collective-permute-start | bytes 589832 | tf_op jit(solution)/shard_map/ppermute | solution.py:205
  212.1 21.5 %collective-permute-start.16 = (bf16[512,192]{1,0:T(8,128)(2,1)S(1)}, bf16[512,192]{1,0:T(8,128)(2,1)}, u32[]{:S(2)}, u32[]{:S(2)}) collective-permute-start(bf16[512,192]{1,0:T(8,128)(2,1)S(1)} %bitcast.38), channel_id=1, source_target_pairs={{0,3},{1,0},{2,1},{3,2},{4,7},{5,4},{6,5},{7,6},{8,11},{9,8},{10,9... | collective-permute-start | bytes 589832 | tf_op jit(solution)/shard_map/ppermute | solution.py:205
  218.4 15.3 %copy-start.2 = (bf16[768,768]{1,0:T(8,128)(2,1)S(1)}, bf16[768,768]{1,0:T(8,128)(2,1)}, u32[]{:S(2)}) copy-start(bf16[768,768]{1,0:T(8,128)(2,1)} %bitcast_select_fusion) | copy-start | bytes 3538948

commit v12 on v7

--- a/solution.py
+++ b/solution.py
@@ -143,9 +143,25 @@
     kv_w = jnp.concatenate([key_w, value_w], axis=1)
     kva = window_of(project_kv(tokens, kv_w), 0)
 
-    gathered = lax.all_gather(tokens, "head", axis=0, tiled=True)
-    rest_tokens = jnp.roll(gathered, -head_rank * own_rows, axis=0)[own_rows:]
-    kvb = window_of(project_kv(rest_tokens, kv_w), 0)
+    def fetch_chunk(source, k):
+        pairs = [(z, (z - k) % head_count) for z in range(head_count)]
+        return lax.ppermute(source, "head", pairs)
+
+    near_k = sorted({1, head_count - 1})
+    groups = [near_k] + ([[k for k in range(1, head_count) if k not in near_k]]
+                         if head_count > 3 else [])
+    group_of, slot_of, size_of = [0] * head_count, [0] * head_count, [0] * head_count
+    kv_groups = []
+    received = {}
+    source = tokens
+    for g, members in enumerate(groups):
+        for p, k in enumerate(members):
+            group_of[k], slot_of[k], size_of[k] = g, p, len(members)
+            received[k] = fetch_chunk(source, k)
+        kv = project_kv(jnp.concatenate([received[k] for k in members], axis=0), kv_w)
+        source, kv = lax.optimization_barrier((tokens, kv))
+        kv_groups.append(window_of(kv, 0))
+    rest_tokens = jnp.concatenate([received[k] for k in range(1, head_count)], axis=0)
     rolled_tokens = jnp.concatenate([tokens, rest_tokens], axis=0)
     queries = jnp.dot(rolled_tokens, query_w, preferred_element_type=jnp.float32).astype(
         jnp.bfloat16
@@ -153,7 +169,9 @@
 
     seq_count = lax.axis_size("seq")
     seq_rank = lax.axis_index("seq")
-    kvanc = gather_all(project_kv(gathered[:BLK], kv_w), "seq")
+    first_at = ((head_count - head_rank) % head_count) * own_rows
+    first_rows = lax.dynamic_slice_in_dim(rolled_tokens, first_at, BLK, 0)
+    kvanc = gather_all(project_kv(first_rows, kv_w), "seq")
     held_count = kvanc.shape[0]
     kvanc = kvanc.reshape(held_count * BLK, 2 * width_here)
     first_block = (seq_rank - 2) * block_count
@@ -170,10 +188,13 @@
     inner = within % own_blocks
     mine = chunk == head_rank
     row_a = offset_idx * own_blocks + inner
-    row_b = (offset_idx * (block_count - own_blocks)
-             + ((chunk - head_rank) % head_count - 1) * own_blocks + inner)
+    hop = (chunk - head_rank) % head_count
+    hop_group = jnp.asarray(group_of, jnp.int32)[hop]
+    hop_slot = jnp.asarray(slot_of, jnp.int32)[hop]
+    hop_size = jnp.asarray(size_of, jnp.int32)[hop]
+    row_b = (offset_idx * hop_size + hop_slot) * own_blocks + inner
     near_row = jnp.where(mine, row_a, row_b)
-    near_src = jnp.where(mine, 0, 1)
+    near_src = jnp.where(mine, 0, 1 + hop_group)
     owner = jnp.clip(anchors // block_count, 0, seq_count - 1)
     anch_row = (owner - seq_rank + held_count - 1) % seq_count
     near_used = jnp.arange(neigh)[None, :] < near_count[:, None]
@@ -183,12 +204,12 @@
     valid = jnp.concatenate([near_used, jnp.logical_not(repeated)], axis=1)
     order = jnp.argsort(jnp.logical_not(valid).astype(jnp.int32), axis=1, stable=True)
     every_row = jnp.concatenate([near_row, anch_row], axis=1)
-    every_src = jnp.concatenate([near_src, jnp.full_like(anch_row, 2)], axis=1)
+    every_src = jnp.concatenate([near_src, jnp.full_like(anch_row, 1 + len(groups))], axis=1)
     rows = jnp.take_along_axis(every_row, order, axis=1).astype(jnp.int32)
     source = jnp.take_along_axis(every_src, order, axis=1).astype(jnp.int32)
     count = jnp.sum(valid.astype(jnp.int32), axis=1).astype(jnp.int32)
 
-    tables = (kva, kvb, kvanc)
+    tables = (kva, *kv_groups, kvanc)
     away = attention(queries[own_blocks:], tables, count[own_blocks:], source[own_blocks:],
                      rows[own_blocks:])
     away = away.reshape(head_count - 1, own_rows, width_here)

time: 254 us -> 222 us (0.87)
  waiting for transfers between devices: 87.7 us -> 29.9 us
  starting transfers between devices: 43.7 us -> 69.7 us
  between operations: 13.9 us -> 0.57 us
  local copies, waits for them, and re-layouts: 40.3 us -> 48.7 us
  matrix products: 9.43 us -> 13.6 us
  other arithmetic: 9 us -> 5 us
  Pallas kernels: 50.4 us -> 53.2 us
    all_gather x1 -> x0, waiting for transfers between devices: 39.8 us -> none  [shards(): gathered = lax.all_gather(tokens, 'head', axis=0, tiled=True)]
    ppermute x3, starting transfers between devices: 3.95 us -> 27.1 us  [gather_all(): got = lax.ppermute(held, axis, pairs)]
    ppermute x8 -> x12, waiting for transfers between devices: 21.2 us -> 1.17 us  [shifted(): return lax.ppermute(x, axis, pairs)]
    ppermute x0 -> x3, waiting for transfers between devices: none -> 19 us  [fetch_chunk(): return lax.ppermute(source, 'head', pairs)]
    ppermute x3, waiting for transfers between devices: 25.9 us -> 9.67 us  [gather_all(): got = lax.ppermute(held, axis, pairs)]
    gather x0 -> x5, local copies, waits for them, and re-layouts: none -> 4.81 us  [the longest x2 1.63 us: shards(): hop_size = jnp.asarray(size_of, jnp.int32)[hop]]
    ppermute x0 -> x3, starting transfers between devices: none -> 4.33 us  [fetch_chunk(): return lax.ppermute(source, 'head', pairs)]
    concatenate x1 -> x0, other arithmetic: 4.05 us -> none  [shards(): rest_tokens = jnp.roll(gathered, -head_rank * own_rows, axis=0)[own_rows:]]
  transfers between devices with their start and end apart: 15 -> 21, of which waited for: 5 -> 5; matrix products, arithmetic and copies ran while one was open for 20% -> 27% of each run, Pallas kernels for 6% -> 8%
where the time goes in v12:
time: 222 us; the launch traced here: 221 us
  starting transfers between devices  69.7 us (31%)
  Pallas kernels  53.2 us (24%)
  local copies, waits for them, and re-layouts  48.7 us (22%)
  waiting for transfers between devices  29.9 us (13%)
  matrix products  13.6 us (6%)
  other arithmetic  5 us (2%)
    pallas_call x2, Pallas kernels, attention(): pl.pallas_call(kernel, out_shape=jax.ShapeDtypeStruct(queries.shape, jnp....  53.2 us
    ppermute x12, starting transfers between devices, shifted(): return lax.ppermute(x, axis, pairs)  31.1 us
    ppermute x3, starting transfers between devices, gather_all(): got = lax.ppermute(held, axis, pairs)  27.1 us
    unnamed x56, local copies, waits for them, and re-layouts  19.1 us
    ppermute x3, waiting for transfers between devices, fetch_chunk(): return lax.ppermute(source, 'head', pairs)  19 us
    ppermute x3, waiting for transfers between devices, gather_all(): got = lax.ppermute(held, axis, pairs)  9.67 us
    dot_general x4, matrix products, project_kv(): jnp.dot(x, kv_w, preferred_element_type=jnp.float32).astype(jnp.bfloat16)  8.28 us
    ppermute x3, starting transfers between devices, shards(): received[j] = lax.ppermute(away[j - 1], 'head', pairs)  7.15 us
  transfers between devices with their start and end apart: 21, of which 5 were waited for; matrix products, arithmetic and copies ran while one was open for 27% of the time, Pallas kernels for 8%

profile of v12, /device:TPU:2, one launch (start us, length us, event | category | flops | bytes accessed | tf_op | source)
XLA Modules:
  0.0 220.6 jit_solution(17563777117190018456)
XLA Ops:
  0.0 3.6 %collective-permute-start = (bf16[512,768]{1,0:T(8,128)(2,1)}, bf16[512,768]{1,0:T(8,128)(2,1)}, u32[]{:S(2)}, u32[]{:S(2)}) collective-permute-start(bf16[512,768]{1,0:T(8,128)(2,1)} %param.11), channel_id=1, source_target_pairs={{0,3},{1,0},{2,1},{3,2},{4,7},{5,4},{6,5},{7,6},{8,11},{9,8},{10,9... | collective-permute-start | bytes 2359304 | tf_op jit(solution)/shard_map/ppermute | solution.py:148
  3.6 3.2 %fusion.39 = (bf16[768,1,768]{2,0,1:T(8,128)(2,1)}, bf16[768,1,768]{2,0,1:T(8,128)(2,1)S(1)}, bf16[768,1,768]{2,0,1:T(8,128)(2,1)S(1)}) fusion(bf16[768,3,768]{2,0,1:T(8,128)(2,1)} %param.12), kind=kLoop, calls=%fused_computation.130 | loop fusion | bytes 7077888 | tf_op jit(solution)/shard_map/slice | solution.py:139
  7.2 2.1 fusion.7
  9.3 3.4 %collective-permute-start.3 = (bf16[512,384]{1,0:T(8,128)(2,1)S(1)}, bf16[512,384]{1,0:T(8,128)(2,1)}, u32[]{:S(2)}, u32[]{:S(2)}) collective-permute-start(bf16[512,384]{1,0:T(8,128)(2,1)S(1)} %fusion.7), channel_id=1, source_target_pairs={{0,8},{4,12},{8,16},{12,20},{16,24},{20,28},{1,9},{5,13},{9,17},{1... | collective-permute-start | bytes 1179656 | tf_op jit(solution)/shard_map/ppermute | solution.py:18
  12.7 1.9 collective-permute-start.4
  14.6 3.6 %collective-permute-start.5 = (bf16[512,384]{1,0:T(8,128)(2,1)S(1)}, bf16[512,384]{1,0:T(8,128)(2,1)}, u32[]{:S(2)}, u32[]{:S(2)}) collective-permute-start(bf16[512,384]{1,0:T(8,128)(2,1)S(1)} %fusion.7), channel_id=1, source_target_pairs={{4,0},{8,4},{12,8},{16,12},{20,16},{24,20},{28,24},{5,1},{9,5},{13... | collective-permute-start | bytes 1179656 | tf_op jit(solution)/shard_map/ppermute | solution.py:18
  18.5 1.6 gather_fusion.1
  20.7 1.5 gather_fusion.2
  22.9 1.5 gather_fusion
  26.2 2.5 %gather_fusion.4 = s32[320]{0:T(512)S(1)} fusion(s32[16,20]{1,0:T(8,128)S(1)} %concatenate.57, s32[320]{0:T(512)S(1)} %reshape.172), kind=kCustom, calls=%fused_computation.clone | custom fusion | bytes 5120 | tf_op jit(solution)/shard_map/jit(take_along_axis)/gather | solution.py:209
  28.9 2.5 %gather_fusion.5 = s32[320]{0:T(512)S(1)} fusion(s32[16,20]{1,0:T(8,128)S(1)} %pad_add_fusion.1, s32[320]{0:T(512)S(1)} %reshape.172), kind=kCustom, calls=%fused_computation.1.clone | custom fusion | bytes 5120 | tf_op jit(solution)/shard_map/jit(take_along_axis)/gather | solution.py:208
  33.1 1.9 collective-permute-start.6
  35.0 3.4 %collective-permute-done.1 = bf16[512,768]{1,0:T(8,128)(2,1)} collective-permute-done((bf16[512,768]{1,0:T(8,128)(2,1)}, bf16[512,768]{1,0:T(8,128)(2,1)}, u32[]{:S(2)}, u32[]{:S(2)}) %collective-permute-start.1) | collective-permute-done | bytes 786464 | tf_op jit(solution)/shard_map/ppermute | solution.py:148
  38.5 3.3 %fusion.4 = bf16[1024,384]{1,0:T(8,128)(2,1)} fusion(bf16[512,768]{1,0:T(8,128)(2,1)} %collective-permute-done.1, bf16[512,768]{1,0:T(8,128)(2,1)} %collective-permute-done, bf16[768,192]{1,0:T(8,128)(2,1)S(1)} %copy-done.10, bf16[768,192]{1,0:T(8,128)(2,1)S(1)} %copy-done.13), kind=kOutput, calls=%fused_computation.12 | convolution fusion | flops 608698368 | bytes 2949120 | tf_op jit(solution)/shard_map/dot_general | solution.py:119
  45.8 1.2 constant_dynamic-update-slice_fusion.8
  49.3 3.4 %collective-permute-start.7 = (bf16[1024,384]{1,0:T(8,128)(2,1)}, bf16[1024,384]{1,0:T(8,128)(2,1)S(1)}, u32[]{:S(2)}, u32[]{:S(2)}) collective-permute-start(bf16[1024,384]{1,0:T(8,128)(2,1)} %fusion.4), channel_id=1, source_target_pairs={{0,8},{4,12},{8,16},{12,20},{16,24},{20,28},{1,9},{5,13},{9,17},{1... | collective-permute-start | bytes 2359304 | tf_op jit(solution)/shard_map/ppermute | solution.py:18
  53.8 1.9 collective-permute-start.8
  55.7 3.6 %collective-permute-start.9 = (bf16[1024,384]{1,0:T(8,128)(2,1)}, bf16[1024,384]{1,0:T(8,128)(2,1)S(1)}, u32[]{:S(2)}, u32[]{:S(2)}) collective-permute-start(bf16[1024,384]{1,0:T(8,128)(2,1)} %fusion.4), channel_id=1, source_target_pairs={{4,0},{8,4},{12,8},{16,12},{20,16},{24,20},{28,24},{5,1},{9,5},{13... | collective-permute-start | bytes 2359304 | tf_op jit(solution)/shard_map/ppermute | solution.py:18
  59.4 1.9 collective-permute-start.10
  61.3 1.2 constant_dynamic-update-slice_fusion.2
  62.5 15.6 %collective-permute-done.2 = bf16[512,768]{1,0:T(8,128)(2,1)} collective-permute-done((bf16[512,768]{1,0:T(8,128)(2,1)S(1)}, bf16[512,768]{1,0:T(8,128)(2,1)}, u32[]{:S(2)}, u32[]{:S(2)}) %collective-permute-start.2) | collective-permute-done | bytes 786464 | tf_op jit(solution)/shard_map/ppermute | solution.py:148
  78.1 2.5 %convolution_convert_fusion.3 = bf16[512,384]{1,0:T(8,128)(2,1)} fusion(bf16[512,768]{1,0:T(8,128)(2,1)} %collective-permute-done.2, bf16[768,192]{1,0:T(8,128)(2,1)S(1)} %copy-done.11, bf16[768,192]{1,0:T(8,128)(2,1)S(1)} %copy-done.14), kind=kOutput, calls=%fused_computation.14 | convolution fusion | flops 303366144 | bytes 1769472 | tf_op jit(solution)/shard_map/dot_general | solution.py:119
  80.6 3.4 %collective-permute-start.11 = (bf16[512,384]{1,0:T(8,128)(2,1)}, bf16[512,384]{1,0:T(8,128)(2,1)}, u32[]{:S(2)}, u32[]{:S(2)}) collective-permute-start(bf16[512,384]{1,0:T(8,128)(2,1)} %convolution_convert_fusion.3), channel_id=1, source_target_pairs={{0,8},{4,12},{8,16},{12,20},{16,24},{20,28},{1,9},{5,13},{9,17},{1... | collective-permute-start | bytes 1179656 | tf_op jit(solution)/shard_map/ppermute | solution.py:18
  84.0 1.2 constant_dynamic-update-slice_fusion.1
  85.2 1.2 constant_dynamic-update-slice_fusion
  86.8 1.9 collective-permute-start.12
  89.7 1.6 collective-permute-start.15
  92.3 2.4 %convolution_convert_fusion = bf16[2048,192]{0,1:T(8,128)(2,1)S(1)} fusion(bf16[2048,768]{1,0:T(8,128)(2,1)S(1)} %constant_dynamic-update-slice_fusion, bf16[768,1,768]{2,0,1:T(8,128)(2,1)} %get-tuple-element.21, s32[]{:T(128)S(6)} %select_n.140), kind=kOutput, calls=%fused_computation.6 | convolution fusion | flops 604372992 | bytes 4325380 | tf_op jit(solution)/shard_map/dot_general | solution.py:166
  95.7 2.2 collective-permute-done.15
  97.8 1.9 collective-permute-start.13
  100.5 23.8 %collective-permute-start.16 = (bf16[2,128,384]{2,1,0:T(8,128)(2,1)}, bf16[2,128,384]{2,1,0:T(8,128)(2,1)S(1)}, u32[]{:S(2)}, u32[]{:S(2)}) collective-permute-start(bf16[2,128,384]{2,1,0:T(8,128)(2,1)} %pad_maximum_fusion.3), channel_id=1, source_target_pairs={{0,8},{4,12},{8,16},{12,20},{16,24},{20,28},{24,0},{28,4},{1,9},{5... | collective-permute-start | bytes 589832 | tf_op jit(solution)/shard_map/ppermute | solution.py:28
  126.1 2.2 %copy.49 = bf16[1536,192]{1,0:T(8,128)(2,1)} copy(bf16[1536,192]{0,1:T(8,128)(2,1)} %slice.84) | data formatting | bytes 1179648 | tf_op jit(solution)/shard_map/slice | solution.py:213
  128.3 2.1 collective-permute-start.14
  130.4 2.1 constant_dynamic-update-slice_fusion.9.refs_1_
  132.6 1.8 collective-permute-start.17
  134.4 1.8 constant_dynamic-update-slice_fusion.18
  136.2 1.8 constant_dynamic-update-slice_fusion.17
  138.0 1.8 constant_dynamic-update-slice_fusion.16
  139.7 1.8 constant_dynamic-update-slice_fusion.15
  141.5 1.1 collective-permute-done.14
  143.5 7.5 %collective-permute-done.17 = bf16[4,128,384]{2,1,0:T(8,128)(2,1)S(1)} collective-permute-done((bf16[4,128,384]{2,1,0:T(8,128)(2,1)S(1)}, bf16[4,128,384]{2,1,0:T(8,128)(2,1)S(1)}, u32[]{:S(2)}, u32[]{:S(2)}) %collective-permute-start.17) | collective-permute-done | bytes 393248 | tf_op jit(solution)/shard_map/ppermute | solution.py:28
  152.0 36.6 %shard_map.92 = bf16[12,128,192]{2,1,0:T(8,128)(2,1)} custom-call(s32[12]{0:T(128)} %slice.59.count, s32[12,20]{1,0:T(8,128)} %slice.82.source, s32[12,20]{1,0:T(8,128)} %slice.83.rows, bf16[12,128,192]{2,1,0:T(8,128)(2,1)} %bitcast.37, bf16[2560,384]{1,0:T(8,128)(2,1)} %copy-done.5, bf16[5120,384]{1,0:T(8,128)(2,1)} %constant_dynamic-update-slice_fusion.9.refs_1_, ...), custom_call_target="tpu_custom_call" | custom-call | flops 3019898880 | bytes 9830400 | tf_op jit(solution)/shard_map/pallas_call | solution.py:95
  188.6 2.0 fusion.40
  190.5 4.3 %collective-permute-start.18 = (bf16[512,192]{1,0:T(8,128)(2,1)}, bf16[512,192]{1,0:T(8,128)(2,1)}, u32[]{:S(2)}, u32[]{:S(2)}) collective-permute-start(bf16[512,192]{1,0:T(8,128)(2,1)} %bitcast.11), channel_id=1, source_target_pairs={{0,1},{1,2},{2,3},{3,0},{4,5},{5,6},{6,7},{7,4},{8,9},{9,10},{10,1... | collective-permute-start | bytes 589832 | tf_op jit(solution)/shard_map/ppermute | solution.py:219
  195.9 1.8 collective-permute-start.20
  197.7 1.3 bitcast_select_fusion
  201.1 16.6 %shard_map.91 = bf16[4,128,192]{2,1,0:T(8,128)(2,1)} custom-call(s32[4]{0:T(128)} %bitcast.40, s32[4,20]{1,0:T(4,128)} %slice.79.source, s32[4,20]{1,0:T(4,128)} %slice.80.rows, bf16[4,128,192]{2,1,0:T(8,128)(2,1)} %bitcast.36, bf16[2560,384]{1,0:T(8,128)(2,1)} %copy-done.5, bf16[5120,384]{1,0:T(8,128)(2,1)} %constant_dynamic-update-slice_fusion.9.refs_1_, ...), custom_call_target="tpu_custom_call" | custom-call | flops 1006632960 | bytes 9043968 | tf_op jit(solution)/shard_map/pallas_call | solution.py:95
  217.7 2.9 %convolution_convert_fusion.1 = bf16[512,768]{1,0:T(8,128)(2,1)} fusion(bf16[768,768]{1,0:T(8,128)(2,1)S(1)} %copy-done.6, bf16[512,192]{1,0:T(8,128)(2,1)} %collective-permute-done.20, bf16[512,192]{1,0:T(8,128)(2,1)} %collective-permute-done.19, bf16[512,192]{1,0:T(8,128)(2,1)} %collective-permute-done.18, bf16[512,192]{1,0:T(8,128)(2,1)} %bitcast.38), kind=kOutput, calls=%fused_computation.11 | convolution fusion | flops 607518720 | bytes 2752512 | tf_op jit(solution)/shard_map/dot_general | solution.py:225
  (120 shorter events, 23.5 us)
Async XLA Ops:
  0.0 45.0 %copy-start = (bf16[768,768]{1,0:T(8,128)(2,1)S(1)}, bf16[768,768]{1,0:T(8,128)(2,1)}, u32[]{:S(2)}) copy-start(bf16[768,768]{1,0:T(8,128)(2,1)} %param.13) | copy-start | bytes 3538948
  0.0 33.1 %collective-permute-start = (bf16[512,768]{1,0:T(8,128)(2,1)}, bf16[512,768]{1,0:T(8,128)(2,1)}, u32[]{:S(2)}, u32[]{:S(2)}) collective-permute-start(bf16[512,768]{1,0:T(8,128)(2,1)} %param.11), channel_id=1, source_target_pairs={{0,3},{1,0},{2,1},{3,2},{4,7},{5,4},{6,5},{7,6},{8,11},{9,8},{10,9... | collective-permute-start | bytes 2359304 | tf_op jit(solution)/shard_map/ppermute | solution.py:148
  3.6 34.9 %collective-permute-start.1 = (bf16[512,768]{1,0:T(8,128)(2,1)}, bf16[512,768]{1,0:T(8,128)(2,1)}, u32[]{:S(2)}, u32[]{:S(2)}) collective-permute-start(bf16[512,768]{1,0:T(8,128)(2,1)} %param.11), channel_id=1, source_target_pairs={{0,1},{1,2},{2,3},{3,0},{4,5},{5,6},{6,7},{7,4},{8,9},{9,10},{10,1... | collective-permute-start | bytes 2359304 | tf_op jit(solution)/shard_map/ppermute | solution.py:148
  6.9 11.5 %copy-start.15 = (s32[16,12]{1,0:T(8,128)S(1)}, s32[16,12]{1,0:T(8,128)}, u32[]{:S(2)}) copy-start(s32[16,12]{1,0:T(8,128)} %param.14) | copy-start | bytes 2308
  6.9 11.6 %copy-start.3 = (s32[4]{0:T(128)S(1)}, s32[4]{0:T(128)}, u32[]{:S(2)}) copy-start(s32[4]{0:T(128)} %constant.195.clone) | copy-start | bytes 52
  7.2 5.5 %copy-start.9 = (bf16[768,192]{1,0:T(8,128)(2,1)}, bf16[768,192]{1,0:T(8,128)(2,1)S(1)}, u32[]{:S(2)}) copy-start(bf16[768,192]{1,0:T(8,128)(2,1)S(1)} %get-tuple-element.27) | copy-start | bytes 884740
  7.2 7.4 %copy-start.12 = (bf16[768,192]{1,0:T(8,128)(2,1)}, bf16[768,192]{1,0:T(8,128)(2,1)S(1)}, u32[]{:S(2)}) copy-start(bf16[768,192]{1,0:T(8,128)(2,1)S(1)} %get-tuple-element.28) | copy-start | bytes 884740
  9.3 36.5 %collective-permute-start.3 = (bf16[512,384]{1,0:T(8,128)(2,1)S(1)}, bf16[512,384]{1,0:T(8,128)(2,1)}, u32[]{:S(2)}, u32[]{:S(2)}) collective-permute-start(bf16[512,384]{1,0:T(8,128)(2,1)S(1)} %fusion.7), channel_id=1, source_target_pairs={{0,8},{4,12},{8,16},{12,20},{16,24},{20,28},{1,9},{5,13},{9,17},{1... | collective-permute-start | bytes 1179656 | tf_op jit(solution)/shard_map/ppermute | solution.py:18
  12.7 34.3 %collective-permute-start.4 = (bf16[512,384]{1,0:T(8,128)(2,1)S(1)}, bf16[512,384]{1,0:T(8,128)(2,1)}, u32[]{:S(2)}, u32[]{:S(2)}) collective-permute-start(bf16[512,384]{1,0:T(8,128)(2,1)S(1)} %fusion.7), channel_id=1, source_target_pairs={{0,4},{4,8},{8,12},{12,16},{16,20},{20,24},{24,28},{1,5},{5,9},{9,... | collective-permute-start | bytes 1179656 | tf_op jit(solution)/shard_map/ppermute | solution.py:18
  14.6 33.5 %collective-permute-start.5 = (bf16[512,384]{1,0:T(8,128)(2,1)S(1)}, bf16[512,384]{1,0:T(8,128)(2,1)}, u32[]{:S(2)}, u32[]{:S(2)}) collective-permute-start(bf16[512,384]{1,0:T(8,128)(2,1)S(1)} %fusion.7), channel_id=1, source_target_pairs={{4,0},{8,4},{12,8},{16,12},{20,16},{24,20},{28,24},{5,1},{9,5},{13... | collective-permute-start | bytes 1179656 | tf_op jit(solution)/shard_map/ppermute | solution.py:18
  20.1 0.7 copy-start.2
  22.3 0.7 copy-start.1
  22.9 1.7 copy-start.17
  22.9 1.9 copy-start.19
  28.9 2.6 %copy-start.7 = (bf16[512,768]{1,0:T(8,128)(2,1)S(1)}, bf16[512,768]{1,0:T(8,128)(2,1)}, u32[]{:S(2)}) copy-start(bf16[512,768]{1,0:T(8,128)(2,1)} %param.11) | copy-start | bytes 2359300
  28.9 9.6 %copy-start.10 = (bf16[768,192]{1,0:T(8,128)(2,1)S(1)}, bf16[768,192]{1,0:T(8,128)(2,1)}, u32[]{:S(2)}) copy-start(bf16[768,192]{1,0:T(8,128)(2,1)} %copy-done.9) | copy-start | bytes 884740
  28.9 9.6 %copy-start.13 = (bf16[768,192]{1,0:T(8,128)(2,1)S(1)}, bf16[768,192]{1,0:T(8,128)(2,1)}, u32[]{:S(2)}) copy-start(bf16[768,192]{1,0:T(8,128)(2,1)} %copy-done.12) | copy-start | bytes 884740
  33.1 19.6 %collective-permute-start.6 = (bf16[512,384]{1,0:T(8,128)(2,1)S(1)}, bf16[512,384]{1,0:T(8,128)(2,1)}, u32[]{:S(2)}, u32[]{:S(2)}) collective-permute-start(bf16[512,384]{1,0:T(8,128)(2,1)S(1)} %fusion.7), channel_id=1, source_target_pairs={{8,0},{12,4},{16,8},{20,12},{24,16},{28,20},{9,1},{13,5},{17,9},{2... | collective-permute-start | bytes 1179656 | tf_op jit(solution)/shard_map/ppermute | solution.py:18
  41.8 36.3 %collective-permute-start.2 = (bf16[512,768]{1,0:T(8,128)(2,1)S(1)}, bf16[512,768]{1,0:T(8,128)(2,1)}, u32[]{:S(2)}, u32[]{:S(2)}) collective-permute-start(bf16[512,768]{1,0:T(8,128)(2,1)S(1)} %copy-done.7), channel_id=1, source_target_pairs={{0,2},{1,3},{2,0},{3,1},{4,6},{5,7},{6,4},{7,5},{8,10},{9,11},{10,... | collective-permute-start | bytes 2359304 | tf_op jit(solution)/shard_map/ppermute | solution.py:148
  43.8 1.2 copy-start.18
  45.8 15.5 %copy-start.4 = (bf16[2048,768]{1,0:T(8,128)(2,1)S(1)}, bf16[2048,768]{1,0:T(8,128)(2,1)}, u32[]{:S(2)}) copy-start(bf16[2048,768]{1,0:T(8,128)(2,1)} %constant_dynamic-update-slice_fusion.3) | copy-start | bytes 9437188
  48.1 30.0 %copy-start.11 = (bf16[768,192]{1,0:T(8,128)(2,1)S(1)}, bf16[768,192]{1,0:T(8,128)(2,1)}, u32[]{:S(2)}) copy-start(bf16[768,192]{1,0:T(8,128)(2,1)} %copy-done.9) | copy-start | bytes 884740
  48.1 30.0 %copy-start.14 = (bf16[768,192]{1,0:T(8,128)(2,1)S(1)}, bf16[768,192]{1,0:T(8,128)(2,1)}, u32[]{:S(2)}) copy-start(bf16[768,192]{1,0:T(8,128)(2,1)} %copy-done.12) | copy-start | bytes 884740
  49.3 37.5 %collective-permute-start.7 = (bf16[1024,384]{1,0:T(8,128)(2,1)}, bf16[1024,384]{1,0:T(8,128)(2,1)S(1)}, u32[]{:S(2)}, u32[]{:S(2)}) collective-permute-start(bf16[1024,384]{1,0:T(8,128)(2,1)} %fusion.4), channel_id=1, source_target_pairs={{0,8},{4,12},{8,16},{12,20},{16,24},{20,28},{1,9},{5,13},{9,17},{1... | collective-permute-start | bytes 2359304 | tf_op jit(solution)/shard_map/ppermute | solution.py:18
  53.8 5.6 %copy-start.5 = (bf16[2560,384]{1,0:T(8,128)(2,1)}, bf16[2560,384]{1,0:T(8,128)(2,1)S(1)}, u32[]{:S(2)}) copy-start(bf16[2560,384]{1,0:T(8,128)(2,1)S(1)} %constant_dynamic-update-slice_fusion.4.refs_0_) | copy-start | bytes 5898244
  53.8 35.9 %collective-permute-start.8 = (bf16[1024,384]{1,0:T(8,128)(2,1)}, bf16[1024,384]{1,0:T(8,128)(2,1)S(1)}, u32[]{:S(2)}, u32[]{:S(2)}) collective-permute-start(bf16[1024,384]{1,0:T(8,128)(2,1)} %fusion.4), channel_id=1, source_target_pairs={{0,4},{4,8},{8,12},{12,16},{16,20},{20,24},{24,28},{1,5},{5,9},{9,... | collective-permute-start | bytes 2359304 | tf_op jit(solution)/shard_map/ppermute | solution.py:18
  55.7 44.8 %collective-permute-start.9 = (bf16[1024,384]{1,0:T(8,128)(2,1)}, bf16[1024,384]{1,0:T(8,128)(2,1)S(1)}, u32[]{:S(2)}, u32[]{:S(2)}) collective-permute-start(bf16[1024,384]{1,0:T(8,128)(2,1)} %fusion.4), channel_id=1, source_target_pairs={{4,0},{8,4},{12,8},{16,12},{20,16},{24,20},{28,24},{5,1},{9,5},{13... | collective-permute-start | bytes 2359304 | tf_op jit(solution)/shard_map/ppermute | solution.py:18
  59.4 69.0 %collective-permute-start.10 = (bf16[1024,384]{1,0:T(8,128)(2,1)}, bf16[1024,384]{1,0:T(8,128)(2,1)}, u32[]{:S(2)}, u32[]{:S(2)}) collective-permute-start(bf16[1024,384]{1,0:T(8,128)(2,1)} %fusion.4), channel_id=1, source_target_pairs={{8,0},{12,4},{16,8},{20,12},{24,16},{28,20},{9,1},{13,5},{17,9},{2... | collective-permute-start | bytes 2359304 | tf_op jit(solution)/shard_map/ppermute | solution.py:18
  80.6 53.7 %collective-permute-start.11 = (bf16[512,384]{1,0:T(8,128)(2,1)}, bf16[512,384]{1,0:T(8,128)(2,1)}, u32[]{:S(2)}, u32[]{:S(2)}) collective-permute-start(bf16[512,384]{1,0:T(8,128)(2,1)} %convolution_convert_fusion.3), channel_id=1, source_target_pairs={{0,8},{4,12},{8,16},{12,20},{16,24},{20,28},{1,9},{5,13},{9,17},{1... | collective-permute-start | bytes 1179656 | tf_op jit(solution)/shard_map/ppermute | solution.py:18
  86.8 49.4 %collective-permute-start.12 = (bf16[512,384]{1,0:T(8,128)(2,1)}, bf16[512,384]{1,0:T(8,128)(2,1)}, u32[]{:S(2)}, u32[]{:S(2)}) collective-permute-start(bf16[512,384]{1,0:T(8,128)(2,1)} %convolution_convert_fusion.3), channel_id=1, source_target_pairs={{0,4},{4,8},{8,12},{12,16},{16,20},{20,24},{24,28},{1,5},{5,9},{9,... | collective-permute-start | bytes 1179656 | tf_op jit(solution)/shard_map/ppermute | solution.py:18
  89.7 8.2 %collective-permute-start.15 = (bf16[1,128,384]{2,1,0:T(8,128)(2,1)S(1)}, bf16[1,128,384]{2,1,0:T(8,128)(2,1)S(1)}, u32[]{:S(2)}, u32[]{:S(2)}) collective-permute-start(bf16[1,128,384]{2,1,0:T(8,128)(2,1)S(1)} %fusion.8), channel_id=1, source_target_pairs={{0,4},{4,8},{8,12},{12,16},{16,20},{20,24},{24,28},{28,0},{1,5},{5... | collective-permute-start | bytes 294920 | tf_op jit(solution)/shard_map/ppermute | solution.py:28
  92.3 2.4 %copy-start.8 = (bf16[1024,384]{1,0:T(8,128)(2,1)S(1)}, bf16[1024,384]{1,0:T(8,128)(2,1)}, u32[]{:S(2)}) copy-start(bf16[1024,384]{1,0:T(8,128)(2,1)} %fusion.4) | copy-start | bytes 2359300
  97.8 41.9 %collective-permute-start.13 = (bf16[512,384]{1,0:T(8,128)(2,1)}, bf16[512,384]{1,0:T(8,128)(2,1)}, u32[]{:S(2)}, u32[]{:S(2)}) collective-permute-start(bf16[512,384]{1,0:T(8,128)(2,1)} %convolution_convert_fusion.3), channel_id=1, source_target_pairs={{4,0},{8,4},{12,8},{16,12},{20,16},{24,20},{28,24},{5,1},{9,5},{13... | collective-permute-start | bytes 1179656 | tf_op jit(solution)/shard_map/ppermute | solution.py:18
  100.5 32.1 %collective-permute-start.16 = (bf16[2,128,384]{2,1,0:T(8,128)(2,1)}, bf16[2,128,384]{2,1,0:T(8,128)(2,1)S(1)}, u32[]{:S(2)}, u32[]{:S(2)}) collective-permute-start(bf16[2,128,384]{2,1,0:T(8,128)(2,1)} %pad_maximum_fusion.3), channel_id=1, source_target_pairs={{0,8},{4,12},{8,16},{12,20},{16,24},{20,28},{24,0},{28,4},{1,9},{5... | collective-permute-start | bytes 589832 | tf_op jit(solution)/shard_map/ppermute | solution.py:28
  128.3 14.3 %collective-permute-start.14 = (bf16[512,384]{1,0:T(8,128)(2,1)}, bf16[512,384]{1,0:T(8,128)(2,1)S(1)}, u32[]{:S(2)}, u32[]{:S(2)}) collective-permute-start(bf16[512,384]{1,0:T(8,128)(2,1)} %convolution_convert_fusion.3), channel_id=1, source_target_pairs={{8,0},{12,4},{16,8},{20,12},{24,16},{28,20},{9,1},{13,5},{17,9},{2... | collective-permute-start | bytes 1179656 | tf_op jit(solution)/shard_map/ppermute | solution.py:18
  132.6 18.4 %collective-permute-start.17 = (bf16[4,128,384]{2,1,0:T(8,128)(2,1)S(1)}, bf16[4,128,384]{2,1,0:T(8,128)(2,1)S(1)}, u32[]{:S(2)}, u32[]{:S(2)}) collective-permute-start(bf16[4,128,384]{2,1,0:T(8,128)(2,1)S(1)} %pad_maximum_fusion.2), channel_id=1, source_target_pairs={{0,16},{4,20},{8,24},{12,28},{16,0},{20,4},{24,8},{28,12},{1,17},{... | collective-permute-start | bytes 1179656 | tf_op jit(solution)/shard_map/ppermute | solution.py:28
  152.0 45.7 %copy-start.16 = (pred[768]{0:T(1024)(128)(4,1)S(1)}, pred[768]{0:T(1024)(128)(4,1)}, u32[]{:S(2)}) copy-start(pred[768]{0:T(1024)(128)(4,1)} %broadcast_in_dim.36) | copy-start | bytes 2308
  190.5 27.1 %collective-permute-start.18 = (bf16[512,192]{1,0:T(8,128)(2,1)}, bf16[512,192]{1,0:T(8,128)(2,1)}, u32[]{:S(2)}, u32[]{:S(2)}) collective-permute-start(bf16[512,192]{1,0:T(8,128)(2,1)} %bitcast.11), channel_id=1, source_target_pairs={{0,1},{1,2},{2,3},{3,0},{4,5},{5,6},{6,7},{7,4},{8,9},{9,10},{10,1... | collective-permute-start | bytes 589832 | tf_op jit(solution)/shard_map/ppermute | solution.py:219
  194.8 22.8 %collective-permute-start.19 = (bf16[512,192]{1,0:T(8,128)(2,1)}, bf16[512,192]{1,0:T(8,128)(2,1)}, u32[]{:S(2)}, u32[]{:S(2)}) collective-permute-start(bf16[512,192]{1,0:T(8,128)(2,1)} %bitcast.12), channel_id=1, source_target_pairs={{0,2},{1,3},{2,0},{3,1},{4,6},{5,7},{6,4},{7,5},{8,10},{9,11},{10,... | collective-permute-start | bytes 589832 | tf_op jit(solution)/shard_map/ppermute | solution.py:219
  195.9 21.8 %collective-permute-start.20 = (bf16[512,192]{1,0:T(8,128)(2,1)S(1)}, bf16[512,192]{1,0:T(8,128)(2,1)}, u32[]{:S(2)}, u32[]{:S(2)}) collective-permute-start(bf16[512,192]{1,0:T(8,128)(2,1)S(1)} %bitcast.39), channel_id=1, source_target_pairs={{0,3},{1,0},{2,1},{3,2},{4,7},{5,4},{6,5},{7,6},{8,11},{9,8},{10,9... | collective-permute-start | bytes 589832 | tf_op jit(solution)/shard_map/ppermute | solution.py:219
  201.1 16.6 %copy-start.6 = (bf16[768,768]{1,0:T(8,128)(2,1)S(1)}, bf16[768,768]{1,0:T(8,128)(2,1)}, u32[]{:S(2)}) copy-start(bf16[768,768]{1,0:T(8,128)(2,1)} %bitcast_select_fusion) | copy-start | bytes 3538948

commit v13 on v12

--- a/solution.py
+++ b/solution.py
@@ -169,8 +169,16 @@
 
     seq_count = lax.axis_size("seq")
     seq_rank = lax.axis_index("seq")
-    first_at = ((head_count - head_rank) % head_count) * own_rows
-    first_rows = lax.dynamic_slice_in_dim(rolled_tokens, first_at, BLK, 0)
+    late = [k for members in groups[1:] for k in members]
+    first_hop = (-head_rank) % head_count
+    first_rows = tokens[:BLK]
+    if late:
+        early_first = lax.ppermute(tokens[:BLK], "head",
+                                   [(0, (-k) % head_count) for k in late])
+        for k in late:
+            first_rows = jnp.where(first_hop == k, early_first, first_rows)
+    for k in groups[0]:
+        first_rows = jnp.where(first_hop == k, received[k][:BLK], first_rows)
     kvanc = gather_all(project_kv(first_rows, kv_w), "seq")
     held_count = kvanc.shape[0]
     kvanc = kvanc.reshape(held_count * BLK, 2 * width_here)

time: 222 us -> 221 us (level); the launches traced: 221 us -> 217 us
  starting transfers between devices: 69.7 us -> 77.7 us
  local copies, waits for them, and re-layouts: 48.7 us -> 44.8 us
  waiting for transfers between devices: 29.9 us -> 27.2 us
  other arithmetic: 5 us -> 2.67 us
    ppermute x12, starting transfers between devices: 31.1 us -> 53.5 us  [shifted(): return lax.ppermute(x, axis, pairs)]
    ppermute x3, waiting for transfers between devices: 19 us -> 0.01 us  [fetch_chunk(): return lax.ppermute(source, 'head', pairs)]
    ppermute x3, starting transfers between devices: 27.1 us -> 10.4 us  [gather_all(): got = lax.ppermute(held, axis, pairs)]
    ppermute x12, waiting for transfers between devices: 1.17 us -> 16.6 us  [shifted(): return lax.ppermute(x, axis, pairs)]
    ppermute x0 -> x1, waiting for transfers between devices: none -> 8.66 us  [shards(): lax.ppermute(tokens[:BLK], 'head', [(0, -k % head_count) for k in late])]
    ppermute x3, waiting for transfers between devices: 9.67 us -> 1.96 us  [gather_all(): got = lax.ppermute(held, axis, pairs)]
    ppermute x3, starting transfers between devices: 7.15 us -> 3.83 us  [shards(): received[j] = lax.ppermute(away[j - 1], 'head', pairs)]
    unnamed x56 -> x49, local copies, waits for them, and re-layouts: 19.1 us -> 16.1 us
  transfers between devices with their start and end apart: 21 -> 22, of which waited for: 5 -> 6; matrix products, arithmetic and copies ran while one was open for 27% -> 24% of each run, Pallas kernels for 8% -> 7%
where the time goes in v13:
time: 221 us; the launch traced here: 217 us
  starting transfers between devices  77.7 us (35%)
  Pallas kernels  51.8 us (23%)
  local copies, waits for them, and re-layouts  44.8 us (20%)
  waiting for transfers between devices  27.2 us (12%)
  matrix products  12.5 us (6%)
  other arithmetic  2.67 us (1%)
    ppermute x12, starting transfers between devices, shifted(): return lax.ppermute(x, axis, pairs)  53.5 us
    pallas_call x2, Pallas kernels, attention(): pl.pallas_call(kernel, out_shape=jax.ShapeDtypeStruct(queries.shape, jnp....  51.8 us
    ppermute x12, waiting for transfers between devices, shifted(): return lax.ppermute(x, axis, pairs)  16.6 us
    unnamed x49, local copies, waits for them, and re-layouts  16.1 us
    ppermute x3, starting transfers between devices, gather_all(): got = lax.ppermute(held, axis, pairs)  10.4 us
    ppermute x1, waiting for transfers between devices, shards(): lax.ppermute(tokens[:BLK], 'head', [(0, -k % head_count) for k in late])  8.66 us
    ppermute x3, starting transfers between devices, fetch_chunk(): return lax.ppermute(source, 'head', pairs)  7.05 us
    dot_general x4, matrix products, project_kv(): jnp.dot(x, kv_w, preferred_element_type=jnp.float32).astype(jnp.bfloat16)  6.82 us
  transfers between devices with their start and end apart: 22, of which 6 were waited for; matrix products, arithmetic and copies ran while one was open for 24% of the time, Pallas kernels for 7%

profile of v13, /device:TPU:2, one launch (start us, length us, event | category | flops | bytes accessed | tf_op | source)
XLA Modules:
  0.0 217.3 jit_solution(12454864359107605539)
XLA Ops:
  0.0 3.6 %collective-permute-start = (bf16[512,768]{1,0:T(8,128)(2,1)}, bf16[512,768]{1,0:T(8,128)(2,1)}, u32[]{:S(2)}, u32[]{:S(2)}) collective-permute-start(bf16[512,768]{1,0:T(8,128)(2,1)} %param.11), channel_id=1, source_target_pairs={{0,3},{1,0},{2,1},{3,2},{4,7},{5,4},{6,5},{7,6},{8,11},{9,8},{10,9... | collective-permute-start | bytes 2359304 | tf_op jit(solution)/shard_map/ppermute | solution.py:148
  3.6 3.3 %fusion.57 = (bf16[768,1,768]{2,0,1:T(8,128)(2,1)}, bf16[768,1,768]{2,0,1:T(8,128)(2,1)S(1)}, bf16[768,1,768]{2,0,1:T(8,128)(2,1)S(1)}) fusion(bf16[768,3,768]{2,0,1:T(8,128)(2,1)} %param.12), kind=kLoop, calls=%fused_computation.141 | loop fusion | bytes 7077888 | tf_op jit(solution)/shard_map/slice | solution.py:139
  7.2 2.1 fusion.18
  9.3 3.4 %collective-permute-start.3 = (bf16[512,384]{1,0:T(8,128)(2,1)S(1)}, bf16[512,384]{1,0:T(8,128)(2,1)}, u32[]{:S(2)}, u32[]{:S(2)}) collective-permute-start(bf16[512,384]{1,0:T(8,128)(2,1)S(1)} %fusion.18), channel_id=1, source_target_pairs={{0,8},{4,12},{8,16},{12,20},{16,24},{20,28},{1,9},{5,13},{9,17},{1... | collective-permute-start | bytes 1179656 | tf_op jit(solution)/shard_map/ppermute | solution.py:18
  12.7 1.9 collective-permute-start.4
  15.6 2.9 %collective-permute-start.15 = (bf16[128,768]{1,0:T(8,128)(2,1)S(1)}, bf16[128,768]{1,0:T(8,128)(2,1)S(1)}, u32[]{:S(2)}, u32[]{:S(2)}) collective-permute-start(bf16[128,768]{1,0:T(8,128)(2,1)S(1)} %slice.71), channel_id=1, source_target_pairs={{0,2},{4,6},{8,10},{12,14},{16,18},{20,22},{24,26},{28,30}} | collective-permute-start | bytes 589832 | tf_op jit(solution)/shard_map/ppermute | solution.py:176
  18.8 1.6 gather_fusion.1
  21.0 1.5 gather_fusion.2
  24.2 1.6 gather_fusion
  25.9 2.5 %gather_fusion.5 = s32[320]{0:T(512)S(1)} fusion(s32[16,20]{1,0:T(8,128)S(1)} %pad_add_fusion.1, s32[320]{0:T(512)S(1)} %reshape.172), kind=kCustom, calls=%fused_computation.1.clone | custom fusion | bytes 5120 | tf_op jit(solution)/shard_map/jit(take_along_axis)/gather | solution.py:216
  28.6 2.5 %gather_fusion.4 = s32[320]{0:T(512)S(1)} fusion(s32[16,20]{1,0:T(8,128)S(1)} %concatenate.57, s32[320]{0:T(512)S(1)} %reshape.172), kind=kCustom, calls=%fused_computation.clone | custom fusion | bytes 5120 | tf_op jit(solution)/shard_map/jit(take_along_axis)/gather | solution.py:217
  33.1 8.7 %collective-permute-done.15 = bf16[128,768]{1,0:T(8,128)(2,1)S(1)} collective-permute-done((bf16[128,768]{1,0:T(8,128)(2,1)S(1)}, bf16[128,768]{1,0:T(8,128)(2,1)S(1)}, u32[]{:S(2)}, u32[]{:S(2)}) %collective-permute-start.15) | collective-permute-done | bytes 196640 | tf_op jit(solution)/shard_map/ppermute | solution.py:176
  41.7 1.9 collective-permute-start.5
  43.7 1.9 collective-permute-start.6
  45.6 1.5 fusion.19
  49.2 2.0 collective-permute-done.16
  51.3 9.5 %collective-permute-start.17 = (bf16[2,128,384]{2,1,0:T(8,128)(2,1)S(1)}, bf16[2,128,384]{2,1,0:T(8,128)(2,1)S(1)}, u32[]{:S(2)}, u32[]{:S(2)}) collective-permute-start(bf16[2,128,384]{2,1,0:T(8,128)(2,1)S(1)} %pad_maximum_fusion.3), channel_id=1, source_target_pairs={{0,8},{4,12},{8,16},{12,20},{16,24},{20,28},{24,0},{28,4},{1,9},{5... | collective-permute-start | bytes 589832 | tf_op jit(solution)/shard_map/ppermute | solution.py:28
  60.8 2.6 %fusion.15 = bf16[1024,384]{1,0:T(8,128)(2,1)S(1)} fusion(bf16[512,768]{1,0:T(8,128)(2,1)} %collective-permute-done.1, bf16[512,768]{1,0:T(8,128)(2,1)} %collective-permute-done, bf16[768,192]{1,0:T(8,128)(2,1)} %copy-done.5, bf16[768,192]{1,0:T(8,128)(2,1)} %copy-done.8), kind=kOutput, calls=%fused_computation.20 | convolution fusion | flops 608698368 | bytes 2949120 | tf_op jit(solution)/shard_map/dot_general | solution.py:119
  63.4 3.4 %collective-permute-start.2 = (bf16[512,768]{1,0:T(8,128)(2,1)S(1)}, bf16[512,768]{1,0:T(8,128)(2,1)S(1)}, u32[]{:S(2)}, u32[]{:S(2)}) collective-permute-start(bf16[512,768]{1,0:T(8,128)(2,1)S(1)} %copy-done.11), channel_id=1, source_target_pairs={{0,2},{1,3},{2,0},{3,1},{4,6},{5,7},{6,4},{7,5},{8,10},{9,11},{10,... | collective-permute-start | bytes 2359304 | tf_op jit(solution)/shard_map/ppermute | solution.py:148
  66.9 1.8 constant_dynamic-update-slice_fusion.4
  68.7 3.4 %collective-permute-start.7 = (bf16[1024,384]{1,0:T(8,128)(2,1)S(1)}, bf16[1024,384]{1,0:T(8,128)(2,1)S(1)}, u32[]{:S(2)}, u32[]{:S(2)}) collective-permute-start(bf16[1024,384]{1,0:T(8,128)(2,1)S(1)} %fusion.15), channel_id=1, source_target_pairs={{0,8},{4,12},{8,16},{12,20},{16,24},{20,28},{1,9},{5,13},{9,17},{1... | collective-permute-start | bytes 2359304 | tf_op jit(solution)/shard_map/ppermute | solution.py:18
  73.0 2.0 collective-permute-start.8
  75.9 1.8 constant_dynamic-update-slice_fusion.1
  77.6 1.8 constant_dynamic-update-slice_fusion.refs_0_
  79.4 3.6 %collective-permute-start.9 = (bf16[1024,384]{1,0:T(8,128)(2,1)S(1)}, bf16[1024,384]{1,0:T(8,128)(2,1)S(1)}, u32[]{:S(2)}, u32[]{:S(2)}) collective-permute-start(bf16[1024,384]{1,0:T(8,128)(2,1)S(1)} %fusion.15), channel_id=1, source_target_pairs={{4,0},{8,4},{12,8},{16,12},{20,16},{24,20},{28,24},{5,1},{9,5},{13... | collective-permute-start | bytes 2359304 | tf_op jit(solution)/shard_map/ppermute | solution.py:18
  83.1 23.8 %collective-permute-start.10 = (bf16[1024,384]{1,0:T(8,128)(2,1)S(1)}, bf16[1024,384]{1,0:T(8,128)(2,1)S(1)}, u32[]{:S(2)}, u32[]{:S(2)}) collective-permute-start(bf16[1024,384]{1,0:T(8,128)(2,1)S(1)} %fusion.15), channel_id=1, source_target_pairs={{8,0},{12,4},{16,8},{20,12},{24,16},{28,20},{9,1},{13,5},{17,9},{2... | collective-permute-start | bytes 2359304 | tf_op jit(solution)/shard_map/ppermute | solution.py:18
  106.9 1.1 pad_maximum_fusion
  108.6 3.8 %collective-permute-start.11 = (bf16[512,384]{1,0:T(8,128)(2,1)S(1)}, bf16[512,384]{1,0:T(8,128)(2,1)}, u32[]{:S(2)}, u32[]{:S(2)}) collective-permute-start(bf16[512,384]{1,0:T(8,128)(2,1)S(1)} %convolution_convert_fusion.2), channel_id=1, source_target_pairs={{0,8},{4,12},{8,16},{12,20},{16,24},{20,28},{1,9},{5,13},{9,17},{1... | collective-permute-start | bytes 1179656 | tf_op jit(solution)/shard_map/ppermute | solution.py:18
  112.5 1.9 collective-permute-start.12
  114.4 1.0 constant_dynamic-update-slice_fusion.9
  115.4 3.6 %collective-permute-start.13 = (bf16[512,384]{1,0:T(8,128)(2,1)S(1)}, bf16[512,384]{1,0:T(8,128)(2,1)}, u32[]{:S(2)}, u32[]{:S(2)}) collective-permute-start(bf16[512,384]{1,0:T(8,128)(2,1)S(1)} %convolution_convert_fusion.2), channel_id=1, source_target_pairs={{4,0},{8,4},{12,8},{16,12},{20,16},{24,20},{28,24},{5,1},{9,5},{13... | collective-permute-start | bytes 1179656 | tf_op jit(solution)/shard_map/ppermute | solution.py:18
  119.0 1.0 constant_dynamic-update-slice_fusion.8
  120.1 2.8 %fusion.8 = bf16[2048,192]{0,1:T(8,128)(2,1)S(1)} fusion(bf16[512,768]{1,0:T(8,128)(2,1)} %collective-permute-done.1, bf16[512,768]{1,0:T(8,128)(2,1)S(1)} %collective-permute-done.2, bf16[512,768]{1,0:T(8,128)(2,1)} %collective-permute-done, bf16[512,768]{1,0:T(8,128)(2,1)S(1)} %copy-done.11, bf16[768,1,768]{2,0,1:T(8,128)(2,1)} %get-tuple-element.21, ...), kind=kOutput, calls=%fused_computation.14 | convolution fusion | flops 616955904 | bytes 4325380 | tf_op jit(solution)/shard_map/dot_general | solution.py:166
  122.9 1.1 constant_dynamic-update-slice_fusion.7
  123.9 2.1 collective-permute-start.14
  128.2 1.2 copy.49
  129.3 3.9 %collective-permute-done.11 = bf16[512,384]{1,0:T(8,128)(2,1)} collective-permute-done((bf16[512,384]{1,0:T(8,128)(2,1)S(1)}, bf16[512,384]{1,0:T(8,128)(2,1)}, u32[]{:S(2)}, u32[]{:S(2)}) %collective-permute-start.11) | collective-permute-done | bytes 393248 | tf_op jit(solution)/shard_map/ppermute | solution.py:18
  133.2 1.8 constant_dynamic-update-slice_fusion.14
  135.0 1.8 constant_dynamic-update-slice_fusion.13
  137.6 4.0 %collective-permute-done.13 = bf16[512,384]{1,0:T(8,128)(2,1)} collective-permute-done((bf16[512,384]{1,0:T(8,128)(2,1)S(1)}, bf16[512,384]{1,0:T(8,128)(2,1)}, u32[]{:S(2)}, u32[]{:S(2)}) %collective-permute-start.13) | collective-permute-done | bytes 393248 | tf_op jit(solution)/shard_map/ppermute | solution.py:18
  141.6 1.8 constant_dynamic-update-slice_fusion.11
  143.4 8.5 %collective-permute-done.14 = bf16[512,384]{1,0:T(8,128)(2,1)} collective-permute-done((bf16[512,384]{1,0:T(8,128)(2,1)S(1)}, bf16[512,384]{1,0:T(8,128)(2,1)}, u32[]{:S(2)}, u32[]{:S(2)}) %collective-permute-start.14) | collective-permute-done | bytes 393248 | tf_op jit(solution)/shard_map/ppermute | solution.py:18
  151.9 1.8 constant_dynamic-update-slice_fusion.10.refs_2_
  153.7 36.1 %shard_map.92 = bf16[12,128,192]{2,1,0:T(8,128)(2,1)} custom-call(s32[12]{0:T(128)} %slice.72.count, s32[12,20]{1,0:T(8,128)} %slice.97.source, s32[12,20]{1,0:T(8,128)} %slice.98.rows, bf16[12,128,192]{2,1,0:T(8,128)(2,1)} %bitcast.36, bf16[2560,384]{1,0:T(8,128)(2,1)} %constant_dynamic-update-slice_fusion.refs_0_, ...), custom_call_target="tpu_custom_call" | custom-call | flops 3019898880 | bytes 9830400 | tf_op jit(solution)/shard_map/pallas_call | solution.py:95
  189.8 2.0 fusion.58
  192.0 3.6 %collective-permute-start.21 = (bf16[512,192]{1,0:T(8,128)(2,1)}, bf16[512,192]{1,0:T(8,128)(2,1)}, u32[]{:S(2)}, u32[]{:S(2)}) collective-permute-start(bf16[512,192]{1,0:T(8,128)(2,1)} %bitcast.13), channel_id=1, source_target_pairs={{0,3},{1,0},{2,1},{3,2},{4,7},{5,4},{6,5},{7,6},{8,11},{9,8},{10,9... | collective-permute-start | bytes 589832 | tf_op jit(solution)/shard_map/ppermute | solution.py:227
  198.7 15.7 %shard_map.91 = bf16[4,128,192]{2,1,0:T(8,128)(2,1)} custom-call(s32[4]{0:T(128)} %bitcast.38, s32[4,20]{1,0:T(4,128)} %slice.92.source, s32[4,20]{1,0:T(4,128)} %slice.93.rows, bf16[4,128,192]{2,1,0:T(8,128)(2,1)} %bitcast.35, bf16[2560,384]{1,0:T(8,128)(2,1)} %constant_dynamic-update-slice_fusion.refs_0_, ...), custom_call_target="tpu_custom_call" | custom-call | flops 1006632960 | bytes 9043968 | tf_op jit(solution)/shard_map/pallas_call | solution.py:95
  214.4 2.9 %convolution_convert_fusion = bf16[512,768]{1,0:T(8,128)(2,1)} fusion(bf16[768,768]{1,0:T(8,128)(2,1)S(1)} %bitcast_select_fusion, bf16[512,192]{1,0:T(8,128)(2,1)} %collective-permute-done.21, bf16[512,192]{1,0:T(8,128)(2,1)} %collective-permute-done.20, bf16[512,192]{1,0:T(8,128)(2,1)} %collective-permute-done.19, bf16[512,192]{1,0:T(8,128)(2,1)} %bitcast.37), kind=kOutput, calls=%fused_computation.19 | convolution fusion | flops 607518720 | bytes 2752512 | tf_op jit(solution)/shard_map/dot_general | solution.py:233
  (114 shorter events, 16.7 us)
Async XLA Ops:
  0.0 48.6 %copy-start = (bf16[768,768]{1,0:T(8,128)(2,1)S(1)}, bf16[768,768]{1,0:T(8,128)(2,1)}, u32[]{:S(2)}) copy-start(bf16[768,768]{1,0:T(8,128)(2,1)} %param.13) | copy-start | bytes 3538948
  0.0 43.6 %collective-permute-start = (bf16[512,768]{1,0:T(8,128)(2,1)}, bf16[512,768]{1,0:T(8,128)(2,1)}, u32[]{:S(2)}, u32[]{:S(2)}) collective-permute-start(bf16[512,768]{1,0:T(8,128)(2,1)} %param.11), channel_id=1, source_target_pairs={{0,3},{1,0},{2,1},{3,2},{4,7},{5,4},{6,5},{7,6},{8,11},{9,8},{10,9... | collective-permute-start | bytes 2359304 | tf_op jit(solution)/shard_map/ppermute | solution.py:148
  3.6 42.0 %collective-permute-start.1 = (bf16[512,768]{1,0:T(8,128)(2,1)}, bf16[512,768]{1,0:T(8,128)(2,1)}, u32[]{:S(2)}, u32[]{:S(2)}) collective-permute-start(bf16[512,768]{1,0:T(8,128)(2,1)} %param.11), channel_id=1, source_target_pairs={{0,1},{1,2},{2,3},{3,0},{4,5},{5,6},{6,7},{7,4},{8,9},{9,10},{10,1... | collective-permute-start | bytes 2359304 | tf_op jit(solution)/shard_map/ppermute | solution.py:148
  6.9 11.8 %copy-start.12 = (s32[16,12]{1,0:T(8,128)S(1)}, s32[16,12]{1,0:T(8,128)}, u32[]{:S(2)}) copy-start(s32[16,12]{1,0:T(8,128)} %param.14) | copy-start | bytes 2308
  6.9 11.9 %copy-start.3 = (s32[4]{0:T(128)S(1)}, s32[4]{0:T(128)}, u32[]{:S(2)}) copy-start(s32[4]{0:T(128)} %constant.193.clone) | copy-start | bytes 52
  7.2 2.1 copy-start.5
  7.2 5.5 %copy-start.8 = (bf16[768,192]{1,0:T(8,128)(2,1)}, bf16[768,192]{1,0:T(8,128)(2,1)S(1)}, u32[]{:S(2)}) copy-start(bf16[768,192]{1,0:T(8,128)(2,1)S(1)} %get-tuple-element.30) | copy-start | bytes 884740
  9.3 54.1 %collective-permute-start.3 = (bf16[512,384]{1,0:T(8,128)(2,1)S(1)}, bf16[512,384]{1,0:T(8,128)(2,1)}, u32[]{:S(2)}, u32[]{:S(2)}) collective-permute-start(bf16[512,384]{1,0:T(8,128)(2,1)S(1)} %fusion.18), channel_id=1, source_target_pairs={{0,8},{4,12},{8,16},{12,20},{16,24},{20,28},{1,9},{5,13},{9,17},{1... | collective-permute-start | bytes 1179656 | tf_op jit(solution)/shard_map/ppermute | solution.py:18
  12.7 59.4 %collective-permute-start.4 = (bf16[512,384]{1,0:T(8,128)(2,1)S(1)}, bf16[512,384]{1,0:T(8,128)(2,1)S(1)}, u32[]{:S(2)}, u32[]{:S(2)}) collective-permute-start(bf16[512,384]{1,0:T(8,128)(2,1)S(1)} %fusion.18), channel_id=1, source_target_pairs={{0,4},{4,8},{8,12},{12,16},{16,20},{20,24},{24,28},{1,5},{5,9},{9,... | collective-permute-start | bytes 1179656 | tf_op jit(solution)/shard_map/ppermute | solution.py:18
  15.6 26.1 %collective-permute-start.15 = (bf16[128,768]{1,0:T(8,128)(2,1)S(1)}, bf16[128,768]{1,0:T(8,128)(2,1)S(1)}, u32[]{:S(2)}, u32[]{:S(2)}) collective-permute-start(bf16[128,768]{1,0:T(8,128)(2,1)S(1)} %slice.71), channel_id=1, source_target_pairs={{0,2},{4,6},{8,10},{12,14},{16,18},{20,22},{24,26},{28,30}} | collective-permute-start | bytes 589832 | tf_op jit(solution)/shard_map/ppermute | solution.py:176
  20.4 0.7 copy-start.2
  21.0 1.7 copy-start.14
  21.0 2.0 copy-start.17
  22.6 1.6 copy-start.1
  28.6 17.0 %copy-start.6 = (bf16[768,192]{1,0:T(8,128)(2,1)S(1)}, bf16[768,192]{1,0:T(8,128)(2,1)}, u32[]{:S(2)}) copy-start(bf16[768,192]{1,0:T(8,128)(2,1)} %copy-done.5) | copy-start | bytes 884740
  28.6 17.0 %copy-start.9 = (bf16[768,192]{1,0:T(8,128)(2,1)S(1)}, bf16[768,192]{1,0:T(8,128)(2,1)}, u32[]{:S(2)}) copy-start(bf16[768,192]{1,0:T(8,128)(2,1)} %copy-done.8) | copy-start | bytes 884740
  32.5 16.7 %copy-start.15 = (s32[16]{0:T(128)}, s32[16]{0:T(128)S(1)}, u32[]{:S(2)}) copy-start(s32[16]{0:T(128)S(1)} %convert_reduce_fusion) | copy-start | bytes 196
  41.7 3.9 %copy-start.16 = (bf16[128,768]{1,0:T(8,128)(2,1)}, bf16[128,768]{1,0:T(8,128)(2,1)S(1)}, u32[]{:S(2)}) copy-start(bf16[128,768]{1,0:T(8,128)(2,1)S(1)} %collective-permute-done.15) | copy-start | bytes 589828
  41.7 31.3 %collective-permute-start.5 = (bf16[512,384]{1,0:T(8,128)(2,1)S(1)}, bf16[512,384]{1,0:T(8,128)(2,1)}, u32[]{:S(2)}, u32[]{:S(2)}) collective-permute-start(bf16[512,384]{1,0:T(8,128)(2,1)S(1)} %fusion.18), channel_id=1, source_target_pairs={{4,0},{8,4},{12,8},{16,12},{20,16},{24,20},{28,24},{5,1},{9,5},{13... | collective-permute-start | bytes 1179656 | tf_op jit(solution)/shard_map/ppermute | solution.py:18
  43.7 34.0 %collective-permute-start.6 = (bf16[512,384]{1,0:T(8,128)(2,1)S(1)}, bf16[512,384]{1,0:T(8,128)(2,1)}, u32[]{:S(2)}, u32[]{:S(2)}) collective-permute-start(bf16[512,384]{1,0:T(8,128)(2,1)S(1)} %fusion.18), channel_id=1, source_target_pairs={{8,0},{12,4},{16,8},{20,12},{24,16},{28,20},{9,1},{13,5},{17,9},{2... | collective-permute-start | bytes 1179656 | tf_op jit(solution)/shard_map/ppermute | solution.py:18
  47.1 4.1 %collective-permute-start.16 = (bf16[1,128,384]{2,1,0:T(8,128)(2,1)S(1)}, bf16[1,128,384]{2,1,0:T(8,128)(2,1)S(1)}, u32[]{:S(2)}, u32[]{:S(2)}) collective-permute-start(bf16[1,128,384]{2,1,0:T(8,128)(2,1)S(1)} %fusion.19), channel_id=1, source_target_pairs={{0,4},{4,8},{8,12},{12,16},{16,20},{20,24},{24,28},{28,0},{1,5},{5... | collective-permute-start | bytes 294920 | tf_op jit(solution)/shard_map/ppermute | solution.py:28
  51.2 12.2 %copy-start.11 = (bf16[512,768]{1,0:T(8,128)(2,1)S(1)}, bf16[512,768]{1,0:T(8,128)(2,1)}, u32[]{:S(2)}) copy-start(bf16[512,768]{1,0:T(8,128)(2,1)} %param.11) | copy-start | bytes 2359300
  51.3 17.4 %collective-permute-start.17 = (bf16[2,128,384]{2,1,0:T(8,128)(2,1)S(1)}, bf16[2,128,384]{2,1,0:T(8,128)(2,1)S(1)}, u32[]{:S(2)}, u32[]{:S(2)}) collective-permute-start(bf16[2,128,384]{2,1,0:T(8,128)(2,1)S(1)} %pad_maximum_fusion.3), channel_id=1, source_target_pairs={{0,8},{4,12},{8,16},{12,20},{16,24},{20,28},{24,0},{28,4},{1,9},{5... | collective-permute-start | bytes 589832 | tf_op jit(solution)/shard_map/ppermute | solution.py:28
  63.4 44.5 %collective-permute-start.2 = (bf16[512,768]{1,0:T(8,128)(2,1)S(1)}, bf16[512,768]{1,0:T(8,128)(2,1)S(1)}, u32[]{:S(2)}, u32[]{:S(2)}) collective-permute-start(bf16[512,768]{1,0:T(8,128)(2,1)S(1)} %copy-done.11), channel_id=1, source_target_pairs={{0,2},{1,3},{2,0},{3,1},{4,6},{5,7},{6,4},{7,5},{8,10},{9,11},{10,... | collective-permute-start | bytes 2359304 | tf_op jit(solution)/shard_map/ppermute | solution.py:148
  68.7 43.8 %collective-permute-start.7 = (bf16[1024,384]{1,0:T(8,128)(2,1)S(1)}, bf16[1024,384]{1,0:T(8,128)(2,1)S(1)}, u32[]{:S(2)}, u32[]{:S(2)}) collective-permute-start(bf16[1024,384]{1,0:T(8,128)(2,1)S(1)} %fusion.15), channel_id=1, source_target_pairs={{0,8},{4,12},{8,16},{12,20},{16,24},{20,28},{1,9},{5,13},{9,17},{1... | collective-permute-start | bytes 2359304 | tf_op jit(solution)/shard_map/ppermute | solution.py:18
  72.1 11.0 %collective-permute-start.18 = (bf16[4,128,384]{2,1,0:T(8,128)(2,1)S(1)}, bf16[4,128,384]{2,1,0:T(8,128)(2,1)S(1)}, u32[]{:S(2)}, u32[]{:S(2)}) collective-permute-start(bf16[4,128,384]{2,1,0:T(8,128)(2,1)S(1)} %pad_maximum_fusion.2), channel_id=1, source_target_pairs={{0,16},{4,20},{8,24},{12,28},{16,0},{20,4},{24,8},{28,12},{1,17},{... | collective-permute-start | bytes 1179656 | tf_op jit(solution)/shard_map/ppermute | solution.py:28
  73.0 35.0 %copy-start.7 = (bf16[768,192]{1,0:T(8,128)(2,1)S(1)}, bf16[768,192]{1,0:T(8,128)(2,1)}, u32[]{:S(2)}) copy-start(bf16[768,192]{1,0:T(8,128)(2,1)} %copy-done.5) | copy-start | bytes 884740
  73.0 35.0 %copy-start.10 = (bf16[768,192]{1,0:T(8,128)(2,1)S(1)}, bf16[768,192]{1,0:T(8,128)(2,1)}, u32[]{:S(2)}) copy-start(bf16[768,192]{1,0:T(8,128)(2,1)} %copy-done.8) | copy-start | bytes 884740
  73.0 42.4 %collective-permute-start.8 = (bf16[1024,384]{1,0:T(8,128)(2,1)S(1)}, bf16[1024,384]{1,0:T(8,128)(2,1)S(1)}, u32[]{:S(2)}, u32[]{:S(2)}) collective-permute-start(bf16[1024,384]{1,0:T(8,128)(2,1)S(1)} %fusion.15), channel_id=1, source_target_pairs={{0,4},{4,8},{8,12},{12,16},{16,20},{20,24},{24,28},{1,5},{5,9},{9,... | collective-permute-start | bytes 2359304 | tf_op jit(solution)/shard_map/ppermute | solution.py:18
  79.4 44.5 %collective-permute-start.9 = (bf16[1024,384]{1,0:T(8,128)(2,1)S(1)}, bf16[1024,384]{1,0:T(8,128)(2,1)S(1)}, u32[]{:S(2)}, u32[]{:S(2)}) collective-permute-start(bf16[1024,384]{1,0:T(8,128)(2,1)S(1)} %fusion.15), channel_id=1, source_target_pairs={{4,0},{8,4},{12,8},{16,12},{20,16},{24,20},{28,24},{5,1},{9,5},{13... | collective-permute-start | bytes 2359304 | tf_op jit(solution)/shard_map/ppermute | solution.py:18
  83.1 44.0 %collective-permute-start.10 = (bf16[1024,384]{1,0:T(8,128)(2,1)S(1)}, bf16[1024,384]{1,0:T(8,128)(2,1)S(1)}, u32[]{:S(2)}, u32[]{:S(2)}) collective-permute-start(bf16[1024,384]{1,0:T(8,128)(2,1)S(1)} %fusion.15), channel_id=1, source_target_pairs={{8,0},{12,4},{16,8},{20,12},{24,16},{28,20},{9,1},{13,5},{17,9},{2... | collective-permute-start | bytes 2359304 | tf_op jit(solution)/shard_map/ppermute | solution.py:18
  108.6 24.6 %collective-permute-start.11 = (bf16[512,384]{1,0:T(8,128)(2,1)S(1)}, bf16[512,384]{1,0:T(8,128)(2,1)}, u32[]{:S(2)}, u32[]{:S(2)}) collective-permute-start(bf16[512,384]{1,0:T(8,128)(2,1)S(1)} %convolution_convert_fusion.2), channel_id=1, source_target_pairs={{0,8},{4,12},{8,16},{12,20},{16,24},{20,28},{1,9},{5,13},{9,17},{1... | collective-permute-start | bytes 1179656 | tf_op jit(solution)/shard_map/ppermute | solution.py:18
  112.5 22.5 %collective-permute-start.12 = (bf16[512,384]{1,0:T(8,128)(2,1)S(1)}, bf16[512,384]{1,0:T(8,128)(2,1)}, u32[]{:S(2)}, u32[]{:S(2)}) collective-permute-start(bf16[512,384]{1,0:T(8,128)(2,1)S(1)} %convolution_convert_fusion.2), channel_id=1, source_target_pairs={{0,4},{4,8},{8,12},{12,16},{16,20},{20,24},{24,28},{1,5},{5,9},{9,... | collective-permute-start | bytes 1179656 | tf_op jit(solution)/shard_map/ppermute | solution.py:18
  115.4 26.2 %collective-permute-start.13 = (bf16[512,384]{1,0:T(8,128)(2,1)S(1)}, bf16[512,384]{1,0:T(8,128)(2,1)}, u32[]{:S(2)}, u32[]{:S(2)}) collective-permute-start(bf16[512,384]{1,0:T(8,128)(2,1)S(1)} %convolution_convert_fusion.2), channel_id=1, source_target_pairs={{4,0},{8,4},{12,8},{16,12},{20,16},{24,20},{28,24},{5,1},{9,5},{13... | collective-permute-start | bytes 1179656 | tf_op jit(solution)/shard_map/ppermute | solution.py:18
  122.8 5.3 %copy-start.4 = (bf16[2048,192]{0,1:T(8,128)(2,1)}, bf16[2048,192]{0,1:T(8,128)(2,1)S(1)}, u32[]{:S(2)}) copy-start(bf16[2048,192]{0,1:T(8,128)(2,1)S(1)} %fusion.8) | copy-start | bytes 2359300
  123.9 28.0 %collective-permute-start.14 = (bf16[512,384]{1,0:T(8,128)(2,1)S(1)}, bf16[512,384]{1,0:T(8,128)(2,1)}, u32[]{:S(2)}, u32[]{:S(2)}) collective-permute-start(bf16[512,384]{1,0:T(8,128)(2,1)S(1)} %convolution_convert_fusion.2), channel_id=1, source_target_pairs={{8,0},{12,4},{16,8},{20,12},{24,16},{28,20},{9,1},{13,5},{17,9},{2... | collective-permute-start | bytes 1179656 | tf_op jit(solution)/shard_map/ppermute | solution.py:18
  153.7 41.9 %copy-start.13 = (pred[768]{0:T(1024)(128)(4,1)S(1)}, pred[768]{0:T(1024)(128)(4,1)}, u32[]{:S(2)}) copy-start(pred[768]{0:T(1024)(128)(4,1)} %broadcast_in_dim.36) | copy-start | bytes 2308
  191.8 22.6 %collective-permute-start.19 = (bf16[512,192]{1,0:T(8,128)(2,1)}, bf16[512,192]{1,0:T(8,128)(2,1)}, u32[]{:S(2)}, u32[]{:S(2)}) collective-permute-start(bf16[512,192]{1,0:T(8,128)(2,1)} %bitcast.11), channel_id=1, source_target_pairs={{0,1},{1,2},{2,3},{3,0},{4,5},{5,6},{6,7},{7,4},{8,9},{9,10},{10,1... | collective-permute-start | bytes 589832 | tf_op jit(solution)/shard_map/ppermute | solution.py:227
  191.8 22.6 %collective-permute-start.20 = (bf16[512,192]{1,0:T(8,128)(2,1)}, bf16[512,192]{1,0:T(8,128)(2,1)}, u32[]{:S(2)}, u32[]{:S(2)}) collective-permute-start(bf16[512,192]{1,0:T(8,128)(2,1)} %bitcast.12), channel_id=1, source_target_pairs={{0,2},{1,3},{2,0},{3,1},{4,6},{5,7},{6,4},{7,5},{8,10},{9,11},{10,... | collective-permute-start | bytes 589832 | tf_op jit(solution)/shard_map/ppermute | solution.py:227
  192.0 22.4 %collective-permute-start.21 = (bf16[512,192]{1,0:T(8,128)(2,1)}, bf16[512,192]{1,0:T(8,128)(2,1)}, u32[]{:S(2)}, u32[]{:S(2)}) collective-permute-start(bf16[512,192]{1,0:T(8,128)(2,1)} %bitcast.13), channel_id=1, source_target_pairs={{0,3},{1,0},{2,1},{3,2},{4,7},{5,4},{6,5},{7,6},{8,11},{9,8},{10,9... | collective-permute-start | bytes 589832 | tf_op jit(solution)/shard_map/ppermute | solution.py:227

commit v14 on v13

--- a/solution.py
+++ b/solution.py
@@ -20,8 +20,13 @@
 
 def gather_all(x, axis):
     size = lax.axis_size(axis)
-    rank = lax.axis_index(axis)
     held = x[None]
+    if size <= 8:
+        got = [
+            lax.ppermute(held, axis, [(i, (i + d) % size) for i in range(size)])
+            for d in range(size - 1, 0, -1)
+        ]
+        return jnp.concatenate(got + [held], axis=0)
     step = 1
     while step < size:
         pairs = [(i, (i + step) % size) for i in range(size)]

time: 221 us -> 217 us (0.982)
  the two profiles are of different devices: /device:TPU:2 before, /device:TPU:11 now
where the time goes in v14:
time: 217 us; the launch traced here: 214 us
  waiting for transfers between devices  51 us (24%)
  Pallas kernels  50.4 us (23%)
  local copies, waits for them, and re-layouts  49.6 us (23%)
  starting transfers between devices  48.5 us (22%)
  matrix products  12.2 us (6%)
    pallas_call x2, Pallas kernels, attention(): pl.pallas_call(kernel, out_shape=jax.ShapeDtypeStruct(queries.shape, jnp....  50.4 us
    ppermute x12, starting transfers between devices, shifted(): return lax.ppermute(x, axis, pairs)  32.7 us
    ppermute x12, waiting for transfers between devices, shifted(): return lax.ppermute(x, axis, pairs)  29.7 us
    unnamed x50, local copies, waits for them, and re-layouts  20.2 us
    ppermute x3, waiting for transfers between devices, fetch_chunk(): return lax.ppermute(source, 'head', pairs)  16.9 us
    ppermute x7, starting transfers between devices, gather_all(): lax.ppermute(held, axis, [(i, (i + d) % size) for i in range(size)])  7.71 us
    dot_general x4, matrix products, project_kv(): jnp.dot(x, kv_w, preferred_element_type=jnp.float32).astype(jnp.bfloat16)  6.52 us
    ppermute x3, starting transfers between devices, fetch_chunk(): return lax.ppermute(source, 'head', pairs)  5.55 us
  transfers between devices with their start and end apart: 26, of which 8 were waited for; matrix products, arithmetic and copies ran while one was open for 25% of the time, Pallas kernels for 7%

profile of v14, /device:TPU:11, one launch (start us, length us, event | category | flops | bytes accessed | tf_op | source)
XLA Modules:
  0.0 214.3 jit_solution(7876100564039658423)
XLA Ops:
  0.2 1.3 collective-permute-start.1
  1.5 3.2 %fusion.57 = (bf16[768,1,768]{2,0,1:T(8,128)(2,1)}, bf16[768,1,768]{2,0,1:T(8,128)(2,1)S(1)}, bf16[768,1,768]{2,0,1:T(8,128)(2,1)S(1)}) fusion(bf16[768,3,768]{2,0,1:T(8,128)(2,1)} %param.12), kind=kLoop, calls=%fused_computation.146 | loop fusion | bytes 7077888 | tf_op jit(solution)/shard_map/slice | solution.py:144
  5.1 2.1 fusion.18
  7.2 3.1 %collective-permute-start.3 = (bf16[512,384]{1,0:T(8,128)(2,1)S(1)}, bf16[512,384]{1,0:T(8,128)(2,1)}, u32[]{:S(2)}, u32[]{:S(2)}) collective-permute-start(bf16[512,384]{1,0:T(8,128)(2,1)S(1)} %fusion.18), channel_id=1, source_target_pairs={{0,8},{4,12},{8,16},{12,20},{16,24},{20,28},{1,9},{5,13},{9,17},{1... | collective-permute-start | bytes 1179656 | tf_op jit(solution)/shard_map/ppermute | solution.py:18
  10.3 4.5 %collective-permute-start.4 = (bf16[512,384]{1,0:T(8,128)(2,1)S(1)}, bf16[512,384]{1,0:T(8,128)(2,1)S(1)}, u32[]{:S(2)}, u32[]{:S(2)}) collective-permute-start(bf16[512,384]{1,0:T(8,128)(2,1)S(1)} %fusion.18), channel_id=1, source_target_pairs={{0,4},{4,8},{8,12},{12,16},{16,20},{20,24},{24,28},{1,5},{5,9},{9,... | collective-permute-start | bytes 1179656 | tf_op jit(solution)/shard_map/ppermute | solution.py:18
  14.8 1.9 collective-permute-start.5
  17.6 1.5 gather_fusion.1
  19.8 1.5 gather_fusion.2
  23.1 2.5 %gather_fusion.5 = s32[320]{0:T(512)S(1)} fusion(s32[16,20]{1,0:T(8,128)S(1)} %pad_add_fusion.1, s32[320]{0:T(512)S(1)} %reshape.172), kind=kCustom, calls=%fused_computation.1.clone | custom fusion | bytes 5120 | tf_op jit(solution)/shard_map/jit(take_along_axis)/gather | solution.py:221
  26.3 1.5 gather_fusion
  28.0 2.5 %gather_fusion.4 = s32[320]{0:T(512)S(1)} fusion(s32[16,20]{1,0:T(8,128)S(1)} %concatenate.49, s32[320]{0:T(512)S(1)} %reshape.172), kind=kCustom, calls=%fused_computation.clone | custom fusion | bytes 5120 | tf_op jit(solution)/shard_map/jit(take_along_axis)/gather | solution.py:222
  30.6 1.6 slice.71
  35.6 2.3 %collective-permute-start.6 = (bf16[512,384]{1,0:T(8,128)(2,1)S(1)}, bf16[512,384]{1,0:T(8,128)(2,1)S(1)}, u32[]{:S(2)}, u32[]{:S(2)}) collective-permute-start(bf16[512,384]{1,0:T(8,128)(2,1)S(1)} %fusion.18), channel_id=1, source_target_pairs={{8,0},{12,4},{16,8},{20,12},{24,16},{28,20},{9,1},{13,5},{17,9},{2... | collective-permute-start | bytes 1179656 | tf_op jit(solution)/shard_map/ppermute | solution.py:18
  37.9 1.8 constant_dynamic-update-slice_fusion.4
  42.7 5.8 %collective-permute-done.6 = bf16[512,384]{1,0:T(8,128)(2,1)S(1)} collective-permute-done((bf16[512,384]{1,0:T(8,128)(2,1)S(1)}, bf16[512,384]{1,0:T(8,128)(2,1)S(1)}, u32[]{:S(2)}, u32[]{:S(2)}) %collective-permute-start.6) | collective-permute-done | bytes 393248 | tf_op jit(solution)/shard_map/ppermute | solution.py:18
  49.4 1.4 fusion.19
  50.8 1.6 collective-permute-start.16
  52.3 2.9 %collective-permute-start.19 = (bf16[1,128,384]{2,1,0:T(8,128)(2,1)S(1)}, bf16[1,128,384]{2,1,0:T(8,128)(2,1)S(1)}, u32[]{:S(2)}, u32[]{:S(2)}) collective-permute-start(bf16[1,128,384]{2,1,0:T(8,128)(2,1)S(1)} %fusion.19), channel_id=1, source_target_pairs={{0,16},{4,20},{8,24},{12,28},{16,0},{20,4},{24,8},{28,12},{1,17},{... | collective-permute-start | bytes 294920 | tf_op jit(solution)/shard_map/ppermute | solution.py:26
  55.2 2.4 %fusion.15 = bf16[1024,384]{1,0:T(8,128)(2,1)S(1)} fusion(bf16[512,768]{1,0:T(8,128)(2,1)} %collective-permute-done.1, bf16[512,768]{1,0:T(8,128)(2,1)} %collective-permute-done, bf16[768,192]{1,0:T(8,128)(2,1)S(1)} %copy-done.6, bf16[768,192]{1,0:T(8,128)(2,1)S(1)} %copy-done.8), kind=kOutput, calls=%fused_computation.20 | convolution fusion | flops 608698368 | bytes 2949120 | tf_op jit(solution)/shard_map/dot_general | solution.py:124
  57.7 1.5 collective-permute-start.21
  59.8 4.1 %collective-permute-start.2 = (bf16[512,768]{1,0:T(8,128)(2,1)S(1)}, bf16[512,768]{1,0:T(8,128)(2,1)S(1)}, u32[]{:S(2)}, u32[]{:S(2)}) collective-permute-start(bf16[512,768]{1,0:T(8,128)(2,1)S(1)} %copy-done.9), channel_id=1, source_target_pairs={{0,2},{1,3},{2,0},{3,1},{4,6},{5,7},{6,4},{7,5},{8,10},{9,11},{10,... | collective-permute-start | bytes 2359304 | tf_op jit(solution)/shard_map/ppermute | solution.py:153
  64.6 1.8 collective-permute-start.22
  67.0 3.4 %collective-permute-start.7 = (bf16[1024,384]{1,0:T(8,128)(2,1)S(1)}, bf16[1024,384]{1,0:T(8,128)(2,1)S(1)}, u32[]{:S(2)}, u32[]{:S(2)}) collective-permute-start(bf16[1024,384]{1,0:T(8,128)(2,1)S(1)} %fusion.15), channel_id=1, source_target_pairs={{0,8},{4,12},{8,16},{12,20},{16,24},{20,28},{1,9},{5,13},{9,17},{1... | collective-permute-start | bytes 2359304 | tf_op jit(solution)/shard_map/ppermute | solution.py:18
  71.0 2.2 %collective-permute-start.8 = (bf16[1024,384]{1,0:T(8,128)(2,1)S(1)}, bf16[1024,384]{1,0:T(8,128)(2,1)S(1)}, u32[]{:S(2)}, u32[]{:S(2)}) collective-permute-start(bf16[1024,384]{1,0:T(8,128)(2,1)S(1)} %fusion.15), channel_id=1, source_target_pairs={{0,4},{4,8},{8,12},{12,16},{16,20},{20,24},{24,28},{1,5},{5,9},{9,... | collective-permute-start | bytes 2359304 | tf_op jit(solution)/shard_map/ppermute | solution.py:18
  73.8 2.1 collective-permute-start.9
  76.6 2.0 collective-permute-start.10
  79.9 16.8 %collective-permute-done.2 = bf16[512,768]{1,0:T(8,128)(2,1)S(1)} collective-permute-done((bf16[512,768]{1,0:T(8,128)(2,1)S(1)}, bf16[512,768]{1,0:T(8,128)(2,1)S(1)}, u32[]{:S(2)}, u32[]{:S(2)}) %collective-permute-start.2) | collective-permute-done | bytes 786464 | tf_op jit(solution)/shard_map/ppermute | solution.py:153
  97.4 1.9 collective-permute-start.11
  99.3 4.6 %collective-permute-start.12 = (bf16[512,384]{1,0:T(8,128)(2,1)S(1)}, bf16[512,384]{1,0:T(8,128)(2,1)}, u32[]{:S(2)}, u32[]{:S(2)}) collective-permute-start(bf16[512,384]{1,0:T(8,128)(2,1)S(1)} %convolution_convert_fusion.2), channel_id=1, source_target_pairs={{0,4},{4,8},{8,12},{12,16},{16,20},{20,24},{24,28},{1,5},{5,9},{9,... | collective-permute-start | bytes 1179656 | tf_op jit(solution)/shard_map/ppermute | solution.py:18
  105.0 1.9 collective-permute-start.13
  107.9 2.8 %fusion.8 = bf16[2048,192]{0,1:T(8,128)(2,1)S(1)} fusion(bf16[512,768]{1,0:T(8,128)(2,1)} %collective-permute-done.1, bf16[512,768]{1,0:T(8,128)(2,1)S(1)} %collective-permute-done.2, bf16[512,768]{1,0:T(8,128)(2,1)} %collective-permute-done, bf16[512,768]{1,0:T(8,128)(2,1)S(1)} %copy-done.9, bf16[768,1,768]{2,0,1:T(8,128)(2,1)} %get-tuple-element.21, ...), kind=kOutput, calls=%fused_computation.14 | convolution fusion | flops 616955904 | bytes 4325380 | tf_op jit(solution)/shard_map/dot_general | solution.py:171
  110.7 1.1 constant_dynamic-update-slice_fusion.7
  111.8 2.8 %collective-permute-start.14 = (bf16[512,384]{1,0:T(8,128)(2,1)S(1)}, bf16[512,384]{1,0:T(8,128)(2,1)}, u32[]{:S(2)}, u32[]{:S(2)}) collective-permute-start(bf16[512,384]{1,0:T(8,128)(2,1)S(1)} %convolution_convert_fusion.2), channel_id=1, source_target_pairs={{8,0},{12,4},{16,8},{20,12},{24,16},{28,20},{9,1},{13,5},{17,9},{2... | collective-permute-start | bytes 1179656 | tf_op jit(solution)/shard_map/ppermute | solution.py:18
  115.5 7.4 %collective-permute-done.10 = bf16[1024,384]{1,0:T(8,128)(2,1)S(1)} collective-permute-done((bf16[1024,384]{1,0:T(8,128)(2,1)S(1)}, bf16[1024,384]{1,0:T(8,128)(2,1)S(1)}, u32[]{:S(2)}, u32[]{:S(2)}) %collective-permute-start.10) | collective-permute-done | bytes 786464 | tf_op jit(solution)/shard_map/ppermute | solution.py:18
  124.0 1.2 copy.49
  125.1 4.7 %collective-permute-done.11 = bf16[512,384]{1,0:T(8,128)(2,1)} collective-permute-done((bf16[512,384]{1,0:T(8,128)(2,1)S(1)}, bf16[512,384]{1,0:T(8,128)(2,1)}, u32[]{:S(2)}, u32[]{:S(2)}) %collective-permute-start.11) | collective-permute-done | bytes 393248 | tf_op jit(solution)/shard_map/ppermute | solution.py:18
  129.8 1.8 constant_dynamic-update-slice_fusion.14
  131.6 6.6 %collective-permute-done.12 = bf16[512,384]{1,0:T(8,128)(2,1)} collective-permute-done((bf16[512,384]{1,0:T(8,128)(2,1)S(1)}, bf16[512,384]{1,0:T(8,128)(2,1)}, u32[]{:S(2)}, u32[]{:S(2)}) %collective-permute-start.12) | collective-permute-done | bytes 393248 | tf_op jit(solution)/shard_map/ppermute | solution.py:18
  138.2 1.8 constant_dynamic-update-slice_fusion.13
  140.8 1.8 constant_dynamic-update-slice_fusion.11
  142.6 5.2 %collective-permute-done.14 = bf16[512,384]{1,0:T(8,128)(2,1)} collective-permute-done((bf16[512,384]{1,0:T(8,128)(2,1)S(1)}, bf16[512,384]{1,0:T(8,128)(2,1)}, u32[]{:S(2)}, u32[]{:S(2)}) %collective-permute-start.14) | collective-permute-done | bytes 393248 | tf_op jit(solution)/shard_map/ppermute | solution.py:18
  147.8 1.8 constant_dynamic-update-slice_fusion.10.refs_2_
  149.6 35.0 %shard_map.92 = bf16[12,128,192]{2,1,0:T(8,128)(2,1)} custom-call(s32[12]{0:T(128)} %slice.72.count, s32[12,20]{1,0:T(8,128)} %slice.97.source, s32[12,20]{1,0:T(8,128)} %slice.98.rows, bf16[12,128,192]{2,1,0:T(8,128)(2,1)} %bitcast.34, bf16[2560,384]{1,0:T(8,128)(2,1)} %constant_dynamic-update-slice_fusion.refs_0_, ...), custom_call_target="tpu_custom_call" | custom-call | flops 3019898880 | bytes 9830400 | tf_op jit(solution)/shard_map/pallas_call | solution.py:100
  184.6 2.0 fusion.58
  191.6 15.3 %shard_map.91 = bf16[4,128,192]{2,1,0:T(8,128)(2,1)} custom-call(s32[4]{0:T(128)} %bitcast.36, s32[4,20]{1,0:T(4,128)} %slice.92.source, s32[4,20]{1,0:T(4,128)} %slice.93.rows, bf16[4,128,192]{2,1,0:T(8,128)(2,1)} %bitcast.33, bf16[2560,384]{1,0:T(8,128)(2,1)} %constant_dynamic-update-slice_fusion.refs_0_, ...), custom_call_target="tpu_custom_call" | custom-call | flops 1006632960 | bytes 9043968 | tf_op jit(solution)/shard_map/pallas_call | solution.py:100
  207.0 2.6 %collective-permute-done.24 = bf16[512,192]{1,0:T(8,128)(2,1)} collective-permute-done((bf16[512,192]{1,0:T(8,128)(2,1)}, bf16[512,192]{1,0:T(8,128)(2,1)}, u32[]{:S(2)}, u32[]{:S(2)}) %collective-permute-start.24) | collective-permute-done | bytes 196640 | tf_op jit(solution)/shard_map/ppermute | solution.py:232
  209.6 1.8 collective-permute-done.25
  211.4 2.9 %convolution_convert_fusion = bf16[512,768]{1,0:T(8,128)(2,1)} fusion(bf16[768,768]{1,0:T(8,128)(2,1)S(1)} %bitcast_select_fusion, bf16[512,192]{1,0:T(8,128)(2,1)} %collective-permute-done.25, bf16[512,192]{1,0:T(8,128)(2,1)} %collective-permute-done.24, bf16[512,192]{1,0:T(8,128)(2,1)} %collective-permute-done.23, bf16[512,192]{1,0:T(8,128)(2,1)} %bitcast.35), kind=kOutput, calls=%fused_computation.19 | convolution fusion | flops 607518720 | bytes 2752512 | tf_op jit(solution)/shard_map/dot_general | solution.py:238
  (121 shorter events, 27.3 us)
Async XLA Ops:
  0.0 34.8 %copy-start = (bf16[768,768]{1,0:T(8,128)(2,1)S(1)}, bf16[768,768]{1,0:T(8,128)(2,1)}, u32[]{:S(2)}) copy-start(bf16[768,768]{1,0:T(8,128)(2,1)} %param.13) | copy-start | bytes 3538948
  0.0 49.3 %collective-permute-start = (bf16[512,768]{1,0:T(8,128)(2,1)}, bf16[512,768]{1,0:T(8,128)(2,1)}, u32[]{:S(2)}, u32[]{:S(2)}) collective-permute-start(bf16[512,768]{1,0:T(8,128)(2,1)} %param.11), channel_id=1, source_target_pairs={{0,3},{1,0},{2,1},{3,2},{4,7},{5,4},{6,5},{7,6},{8,11},{9,8},{10,9... | collective-permute-start | bytes 2359304 | tf_op jit(solution)/shard_map/ppermute | solution.py:153
  0.2 49.2 %collective-permute-start.1 = (bf16[512,768]{1,0:T(8,128)(2,1)}, bf16[512,768]{1,0:T(8,128)(2,1)}, u32[]{:S(2)}, u32[]{:S(2)}) collective-permute-start(bf16[512,768]{1,0:T(8,128)(2,1)} %param.11), channel_id=1, source_target_pairs={{0,1},{1,2},{2,3},{3,0},{4,5},{5,6},{6,7},{7,4},{8,9},{9,10},{10,1... | collective-permute-start | bytes 2359304 | tf_op jit(solution)/shard_map/ppermute | solution.py:153
  4.7 12.1 %copy-start.10 = (s32[16,12]{1,0:T(8,128)S(1)}, s32[16,12]{1,0:T(8,128)}, u32[]{:S(2)}) copy-start(s32[16,12]{1,0:T(8,128)} %param.14) | copy-start | bytes 2308
  4.7 12.9 %copy-start.3 = (s32[4]{0:T(128)S(1)}, s32[4]{0:T(128)}, u32[]{:S(2)}) copy-start(s32[4]{0:T(128)} %constant.193.clone) | copy-start | bytes 52
  5.1 5.2 %copy-start.5 = (bf16[768,192]{1,0:T(8,128)(2,1)}, bf16[768,192]{1,0:T(8,128)(2,1)S(1)}, u32[]{:S(2)}) copy-start(bf16[768,192]{1,0:T(8,128)(2,1)S(1)} %get-tuple-element.29) | copy-start | bytes 884740
  5.1 9.7 %copy-start.7 = (bf16[768,192]{1,0:T(8,128)(2,1)}, bf16[768,192]{1,0:T(8,128)(2,1)S(1)}, u32[]{:S(2)}) copy-start(bf16[768,192]{1,0:T(8,128)(2,1)S(1)} %get-tuple-element.30) | copy-start | bytes 884740
  7.2 28.4 %collective-permute-start.3 = (bf16[512,384]{1,0:T(8,128)(2,1)S(1)}, bf16[512,384]{1,0:T(8,128)(2,1)}, u32[]{:S(2)}, u32[]{:S(2)}) collective-permute-start(bf16[512,384]{1,0:T(8,128)(2,1)S(1)} %fusion.18), channel_id=1, source_target_pairs={{0,8},{4,12},{8,16},{12,20},{16,24},{20,28},{1,9},{5,13},{9,17},{1... | collective-permute-start | bytes 1179656 | tf_op jit(solution)/shard_map/ppermute | solution.py:18
  10.3 29.4 %collective-permute-start.4 = (bf16[512,384]{1,0:T(8,128)(2,1)S(1)}, bf16[512,384]{1,0:T(8,128)(2,1)S(1)}, u32[]{:S(2)}, u32[]{:S(2)}) collective-permute-start(bf16[512,384]{1,0:T(8,128)(2,1)S(1)} %fusion.18), channel_id=1, source_target_pairs={{0,4},{4,8},{8,12},{12,16},{16,20},{20,24},{24,28},{1,5},{5,9},{9,... | collective-permute-start | bytes 1179656 | tf_op jit(solution)/shard_map/ppermute | solution.py:18
  14.8 27.1 %collective-permute-start.5 = (bf16[512,384]{1,0:T(8,128)(2,1)S(1)}, bf16[512,384]{1,0:T(8,128)(2,1)S(1)}, u32[]{:S(2)}, u32[]{:S(2)}) collective-permute-start(bf16[512,384]{1,0:T(8,128)(2,1)S(1)} %fusion.18), channel_id=1, source_target_pairs={{4,0},{8,4},{12,8},{16,12},{20,16},{24,20},{28,24},{5,1},{9,5},{13... | collective-permute-start | bytes 1179656 | tf_op jit(solution)/shard_map/ppermute | solution.py:18
  19.1 0.7 copy-start.2
  19.8 1.6 copy-start.12
  19.8 2.0 copy-start.14
  25.6 0.7 copy-start.1
  33.5 1.3 copy-start.13
  35.5 13.8 %copy-start.6 = (bf16[768,192]{1,0:T(8,128)(2,1)S(1)}, bf16[768,192]{1,0:T(8,128)(2,1)}, u32[]{:S(2)}) copy-start(bf16[768,192]{1,0:T(8,128)(2,1)} %copy-done.5) | copy-start | bytes 884740
  35.5 13.8 %copy-start.8 = (bf16[768,192]{1,0:T(8,128)(2,1)S(1)}, bf16[768,192]{1,0:T(8,128)(2,1)}, u32[]{:S(2)}) copy-start(bf16[768,192]{1,0:T(8,128)(2,1)} %copy-done.7) | copy-start | bytes 884740
  35.6 13.8 %copy-start.9 = (bf16[512,768]{1,0:T(8,128)(2,1)S(1)}, bf16[512,768]{1,0:T(8,128)(2,1)}, u32[]{:S(2)}) copy-start(bf16[512,768]{1,0:T(8,128)(2,1)} %param.11) | copy-start | bytes 2359300
  35.6 13.0 %collective-permute-start.6 = (bf16[512,384]{1,0:T(8,128)(2,1)S(1)}, bf16[512,384]{1,0:T(8,128)(2,1)S(1)}, u32[]{:S(2)}, u32[]{:S(2)}) collective-permute-start(bf16[512,384]{1,0:T(8,128)(2,1)S(1)} %fusion.18), channel_id=1, source_target_pairs={{8,0},{12,4},{16,8},{20,12},{24,16},{28,20},{9,1},{13,5},{17,9},{2... | collective-permute-start | bytes 1179656 | tf_op jit(solution)/shard_map/ppermute | solution.py:18
  39.7 9.7 %collective-permute-start.15 = (bf16[128,768]{1,0:T(8,128)(2,1)}, bf16[128,768]{1,0:T(8,128)(2,1)S(1)}, u32[]{:S(2)}, u32[]{:S(2)}) collective-permute-start(bf16[128,768]{1,0:T(8,128)(2,1)} %slice.71), channel_id=1, source_target_pairs={{0,2},{4,6},{8,10},{12,14},{16,18},{20,22},{24,26},{28,30}} | collective-permute-start | bytes 589832 | tf_op jit(solution)/shard_map/ppermute | solution.py:181
  50.8 6.9 %collective-permute-start.16 = (bf16[1,128,384]{2,1,0:T(8,128)(2,1)S(1)}, bf16[1,128,384]{2,1,0:T(8,128)(2,1)S(1)}, u32[]{:S(2)}, u32[]{:S(2)}) collective-permute-start(bf16[1,128,384]{2,1,0:T(8,128)(2,1)S(1)} %fusion.19), channel_id=1, source_target_pairs={{0,28},{4,0},{8,4},{12,8},{16,12},{20,16},{24,20},{28,24},{1,29},{... | collective-permute-start | bytes 294920 | tf_op jit(solution)/shard_map/ppermute | solution.py:26
  52.3 7.5 %collective-permute-start.17 = (bf16[1,128,384]{2,1,0:T(8,128)(2,1)S(1)}, bf16[1,128,384]{2,1,0:T(8,128)(2,1)S(1)}, u32[]{:S(2)}, u32[]{:S(2)}) collective-permute-start(bf16[1,128,384]{2,1,0:T(8,128)(2,1)S(1)} %fusion.19), channel_id=1, source_target_pairs={{0,24},{4,28},{8,0},{12,4},{16,8},{20,12},{24,16},{28,20},{1,25},{... | collective-permute-start | bytes 294920 | tf_op jit(solution)/shard_map/ppermute | solution.py:26
  52.3 12.2 %collective-permute-start.18 = (bf16[1,128,384]{2,1,0:T(8,128)(2,1)S(1)}, bf16[1,128,384]{2,1,0:T(8,128)(2,1)S(1)}, u32[]{:S(2)}, u32[]{:S(2)}) collective-permute-start(bf16[1,128,384]{2,1,0:T(8,128)(2,1)S(1)} %fusion.19), channel_id=1, source_target_pairs={{0,20},{4,24},{8,28},{12,0},{16,4},{20,8},{24,12},{28,16},{1,21},{... | collective-permute-start | bytes 294920 | tf_op jit(solution)/shard_map/ppermute | solution.py:26
  52.3 14.6 %collective-permute-start.19 = (bf16[1,128,384]{2,1,0:T(8,128)(2,1)S(1)}, bf16[1,128,384]{2,1,0:T(8,128)(2,1)S(1)}, u32[]{:S(2)}, u32[]{:S(2)}) collective-permute-start(bf16[1,128,384]{2,1,0:T(8,128)(2,1)S(1)} %fusion.19), channel_id=1, source_target_pairs={{0,16},{4,20},{8,24},{12,28},{16,0},{20,4},{24,8},{28,12},{1,17},{... | collective-permute-start | bytes 294920 | tf_op jit(solution)/shard_map/ppermute | solution.py:26
  55.2 15.8 %collective-permute-start.20 = (bf16[1,128,384]{2,1,0:T(8,128)(2,1)S(1)}, bf16[1,128,384]{2,1,0:T(8,128)(2,1)S(1)}, u32[]{:S(2)}, u32[]{:S(2)}) collective-permute-start(bf16[1,128,384]{2,1,0:T(8,128)(2,1)S(1)} %fusion.19), channel_id=1, source_target_pairs={{0,12},{4,16},{8,20},{12,24},{16,28},{20,0},{24,4},{28,8},{1,13},{... | collective-permute-start | bytes 294920 | tf_op jit(solution)/shard_map/ppermute | solution.py:26
  57.7 16.1 %collective-permute-start.21 = (bf16[1,128,384]{2,1,0:T(8,128)(2,1)S(1)}, bf16[1,128,384]{2,1,0:T(8,128)(2,1)S(1)}, u32[]{:S(2)}, u32[]{:S(2)}) collective-permute-start(bf16[1,128,384]{2,1,0:T(8,128)(2,1)S(1)} %fusion.19), channel_id=1, source_target_pairs={{0,8},{4,12},{8,16},{12,20},{16,24},{20,28},{24,0},{28,4},{1,9},{5... | collective-permute-start | bytes 294920 | tf_op jit(solution)/shard_map/ppermute | solution.py:26
  59.8 36.9 %collective-permute-start.2 = (bf16[512,768]{1,0:T(8,128)(2,1)S(1)}, bf16[512,768]{1,0:T(8,128)(2,1)S(1)}, u32[]{:S(2)}, u32[]{:S(2)}) collective-permute-start(bf16[512,768]{1,0:T(8,128)(2,1)S(1)} %copy-done.9), channel_id=1, source_target_pairs={{0,2},{1,3},{2,0},{3,1},{4,6},{5,7},{6,4},{7,5},{8,10},{9,11},{10,... | collective-permute-start | bytes 2359304 | tf_op jit(solution)/shard_map/ppermute | solution.py:153
  64.6 12.0 %collective-permute-start.22 = (bf16[1,128,384]{2,1,0:T(8,128)(2,1)S(1)}, bf16[1,128,384]{2,1,0:T(8,128)(2,1)S(1)}, u32[]{:S(2)}, u32[]{:S(2)}) collective-permute-start(bf16[1,128,384]{2,1,0:T(8,128)(2,1)S(1)} %fusion.19), channel_id=1, source_target_pairs={{0,4},{4,8},{8,12},{12,16},{16,20},{20,24},{24,28},{28,0},{1,5},{5... | collective-permute-start | bytes 294920 | tf_op jit(solution)/shard_map/ppermute | solution.py:26
  67.0 32.4 %collective-permute-start.7 = (bf16[1024,384]{1,0:T(8,128)(2,1)S(1)}, bf16[1024,384]{1,0:T(8,128)(2,1)S(1)}, u32[]{:S(2)}, u32[]{:S(2)}) collective-permute-start(bf16[1024,384]{1,0:T(8,128)(2,1)S(1)} %fusion.15), channel_id=1, source_target_pairs={{0,8},{4,12},{8,16},{12,20},{16,24},{20,28},{1,9},{5,13},{9,17},{1... | collective-permute-start | bytes 2359304 | tf_op jit(solution)/shard_map/ppermute | solution.py:18
  71.0 34.0 %collective-permute-start.8 = (bf16[1024,384]{1,0:T(8,128)(2,1)S(1)}, bf16[1024,384]{1,0:T(8,128)(2,1)S(1)}, u32[]{:S(2)}, u32[]{:S(2)}) collective-permute-start(bf16[1024,384]{1,0:T(8,128)(2,1)S(1)} %fusion.15), channel_id=1, source_target_pairs={{0,4},{4,8},{8,12},{12,16},{16,20},{20,24},{24,28},{1,5},{5,9},{9,... | collective-permute-start | bytes 2359304 | tf_op jit(solution)/shard_map/ppermute | solution.py:18
  73.8 38.0 %collective-permute-start.9 = (bf16[1024,384]{1,0:T(8,128)(2,1)S(1)}, bf16[1024,384]{1,0:T(8,128)(2,1)S(1)}, u32[]{:S(2)}, u32[]{:S(2)}) collective-permute-start(bf16[1024,384]{1,0:T(8,128)(2,1)S(1)} %fusion.15), channel_id=1, source_target_pairs={{4,0},{8,4},{12,8},{16,12},{20,16},{24,20},{28,24},{5,1},{9,5},{13... | collective-permute-start | bytes 2359304 | tf_op jit(solution)/shard_map/ppermute | solution.py:18
  76.6 46.3 %collective-permute-start.10 = (bf16[1024,384]{1,0:T(8,128)(2,1)S(1)}, bf16[1024,384]{1,0:T(8,128)(2,1)S(1)}, u32[]{:S(2)}, u32[]{:S(2)}) collective-permute-start(bf16[1024,384]{1,0:T(8,128)(2,1)S(1)} %fusion.15), channel_id=1, source_target_pairs={{8,0},{12,4},{16,8},{20,12},{24,16},{28,20},{9,1},{13,5},{17,9},{2... | collective-permute-start | bytes 2359304 | tf_op jit(solution)/shard_map/ppermute | solution.py:18
  97.4 32.4 %collective-permute-start.11 = (bf16[512,384]{1,0:T(8,128)(2,1)S(1)}, bf16[512,384]{1,0:T(8,128)(2,1)}, u32[]{:S(2)}, u32[]{:S(2)}) collective-permute-start(bf16[512,384]{1,0:T(8,128)(2,1)S(1)} %convolution_convert_fusion.2), channel_id=1, source_target_pairs={{0,8},{4,12},{8,16},{12,20},{16,24},{20,28},{1,9},{5,13},{9,17},{1... | collective-permute-start | bytes 1179656 | tf_op jit(solution)/shard_map/ppermute | solution.py:18
  99.3 38.9 %collective-permute-start.12 = (bf16[512,384]{1,0:T(8,128)(2,1)S(1)}, bf16[512,384]{1,0:T(8,128)(2,1)}, u32[]{:S(2)}, u32[]{:S(2)}) collective-permute-start(bf16[512,384]{1,0:T(8,128)(2,1)S(1)} %convolution_convert_fusion.2), channel_id=1, source_target_pairs={{0,4},{4,8},{8,12},{12,16},{16,20},{20,24},{24,28},{1,5},{5,9},{9,... | collective-permute-start | bytes 1179656 | tf_op jit(solution)/shard_map/ppermute | solution.py:18
  105.0 35.8 %collective-permute-start.13 = (bf16[512,384]{1,0:T(8,128)(2,1)S(1)}, bf16[512,384]{1,0:T(8,128)(2,1)}, u32[]{:S(2)}, u32[]{:S(2)}) collective-permute-start(bf16[512,384]{1,0:T(8,128)(2,1)S(1)} %convolution_convert_fusion.2), channel_id=1, source_target_pairs={{4,0},{8,4},{12,8},{16,12},{20,16},{24,20},{28,24},{5,1},{9,5},{13... | collective-permute-start | bytes 1179656 | tf_op jit(solution)/shard_map/ppermute | solution.py:18
  110.7 13.2 %copy-start.4 = (bf16[2048,192]{0,1:T(8,128)(2,1)}, bf16[2048,192]{0,1:T(8,128)(2,1)S(1)}, u32[]{:S(2)}) copy-start(bf16[2048,192]{0,1:T(8,128)(2,1)S(1)} %fusion.8) | copy-start | bytes 2359300
  111.8 36.0 %collective-permute-start.14 = (bf16[512,384]{1,0:T(8,128)(2,1)S(1)}, bf16[512,384]{1,0:T(8,128)(2,1)}, u32[]{:S(2)}, u32[]{:S(2)}) collective-permute-start(bf16[512,384]{1,0:T(8,128)(2,1)S(1)} %convolution_convert_fusion.2), channel_id=1, source_target_pairs={{8,0},{12,4},{16,8},{20,12},{24,16},{28,20},{9,1},{13,5},{17,9},{2... | collective-permute-start | bytes 1179656 | tf_op jit(solution)/shard_map/ppermute | solution.py:18
  149.6 38.9 %copy-start.11 = (pred[768]{0:T(1024)(128)(4,1)S(1)}, pred[768]{0:T(1024)(128)(4,1)}, u32[]{:S(2)}) copy-start(pred[768]{0:T(1024)(128)(4,1)} %broadcast_in_dim.36) | copy-start | bytes 2308
  186.6 20.4 %collective-permute-start.23 = (bf16[512,192]{1,0:T(8,128)(2,1)}, bf16[512,192]{1,0:T(8,128)(2,1)}, u32[]{:S(2)}, u32[]{:S(2)}) collective-permute-start(bf16[512,192]{1,0:T(8,128)(2,1)} %bitcast.11), channel_id=1, source_target_pairs={{0,1},{1,2},{2,3},{3,0},{4,5},{5,6},{6,7},{7,4},{8,9},{9,10},{10,1... | collective-permute-start | bytes 589832 | tf_op jit(solution)/shard_map/ppermute | solution.py:232
  186.6 23.0 %collective-permute-start.24 = (bf16[512,192]{1,0:T(8,128)(2,1)}, bf16[512,192]{1,0:T(8,128)(2,1)}, u32[]{:S(2)}, u32[]{:S(2)}) collective-permute-start(bf16[512,192]{1,0:T(8,128)(2,1)} %bitcast.12), channel_id=1, source_target_pairs={{0,2},{1,3},{2,0},{3,1},{4,6},{5,7},{6,4},{7,5},{8,10},{9,11},{10,... | collective-permute-start | bytes 589832 | tf_op jit(solution)/shard_map/ppermute | solution.py:232
  187.4 24.0 %collective-permute-start.25 = (bf16[512,192]{1,0:T(8,128)(2,1)}, bf16[512,192]{1,0:T(8,128)(2,1)}, u32[]{:S(2)}, u32[]{:S(2)}) collective-permute-start(bf16[512,192]{1,0:T(8,128)(2,1)} %bitcast.13), channel_id=1, source_target_pairs={{0,3},{1,0},{2,1},{3,2},{4,7},{5,4},{6,5},{7,6},{8,11},{9,8},{10,9... | collective-permute-start | bytes 589832 | tf_op jit(solution)/shard_map/ppermute | solution.py:232

commit v15 on v12

--- a/solution.py
+++ b/solution.py
@@ -20,8 +20,13 @@
 
 def gather_all(x, axis):
     size = lax.axis_size(axis)
-    rank = lax.axis_index(axis)
     held = x[None]
+    if size <= 8:
+        got = [
+            lax.ppermute(held, axis, [(i, (i + d) % size) for i in range(size)])
+            for d in range(size - 1, 0, -1)
+        ]
+        return jnp.concatenate(got + [held], axis=0)
     step = 1
     while step < size:
         pairs = [(i, (i + step) % size) for i in range(size)]

time: 222 us -> 211 us (0.950)
  starting transfers between devices: 69.7 us -> 48.6 us
  waiting for transfers between devices: 29.9 us -> 46.1 us
  Pallas kernels: 53.2 us -> 50.1 us
  local copies, waits for them, and re-layouts: 48.7 us -> 45.8 us
    ppermute x12, waiting for transfers between devices: 1.17 us -> 27 us  [shifted(): return lax.ppermute(x, axis, pairs)]
    ppermute x3 -> x7, starting transfers between devices: 27.1 us -> 4.25 us  [gather_all(): lax.ppermute(held, axis, [(i, (i + d) % size) for i in range(size)])]
    ppermute x3 -> x7, waiting for transfers between devices: 9.67 us -> 0.02 us  [gather_all(): lax.ppermute(held, axis, [(i, (i + d) % size) for i in range(size)])]
    pallas_call x2, Pallas kernels: 53.2 us -> 50.1 us  [attention(): pl.pallas_call(kernel, out_shape=jax.ShapeDtypeStruct(queries.shape, jnp....]
    unnamed x56 -> x67, local copies, waits for them, and re-layouts: 19.1 us -> 16.2 us
  transfers between devices with their start and end apart: 21 -> 25, of which waited for: 5 -> 7; matrix products, arithmetic and copies ran while one was open for 27% -> 27% of each run, Pallas kernels for 8% -> 8%
where the time goes in v15:
time: 211 us; the launch traced here: 208 us
  Pallas kernels  50.1 us (24%)
  starting transfers between devices  48.6 us (23%)
  waiting for transfers between devices  46.1 us (22%)
  local copies, waits for them, and re-layouts  45.8 us (22%)
  matrix products  13.5 us (6%)
  other arithmetic  3.21 us (2%)
    pallas_call x2, Pallas kernels, attention(): pl.pallas_call(kernel, out_shape=jax.ShapeDtypeStruct(queries.shape, jnp....  50.1 us
    ppermute x12, starting transfers between devices, shifted(): return lax.ppermute(x, axis, pairs)  32.9 us
    ppermute x12, waiting for transfers between devices, shifted(): return lax.ppermute(x, axis, pairs)  27 us
    ppermute x3, waiting for transfers between devices, fetch_chunk(): return lax.ppermute(source, 'head', pairs)  19.1 us
    unnamed x67, local copies, waits for them, and re-layouts  16.2 us
    dot_general x4, matrix products, project_kv(): jnp.dot(x, kv_w, preferred_element_type=jnp.float32).astype(jnp.bfloat16)  8.2 us
    ppermute x3, starting transfers between devices, shards(): received[j] = lax.ppermute(away[j - 1], 'head', pairs)  7.12 us
    ppermute x3, starting transfers between devices, fetch_chunk(): return lax.ppermute(source, 'head', pairs)  4.33 us
  transfers between devices with their start and end apart: 25, of which 7 were waited for; matrix products, arithmetic and copies ran while one was open for 27% of the time, Pallas kernels for 8%

profile of v15, /device:TPU:2, one launch (start us, length us, event | category | flops | bytes accessed | tf_op | source)
XLA Modules:
  0.0 208.0 jit_solution(13087644877465959666)
XLA Ops:
  0.0 3.6 %collective-permute-start = (bf16[512,768]{1,0:T(8,128)(2,1)}, bf16[512,768]{1,0:T(8,128)(2,1)}, u32[]{:S(2)}, u32[]{:S(2)}) collective-permute-start(bf16[512,768]{1,0:T(8,128)(2,1)} %param.11), channel_id=1, source_target_pairs={{0,3},{1,0},{2,1},{3,2},{4,7},{5,4},{6,5},{7,6},{8,11},{9,8},{10,9... | collective-permute-start | bytes 2359304 | tf_op jit(solution)/shard_map/ppermute | solution.py:153
  3.6 3.2 %fusion.39 = (bf16[768,1,768]{2,0,1:T(8,128)(2,1)}, bf16[768,1,768]{2,0,1:T(8,128)(2,1)S(1)}, bf16[768,1,768]{2,0,1:T(8,128)(2,1)S(1)}) fusion(bf16[768,3,768]{2,0,1:T(8,128)(2,1)} %param.12), kind=kLoop, calls=%fused_computation.135 | loop fusion | bytes 7077888 | tf_op jit(solution)/shard_map/slice | solution.py:144
  7.2 2.1 fusion.7
  9.3 3.4 %collective-permute-start.3 = (bf16[512,384]{1,0:T(8,128)(2,1)S(1)}, bf16[512,384]{1,0:T(8,128)(2,1)}, u32[]{:S(2)}, u32[]{:S(2)}) collective-permute-start(bf16[512,384]{1,0:T(8,128)(2,1)S(1)} %fusion.7), channel_id=1, source_target_pairs={{0,8},{4,12},{8,16},{12,20},{16,24},{20,28},{1,9},{5,13},{9,17},{1... | collective-permute-start | bytes 1179656 | tf_op jit(solution)/shard_map/ppermute | solution.py:18
  12.7 1.9 collective-permute-start.4
  14.6 3.6 %collective-permute-start.5 = (bf16[512,384]{1,0:T(8,128)(2,1)S(1)}, bf16[512,384]{1,0:T(8,128)(2,1)}, u32[]{:S(2)}, u32[]{:S(2)}) collective-permute-start(bf16[512,384]{1,0:T(8,128)(2,1)S(1)} %fusion.7), channel_id=1, source_target_pairs={{4,0},{8,4},{12,8},{16,12},{20,16},{24,20},{28,24},{5,1},{9,5},{13... | collective-permute-start | bytes 1179656 | tf_op jit(solution)/shard_map/ppermute | solution.py:18
  18.5 1.6 gather_fusion.1
  20.7 1.5 gather_fusion.2
  22.9 1.5 gather_fusion
  26.1 2.5 %gather_fusion.4 = s32[320]{0:T(512)S(1)} fusion(s32[16,20]{1,0:T(8,128)S(1)} %concatenate.49, s32[320]{0:T(512)S(1)} %reshape.172), kind=kCustom, calls=%fused_computation.clone | custom fusion | bytes 5120 | tf_op jit(solution)/shard_map/jit(take_along_axis)/gather | solution.py:214
  28.9 2.5 %gather_fusion.5 = s32[320]{0:T(512)S(1)} fusion(s32[16,20]{1,0:T(8,128)S(1)} %pad_add_fusion.1, s32[320]{0:T(512)S(1)} %reshape.172), kind=kCustom, calls=%fused_computation.1.clone | custom fusion | bytes 5120 | tf_op jit(solution)/shard_map/jit(take_along_axis)/gather | solution.py:213
  33.1 1.9 collective-permute-start.6
  35.0 3.5 %collective-permute-done.1 = bf16[512,768]{1,0:T(8,128)(2,1)} collective-permute-done((bf16[512,768]{1,0:T(8,128)(2,1)}, bf16[512,768]{1,0:T(8,128)(2,1)}, u32[]{:S(2)}, u32[]{:S(2)}) %collective-permute-start.1) | collective-permute-done | bytes 786464 | tf_op jit(solution)/shard_map/ppermute | solution.py:153
  38.5 3.4 %fusion.4 = bf16[1024,384]{1,0:T(8,128)(2,1)} fusion(bf16[512,768]{1,0:T(8,128)(2,1)} %collective-permute-done.1, bf16[512,768]{1,0:T(8,128)(2,1)} %collective-permute-done, bf16[768,192]{1,0:T(8,128)(2,1)S(1)} %copy-done.12, bf16[768,192]{1,0:T(8,128)(2,1)S(1)} %copy-done.15), kind=kOutput, calls=%fused_computation.12 | convolution fusion | flops 608698368 | bytes 2949120 | tf_op jit(solution)/shard_map/dot_general | solution.py:124
  45.9 1.2 constant_dynamic-update-slice_fusion.8
  50.4 3.4 %collective-permute-start.7 = (bf16[1024,384]{1,0:T(8,128)(2,1)}, bf16[1024,384]{1,0:T(8,128)(2,1)}, u32[]{:S(2)}, u32[]{:S(2)}) collective-permute-start(bf16[1024,384]{1,0:T(8,128)(2,1)} %fusion.4), channel_id=1, source_target_pairs={{0,8},{4,12},{8,16},{12,20},{16,24},{20,28},{1,9},{5,13},{9,17},{1... | collective-permute-start | bytes 2359304 | tf_op jit(solution)/shard_map/ppermute | solution.py:18
  53.8 1.9 collective-permute-start.8
  55.7 3.6 %collective-permute-start.9 = (bf16[1024,384]{1,0:T(8,128)(2,1)}, bf16[1024,384]{1,0:T(8,128)(2,1)}, u32[]{:S(2)}, u32[]{:S(2)}) collective-permute-start(bf16[1024,384]{1,0:T(8,128)(2,1)} %fusion.4), channel_id=1, source_target_pairs={{4,0},{8,4},{12,8},{16,12},{20,16},{24,20},{28,24},{5,1},{9,5},{13... | collective-permute-start | bytes 2359304 | tf_op jit(solution)/shard_map/ppermute | solution.py:18
  59.4 1.9 collective-permute-start.10
  61.3 1.2 constant_dynamic-update-slice_fusion.2
  62.5 15.6 %collective-permute-done.2 = bf16[512,768]{1,0:T(8,128)(2,1)} collective-permute-done((bf16[512,768]{1,0:T(8,128)(2,1)S(1)}, bf16[512,768]{1,0:T(8,128)(2,1)}, u32[]{:S(2)}, u32[]{:S(2)}) %collective-permute-start.2) | collective-permute-done | bytes 786464 | tf_op jit(solution)/shard_map/ppermute | solution.py:153
  79.3 1.2 constant_dynamic-update-slice_fusion
  81.5 1.8 convolution_convert_fusion.3
  83.3 2.3 %convolution_convert_fusion = bf16[2048,192]{0,1:T(8,128)(2,1)S(1)} fusion(bf16[2048,768]{1,0:T(8,128)(2,1)S(1)} %constant_dynamic-update-slice_fusion, bf16[768,1,768]{2,0,1:T(8,128)(2,1)} %get-tuple-element.21, s32[]{:T(128)S(6)} %select_n.140), kind=kOutput, calls=%fused_computation.6 | convolution fusion | flops 604372992 | bytes 4325380 | tf_op jit(solution)/shard_map/dot_general | solution.py:171
  86.5 2.2 %copy.49 = bf16[1536,192]{1,0:T(8,128)(2,1)} copy(bf16[1536,192]{0,1:T(8,128)(2,1)} %slice.84) | data formatting | bytes 1179648 | tf_op jit(solution)/shard_map/slice | solution.py:218
  88.7 1.4 collective-permute-start.16
  90.1 1.2 constant_dynamic-update-slice_fusion.13
  91.9 1.3 constant_dynamic-update-slice_fusion.12
  93.9 1.3 constant_dynamic-update-slice_fusion.10
  95.2 12.0 %collective-permute-done.10 = bf16[1024,384]{1,0:T(8,128)(2,1)} collective-permute-done((bf16[1024,384]{1,0:T(8,128)(2,1)}, bf16[1024,384]{1,0:T(8,128)(2,1)}, u32[]{:S(2)}, u32[]{:S(2)}) %collective-permute-start.10) | collective-permute-done | bytes 786464 | tf_op jit(solution)/shard_map/ppermute | solution.py:18
  107.3 1.3 constant_dynamic-update-slice_fusion.9.refs_1_
  109.6 1.7 collective-permute-start.21
  111.3 3.5 %collective-permute-start.11 = (bf16[512,384]{1,0:T(8,128)(2,1)S(1)}, bf16[512,384]{1,0:T(8,128)(2,1)S(1)}, u32[]{:S(2)}, u32[]{:S(2)}) collective-permute-start(bf16[512,384]{1,0:T(8,128)(2,1)S(1)} %convolution_convert_fusion.3), channel_id=1, source_target_pairs={{0,8},{4,12},{8,16},{12,20},{16,24},{20,28},{1,9},{5,13},{9,17},{1... | collective-permute-start | bytes 1179656 | tf_op jit(solution)/shard_map/ppermute | solution.py:18
  114.9 1.9 collective-permute-start.12
  116.9 3.6 %collective-permute-start.13 = (bf16[512,384]{1,0:T(8,128)(2,1)S(1)}, bf16[512,384]{1,0:T(8,128)(2,1)S(1)}, u32[]{:S(2)}, u32[]{:S(2)}) collective-permute-start(bf16[512,384]{1,0:T(8,128)(2,1)S(1)} %convolution_convert_fusion.3), channel_id=1, source_target_pairs={{4,0},{8,4},{12,8},{16,12},{20,16},{24,20},{28,24},{5,1},{9,5},{13... | collective-permute-start | bytes 1179656 | tf_op jit(solution)/shard_map/ppermute | solution.py:18
  120.5 2.1 %collective-permute-start.14 = (bf16[512,384]{1,0:T(8,128)(2,1)S(1)}, bf16[512,384]{1,0:T(8,128)(2,1)S(1)}, u32[]{:S(2)}, u32[]{:S(2)}) collective-permute-start(bf16[512,384]{1,0:T(8,128)(2,1)S(1)} %convolution_convert_fusion.3), channel_id=1, source_target_pairs={{8,0},{12,4},{16,8},{20,12},{24,16},{28,20},{9,1},{13,5},{17,9},{2... | collective-permute-start | bytes 1179656 | tf_op jit(solution)/shard_map/ppermute | solution.py:18
  123.6 1.6 collective-permute-done.11
  126.0 2.5 %collective-permute-done.12 = bf16[512,384]{1,0:T(8,128)(2,1)S(1)} collective-permute-done((bf16[512,384]{1,0:T(8,128)(2,1)S(1)}, bf16[512,384]{1,0:T(8,128)(2,1)S(1)}, u32[]{:S(2)}, u32[]{:S(2)}) %collective-permute-start.12) | collective-permute-done | bytes 393248 | tf_op jit(solution)/shard_map/ppermute | solution.py:18
  130.1 2.7 %collective-permute-done.13 = bf16[512,384]{1,0:T(8,128)(2,1)S(1)} collective-permute-done((bf16[512,384]{1,0:T(8,128)(2,1)S(1)}, bf16[512,384]{1,0:T(8,128)(2,1)S(1)}, u32[]{:S(2)}, u32[]{:S(2)}) %collective-permute-start.13) | collective-permute-done | bytes 393248 | tf_op jit(solution)/shard_map/ppermute | solution.py:18
  133.5 8.2 %collective-permute-done.14 = bf16[512,384]{1,0:T(8,128)(2,1)S(1)} collective-permute-done((bf16[512,384]{1,0:T(8,128)(2,1)S(1)}, bf16[512,384]{1,0:T(8,128)(2,1)S(1)}, u32[]{:S(2)}, u32[]{:S(2)}) %collective-permute-start.14) | collective-permute-done | bytes 393248 | tf_op jit(solution)/shard_map/ppermute | solution.py:18
  142.6 33.6 %shard_map.92 = bf16[12,128,192]{2,1,0:T(8,128)(2,1)} custom-call(s32[12]{0:T(128)} %slice.59.count, s32[12,20]{1,0:T(8,128)} %slice.82.source, s32[12,20]{1,0:T(8,128)} %slice.83.rows, bf16[12,128,192]{2,1,0:T(8,128)(2,1)} %bitcast.37, bf16[2560,384]{1,0:T(8,128)(2,1)} %copy-done.6, bf16[5120,384]{1,0:T(8,128)(2,1)} %copy-done.4, ...), custom_call_target="tpu_custom_call" | custom-call | flops 3019898880 | bytes 9830400 | tf_op jit(solution)/shard_map/pallas_call | solution.py:100
  176.2 2.0 fusion.40
  178.1 4.4 %collective-permute-start.22 = (bf16[512,192]{1,0:T(8,128)(2,1)}, bf16[512,192]{1,0:T(8,128)(2,1)}, u32[]{:S(2)}, u32[]{:S(2)}) collective-permute-start(bf16[512,192]{1,0:T(8,128)(2,1)} %bitcast.11), channel_id=1, source_target_pairs={{0,1},{1,2},{2,3},{3,0},{4,5},{5,6},{6,7},{7,4},{8,9},{9,10},{10,1... | collective-permute-start | bytes 589832 | tf_op jit(solution)/shard_map/ppermute | solution.py:224
  182.5 1.3 collective-permute-start.23
  183.8 1.5 collective-permute-start.24
  185.3 1.3 bitcast_select_fusion
  188.6 16.5 %shard_map.91 = bf16[4,128,192]{2,1,0:T(8,128)(2,1)} custom-call(s32[4]{0:T(128)} %bitcast.40, s32[4,20]{1,0:T(4,128)} %slice.79.source, s32[4,20]{1,0:T(4,128)} %slice.80.rows, bf16[4,128,192]{2,1,0:T(8,128)(2,1)} %bitcast.34, bf16[2560,384]{1,0:T(8,128)(2,1)} %copy-done.6, bf16[5120,384]{1,0:T(8,128)(2,1)} %copy-done.4, ...), custom_call_target="tpu_custom_call" | custom-call | flops 1006632960 | bytes 9043968 | tf_op jit(solution)/shard_map/pallas_call | solution.py:100
  205.1 2.9 %convolution_convert_fusion.1 = bf16[512,768]{1,0:T(8,128)(2,1)} fusion(bf16[768,768]{1,0:T(8,128)(2,1)S(1)} %copy-done.7, bf16[512,192]{1,0:T(8,128)(2,1)} %collective-permute-done.24, bf16[512,192]{1,0:T(8,128)(2,1)} %collective-permute-done.23, bf16[512,192]{1,0:T(8,128)(2,1)} %collective-permute-done.22, bf16[512,192]{1,0:T(8,128)(2,1)} %bitcast.38), kind=kOutput, calls=%fused_computation.11 | convolution fusion | flops 607518720 | bytes 2752512 | tf_op jit(solution)/shard_map/dot_general | solution.py:230
  (137 shorter events, 24.9 us)
Async XLA Ops:
  0.0 45.1 %copy-start = (bf16[768,768]{1,0:T(8,128)(2,1)S(1)}, bf16[768,768]{1,0:T(8,128)(2,1)}, u32[]{:S(2)}) copy-start(bf16[768,768]{1,0:T(8,128)(2,1)} %param.13) | copy-start | bytes 3538948
  0.0 33.1 %collective-permute-start = (bf16[512,768]{1,0:T(8,128)(2,1)}, bf16[512,768]{1,0:T(8,128)(2,1)}, u32[]{:S(2)}, u32[]{:S(2)}) collective-permute-start(bf16[512,768]{1,0:T(8,128)(2,1)} %param.11), channel_id=1, source_target_pairs={{0,3},{1,0},{2,1},{3,2},{4,7},{5,4},{6,5},{7,6},{8,11},{9,8},{10,9... | collective-permute-start | bytes 2359304 | tf_op jit(solution)/shard_map/ppermute | solution.py:153
  3.6 34.9 %collective-permute-start.1 = (bf16[512,768]{1,0:T(8,128)(2,1)}, bf16[512,768]{1,0:T(8,128)(2,1)}, u32[]{:S(2)}, u32[]{:S(2)}) collective-permute-start(bf16[512,768]{1,0:T(8,128)(2,1)} %param.11), channel_id=1, source_target_pairs={{0,1},{1,2},{2,3},{3,0},{4,5},{5,6},{6,7},{7,4},{8,9},{9,10},{10,1... | collective-permute-start | bytes 2359304 | tf_op jit(solution)/shard_map/ppermute | solution.py:153
  6.8 11.5 %copy-start.17 = (s32[16,12]{1,0:T(8,128)S(1)}, s32[16,12]{1,0:T(8,128)}, u32[]{:S(2)}) copy-start(s32[16,12]{1,0:T(8,128)} %param.14) | copy-start | bytes 2308
  6.8 11.6 %copy-start.3 = (s32[4]{0:T(128)S(1)}, s32[4]{0:T(128)}, u32[]{:S(2)}) copy-start(s32[4]{0:T(128)} %constant.195.clone) | copy-start | bytes 52
  7.2 5.5 %copy-start.11 = (bf16[768,192]{1,0:T(8,128)(2,1)}, bf16[768,192]{1,0:T(8,128)(2,1)S(1)}, u32[]{:S(2)}) copy-start(bf16[768,192]{1,0:T(8,128)(2,1)S(1)} %get-tuple-element.27) | copy-start | bytes 884740
  7.2 7.4 %copy-start.14 = (bf16[768,192]{1,0:T(8,128)(2,1)}, bf16[768,192]{1,0:T(8,128)(2,1)S(1)}, u32[]{:S(2)}) copy-start(bf16[768,192]{1,0:T(8,128)(2,1)S(1)} %get-tuple-element.28) | copy-start | bytes 884740
  9.3 36.6 %collective-permute-start.3 = (bf16[512,384]{1,0:T(8,128)(2,1)S(1)}, bf16[512,384]{1,0:T(8,128)(2,1)}, u32[]{:S(2)}, u32[]{:S(2)}) collective-permute-start(bf16[512,384]{1,0:T(8,128)(2,1)S(1)} %fusion.7), channel_id=1, source_target_pairs={{0,8},{4,12},{8,16},{12,20},{16,24},{20,28},{1,9},{5,13},{9,17},{1... | collective-permute-start | bytes 1179656 | tf_op jit(solution)/shard_map/ppermute | solution.py:18
  12.7 34.4 %collective-permute-start.4 = (bf16[512,384]{1,0:T(8,128)(2,1)S(1)}, bf16[512,384]{1,0:T(8,128)(2,1)}, u32[]{:S(2)}, u32[]{:S(2)}) collective-permute-start(bf16[512,384]{1,0:T(8,128)(2,1)S(1)} %fusion.7), channel_id=1, source_target_pairs={{0,4},{4,8},{8,12},{12,16},{16,20},{20,24},{24,28},{1,5},{5,9},{9,... | collective-permute-start | bytes 1179656 | tf_op jit(solution)/shard_map/ppermute | solution.py:18
  14.6 33.6 %collective-permute-start.5 = (bf16[512,384]{1,0:T(8,128)(2,1)S(1)}, bf16[512,384]{1,0:T(8,128)(2,1)}, u32[]{:S(2)}, u32[]{:S(2)}) collective-permute-start(bf16[512,384]{1,0:T(8,128)(2,1)S(1)} %fusion.7), channel_id=1, source_target_pairs={{4,0},{8,4},{12,8},{16,12},{20,16},{24,20},{28,24},{5,1},{9,5},{13... | collective-permute-start | bytes 1179656 | tf_op jit(solution)/shard_map/ppermute | solution.py:18
  20.0 0.7 copy-start.2
  22.3 0.7 copy-start.1
  22.9 1.7 copy-start.19
  22.9 1.9 copy-start.21
  28.9 2.6 %copy-start.9 = (bf16[512,768]{1,0:T(8,128)(2,1)S(1)}, bf16[512,768]{1,0:T(8,128)(2,1)}, u32[]{:S(2)}) copy-start(bf16[512,768]{1,0:T(8,128)(2,1)} %param.11) | copy-start | bytes 2359300
  28.9 9.6 %copy-start.12 = (bf16[768,192]{1,0:T(8,128)(2,1)S(1)}, bf16[768,192]{1,0:T(8,128)(2,1)}, u32[]{:S(2)}) copy-start(bf16[768,192]{1,0:T(8,128)(2,1)} %copy-done.11) | copy-start | bytes 884740
  28.9 9.6 %copy-start.15 = (bf16[768,192]{1,0:T(8,128)(2,1)S(1)}, bf16[768,192]{1,0:T(8,128)(2,1)}, u32[]{:S(2)}) copy-start(bf16[768,192]{1,0:T(8,128)(2,1)} %copy-done.14) | copy-start | bytes 884740
  33.1 16.2 %collective-permute-start.6 = (bf16[512,384]{1,0:T(8,128)(2,1)S(1)}, bf16[512,384]{1,0:T(8,128)(2,1)}, u32[]{:S(2)}, u32[]{:S(2)}) collective-permute-start(bf16[512,384]{1,0:T(8,128)(2,1)S(1)} %fusion.7), channel_id=1, source_target_pairs={{8,0},{12,4},{16,8},{20,12},{24,16},{28,20},{9,1},{13,5},{17,9},{2... | collective-permute-start | bytes 1179656 | tf_op jit(solution)/shard_map/ppermute | solution.py:18
  41.9 36.3 %collective-permute-start.2 = (bf16[512,768]{1,0:T(8,128)(2,1)S(1)}, bf16[512,768]{1,0:T(8,128)(2,1)}, u32[]{:S(2)}, u32[]{:S(2)}) collective-permute-start(bf16[512,768]{1,0:T(8,128)(2,1)S(1)} %copy-done.9), channel_id=1, source_target_pairs={{0,2},{1,3},{2,0},{3,1},{4,6},{5,7},{6,4},{7,5},{8,10},{9,11},{10,... | collective-permute-start | bytes 2359304 | tf_op jit(solution)/shard_map/ppermute | solution.py:153
  43.8 1.3 copy-start.20
  45.8 15.4 %copy-start.5 = (bf16[2048,768]{1,0:T(8,128)(2,1)S(1)}, bf16[2048,768]{1,0:T(8,128)(2,1)}, u32[]{:S(2)}) copy-start(bf16[2048,768]{1,0:T(8,128)(2,1)} %constant_dynamic-update-slice_fusion.3) | copy-start | bytes 9437188
  50.3 9.0 %copy-start.6 = (bf16[2560,384]{1,0:T(8,128)(2,1)}, bf16[2560,384]{1,0:T(8,128)(2,1)S(1)}, u32[]{:S(2)}) copy-start(bf16[2560,384]{1,0:T(8,128)(2,1)S(1)} %constant_dynamic-update-slice_fusion.4.refs_0_) | copy-start | bytes 5898244
  50.4 38.4 %collective-permute-start.7 = (bf16[1024,384]{1,0:T(8,128)(2,1)}, bf16[1024,384]{1,0:T(8,128)(2,1)}, u32[]{:S(2)}, u32[]{:S(2)}) collective-permute-start(bf16[1024,384]{1,0:T(8,128)(2,1)} %fusion.4), channel_id=1, source_target_pairs={{0,8},{4,12},{8,16},{12,20},{16,24},{20,28},{1,9},{5,13},{9,17},{1... | collective-permute-start | bytes 2359304 | tf_op jit(solution)/shard_map/ppermute | solution.py:18
  53.8 37.6 %collective-permute-start.8 = (bf16[1024,384]{1,0:T(8,128)(2,1)}, bf16[1024,384]{1,0:T(8,128)(2,1)}, u32[]{:S(2)}, u32[]{:S(2)}) collective-permute-start(bf16[1024,384]{1,0:T(8,128)(2,1)} %fusion.4), channel_id=1, source_target_pairs={{0,4},{4,8},{8,12},{12,16},{16,20},{20,24},{24,28},{1,5},{5,9},{9,... | collective-permute-start | bytes 2359304 | tf_op jit(solution)/shard_map/ppermute | solution.py:18
  55.7 37.7 %collective-permute-start.9 = (bf16[1024,384]{1,0:T(8,128)(2,1)}, bf16[1024,384]{1,0:T(8,128)(2,1)}, u32[]{:S(2)}, u32[]{:S(2)}) collective-permute-start(bf16[1024,384]{1,0:T(8,128)(2,1)} %fusion.4), channel_id=1, source_target_pairs={{4,0},{8,4},{12,8},{16,12},{20,16},{24,20},{28,24},{5,1},{9,5},{13... | collective-permute-start | bytes 2359304 | tf_op jit(solution)/shard_map/ppermute | solution.py:18
  59.4 47.9 %collective-permute-start.10 = (bf16[1024,384]{1,0:T(8,128)(2,1)}, bf16[1024,384]{1,0:T(8,128)(2,1)}, u32[]{:S(2)}, u32[]{:S(2)}) collective-permute-start(bf16[1024,384]{1,0:T(8,128)(2,1)} %fusion.4), channel_id=1, source_target_pairs={{8,0},{12,4},{16,8},{20,12},{24,16},{28,20},{9,1},{13,5},{17,9},{2... | collective-permute-start | bytes 2359304 | tf_op jit(solution)/shard_map/ppermute | solution.py:18
  62.5 18.0 %copy-start.13 = (bf16[768,192]{1,0:T(8,128)(2,1)S(1)}, bf16[768,192]{1,0:T(8,128)(2,1)}, u32[]{:S(2)}) copy-start(bf16[768,192]{1,0:T(8,128)(2,1)} %copy-done.11) | copy-start | bytes 884740
  62.5 18.0 %copy-start.16 = (bf16[768,192]{1,0:T(8,128)(2,1)S(1)}, bf16[768,192]{1,0:T(8,128)(2,1)}, u32[]{:S(2)}) copy-start(bf16[768,192]{1,0:T(8,128)(2,1)} %copy-done.14) | copy-start | bytes 884740
  81.5 27.1 %collective-permute-start.15 = (bf16[1,128,384]{2,1,0:T(8,128)(2,1)}, bf16[1,128,384]{2,1,0:T(8,128)(2,1)}, u32[]{:S(2)}, u32[]{:S(2)}) collective-permute-start(bf16[1,128,384]{2,1,0:T(8,128)(2,1)} %fusion.8), channel_id=1, source_target_pairs={{0,28},{4,0},{8,4},{12,8},{16,12},{20,16},{24,20},{28,24},{1,29},{... | collective-permute-start | bytes 294920 | tf_op jit(solution)/shard_map/ppermute | solution.py:26
  88.7 4.5 %copy-start.10 = (bf16[1024,384]{1,0:T(8,128)(2,1)S(1)}, bf16[1024,384]{1,0:T(8,128)(2,1)}, u32[]{:S(2)}) copy-start(bf16[1024,384]{1,0:T(8,128)(2,1)} %fusion.4) | copy-start | bytes 2359300
  88.7 20.9 %collective-permute-start.16 = (bf16[1,128,384]{2,1,0:T(8,128)(2,1)}, bf16[1,128,384]{2,1,0:T(8,128)(2,1)S(1)}, u32[]{:S(2)}, u32[]{:S(2)}) collective-permute-start(bf16[1,128,384]{2,1,0:T(8,128)(2,1)} %fusion.8), channel_id=1, source_target_pairs={{0,24},{4,28},{8,0},{12,4},{16,8},{20,12},{24,16},{28,20},{1,25},{... | collective-permute-start | bytes 294920 | tf_op jit(solution)/shard_map/ppermute | solution.py:26
  91.4 20.0 %collective-permute-start.17 = (bf16[1,128,384]{2,1,0:T(8,128)(2,1)}, bf16[1,128,384]{2,1,0:T(8,128)(2,1)S(1)}, u32[]{:S(2)}, u32[]{:S(2)}) collective-permute-start(bf16[1,128,384]{2,1,0:T(8,128)(2,1)} %fusion.8), channel_id=1, source_target_pairs={{0,20},{4,24},{8,28},{12,0},{16,4},{20,8},{24,12},{28,16},{1,21},{... | collective-permute-start | bytes 294920 | tf_op jit(solution)/shard_map/ppermute | solution.py:26
  93.4 21.5 %collective-permute-start.18 = (bf16[1,128,384]{2,1,0:T(8,128)(2,1)}, bf16[1,128,384]{2,1,0:T(8,128)(2,1)S(1)}, u32[]{:S(2)}, u32[]{:S(2)}) collective-permute-start(bf16[1,128,384]{2,1,0:T(8,128)(2,1)} %fusion.8), channel_id=1, source_target_pairs={{0,16},{4,20},{8,24},{12,28},{16,0},{20,4},{24,8},{28,12},{1,17},{... | collective-permute-start | bytes 294920 | tf_op jit(solution)/shard_map/ppermute | solution.py:26
  107.2 9.6 %collective-permute-start.19 = (bf16[1,128,384]{2,1,0:T(8,128)(2,1)}, bf16[1,128,384]{2,1,0:T(8,128)(2,1)S(1)}, u32[]{:S(2)}, u32[]{:S(2)}) collective-permute-start(bf16[1,128,384]{2,1,0:T(8,128)(2,1)} %fusion.8), channel_id=1, source_target_pairs={{0,12},{4,16},{8,20},{12,24},{16,28},{20,0},{24,4},{28,8},{1,13},{... | collective-permute-start | bytes 294920 | tf_op jit(solution)/shard_map/ppermute | solution.py:26
  108.5 25.0 %copy-start.4 = (bf16[5120,384]{1,0:T(8,128)(2,1)}, bf16[5120,384]{1,0:T(8,128)(2,1)S(1)}, u32[]{:S(2)}) copy-start(bf16[5120,384]{1,0:T(8,128)(2,1)S(1)} %constant_dynamic-update-slice_fusion.9.refs_1_) | copy-start | bytes 11796484
  108.6 12.0 %collective-permute-start.20 = (bf16[1,128,384]{2,1,0:T(8,128)(2,1)}, bf16[1,128,384]{2,1,0:T(8,128)(2,1)S(1)}, u32[]{:S(2)}, u32[]{:S(2)}) collective-permute-start(bf16[1,128,384]{2,1,0:T(8,128)(2,1)} %fusion.8), channel_id=1, source_target_pairs={{0,8},{4,12},{8,16},{12,20},{16,24},{20,28},{24,0},{28,4},{1,9},{5... | collective-permute-start | bytes 294920 | tf_op jit(solution)/shard_map/ppermute | solution.py:26
  109.6 13.0 %collective-permute-start.21 = (bf16[1,128,384]{2,1,0:T(8,128)(2,1)}, bf16[1,128,384]{2,1,0:T(8,128)(2,1)S(1)}, u32[]{:S(2)}, u32[]{:S(2)}) collective-permute-start(bf16[1,128,384]{2,1,0:T(8,128)(2,1)} %fusion.8), channel_id=1, source_target_pairs={{0,4},{4,8},{8,12},{12,16},{16,20},{20,24},{24,28},{28,0},{1,5},{5... | collective-permute-start | bytes 294920 | tf_op jit(solution)/shard_map/ppermute | solution.py:26
  111.3 13.9 %collective-permute-start.11 = (bf16[512,384]{1,0:T(8,128)(2,1)S(1)}, bf16[512,384]{1,0:T(8,128)(2,1)S(1)}, u32[]{:S(2)}, u32[]{:S(2)}) collective-permute-start(bf16[512,384]{1,0:T(8,128)(2,1)S(1)} %convolution_convert_fusion.3), channel_id=1, source_target_pairs={{0,8},{4,12},{8,16},{12,20},{16,24},{20,28},{1,9},{5,13},{9,17},{1... | collective-permute-start | bytes 1179656 | tf_op jit(solution)/shard_map/ppermute | solution.py:18
  114.9 13.6 %collective-permute-start.12 = (bf16[512,384]{1,0:T(8,128)(2,1)S(1)}, bf16[512,384]{1,0:T(8,128)(2,1)S(1)}, u32[]{:S(2)}, u32[]{:S(2)}) collective-permute-start(bf16[512,384]{1,0:T(8,128)(2,1)S(1)} %convolution_convert_fusion.3), channel_id=1, source_target_pairs={{0,4},{4,8},{8,12},{12,16},{16,20},{20,24},{24,28},{1,5},{5,9},{9,... | collective-permute-start | bytes 1179656 | tf_op jit(solution)/shard_map/ppermute | solution.py:18
  116.9 15.9 %collective-permute-start.13 = (bf16[512,384]{1,0:T(8,128)(2,1)S(1)}, bf16[512,384]{1,0:T(8,128)(2,1)S(1)}, u32[]{:S(2)}, u32[]{:S(2)}) collective-permute-start(bf16[512,384]{1,0:T(8,128)(2,1)S(1)} %convolution_convert_fusion.3), channel_id=1, source_target_pairs={{4,0},{8,4},{12,8},{16,12},{20,16},{24,20},{28,24},{5,1},{9,5},{13... | collective-permute-start | bytes 1179656 | tf_op jit(solution)/shard_map/ppermute | solution.py:18
  120.5 21.2 %collective-permute-start.14 = (bf16[512,384]{1,0:T(8,128)(2,1)S(1)}, bf16[512,384]{1,0:T(8,128)(2,1)S(1)}, u32[]{:S(2)}, u32[]{:S(2)}) collective-permute-start(bf16[512,384]{1,0:T(8,128)(2,1)S(1)} %convolution_convert_fusion.3), channel_id=1, source_target_pairs={{8,0},{12,4},{16,8},{20,12},{24,16},{28,20},{9,1},{13,5},{17,9},{2... | collective-permute-start | bytes 1179656 | tf_op jit(solution)/shard_map/ppermute | solution.py:18
  123.6 18.9 %copy-start.8 = (bf16[8,128,384]{2,1,0:T(8,128)(2,1)}, bf16[8,128,384]{2,1,0:T(8,128)(2,1)S(1)}, u32[]{:S(2)}) copy-start(bf16[8,128,384]{2,1,0:T(8,128)(2,1)S(1)} %constant_dynamic-update-slice_fusion.19) | copy-start | bytes 2359300
  142.6 42.7 %copy-start.18 = (pred[768]{0:T(1024)(128)(4,1)S(1)}, pred[768]{0:T(1024)(128)(4,1)}, u32[]{:S(2)}) copy-start(pred[768]{0:T(1024)(128)(4,1)} %broadcast_in_dim.36) | copy-start | bytes 2308
  178.1 26.9 %collective-permute-start.22 = (bf16[512,192]{1,0:T(8,128)(2,1)}, bf16[512,192]{1,0:T(8,128)(2,1)}, u32[]{:S(2)}, u32[]{:S(2)}) collective-permute-start(bf16[512,192]{1,0:T(8,128)(2,1)} %bitcast.11), channel_id=1, source_target_pairs={{0,1},{1,2},{2,3},{3,0},{4,5},{5,6},{6,7},{7,4},{8,9},{9,10},{10,1... | collective-permute-start | bytes 589832 | tf_op jit(solution)/shard_map/ppermute | solution.py:224
  182.5 22.6 %collective-permute-start.23 = (bf16[512,192]{1,0:T(8,128)(2,1)}, bf16[512,192]{1,0:T(8,128)(2,1)}, u32[]{:S(2)}, u32[]{:S(2)}) collective-permute-start(bf16[512,192]{1,0:T(8,128)(2,1)} %bitcast.12), channel_id=1, source_target_pairs={{0,2},{1,3},{2,0},{3,1},{4,6},{5,7},{6,4},{7,5},{8,10},{9,11},{10,... | collective-permute-start | bytes 589832 | tf_op jit(solution)/shard_map/ppermute | solution.py:224
  183.8 21.3 %collective-permute-start.24 = (bf16[512,192]{1,0:T(8,128)(2,1)S(1)}, bf16[512,192]{1,0:T(8,128)(2,1)}, u32[]{:S(2)}, u32[]{:S(2)}) collective-permute-start(bf16[512,192]{1,0:T(8,128)(2,1)S(1)} %bitcast.39), channel_id=1, source_target_pairs={{0,3},{1,0},{2,1},{3,2},{4,7},{5,4},{6,5},{7,6},{8,11},{9,8},{10,9... | collective-permute-start | bytes 589832 | tf_op jit(solution)/shard_map/ppermute | solution.py:224
  188.6 16.5 %copy-start.7 = (bf16[768,768]{1,0:T(8,128)(2,1)S(1)}, bf16[768,768]{1,0:T(8,128)(2,1)}, u32[]{:S(2)}) copy-start(bf16[768,768]{1,0:T(8,128)(2,1)} %bitcast_select_fusion) | copy-start | bytes 3538948

commit v16 on v15

--- a/solution.py
+++ b/solution.py
@@ -92,7 +92,7 @@
     heads = width // HDIM
     slots = rows.shape[1]
     if widths is None:
-        widths = tuple(w for w in (8, 12, 16) if w < slots) + (slots,)
+        widths = tuple(w for w in (8, 10, 12, 14, 16, 18) if w < slots) + (slots,)
     kernel = functools.partial(attention_kernel, heads=heads, widths=widths,
                                scale=HDIM ** (-0.5))
     whole = pl.BlockSpec(memory_space=pltpu.VMEM)

time: 211 us -> 212 us (level)
  the two profiles are of different devices: /device:TPU:2 before, /device:TPU:9 now
where the time goes in v16:
time: 212 us; the launch traced here: 211 us
  Pallas kernels  52.6 us (25%)
  waiting for transfers between devices  48.8 us (23%)
  starting transfers between devices  46 us (22%)
  local copies, waits for them, and re-layouts  45.9 us (22%)
  matrix products  13.4 us (6%)
  other arithmetic  3.21 us (2%)
    pallas_call x2, Pallas kernels, attention(): pl.pallas_call(kernel, out_shape=jax.ShapeDtypeStruct(queries.shape, jnp....  52.6 us
    ppermute x12, starting transfers between devices, shifted(): return lax.ppermute(x, axis, pairs)  33.2 us
    ppermute x12, waiting for transfers between devices, shifted(): return lax.ppermute(x, axis, pairs)  25.9 us
    ppermute x3, waiting for transfers between devices, fetch_chunk(): return lax.ppermute(source, 'head', pairs)  18.1 us
    unnamed x67, local copies, waits for them, and re-layouts  16.3 us
    ppermute x7, starting transfers between devices, gather_all(): lax.ppermute(held, axis, [(i, (i + d) % size) for i in range(size)])  9.29 us
    dot_general x4, matrix products, project_kv(): jnp.dot(x, kv_w, preferred_element_type=jnp.float32).astype(jnp.bfloat16)  8.19 us
  transfers between devices with their start and end apart: 25, of which 9 were waited for; matrix products, arithmetic and copies ran while one was open for 26% of the time, Pallas kernels for 7%

profile of v16, /device:TPU:9, one launch (start us, length us, event | category | flops | bytes accessed | tf_op | source)
XLA Modules:
  0.0 210.6 jit_solution(4673976324118748556)
XLA Ops:
  0.0 1.5 collective-permute-start.1
  1.5 3.2 %fusion.39 = (bf16[768,1,768]{2,0,1:T(8,128)(2,1)}, bf16[768,1,768]{2,0,1:T(8,128)(2,1)S(1)}, bf16[768,1,768]{2,0,1:T(8,128)(2,1)S(1)}) fusion(bf16[768,3,768]{2,0,1:T(8,128)(2,1)} %param.12), kind=kLoop, calls=%fused_computation.135 | loop fusion | bytes 7077888 | tf_op jit(solution)/shard_map/slice | solution.py:144
  5.1 2.1 fusion.7
  7.1 3.9 %collective-permute-start.3 = (bf16[512,384]{1,0:T(8,128)(2,1)S(1)}, bf16[512,384]{1,0:T(8,128)(2,1)}, u32[]{:S(2)}, u32[]{:S(2)}) collective-permute-start(bf16[512,384]{1,0:T(8,128)(2,1)S(1)} %fusion.7), channel_id=1, source_target_pairs={{0,8},{4,12},{8,16},{12,20},{16,24},{20,28},{1,9},{5,13},{9,17},{1... | collective-permute-start | bytes 1179656 | tf_op jit(solution)/shard_map/ppermute | solution.py:18
  11.0 3.8 %collective-permute-start.4 = (bf16[512,384]{1,0:T(8,128)(2,1)S(1)}, bf16[512,384]{1,0:T(8,128)(2,1)}, u32[]{:S(2)}, u32[]{:S(2)}) collective-permute-start(bf16[512,384]{1,0:T(8,128)(2,1)S(1)} %fusion.7), channel_id=1, source_target_pairs={{0,4},{4,8},{8,12},{12,16},{16,20},{20,24},{24,28},{1,5},{5,9},{9,... | collective-permute-start | bytes 1179656 | tf_op jit(solution)/shard_map/ppermute | solution.py:18
  14.8 1.9 collective-permute-start.5
  16.9 1.6 gather_fusion.1
  19.2 1.5 gather_fusion.2
  21.4 1.5 gather_fusion
  24.6 2.5 %gather_fusion.4 = s32[320]{0:T(512)S(1)} fusion(s32[16,20]{1,0:T(8,128)S(1)} %concatenate.49, s32[320]{0:T(512)S(1)} %reshape.172), kind=kCustom, calls=%fused_computation.clone | custom fusion | bytes 5120 | tf_op jit(solution)/shard_map/jit(take_along_axis)/gather | solution.py:214
  27.3 2.5 %gather_fusion.5 = s32[320]{0:T(512)S(1)} fusion(s32[16,20]{1,0:T(8,128)S(1)} %pad_add_fusion.1, s32[320]{0:T(512)S(1)} %reshape.172), kind=kCustom, calls=%fused_computation.1.clone | custom fusion | bytes 5120 | tf_op jit(solution)/shard_map/jit(take_along_axis)/gather | solution.py:213
  31.5 1.3 collective-permute-start.6
  32.8 4.9 %collective-permute-done.1 = bf16[512,768]{1,0:T(8,128)(2,1)} collective-permute-done((bf16[512,768]{1,0:T(8,128)(2,1)}, bf16[512,768]{1,0:T(8,128)(2,1)}, u32[]{:S(2)}, u32[]{:S(2)}) %collective-permute-start.1) | collective-permute-done | bytes 786464 | tf_op jit(solution)/shard_map/ppermute | solution.py:153
  37.7 3.4 %fusion.4 = bf16[1024,384]{1,0:T(8,128)(2,1)} fusion(bf16[512,768]{1,0:T(8,128)(2,1)} %collective-permute-done.1, bf16[512,768]{1,0:T(8,128)(2,1)} %collective-permute-done, bf16[768,192]{1,0:T(8,128)(2,1)S(1)} %copy-done.12, bf16[768,192]{1,0:T(8,128)(2,1)S(1)} %copy-done.15), kind=kOutput, calls=%fused_computation.12 | convolution fusion | flops 608698368 | bytes 2949120 | tf_op jit(solution)/shard_map/dot_general | solution.py:124
  44.4 1.2 constant_dynamic-update-slice_fusion.8
  48.9 4.1 %collective-permute-start.7 = (bf16[1024,384]{1,0:T(8,128)(2,1)}, bf16[1024,384]{1,0:T(8,128)(2,1)}, u32[]{:S(2)}, u32[]{:S(2)}) collective-permute-start(bf16[1024,384]{1,0:T(8,128)(2,1)} %fusion.4), channel_id=1, source_target_pairs={{0,8},{4,12},{8,16},{12,20},{16,24},{20,28},{1,9},{5,13},{9,17},{1... | collective-permute-start | bytes 2359304 | tf_op jit(solution)/shard_map/ppermute | solution.py:18
  53.0 4.5 %collective-permute-start.8 = (bf16[1024,384]{1,0:T(8,128)(2,1)}, bf16[1024,384]{1,0:T(8,128)(2,1)}, u32[]{:S(2)}, u32[]{:S(2)}) collective-permute-start(bf16[1024,384]{1,0:T(8,128)(2,1)} %fusion.4), channel_id=1, source_target_pairs={{0,4},{4,8},{8,12},{12,16},{16,20},{20,24},{24,28},{1,5},{5,9},{9,... | collective-permute-start | bytes 2359304 | tf_op jit(solution)/shard_map/ppermute | solution.py:18
  57.5 1.9 collective-permute-start.9
  59.4 1.3 collective-permute-start.10
  61.9 13.2 %collective-permute-done.2 = bf16[512,768]{1,0:T(8,128)(2,1)} collective-permute-done((bf16[512,768]{1,0:T(8,128)(2,1)S(1)}, bf16[512,768]{1,0:T(8,128)(2,1)}, u32[]{:S(2)}, u32[]{:S(2)}) %collective-permute-start.2) | collective-permute-done | bytes 786464 | tf_op jit(solution)/shard_map/ppermute | solution.py:153
  76.3 1.2 constant_dynamic-update-slice_fusion
  79.0 1.8 convolution_convert_fusion.3
  80.8 2.3 %convolution_convert_fusion = bf16[2048,192]{0,1:T(8,128)(2,1)S(1)} fusion(bf16[2048,768]{1,0:T(8,128)(2,1)S(1)} %constant_dynamic-update-slice_fusion, bf16[768,1,768]{2,0,1:T(8,128)(2,1)} %get-tuple-element.21, s32[]{:T(128)S(6)} %select_n.140), kind=kOutput, calls=%fused_computation.6 | convolution fusion | flops 604372992 | bytes 4325380 | tf_op jit(solution)/shard_map/dot_general | solution.py:171
  84.0 2.2 %copy.49 = bf16[1536,192]{1,0:T(8,128)(2,1)} copy(bf16[1536,192]{0,1:T(8,128)(2,1)} %slice.84) | data formatting | bytes 1179648 | tf_op jit(solution)/shard_map/slice | solution.py:218
  86.2 2.2 %collective-permute-start.16 = (bf16[1,128,384]{2,1,0:T(8,128)(2,1)}, bf16[1,128,384]{2,1,0:T(8,128)(2,1)S(1)}, u32[]{:S(2)}, u32[]{:S(2)}) collective-permute-start(bf16[1,128,384]{2,1,0:T(8,128)(2,1)} %fusion.8), channel_id=1, source_target_pairs={{0,24},{4,28},{8,0},{12,4},{16,8},{20,12},{24,16},{28,20},{1,25},{... | collective-permute-start | bytes 294920 | tf_op jit(solution)/shard_map/ppermute | solution.py:26
  88.4 1.2 constant_dynamic-update-slice_fusion.13
  89.6 1.5 collective-permute-start.17
  91.1 1.3 constant_dynamic-update-slice_fusion.12
  92.6 1.3 collective-permute-start.18
  93.9 1.3 constant_dynamic-update-slice_fusion.10
  95.2 9.3 %collective-permute-done.10 = bf16[1024,384]{1,0:T(8,128)(2,1)} collective-permute-done((bf16[1024,384]{1,0:T(8,128)(2,1)}, bf16[1024,384]{1,0:T(8,128)(2,1)}, u32[]{:S(2)}, u32[]{:S(2)}) %collective-permute-start.10) | collective-permute-done | bytes 786464 | tf_op jit(solution)/shard_map/ppermute | solution.py:18
  104.6 2.5 %collective-permute-start.19 = (bf16[1,128,384]{2,1,0:T(8,128)(2,1)}, bf16[1,128,384]{2,1,0:T(8,128)(2,1)S(1)}, u32[]{:S(2)}, u32[]{:S(2)}) collective-permute-start(bf16[1,128,384]{2,1,0:T(8,128)(2,1)} %fusion.8), channel_id=1, source_target_pairs={{0,12},{4,16},{8,20},{12,24},{16,28},{20,0},{24,4},{28,8},{1,13},{... | collective-permute-start | bytes 294920 | tf_op jit(solution)/shard_map/ppermute | solution.py:26
  107.0 1.3 constant_dynamic-update-slice_fusion.9.refs_1_
  111.5 3.7 %collective-permute-start.11 = (bf16[512,384]{1,0:T(8,128)(2,1)S(1)}, bf16[512,384]{1,0:T(8,128)(2,1)S(1)}, u32[]{:S(2)}, u32[]{:S(2)}) collective-permute-start(bf16[512,384]{1,0:T(8,128)(2,1)S(1)} %convolution_convert_fusion.3), channel_id=1, source_target_pairs={{0,8},{4,12},{8,16},{12,20},{16,24},{20,28},{1,9},{5,13},{9,17},{1... | collective-permute-start | bytes 1179656 | tf_op jit(solution)/shard_map/ppermute | solution.py:18
  115.3 3.4 %collective-permute-start.12 = (bf16[512,384]{1,0:T(8,128)(2,1)S(1)}, bf16[512,384]{1,0:T(8,128)(2,1)S(1)}, u32[]{:S(2)}, u32[]{:S(2)}) collective-permute-start(bf16[512,384]{1,0:T(8,128)(2,1)S(1)} %convolution_convert_fusion.3), channel_id=1, source_target_pairs={{0,4},{4,8},{8,12},{12,16},{16,20},{20,24},{24,28},{1,5},{5,9},{9,... | collective-permute-start | bytes 1179656 | tf_op jit(solution)/shard_map/ppermute | solution.py:18
  118.7 1.9 collective-permute-start.13
  120.7 1.5 collective-permute-start.14
  124.1 4.3 %collective-permute-done.12 = bf16[512,384]{1,0:T(8,128)(2,1)S(1)} collective-permute-done((bf16[512,384]{1,0:T(8,128)(2,1)S(1)}, bf16[512,384]{1,0:T(8,128)(2,1)S(1)}, u32[]{:S(2)}, u32[]{:S(2)}) %collective-permute-start.12) | collective-permute-done | bytes 393248 | tf_op jit(solution)/shard_map/ppermute | solution.py:18
  129.9 4.8 %collective-permute-done.13 = bf16[512,384]{1,0:T(8,128)(2,1)S(1)} collective-permute-done((bf16[512,384]{1,0:T(8,128)(2,1)S(1)}, bf16[512,384]{1,0:T(8,128)(2,1)S(1)}, u32[]{:S(2)}, u32[]{:S(2)}) %collective-permute-start.13) | collective-permute-done | bytes 393248 | tf_op jit(solution)/shard_map/ppermute | solution.py:18
  135.5 7.4 %collective-permute-done.14 = bf16[512,384]{1,0:T(8,128)(2,1)S(1)} collective-permute-done((bf16[512,384]{1,0:T(8,128)(2,1)S(1)}, bf16[512,384]{1,0:T(8,128)(2,1)S(1)}, u32[]{:S(2)}, u32[]{:S(2)}) %collective-permute-start.14) | collective-permute-done | bytes 393248 | tf_op jit(solution)/shard_map/ppermute | solution.py:18
  143.8 37.3 %shard_map.92 = bf16[12,128,192]{2,1,0:T(8,128)(2,1)} custom-call(s32[12]{0:T(128)} %slice.59.count, s32[12,20]{1,0:T(8,128)} %slice.82.source, s32[12,20]{1,0:T(8,128)} %slice.83.rows, bf16[12,128,192]{2,1,0:T(8,128)(2,1)} %bitcast.37, bf16[2560,384]{1,0:T(8,128)(2,1)} %copy-done.6, bf16[5120,384]{1,0:T(8,128)(2,1)} %copy-done.4, ...), custom_call_target="tpu_custom_call" | custom-call | flops 3019898880 | bytes 9830400 | tf_op jit(solution)/shard_map/pallas_call | solution.py:100
  181.0 2.0 fusion.40
  183.7 1.3 collective-permute-start.24
  185.0 1.3 bitcast_select_fusion
  188.3 15.3 %shard_map.91 = bf16[4,128,192]{2,1,0:T(8,128)(2,1)} custom-call(s32[4]{0:T(128)} %bitcast.40, s32[4,20]{1,0:T(4,128)} %slice.79.source, s32[4,20]{1,0:T(4,128)} %slice.80.rows, bf16[4,128,192]{2,1,0:T(8,128)(2,1)} %bitcast.34, bf16[2560,384]{1,0:T(8,128)(2,1)} %copy-done.6, bf16[5120,384]{1,0:T(8,128)(2,1)} %copy-done.4, ...), custom_call_target="tpu_custom_call" | custom-call | flops 1006632960 | bytes 9043968 | tf_op jit(solution)/shard_map/pallas_call | solution.py:100
  203.6 1.5 collective-permute-done.23
  205.1 2.6 %collective-permute-done.24 = bf16[512,192]{1,0:T(8,128)(2,1)} collective-permute-done((bf16[512,192]{1,0:T(8,128)(2,1)S(1)}, bf16[512,192]{1,0:T(8,128)(2,1)}, u32[]{:S(2)}, u32[]{:S(2)}) %collective-permute-start.24) | collective-permute-done | bytes 196640 | tf_op jit(solution)/shard_map/ppermute | solution.py:224
  207.7 2.9 %convolution_convert_fusion.1 = bf16[512,768]{1,0:T(8,128)(2,1)} fusion(bf16[768,768]{1,0:T(8,128)(2,1)S(1)} %copy-done.7, bf16[512,192]{1,0:T(8,128)(2,1)} %collective-permute-done.24, bf16[512,192]{1,0:T(8,128)(2,1)} %collective-permute-done.23, bf16[512,192]{1,0:T(8,128)(2,1)} %collective-permute-done.22, bf16[512,192]{1,0:T(8,128)(2,1)} %bitcast.38), kind=kOutput, calls=%fused_computation.11 | convolution fusion | flops 607518720 | bytes 2752512 | tf_op jit(solution)/shard_map/dot_general | solution.py:230
  (137 shorter events, 27.7 us)
Async XLA Ops:
  0.0 43.6 %copy-start = (bf16[768,768]{1,0:T(8,128)(2,1)S(1)}, bf16[768,768]{1,0:T(8,128)(2,1)}, u32[]{:S(2)}) copy-start(bf16[768,768]{1,0:T(8,128)(2,1)} %param.13) | copy-start | bytes 3538948
  0.0 31.5 %collective-permute-start = (bf16[512,768]{1,0:T(8,128)(2,1)}, bf16[512,768]{1,0:T(8,128)(2,1)}, u32[]{:S(2)}, u32[]{:S(2)}) collective-permute-start(bf16[512,768]{1,0:T(8,128)(2,1)} %param.11), channel_id=1, source_target_pairs={{0,3},{1,0},{2,1},{3,2},{4,7},{5,4},{6,5},{7,6},{8,11},{9,8},{10,9... | collective-permute-start | bytes 2359304 | tf_op jit(solution)/shard_map/ppermute | solution.py:153
  0.0 37.7 %collective-permute-start.1 = (bf16[512,768]{1,0:T(8,128)(2,1)}, bf16[512,768]{1,0:T(8,128)(2,1)}, u32[]{:S(2)}, u32[]{:S(2)}) collective-permute-start(bf16[512,768]{1,0:T(8,128)(2,1)} %param.11), channel_id=1, source_target_pairs={{0,1},{1,2},{2,3},{3,0},{4,5},{5,6},{6,7},{7,4},{8,9},{9,10},{10,1... | collective-permute-start | bytes 2359304 | tf_op jit(solution)/shard_map/ppermute | solution.py:153
  4.7 12.1 %copy-start.17 = (s32[16,12]{1,0:T(8,128)S(1)}, s32[16,12]{1,0:T(8,128)}, u32[]{:S(2)}) copy-start(s32[16,12]{1,0:T(8,128)} %param.14) | copy-start | bytes 2308
  4.7 12.2 %copy-start.3 = (s32[4]{0:T(128)S(1)}, s32[4]{0:T(128)}, u32[]{:S(2)}) copy-start(s32[4]{0:T(128)} %constant.195.clone) | copy-start | bytes 52
  5.0 6.0 %copy-start.11 = (bf16[768,192]{1,0:T(8,128)(2,1)}, bf16[768,192]{1,0:T(8,128)(2,1)S(1)}, u32[]{:S(2)}) copy-start(bf16[768,192]{1,0:T(8,128)(2,1)S(1)} %get-tuple-element.27) | copy-start | bytes 884740
  5.0 9.7 %copy-start.14 = (bf16[768,192]{1,0:T(8,128)(2,1)}, bf16[768,192]{1,0:T(8,128)(2,1)S(1)}, u32[]{:S(2)}) copy-start(bf16[768,192]{1,0:T(8,128)(2,1)S(1)} %get-tuple-element.28) | copy-start | bytes 884740
  7.1 37.3 %collective-permute-start.3 = (bf16[512,384]{1,0:T(8,128)(2,1)S(1)}, bf16[512,384]{1,0:T(8,128)(2,1)}, u32[]{:S(2)}, u32[]{:S(2)}) collective-permute-start(bf16[512,384]{1,0:T(8,128)(2,1)S(1)} %fusion.7), channel_id=1, source_target_pairs={{0,8},{4,12},{8,16},{12,20},{16,24},{20,28},{1,9},{5,13},{9,17},{1... | collective-permute-start | bytes 1179656 | tf_op jit(solution)/shard_map/ppermute | solution.py:18
  11.0 34.6 %collective-permute-start.4 = (bf16[512,384]{1,0:T(8,128)(2,1)S(1)}, bf16[512,384]{1,0:T(8,128)(2,1)}, u32[]{:S(2)}, u32[]{:S(2)}) collective-permute-start(bf16[512,384]{1,0:T(8,128)(2,1)S(1)} %fusion.7), channel_id=1, source_target_pairs={{0,4},{4,8},{8,12},{12,16},{16,20},{20,24},{24,28},{1,5},{5,9},{9,... | collective-permute-start | bytes 1179656 | tf_op jit(solution)/shard_map/ppermute | solution.py:18
  14.8 31.9 %collective-permute-start.5 = (bf16[512,384]{1,0:T(8,128)(2,1)S(1)}, bf16[512,384]{1,0:T(8,128)(2,1)}, u32[]{:S(2)}, u32[]{:S(2)}) collective-permute-start(bf16[512,384]{1,0:T(8,128)(2,1)S(1)} %fusion.7), channel_id=1, source_target_pairs={{4,0},{8,4},{12,8},{16,12},{20,16},{24,20},{28,24},{5,1},{9,5},{13... | collective-permute-start | bytes 1179656 | tf_op jit(solution)/shard_map/ppermute | solution.py:18
  18.5 0.7 copy-start.2
  20.7 0.7 copy-start.1
  21.4 1.7 copy-start.19
  21.4 1.9 copy-start.21
  27.3 2.6 %copy-start.9 = (bf16[512,768]{1,0:T(8,128)(2,1)S(1)}, bf16[512,768]{1,0:T(8,128)(2,1)}, u32[]{:S(2)}) copy-start(bf16[512,768]{1,0:T(8,128)(2,1)} %param.11) | copy-start | bytes 2359300
  27.3 10.4 %copy-start.12 = (bf16[768,192]{1,0:T(8,128)(2,1)S(1)}, bf16[768,192]{1,0:T(8,128)(2,1)}, u32[]{:S(2)}) copy-start(bf16[768,192]{1,0:T(8,128)(2,1)} %copy-done.11) | copy-start | bytes 884740
  27.3 10.4 %copy-start.15 = (bf16[768,192]{1,0:T(8,128)(2,1)S(1)}, bf16[768,192]{1,0:T(8,128)(2,1)}, u32[]{:S(2)}) copy-start(bf16[768,192]{1,0:T(8,128)(2,1)} %copy-done.14) | copy-start | bytes 884740
  31.5 16.3 %collective-permute-start.6 = (bf16[512,384]{1,0:T(8,128)(2,1)S(1)}, bf16[512,384]{1,0:T(8,128)(2,1)}, u32[]{:S(2)}, u32[]{:S(2)}) collective-permute-start(bf16[512,384]{1,0:T(8,128)(2,1)S(1)} %fusion.7), channel_id=1, source_target_pairs={{8,0},{12,4},{16,8},{20,12},{24,16},{28,20},{9,1},{13,5},{17,9},{2... | collective-permute-start | bytes 1179656 | tf_op jit(solution)/shard_map/ppermute | solution.py:18
  41.1 34.1 %collective-permute-start.2 = (bf16[512,768]{1,0:T(8,128)(2,1)S(1)}, bf16[512,768]{1,0:T(8,128)(2,1)}, u32[]{:S(2)}, u32[]{:S(2)}) collective-permute-start(bf16[512,768]{1,0:T(8,128)(2,1)S(1)} %copy-done.9), channel_id=1, source_target_pairs={{0,2},{1,3},{2,0},{3,1},{4,6},{5,7},{6,4},{7,5},{8,10},{9,11},{10,... | collective-permute-start | bytes 2359304 | tf_op jit(solution)/shard_map/ppermute | solution.py:153
  42.4 1.3 copy-start.20
  44.4 16.3 %copy-start.5 = (bf16[2048,768]{1,0:T(8,128)(2,1)S(1)}, bf16[2048,768]{1,0:T(8,128)(2,1)}, u32[]{:S(2)}) copy-start(bf16[2048,768]{1,0:T(8,128)(2,1)} %constant_dynamic-update-slice_fusion.3) | copy-start | bytes 9437188
  48.9 10.5 %copy-start.6 = (bf16[2560,384]{1,0:T(8,128)(2,1)}, bf16[2560,384]{1,0:T(8,128)(2,1)S(1)}, u32[]{:S(2)}) copy-start(bf16[2560,384]{1,0:T(8,128)(2,1)S(1)} %constant_dynamic-update-slice_fusion.4.refs_0_) | copy-start | bytes 5898244
  48.9 37.3 %collective-permute-start.7 = (bf16[1024,384]{1,0:T(8,128)(2,1)}, bf16[1024,384]{1,0:T(8,128)(2,1)}, u32[]{:S(2)}, u32[]{:S(2)}) collective-permute-start(bf16[1024,384]{1,0:T(8,128)(2,1)} %fusion.4), channel_id=1, source_target_pairs={{0,8},{4,12},{8,16},{12,20},{16,24},{20,28},{1,9},{5,13},{9,17},{1... | collective-permute-start | bytes 2359304 | tf_op jit(solution)/shard_map/ppermute | solution.py:18
  53.0 36.6 %collective-permute-start.8 = (bf16[1024,384]{1,0:T(8,128)(2,1)}, bf16[1024,384]{1,0:T(8,128)(2,1)}, u32[]{:S(2)}, u32[]{:S(2)}) collective-permute-start(bf16[1024,384]{1,0:T(8,128)(2,1)} %fusion.4), channel_id=1, source_target_pairs={{0,4},{4,8},{8,12},{12,16},{16,20},{20,24},{24,28},{1,5},{5,9},{9,... | collective-permute-start | bytes 2359304 | tf_op jit(solution)/shard_map/ppermute | solution.py:18
  57.5 35.1 %collective-permute-start.9 = (bf16[1024,384]{1,0:T(8,128)(2,1)}, bf16[1024,384]{1,0:T(8,128)(2,1)}, u32[]{:S(2)}, u32[]{:S(2)}) collective-permute-start(bf16[1024,384]{1,0:T(8,128)(2,1)} %fusion.4), channel_id=1, source_target_pairs={{4,0},{8,4},{12,8},{16,12},{20,16},{24,20},{28,24},{5,1},{9,5},{13... | collective-permute-start | bytes 2359304 | tf_op jit(solution)/shard_map/ppermute | solution.py:18
  59.4 45.1 %collective-permute-start.10 = (bf16[1024,384]{1,0:T(8,128)(2,1)}, bf16[1024,384]{1,0:T(8,128)(2,1)}, u32[]{:S(2)}, u32[]{:S(2)}) collective-permute-start(bf16[1024,384]{1,0:T(8,128)(2,1)} %fusion.4), channel_id=1, source_target_pairs={{8,0},{12,4},{16,8},{20,12},{24,16},{28,20},{9,1},{13,5},{17,9},{2... | collective-permute-start | bytes 2359304 | tf_op jit(solution)/shard_map/ppermute | solution.py:18
  61.9 15.6 %copy-start.13 = (bf16[768,192]{1,0:T(8,128)(2,1)S(1)}, bf16[768,192]{1,0:T(8,128)(2,1)}, u32[]{:S(2)}) copy-start(bf16[768,192]{1,0:T(8,128)(2,1)} %copy-done.11) | copy-start | bytes 884740
  61.9 15.6 %copy-start.16 = (bf16[768,192]{1,0:T(8,128)(2,1)S(1)}, bf16[768,192]{1,0:T(8,128)(2,1)}, u32[]{:S(2)}) copy-start(bf16[768,192]{1,0:T(8,128)(2,1)} %copy-done.14) | copy-start | bytes 884740
  78.5 30.6 %collective-permute-start.15 = (bf16[1,128,384]{2,1,0:T(8,128)(2,1)}, bf16[1,128,384]{2,1,0:T(8,128)(2,1)}, u32[]{:S(2)}, u32[]{:S(2)}) collective-permute-start(bf16[1,128,384]{2,1,0:T(8,128)(2,1)} %fusion.8), channel_id=1, source_target_pairs={{0,28},{4,0},{8,4},{12,8},{16,12},{20,16},{24,20},{28,24},{1,29},{... | collective-permute-start | bytes 294920 | tf_op jit(solution)/shard_map/ppermute | solution.py:26
  86.2 6.2 %copy-start.10 = (bf16[1024,384]{1,0:T(8,128)(2,1)S(1)}, bf16[1024,384]{1,0:T(8,128)(2,1)}, u32[]{:S(2)}) copy-start(bf16[1024,384]{1,0:T(8,128)(2,1)} %fusion.4) | copy-start | bytes 2359300
  86.2 24.3 %collective-permute-start.16 = (bf16[1,128,384]{2,1,0:T(8,128)(2,1)}, bf16[1,128,384]{2,1,0:T(8,128)(2,1)S(1)}, u32[]{:S(2)}, u32[]{:S(2)}) collective-permute-start(bf16[1,128,384]{2,1,0:T(8,128)(2,1)} %fusion.8), channel_id=1, source_target_pairs={{0,24},{4,28},{8,0},{12,4},{16,8},{20,12},{24,16},{28,20},{1,25},{... | collective-permute-start | bytes 294920 | tf_op jit(solution)/shard_map/ppermute | solution.py:26
  89.6 21.9 %collective-permute-start.17 = (bf16[1,128,384]{2,1,0:T(8,128)(2,1)}, bf16[1,128,384]{2,1,0:T(8,128)(2,1)S(1)}, u32[]{:S(2)}, u32[]{:S(2)}) collective-permute-start(bf16[1,128,384]{2,1,0:T(8,128)(2,1)} %fusion.8), channel_id=1, source_target_pairs={{0,20},{4,24},{8,28},{12,0},{16,4},{20,8},{24,12},{28,16},{1,21},{... | collective-permute-start | bytes 294920 | tf_op jit(solution)/shard_map/ppermute | solution.py:26
  92.6 22.7 %collective-permute-start.18 = (bf16[1,128,384]{2,1,0:T(8,128)(2,1)}, bf16[1,128,384]{2,1,0:T(8,128)(2,1)S(1)}, u32[]{:S(2)}, u32[]{:S(2)}) collective-permute-start(bf16[1,128,384]{2,1,0:T(8,128)(2,1)} %fusion.8), channel_id=1, source_target_pairs={{0,16},{4,20},{8,24},{12,28},{16,0},{20,4},{24,8},{28,12},{1,17},{... | collective-permute-start | bytes 294920 | tf_op jit(solution)/shard_map/ppermute | solution.py:26
  104.6 14.2 %collective-permute-start.19 = (bf16[1,128,384]{2,1,0:T(8,128)(2,1)}, bf16[1,128,384]{2,1,0:T(8,128)(2,1)S(1)}, u32[]{:S(2)}, u32[]{:S(2)}) collective-permute-start(bf16[1,128,384]{2,1,0:T(8,128)(2,1)} %fusion.8), channel_id=1, source_target_pairs={{0,12},{4,16},{8,20},{12,24},{16,28},{20,0},{24,4},{28,8},{1,13},{... | collective-permute-start | bytes 294920 | tf_op jit(solution)/shard_map/ppermute | solution.py:26
  108.3 27.2 %copy-start.4 = (bf16[5120,384]{1,0:T(8,128)(2,1)}, bf16[5120,384]{1,0:T(8,128)(2,1)S(1)}, u32[]{:S(2)}) copy-start(bf16[5120,384]{1,0:T(8,128)(2,1)S(1)} %constant_dynamic-update-slice_fusion.9.refs_1_) | copy-start | bytes 11796484
  109.1 11.5 %collective-permute-start.20 = (bf16[1,128,384]{2,1,0:T(8,128)(2,1)}, bf16[1,128,384]{2,1,0:T(8,128)(2,1)S(1)}, u32[]{:S(2)}, u32[]{:S(2)}) collective-permute-start(bf16[1,128,384]{2,1,0:T(8,128)(2,1)} %fusion.8), channel_id=1, source_target_pairs={{0,8},{4,12},{8,16},{12,20},{16,24},{20,28},{24,0},{28,4},{1,9},{5... | collective-permute-start | bytes 294920 | tf_op jit(solution)/shard_map/ppermute | solution.py:26
  110.5 11.7 %collective-permute-start.21 = (bf16[1,128,384]{2,1,0:T(8,128)(2,1)}, bf16[1,128,384]{2,1,0:T(8,128)(2,1)S(1)}, u32[]{:S(2)}, u32[]{:S(2)}) collective-permute-start(bf16[1,128,384]{2,1,0:T(8,128)(2,1)} %fusion.8), channel_id=1, source_target_pairs={{0,4},{4,8},{8,12},{12,16},{16,20},{20,24},{24,28},{28,0},{1,5},{5... | collective-permute-start | bytes 294920 | tf_op jit(solution)/shard_map/ppermute | solution.py:26
  111.5 11.7 %collective-permute-start.11 = (bf16[512,384]{1,0:T(8,128)(2,1)S(1)}, bf16[512,384]{1,0:T(8,128)(2,1)S(1)}, u32[]{:S(2)}, u32[]{:S(2)}) collective-permute-start(bf16[512,384]{1,0:T(8,128)(2,1)S(1)} %convolution_convert_fusion.3), channel_id=1, source_target_pairs={{0,8},{4,12},{8,16},{12,20},{16,24},{20,28},{1,9},{5,13},{9,17},{1... | collective-permute-start | bytes 1179656 | tf_op jit(solution)/shard_map/ppermute | solution.py:18
  115.3 13.1 %collective-permute-start.12 = (bf16[512,384]{1,0:T(8,128)(2,1)S(1)}, bf16[512,384]{1,0:T(8,128)(2,1)S(1)}, u32[]{:S(2)}, u32[]{:S(2)}) collective-permute-start(bf16[512,384]{1,0:T(8,128)(2,1)S(1)} %convolution_convert_fusion.3), channel_id=1, source_target_pairs={{0,4},{4,8},{8,12},{12,16},{16,20},{20,24},{24,28},{1,5},{5,9},{9,... | collective-permute-start | bytes 1179656 | tf_op jit(solution)/shard_map/ppermute | solution.py:18
  118.7 16.0 %collective-permute-start.13 = (bf16[512,384]{1,0:T(8,128)(2,1)S(1)}, bf16[512,384]{1,0:T(8,128)(2,1)S(1)}, u32[]{:S(2)}, u32[]{:S(2)}) collective-permute-start(bf16[512,384]{1,0:T(8,128)(2,1)S(1)} %convolution_convert_fusion.3), channel_id=1, source_target_pairs={{4,0},{8,4},{12,8},{16,12},{20,16},{24,20},{28,24},{5,1},{9,5},{13... | collective-permute-start | bytes 1179656 | tf_op jit(solution)/shard_map/ppermute | solution.py:18
  120.7 22.2 %collective-permute-start.14 = (bf16[512,384]{1,0:T(8,128)(2,1)S(1)}, bf16[512,384]{1,0:T(8,128)(2,1)S(1)}, u32[]{:S(2)}, u32[]{:S(2)}) collective-permute-start(bf16[512,384]{1,0:T(8,128)(2,1)S(1)} %convolution_convert_fusion.3), channel_id=1, source_target_pairs={{8,0},{12,4},{16,8},{20,12},{24,16},{28,20},{9,1},{13,5},{17,9},{2... | collective-permute-start | bytes 1179656 | tf_op jit(solution)/shard_map/ppermute | solution.py:18
  123.1 20.6 %copy-start.8 = (bf16[8,128,384]{2,1,0:T(8,128)(2,1)}, bf16[8,128,384]{2,1,0:T(8,128)(2,1)S(1)}, u32[]{:S(2)}) copy-start(bf16[8,128,384]{2,1,0:T(8,128)(2,1)S(1)} %constant_dynamic-update-slice_fusion.19) | copy-start | bytes 2359300
  143.8 41.2 %copy-start.18 = (pred[768]{0:T(1024)(128)(4,1)S(1)}, pred[768]{0:T(1024)(128)(4,1)}, u32[]{:S(2)}) copy-start(pred[768]{0:T(1024)(128)(4,1)} %broadcast_in_dim.36) | copy-start | bytes 2308
  183.0 20.6 %collective-permute-start.22 = (bf16[512,192]{1,0:T(8,128)(2,1)}, bf16[512,192]{1,0:T(8,128)(2,1)}, u32[]{:S(2)}, u32[]{:S(2)}) collective-permute-start(bf16[512,192]{1,0:T(8,128)(2,1)} %bitcast.11), channel_id=1, source_target_pairs={{0,1},{1,2},{2,3},{3,0},{4,5},{5,6},{6,7},{7,4},{8,9},{9,10},{10,1... | collective-permute-start | bytes 589832 | tf_op jit(solution)/shard_map/ppermute | solution.py:224
  183.0 22.1 %collective-permute-start.23 = (bf16[512,192]{1,0:T(8,128)(2,1)}, bf16[512,192]{1,0:T(8,128)(2,1)}, u32[]{:S(2)}, u32[]{:S(2)}) collective-permute-start(bf16[512,192]{1,0:T(8,128)(2,1)} %bitcast.12), channel_id=1, source_target_pairs={{0,2},{1,3},{2,0},{3,1},{4,6},{5,7},{6,4},{7,5},{8,10},{9,11},{10,... | collective-permute-start | bytes 589832 | tf_op jit(solution)/shard_map/ppermute | solution.py:224
  183.7 24.0 %collective-permute-start.24 = (bf16[512,192]{1,0:T(8,128)(2,1)S(1)}, bf16[512,192]{1,0:T(8,128)(2,1)}, u32[]{:S(2)}, u32[]{:S(2)}) collective-permute-start(bf16[512,192]{1,0:T(8,128)(2,1)S(1)} %bitcast.39), channel_id=1, source_target_pairs={{0,3},{1,0},{2,1},{3,2},{4,7},{5,4},{6,5},{7,6},{8,11},{9,8},{10,9... | collective-permute-start | bytes 589832 | tf_op jit(solution)/shard_map/ppermute | solution.py:224
  188.3 19.4 %copy-start.7 = (bf16[768,768]{1,0:T(8,128)(2,1)S(1)}, bf16[768,768]{1,0:T(8,128)(2,1)}, u32[]{:S(2)}) copy-start(bf16[768,768]{1,0:T(8,128)(2,1)} %bitcast_select_fusion) | copy-start | bytes 3538948
